TPU v7x, 512 devices: a whole 4x4x16 slice. The times are simulated.
512 devices in a mesh: group: 4 (over z_hi), shard: 16 (over z_lo, y), tensor: 8 (over x, core).
Axes of the slice: x: 4, y: 4, z: 16 (z_hi: 4, z_lo: 4; z = z_hi * 4 + z_lo), core: 2. Of those that a mesh axis runs over, the one named last changes fastest.
Arguments:
- layer_delta: bfloat16 [4, 2, 4, 224, 4864], P('group', None, None, 'shard', 'tensor'), may hold values from -6 to 6
- emb_left: bfloat16 [4, 4, 19200, 64], P('group', None, ('shard', 'tensor')), may hold values from -6 to 6
- emb_right: bfloat16 [4, 64, 896], P('group'), may hold values from -0.75 to 0.75
- layer_weight: float32 [2, 896, 4864], P(None, ('group', 'shard'), 'tensor'), may hold values from -6 to 6
- layer_momentum: float32 [2, 896, 4864], P(None, ('group', 'shard'), 'tensor'), may hold values from -4 to 4
- emb_weight: float32 [76800, 896], P(('group', 'shard', 'tensor')), may hold values from -6 to 6
- emb_momentum: float32 [76800, 896], P(('group', 'shard', 'tensor')), may hold values from -4 to 4
Outputs:
- new_layer_weight: float32 [2, 896, 4864], P(None, ('group', 'shard'), 'tensor')
- new_layer_momentum: float32 [2, 896, 4864], P(None, ('group', 'shard'), 'tensor')
- layer_blocks: bfloat16 [2, 896, 4864], P(None, None, 'tensor')
- new_emb_weight: float32 [76800, 896], P(('group', 'shard', 'tensor'))
- new_emb_momentum: float32 [76800, 896], P(('group', 'shard', 'tensor'))
All inputs are finite; a program needn't handle non-finite values.
Results may differ from a plain program's by a relative error of at most 0.0095.
Values may be sent and summed in bfloat16 or wider, within the bound.
No kernel may reach another device: no remote copies, remote signals or barrier semaphores. Data moves between devices by JAX's collectives and lax.ppermute only.
A program may use at most 64 MiB of HBM per device.

v0:
```python
import jax
import jax.numpy as jnp
from jax import lax
from jax.sharding import PartitionSpec as P

rate_outer = 0.7
beta_outer = 0.9


def on_device(
    layer_delta, emb_left, emb_right, layer_weight, layer_momentum, emb_weight, emb_momentum
):
    groups = lax.axis_size("group")
    summed = lax.psum_scatter(
        layer_delta.astype(jnp.float32).astype(jnp.bfloat16),
        "group",
        scatter_dimension=2,
        tiled=True,
    ).astype(jnp.float32)
    layer_mean = summed.reshape(layer_weight.shape) / groups
    new_layer_momentum = beta_outer * layer_momentum + layer_mean
    new_layer_weight = layer_weight - rate_outer * (layer_mean + beta_outer * new_layer_momentum)
    pieces = new_layer_weight.astype(jnp.bfloat16)
    layer_blocks = lax.all_gather(pieces, ("group", "shard"), axis=1, tiled=True)
    terms = jnp.einsum("qnr,rd->qnd", emb_left[0], emb_right[0], preferred_element_type=jnp.float32)
    total = lax.psum_scatter(
        terms.astype(jnp.bfloat16), "group", scatter_dimension=0, tiled=True
    ).astype(jnp.float32)[0]
    emb_mean = total / groups
    new_emb_momentum = beta_outer * emb_momentum + emb_mean
    new_emb_weight = emb_weight - rate_outer * (emb_mean + beta_outer * new_emb_momentum)
    return (new_layer_weight, new_layer_momentum, layer_blocks, new_emb_weight, new_emb_momentum)


def solution(mesh):
    placed = (
        P("group", None, None, "shard", "tensor"),
        P("group", None, ("shard", "tensor"), None),
        P("group", None, None),
        P(None, ("group", "shard"), "tensor"),
        P(None, ("group", "shard"), "tensor"),
        P(("group", "shard", "tensor"), None),
        P(("group", "shard", "tensor"), None),
    )
    return jax.shard_map(
        on_device,
        mesh=mesh,
        in_specs=placed,
        out_specs=(
            P(None, ("group", "shard"), "tensor"),
            P(None, ("group", "shard"), "tensor"),
            P(None, None, "tensor"),
            P(("group", "shard", "tensor"), None),
            P(("group", "shard", "tensor"), None),
        ),
        check_vma=False,
    )
```

profile of v0, /device:TPU:6, one launch (start us, length us, event | category | flops | bytes accessed | tf_op | source)
XLA Modules:
  0.0 299.9 jit_solution(9431584884943056190)
XLA Ops:
  7.2 0.0 copy-start
  7.2 0.0 copy-start.4
  7.2 0.0 copy-start.3
  7.2 0.0 copy-start.2
  7.2 0.0 copy-start.1
  7.2 0.0 all-reduce.4.cloned.1.call-start
  7.3 1.8 copy.14
  9.0 0.0 all-reduce.4.cloned.1.call-update
  9.1 0.0 reduce-scatter.5.cloned.1.call-start
  9.1 0.0 copy-done
  9.1 2.4 convolution_convert_fusion
  11.5 0.0 reduce-scatter.5.cloned.1.call-update
  11.5 0.0 all-gather.2.cloned.1.call-start
  11.6 1.3 dynamic-slice
  12.9 70.7 %all-reduce.4.cloned.1.call-done = bf16[1,2,4,14,608]{4,1,3,2,0:T(2,128)(2,1)} async-done(((bf16[1,2,4,14,608]{4,1,3,2,0:T(2,128)(2,1)}), bf16[1,2,4,14,608]{4,1,3,2,0:T(2,128)(2,1)}) %all-reduce.4.cloned.1.call-update) | async-done | bytes 136208
  83.6 0.0 copy-done.4
  83.6 0.0 copy-done.3
  83.6 2.2 fusion.6
  85.8 0.0 all-gather.2.cloned.1.call-update
  85.8 60.7 %reduce-scatter.5.cloned.1.call-done = bf16[1,150,896]{2,1,0:T(8,128)(2,1)} async-done(((bf16[4,150,896]{2,1,0:T(8,128)(2,1)}), bf16[1,150,896]{2,1,0:T(8,128)(2,1)}) %reduce-scatter.5.cloned.1.call-update) | async-done | bytes 268816
  146.5 0.0 copy-done.2
  146.5 0.0 copy-done.1
  146.5 2.1 fusion.1
  148.6 137.4 %all-gather.2.cloned.1.call-done = bf16[2,896,608]{2,0,1:T(2,128)(2,1)} async-done(((bf16[2,14,608]{2,0,1:T(2,128)(2,1)}), bf16[2,896,608]{2,0,1:T(2,128)(2,1)}) %all-gather.2.cloned.1.call-update) | async-done | bytes 2179088 | tf_op jit(solution)/shard_map/all_gather | solution.py:24
  286.0 7.3 %copy.15 = bf16[2,896,608]{1,2,0:T(8,128)(2,1)} copy(bf16[2,896,608]{2,0,1:T(2,128)(2,1)} %all-gather.2.cloned.1.call-done) | data formatting | bytes 4358144
Async XLA Ops:
  7.2 2.0 copy-start
  7.2 76.4 %copy-start.4 = (f32[2,14,608]{2,0,1:T(2,128)S(1)}, f32[2,14,608]{2,0,1:T(2,128)}, u32[]{:S(2)}) copy-start(f32[2,14,608]{2,0,1:T(2,128)} %param.11) | copy-start | bytes 204292
  7.2 76.4 %copy-start.3 = (f32[2,14,608]{2,0,1:T(2,128)S(1)}, f32[2,14,608]{2,0,1:T(2,128)}, u32[]{:S(2)}) copy-start(f32[2,14,608]{2,0,1:T(2,128)} %param.10) | copy-start | bytes 204292
  7.2 139.3 %copy-start.2 = (f32[150,896]{1,0:T(8,128)S(1)}, f32[150,896]{1,0:T(8,128)}, u32[]{:S(2)}) copy-start(f32[150,896]{1,0:T(8,128)} %param.13) | copy-start | bytes 1612804
  7.2 139.3 %copy-start.1 = (f32[150,896]{1,0:T(8,128)S(1)}, f32[150,896]{1,0:T(8,128)}, u32[]{:S(2)}) copy-start(f32[150,896]{1,0:T(8,128)} %param.12) | copy-start | bytes 1612804
  7.2 76.3 %all-reduce.4.cloned.1.call-start = ((), (), s32[]{:S(2)}) async-start(), calls=%async_computation.2 | async-start | bytes 286720
  9.1 137.4 %reduce-scatter.5.cloned.1.call-start = ((), (), s32[]{:S(2)}) async-start(), calls=%async_computation.3 | async-start | bytes 1361920
  11.5 274.5 %all-gather.2.cloned.1.call-start = ((), (), s32[]{:S(2)}) async-start(), calls=%async_computation.1 | async-start | bytes 2329600 | tf_op jit(solution)/shard_map/all_gather | solution.py:24
Sparse Core Ops, SparseCore 0:
  11.5 71.9 all-reduce.3
  87.0 59.4 reduce-scatter.4
  149.5 136.5 all-gather.1
where the time goes:
time: 300 us
  waiting for transfers between devices  269 us (90%)
  between operations  13.8 us (5%)
  local copies, waits for them, and re-layouts  10.4 us (3%)
  other arithmetic  4.27 us (1%)
    all_gather x1, waiting for transfers between devices, on_device(): lax.all_gather(pieces, ('group', 'shard'), axis=1, tiled=True)  137 us
    unnamed x5, waiting for transfers between devices  131 us
    unnamed x13, local copies, waits for them, and re-layouts  10.4 us
  transfers between devices with their start and end apart: 3, of which 3 were waited for; matrix products, arithmetic and copies ran while one was open for 3% of the time, Pallas kernels for 0%

commit v1 on v0

--- a/solution.py
+++ b/solution.py
@@ -6,26 +6,92 @@
 rate_outer = 0.7
 beta_outer = 0.9
 
+Y_SIZE = 4
+
+
+def shift_pairs(n, k):
+    return [(i, (i + k) % n) for i in range(n)]
+
 
 def on_device(
     layer_delta, emb_left, emb_right, layer_weight, layer_momentum, emb_weight, emb_momentum
 ):
+    f32 = jnp.float32
     groups = lax.axis_size("group")
-    summed = lax.psum_scatter(
-        layer_delta.astype(jnp.float32).astype(jnp.bfloat16),
-        "group",
-        scatter_dimension=2,
-        tiled=True,
-    ).astype(jnp.float32)
-    layer_mean = summed.reshape(layer_weight.shape) / groups
+    shards = lax.axis_size("shard")
+    tensors = lax.axis_size("tensor")
+    gi = lax.axis_index("group")
+    si = lax.axis_index("shard")
+    ti = lax.axis_index("tensor")
+
+    delta = layer_delta[0]
+    acc = lax.dynamic_index_in_dim(delta, gi, axis=1, keepdims=False).astype(f32)
+    for k in range(1, groups):
+        piece = lax.dynamic_index_in_dim(delta, (gi + k) % groups, axis=1, keepdims=False)
+        acc = acc + lax.ppermute(piece, "group", shift_pairs(groups, k)).astype(f32)
+    layer_mean = acc.reshape(layer_weight.shape) / groups
     new_layer_momentum = beta_outer * layer_momentum + layer_mean
     new_layer_weight = layer_weight - rate_outer * (layer_mean + beta_outer * new_layer_momentum)
-    pieces = new_layer_weight.astype(jnp.bfloat16)
-    layer_blocks = lax.all_gather(pieces, ("group", "shard"), axis=1, tiled=True)
-    terms = jnp.einsum("qnr,rd->qnd", emb_left[0], emb_right[0], preferred_element_type=jnp.float32)
-    total = lax.psum_scatter(
-        terms.astype(jnp.bfloat16), "group", scatter_dimension=0, tiled=True
-    ).astype(jnp.float32)[0]
+    piece = new_layer_weight.astype(jnp.bfloat16)
+    rows = piece.shape[1]
+
+    yi = si % Y_SIZE
+    ybase = si - yi
+    yblk = jnp.zeros((piece.shape[0], Y_SIZE * rows, piece.shape[2]), piece.dtype)
+    yblk = lax.dynamic_update_slice_in_dim(yblk, piece, yi * rows, axis=1)
+    for k in range(1, Y_SIZE):
+        pairs = [(s, (s - s % Y_SIZE) + (s % Y_SIZE + k) % Y_SIZE) for s in range(shards)]
+        got = lax.ppermute(piece, "shard", pairs)
+        yblk = lax.dynamic_update_slice_in_dim(yblk, got, ((yi - k) % Y_SIZE) * rows, axis=1)
+
+    zlo_size = shards // Y_SIZE
+    nz = groups * zlo_size
+    zi = gi * zlo_size + si // Y_SIZE
+    brows = Y_SIZE * rows
+    n_all = groups * shards
+
+    def zshift(k):
+        pairs = []
+        for idx in range(n_all):
+            z, y = idx // Y_SIZE, idx % Y_SIZE
+            pairs.append((idx, ((z + k) % nz) * Y_SIZE + y))
+        return pairs
+
+    out = jnp.zeros((piece.shape[0], nz * brows, piece.shape[2]), piece.dtype)
+    out = lax.dynamic_update_slice_in_dim(out, yblk, zi * brows, axis=1)
+    fwd = yblk
+    bwd = yblk
+    for step in range(1, nz // 2 + 1):
+        fwd = lax.ppermute(fwd, ("group", "shard"), zshift(1))
+        out = lax.dynamic_update_slice_in_dim(out, fwd, ((zi - step) % nz) * brows, axis=1)
+        if step < nz - nz // 2:
+            bwd = lax.ppermute(bwd, ("group", "shard"), zshift(-1))
+            out = lax.dynamic_update_slice_in_dim(out, bwd, ((zi + step) % nz) * brows, axis=1)
+    layer_blocks = out
+
+    left = emb_left[0]
+    right = emb_right[0]
+    width = right.shape[1]
+    chunk = width // tensors
+    lefts = [None] * groups
+    rights = [None] * groups
+    lefts[0] = lax.dynamic_index_in_dim(left, gi, axis=0, keepdims=False)
+    rchunk = lax.dynamic_slice_in_dim(right, ti * chunk, chunk, axis=1)
+    rights[0] = rchunk
+    for k in range(1, groups):
+        lp = lax.dynamic_index_in_dim(left, (gi + k) % groups, axis=0, keepdims=False)
+        lefts[k] = lax.ppermute(lp, "group", shift_pairs(groups, k))
+        rights[k] = lax.ppermute(rchunk, "group", shift_pairs(groups, k))
+    rstack = jnp.stack(rights, axis=0)
+    full = jnp.zeros((groups, right.shape[0], width), right.dtype)
+    full = lax.dynamic_update_slice_in_dim(full, rstack, ti * chunk, axis=2)
+    for k in range(1, tensors):
+        got = lax.ppermute(rstack, "tensor", shift_pairs(tensors, k))
+        full = lax.dynamic_update_slice_in_dim(full, got, ((ti - k) % tensors) * chunk, axis=2)
+    total = jnp.zeros(emb_weight.shape, f32)
+    for k in range(groups):
+        product = jnp.dot(lefts[k], full[k], preferred_element_type=f32).astype(jnp.bfloat16)
+        total = total + product.astype(f32)
     emb_mean = total / groups
     new_emb_momentum = beta_outer * emb_momentum + emb_mean
     new_emb_weight = emb_weight - rate_outer * (emb_mean + beta_outer * new_emb_momentum)

time: 300 us -> 286 us (0.953)
  the two profiles are of different devices: /device:TPU:6 before, /device:TPU:16 now
where the time goes in v1:
time: 286 us; the launch traced here: 282 us
  starting transfers between devices  141 us (49%)
  local copies, waits for them, and re-layouts  114 us (40%)
  waiting for transfers between devices  20 us (7%)
  matrix products  2.88 us (1%)
    dynamic_update_slice x8, local copies, waits for them, and re-layouts, on_device(): lax.dynamic_update_slice_in_dim(out, fwd, (zi - step) % nz * brows, axis=1)  43.6 us
    dynamic_update_slice x7, local copies, waits for them, and re-layouts, on_device(): lax.dynamic_update_slice_in_dim(out, bwd, (zi + step) % nz * brows, axis=1)  38.1 us
    ppermute x7, starting transfers between devices, on_device(): bwd = lax.ppermute(bwd, ('group', 'shard'), zshift(-1))  37.4 us
    ppermute x3, starting transfers between devices, on_device(): acc = acc + lax.ppermute(piece, 'group', shift_pairs(groups, k)).astype(f32)  25.5 us
    ppermute x3, starting transfers between devices, on_device(): lefts[k] = lax.ppermute(lp, 'group', shift_pairs(groups, k))  18.3 us
    ppermute x7, starting transfers between devices, on_device(): got = lax.ppermute(rstack, 'tensor', shift_pairs(tensors, k))  18.1 us
    ppermute x3, starting transfers between devices, on_device(): rights[k] = lax.ppermute(rchunk, 'group', shift_pairs(groups, k))  17.4 us
    ppermute x8, starting transfers between devices, on_device(): fwd = lax.ppermute(fwd, ('group', 'shard'), zshift(1))  15.5 us
  transfers between devices with their start and end apart: 34, of which 7 were waited for; matrix products, arithmetic and copies ran while one was open for 37% of the time, Pallas kernels for 0%

profile of v1, /device:TPU:16, one launch (start us, length us, event | category | flops | bytes accessed | tf_op | source)
XLA Modules:
  0.0 282.0 jit_solution(1907489874421819573)
XLA Ops:
  2.3 12.7 %collective-permute-start.2 = (bf16[2,14,608]{2,0,1:T(2,128)(2,1)S(1)}, bf16[2,14,608]{2,0,1:T(2,128)(2,1)S(1)}, u32[]{:S(2)}, u32[]{:S(2)}) collective-permute-start(bf16[2,14,608]{2,0,1:T(2,128)(2,1)S(1)} %bitcast.50), channel_id=1, source_target_pairs={{0,384},{128,0},{256,128},{384,256},{1,385},{129,1},{257,129},{385... | collective-permute-start | bytes 102152 | tf_op jit(solution)/shard_map/ppermute | solution.py:31
  15.1 4.9 %collective-permute-start.1 = (bf16[2,14,608]{2,0,1:T(2,128)(2,1)S(1)}, bf16[2,14,608]{2,0,1:T(2,128)(2,1)S(1)}, u32[]{:S(2)}, u32[]{:S(2)}) collective-permute-start(bf16[2,14,608]{2,0,1:T(2,128)(2,1)S(1)} %bitcast.51), channel_id=1, source_target_pairs={{0,256},{128,384},{256,0},{384,128},{1,257},{129,385},{257,1},{385... | collective-permute-start | bytes 102152 | tf_op jit(solution)/shard_map/ppermute | solution.py:31
  20.0 7.8 %collective-permute-start = (bf16[2,14,608]{2,0,1:T(2,128)(2,1)S(1)}, bf16[2,14,608]{2,0,1:T(2,128)(2,1)S(1)}, u32[]{:S(2)}, u32[]{:S(2)}) collective-permute-start(bf16[2,14,608]{2,0,1:T(2,128)(2,1)S(1)} %bitcast.52), channel_id=1, source_target_pairs={{0,128},{128,256},{256,384},{384,0},{1,129},{129,257},{257,385},{3... | collective-permute-start | bytes 102152 | tf_op jit(solution)/shard_map/ppermute | solution.py:31
  27.9 2.0 collective-permute-done.1
  31.5 1.7 multiply_subtract_fusion.1
  33.4 3.2 %collective-permute-start.3 = (bf16[2,14,608]{1,2,0:T(8,128)(2,1)S(1)}, bf16[2,14,608]{1,2,0:T(8,128)(2,1)S(1)}, u32[]{:S(2)}, u32[]{:S(2)}) collective-permute-start(bf16[2,14,608]{1,2,0:T(8,128)(2,1)S(1)} %copy.16), channel_id=1, source_target_pairs={{0,8},{8,16},{16,24},{24,0},{32,40},{40,48},{48,56},{56,32},{64,72... | collective-permute-start | bytes 102152 | tf_op jit(solution)/shard_map/ppermute | solution.py:44
  36.6 2.5 collective-permute-start.4
  39.2 3.4 %collective-permute-start.5 = (bf16[2,14,608]{1,2,0:T(8,128)(2,1)S(1)}, bf16[2,14,608]{1,2,0:T(8,128)(2,1)S(1)}, u32[]{:S(2)}, u32[]{:S(2)}) collective-permute-start(bf16[2,14,608]{1,2,0:T(8,128)(2,1)S(1)} %copy.16), channel_id=1, source_target_pairs={{0,24},{8,0},{16,8},{24,16},{32,56},{40,32},{48,40},{56,48},{64,88... | collective-permute-start | bytes 102152 | tf_op jit(solution)/shard_map/ppermute | solution.py:44
  42.7 4.0 %dynamic_update_slice.84 = bf16[2,56,608]{1,2,0:T(8,128)(2,1)S(1)} dynamic-update-slice(bf16[2,56,608]{1,2,0:T(8,128)(2,1)S(1)} %broadcast_in_dim.10, bf16[2,14,608]{1,2,0:T(8,128)(2,1)S(1)} %copy.16, s32[]{:T(128)} %constant.225.clone.1, s32[]{:T(128)S(6)} %select_n.240, s32[]{:T(128)} %constant.225.clone.1) | dynamic-update-slice | bytes 68100 | tf_op jit(solution)/shard_map/dynamic_update_slice | solution.py:41
  46.7 4.4 %collective-permute-done.3 = bf16[2,14,608]{1,2,0:T(8,128)(2,1)S(1)} collective-permute-done((bf16[2,14,608]{1,2,0:T(8,128)(2,1)S(1)}, bf16[2,14,608]{1,2,0:T(8,128)(2,1)S(1)}, u32[]{:S(2)}, u32[]{:S(2)}) %collective-permute-start.3) | collective-permute-done | bytes 34080 | tf_op jit(solution)/shard_map/ppermute | solution.py:44
  51.1 4.0 %dynamic_update_slice.85 = bf16[2,56,608]{1,2,0:T(8,128)(2,1)S(1)} dynamic-update-slice(bf16[2,56,608]{1,2,0:T(8,128)(2,1)S(1)} %dynamic_update_slice.84, bf16[2,14,608]{1,2,0:T(8,128)(2,1)S(1)} %collective-permute-done.3, s32[]{:T(128)} %constant.225.clone.1, s32[]{:T(128)S(6)} %select_n.242, s32[]{:T(128)} %constant.225.clone.1) | dynamic-update-slice | bytes 68100 | tf_op jit(solution)/shard_map/dynamic_update_slice | solution.py:45
  55.1 2.4 dynamic_update_slice.86
  57.5 4.0 %dynamic_update_slice.87 = bf16[2,56,608]{1,2,0:T(8,128)(2,1)S(1)} dynamic-update-slice(bf16[2,56,608]{1,2,0:T(8,128)(2,1)S(1)} %dynamic_update_slice.86, bf16[2,14,608]{1,2,0:T(8,128)(2,1)S(1)} %collective-permute-done.5, s32[]{:T(128)} %constant.225.clone.1, s32[]{:T(128)S(6)} %select_n.246, s32[]{:T(128)} %constant.225.clone.1) | dynamic-update-slice | bytes 68100 | tf_op jit(solution)/shard_map/dynamic_update_slice | solution.py:45
  61.6 1.9 collective-permute-start.6
  63.5 5.1 %collective-permute-start.7 = (bf16[2,56,608]{1,2,0:T(8,128)(2,1)S(1)}, bf16[2,56,608]{1,2,0:T(8,128)(2,1)S(1)}, u32[]{:S(2)}, u32[]{:S(2)}) collective-permute-start(bf16[2,56,608]{1,2,0:T(8,128)(2,1)S(1)} %dynamic_update_slice.87), channel_id=1, source_target_pairs={{0,480},{8,488},{16,496},{24,504},{32,0},{40,8},{48,16},{56,24},{6... | collective-permute-start | bytes 408584 | tf_op jit(solution)/shard_map/ppermute | solution.py:68
  68.6 2.9 %collective-permute-done.6 = bf16[2,56,608]{1,2,0:T(8,128)(2,1)S(1)} collective-permute-done((bf16[2,56,608]{1,2,0:T(8,128)(2,1)S(1)}, bf16[2,56,608]{1,2,0:T(8,128)(2,1)S(1)}, u32[]{:S(2)}, u32[]{:S(2)}) %collective-permute-start.6) | collective-permute-done | bytes 136224 | tf_op jit(solution)/shard_map/ppermute | solution.py:65
  71.6 1.9 collective-permute-start.8
  73.6 4.3 %collective-permute-start.23 = (bf16[64,112]{1,0:T(8,128)(2,1)S(1)}, bf16[64,112]{1,0:T(8,128)(2,1)S(1)}, u32[]{:S(2)}, u32[]{:S(2)}) collective-permute-start(bf16[64,112]{1,0:T(8,128)(2,1)S(1)} %fusion.17), channel_id=1, source_target_pairs={{0,384},{128,0},{256,128},{384,256},{1,385},{129,1},{257,129},{385... | collective-permute-start | bytes 43016 | tf_op jit(solution)/shard_map/ppermute | solution.py:84
  77.9 7.6 %collective-permute-start.22 = (bf16[64,112]{1,0:T(8,128)(2,1)S(1)}, bf16[64,112]{1,0:T(8,128)(2,1)S(1)}, u32[]{:S(2)}, u32[]{:S(2)}) collective-permute-start(bf16[64,112]{1,0:T(8,128)(2,1)S(1)} %fusion.17), channel_id=1, source_target_pairs={{0,256},{128,384},{256,0},{384,128},{1,257},{129,385},{257,1},{385... | collective-permute-start | bytes 43016 | tf_op jit(solution)/shard_map/ppermute | solution.py:84
  85.5 5.6 %collective-permute-start.21 = (bf16[64,112]{1,0:T(8,128)(2,1)S(1)}, bf16[64,112]{1,0:T(8,128)(2,1)S(1)}, u32[]{:S(2)}, u32[]{:S(2)}) collective-permute-start(bf16[64,112]{1,0:T(8,128)(2,1)S(1)} %fusion.17), channel_id=1, source_target_pairs={{0,128},{128,256},{256,384},{384,0},{1,129},{129,257},{257,385},{3... | collective-permute-start | bytes 43016 | tf_op jit(solution)/shard_map/ppermute | solution.py:84
  91.1 5.1 %collective-permute-start.9 = (bf16[2,56,608]{1,2,0:T(8,128)(2,1)S(1)}, bf16[2,56,608]{1,2,0:T(8,128)(2,1)}, u32[]{:S(2)}, u32[]{:S(2)}) collective-permute-start(bf16[2,56,608]{1,2,0:T(8,128)(2,1)S(1)} %collective-permute-done.7), channel_id=1, source_target_pairs={{0,480},{8,488},{16,496},{24,504},{32,0},{40,8},{48,16},{56,24},{6... | collective-permute-start | bytes 408584 | tf_op jit(solution)/shard_map/ppermute | solution.py:68
  96.3 1.9 collective-permute-start.10
  98.3 3.4 %collective-permute-start.25 = (bf16[4,64,112]{2,1,0:T(8,128)(2,1)S(1)}, bf16[4,64,112]{2,1,0:T(8,128)(2,1)S(1)}, u32[]{:S(2)}, u32[]{:S(2)}) collective-permute-start(bf16[4,64,112]{2,1,0:T(8,128)(2,1)S(1)} %pad_maximum_fusion), channel_id=1, source_target_pairs={{0,2},{1,3},{2,4},{3,5},{4,6},{5,7},{6,0},{7,1},{8,10},{9,11},{10,... | collective-permute-start | bytes 172040 | tf_op jit(solution)/shard_map/ppermute | solution.py:89
  101.7 4.0 %collective-permute-start.26 = (bf16[4,64,112]{2,1,0:T(8,128)(2,1)S(1)}, bf16[4,64,112]{2,1,0:T(8,128)(2,1)S(1)}, u32[]{:S(2)}, u32[]{:S(2)}) collective-permute-start(bf16[4,64,112]{2,1,0:T(8,128)(2,1)S(1)} %pad_maximum_fusion), channel_id=1, source_target_pairs={{0,3},{1,4},{2,5},{3,6},{4,7},{5,0},{6,1},{7,2},{8,11},{9,12},{10,... | collective-permute-start | bytes 172040 | tf_op jit(solution)/shard_map/ppermute | solution.py:89
  105.7 3.9 %collective-permute-start.27 = (bf16[4,64,112]{2,1,0:T(8,128)(2,1)S(1)}, bf16[4,64,112]{2,1,0:T(8,128)(2,1)S(1)}, u32[]{:S(2)}, u32[]{:S(2)}) collective-permute-start(bf16[4,64,112]{2,1,0:T(8,128)(2,1)S(1)} %pad_maximum_fusion), channel_id=1, source_target_pairs={{0,4},{1,5},{2,6},{3,7},{4,0},{5,1},{6,2},{7,3},{8,12},{9,13},{10,... | collective-permute-start | bytes 172040 | tf_op jit(solution)/shard_map/ppermute | solution.py:89
  109.7 5.1 %collective-permute-start.11 = (bf16[2,56,608]{1,2,0:T(8,128)(2,1)}, bf16[2,56,608]{1,2,0:T(8,128)(2,1)}, u32[]{:S(2)}, u32[]{:S(2)}) collective-permute-start(bf16[2,56,608]{1,2,0:T(8,128)(2,1)} %collective-permute-done.9), channel_id=1, source_target_pairs={{0,480},{8,488},{16,496},{24,504},{32,0},{40,8},{48,16},{56,24},{6... | collective-permute-start | bytes 408584 | tf_op jit(solution)/shard_map/ppermute | solution.py:68
  114.8 1.9 collective-permute-start.12
  116.8 3.2 %collective-permute-start.28 = (bf16[4,64,112]{2,1,0:T(8,128)(2,1)S(1)}, bf16[4,64,112]{2,1,0:T(8,128)(2,1)}, u32[]{:S(2)}, u32[]{:S(2)}) collective-permute-start(bf16[4,64,112]{2,1,0:T(8,128)(2,1)S(1)} %pad_maximum_fusion), channel_id=1, source_target_pairs={{0,5},{1,6},{2,7},{3,0},{4,1},{5,2},{6,3},{7,4},{8,13},{9,14},{10,... | collective-permute-start | bytes 172040 | tf_op jit(solution)/shard_map/ppermute | solution.py:89
  120.0 3.3 %collective-permute-start.29 = (bf16[4,64,112]{2,1,0:T(8,128)(2,1)S(1)}, bf16[4,64,112]{2,1,0:T(8,128)(2,1)}, u32[]{:S(2)}, u32[]{:S(2)}) collective-permute-start(bf16[4,64,112]{2,1,0:T(8,128)(2,1)S(1)} %pad_maximum_fusion), channel_id=1, source_target_pairs={{0,6},{1,7},{2,0},{3,1},{4,2},{5,3},{6,4},{7,5},{8,14},{9,15},{10,... | collective-permute-start | bytes 172040 | tf_op jit(solution)/shard_map/ppermute | solution.py:89
  124.9 2.9 %dynamic_update_slice.88 = bf16[2,896,608]{1,2,0:T(8,128)(2,1)S(1)} dynamic-update-slice(bf16[2,896,608]{1,2,0:T(8,128)(2,1)S(1)} %broadcast_in_dim.9, bf16[2,56,608]{1,2,0:T(8,128)(2,1)S(1)} %dynamic_update_slice.87, s32[]{:T(128)} %constant.225.clone.1, s32[]{:T(128)S(6)} %select_n.248, s32[]{:T(128)} %constant.225.clone.1) | dynamic-update-slice | bytes 272388 | tf_op jit(solution)/shard_map/dynamic_update_slice | solution.py:61
  129.7 1.7 dynamic_update_slice.107
  131.5 1.7 dynamic_update_slice.108
  133.2 5.8 %collective-permute-start.33 = (bf16[150,64]{0,1:T(8,128)(2,1)}, bf16[150,64]{0,1:T(8,128)(2,1)S(1)}, u32[]{:S(2)}, u32[]{:S(2)}) collective-permute-start(bf16[150,64]{0,1:T(8,128)(2,1)} %get-tuple-element.15), channel_id=1, source_target_pairs={{0,384},{128,0},{256,128},{384,256},{1,385},{129,1},{257,129},{385... | collective-permute-start | bytes 57608 | tf_op jit(solution)/shard_map/ppermute | solution.py:83
  139.1 1.7 dynamic_update_slice.109
  140.8 3.9 %collective-permute-start.31 = (bf16[150,64]{0,1:T(8,128)(2,1)}, bf16[150,64]{0,1:T(8,128)(2,1)S(1)}, u32[]{:S(2)}, u32[]{:S(2)}) collective-permute-start(bf16[150,64]{0,1:T(8,128)(2,1)} %get-tuple-element.14), channel_id=1, source_target_pairs={{0,128},{128,256},{256,384},{384,0},{1,129},{129,257},{257,385},{3... | collective-permute-start | bytes 57608 | tf_op jit(solution)/shard_map/ppermute | solution.py:83
  144.7 1.7 dynamic_update_slice.110
  146.5 8.5 %collective-permute-start.32 = (bf16[150,64]{0,1:T(8,128)(2,1)S(1)}, bf16[150,64]{0,1:T(8,128)(2,1)S(1)}, u32[]{:S(2)}, u32[]{:S(2)}) collective-permute-start(bf16[150,64]{0,1:T(8,128)(2,1)S(1)} %get-tuple-element.13), channel_id=1, source_target_pairs={{0,256},{128,384},{256,0},{384,128},{1,257},{129,385},{257,1},{385... | collective-permute-start | bytes 57608 | tf_op jit(solution)/shard_map/ppermute | solution.py:83
  155.0 1.7 dynamic_update_slice.111
  156.8 5.3 %collective-permute-start.13 = (bf16[2,56,608]{1,2,0:T(8,128)(2,1)}, bf16[2,56,608]{1,2,0:T(8,128)(2,1)S(1)}, u32[]{:S(2)}, u32[]{:S(2)}) collective-permute-start(bf16[2,56,608]{1,2,0:T(8,128)(2,1)} %collective-permute-done.11), channel_id=1, source_target_pairs={{0,480},{8,488},{16,496},{24,504},{32,0},{40,8},{48,16},{56,24},{6... | collective-permute-start | bytes 408584 | tf_op jit(solution)/shard_map/ppermute | solution.py:68
  162.0 1.9 collective-permute-start.14
  165.0 3.6 %collective-permute-done.13 = bf16[2,56,608]{1,2,0:T(8,128)(2,1)S(1)} collective-permute-done((bf16[2,56,608]{1,2,0:T(8,128)(2,1)}, bf16[2,56,608]{1,2,0:T(8,128)(2,1)S(1)}, u32[]{:S(2)}, u32[]{:S(2)}) %collective-permute-start.13) | collective-permute-done | bytes 136224 | tf_op jit(solution)/shard_map/ppermute | solution.py:68
  168.6 5.5 %collective-permute-start.15 = (bf16[2,56,608]{1,2,0:T(8,128)(2,1)S(1)}, bf16[2,56,608]{1,2,0:T(8,128)(2,1)S(1)}, u32[]{:S(2)}, u32[]{:S(2)}) collective-permute-start(bf16[2,56,608]{1,2,0:T(8,128)(2,1)S(1)} %collective-permute-done.13), channel_id=1, source_target_pairs={{0,480},{8,488},{16,496},{24,504},{32,0},{40,8},{48,16},{56,24},{6... | collective-permute-start | bytes 408584 | tf_op jit(solution)/shard_map/ppermute | solution.py:68
  174.1 1.9 collective-permute-start.16
  176.3 3.1 %collective-permute-done.15 = bf16[2,56,608]{1,2,0:T(8,128)(2,1)S(1)} collective-permute-done((bf16[2,56,608]{1,2,0:T(8,128)(2,1)S(1)}, bf16[2,56,608]{1,2,0:T(8,128)(2,1)S(1)}, u32[]{:S(2)}, u32[]{:S(2)}) %collective-permute-start.15) | collective-permute-done | bytes 136224 | tf_op jit(solution)/shard_map/ppermute | solution.py:68
  179.4 5.6 %collective-permute-start.17 = (bf16[2,56,608]{1,2,0:T(8,128)(2,1)S(1)}, bf16[2,56,608]{1,2,0:T(8,128)(2,1)}, u32[]{:S(2)}, u32[]{:S(2)}) collective-permute-start(bf16[2,56,608]{1,2,0:T(8,128)(2,1)S(1)} %collective-permute-done.15), channel_id=1, source_target_pairs={{0,480},{8,488},{16,496},{24,504},{32,0},{40,8},{48,16},{56,24},{6... | collective-permute-start | bytes 408584 | tf_op jit(solution)/shard_map/ppermute | solution.py:68
  185.1 1.9 collective-permute-start.18
  187.3 2.3 collective-permute-done.17
  189.5 5.7 %collective-permute-start.19 = (bf16[2,56,608]{1,2,0:T(8,128)(2,1)}, bf16[2,56,608]{1,2,0:T(8,128)(2,1)}, u32[]{:S(2)}, u32[]{:S(2)}) collective-permute-start(bf16[2,56,608]{1,2,0:T(8,128)(2,1)} %collective-permute-done.17), channel_id=1, source_target_pairs={{0,480},{8,488},{16,496},{24,504},{32,0},{40,8},{48,16},{56,24},{6... | collective-permute-start | bytes 408584 | tf_op jit(solution)/shard_map/ppermute | solution.py:68
  195.3 2.1 collective-permute-start.20
  198.8 5.6 %dynamic_update_slice.89 = bf16[2,896,608]{1,2,0:T(8,128)(2,1)S(1)} dynamic-update-slice(bf16[2,896,608]{1,2,0:T(8,128)(2,1)S(1)} %dynamic_update_slice.88, bf16[2,56,608]{1,2,0:T(8,128)(2,1)} %copy-done.4, s32[]{:T(128)} %constant.225.clone.1, s32[]{:T(128)S(6)} %select_n.250, s32[]{:T(128)} %constant.225.clone.1) | dynamic-update-slice | bytes 272388 | tf_op jit(solution)/shard_map/dynamic_update_slice | solution.py:66
  204.4 5.8 %dynamic_update_slice.90 = bf16[2,896,608]{1,2,0:T(8,128)(2,1)S(1)} dynamic-update-slice(bf16[2,896,608]{1,2,0:T(8,128)(2,1)S(1)} %dynamic_update_slice.89, bf16[2,56,608]{1,2,0:T(8,128)(2,1)} %copy-done.5, s32[]{:T(128)} %constant.225.clone.1, s32[]{:T(128)S(6)} %select_n.252, s32[]{:T(128)} %constant.225.clone.1) | dynamic-update-slice | bytes 272388 | tf_op jit(solution)/shard_map/dynamic_update_slice | solution.py:69
  210.3 5.7 %dynamic_update_slice.91 = bf16[2,896,608]{1,2,0:T(8,128)(2,1)S(1)} dynamic-update-slice(bf16[2,896,608]{1,2,0:T(8,128)(2,1)S(1)} %dynamic_update_slice.90, bf16[2,56,608]{1,2,0:T(8,128)(2,1)} %copy-done.6, s32[]{:T(128)} %constant.225.clone.1, s32[]{:T(128)S(6)} %select_n.254, s32[]{:T(128)} %constant.225.clone.1) | dynamic-update-slice | bytes 272388 | tf_op jit(solution)/shard_map/dynamic_update_slice | solution.py:66
  216.0 5.8 %dynamic_update_slice.92 = bf16[2,896,608]{1,2,0:T(8,128)(2,1)S(1)} dynamic-update-slice(bf16[2,896,608]{1,2,0:T(8,128)(2,1)S(1)} %dynamic_update_slice.91, bf16[2,56,608]{1,2,0:T(8,128)(2,1)} %collective-permute-done.9, s32[]{:T(128)} %constant.225.clone.1, s32[]{:T(128)S(6)} %select_n.256, s32[]{:T(128)} %constant.225.clone.1) | dynamic-update-slice | bytes 272388 | tf_op jit(solution)/shard_map/dynamic_update_slice | solution.py:69
  221.8 5.8 %dynamic_update_slice.93 = bf16[2,896,608]{1,2,0:T(8,128)(2,1)S(1)} dynamic-update-slice(bf16[2,896,608]{1,2,0:T(8,128)(2,1)S(1)} %dynamic_update_slice.92, bf16[2,56,608]{1,2,0:T(8,128)(2,1)} %collective-permute-done.10, s32[]{:T(128)} %constant.225.clone.1, s32[]{:T(128)S(6)} %select_n.258, s32[]{:T(128)} %constant.225.clone.1) | dynamic-update-slice | bytes 272388 | tf_op jit(solution)/shard_map/dynamic_update_slice | solution.py:66
  227.6 5.8 %dynamic_update_slice.94 = bf16[2,896,608]{1,2,0:T(8,128)(2,1)S(1)} dynamic-update-slice(bf16[2,896,608]{1,2,0:T(8,128)(2,1)S(1)} %dynamic_update_slice.93, bf16[2,56,608]{1,2,0:T(8,128)(2,1)} %collective-permute-done.11, s32[]{:T(128)} %constant.225.clone.1, s32[]{:T(128)S(6)} %select_n.260, s32[]{:T(128)} %constant.225.clone.1) | dynamic-update-slice | bytes 272388 | tf_op jit(solution)/shard_map/dynamic_update_slice | solution.py:69
  233.4 5.8 %dynamic_update_slice.95 = bf16[2,896,608]{1,2,0:T(8,128)(2,1)S(1)} dynamic-update-slice(bf16[2,896,608]{1,2,0:T(8,128)(2,1)S(1)} %dynamic_update_slice.94, bf16[2,56,608]{1,2,0:T(8,128)(2,1)} %collective-permute-done.12, s32[]{:T(128)} %constant.225.clone.1, s32[]{:T(128)S(6)} %select_n.262, s32[]{:T(128)} %constant.225.clone.1) | dynamic-update-slice | bytes 272388 | tf_op jit(solution)/shard_map/dynamic_update_slice | solution.py:66
  239.2 4.5 %dynamic_update_slice.96 = bf16[2,896,608]{1,2,0:T(8,128)(2,1)S(1)} dynamic-update-slice(bf16[2,896,608]{1,2,0:T(8,128)(2,1)S(1)} %dynamic_update_slice.95, bf16[2,56,608]{1,2,0:T(8,128)(2,1)S(1)} %copy-done.8, s32[]{:T(128)} %constant.225.clone.1, s32[]{:T(128)S(6)} %select_n.264, s32[]{:T(128)} %constant.225.clone.1) | dynamic-update-slice | bytes 272388 | tf_op jit(solution)/shard_map/dynamic_update_slice | solution.py:69
  243.8 4.5 %dynamic_update_slice.97 = bf16[2,896,608]{1,2,0:T(8,128)(2,1)S(1)} dynamic-update-slice(bf16[2,896,608]{1,2,0:T(8,128)(2,1)S(1)} %dynamic_update_slice.96, bf16[2,56,608]{1,2,0:T(8,128)(2,1)S(1)} %copy-done.10, s32[]{:T(128)} %constant.225.clone.1, s32[]{:T(128)S(6)} %select_n.266, s32[]{:T(128)} %constant.225.clone.1) | dynamic-update-slice | bytes 272388 | tf_op jit(solution)/shard_map/dynamic_update_slice | solution.py:66
  248.3 4.5 %dynamic_update_slice.98 = bf16[2,896,608]{1,2,0:T(8,128)(2,1)S(1)} dynamic-update-slice(bf16[2,896,608]{1,2,0:T(8,128)(2,1)S(1)} %dynamic_update_slice.97, bf16[2,56,608]{1,2,0:T(8,128)(2,1)S(1)} %copy-done.12, s32[]{:T(128)} %constant.225.clone.1, s32[]{:T(128)S(6)} %select_n.268, s32[]{:T(128)} %constant.225.clone.1) | dynamic-update-slice | bytes 272388 | tf_op jit(solution)/shard_map/dynamic_update_slice | solution.py:69
  252.8 4.5 %dynamic_update_slice.99 = bf16[2,896,608]{1,2,0:T(8,128)(2,1)S(1)} dynamic-update-slice(bf16[2,896,608]{1,2,0:T(8,128)(2,1)S(1)} %dynamic_update_slice.98, bf16[2,56,608]{1,2,0:T(8,128)(2,1)S(1)} %copy-done.14, s32[]{:T(128)} %constant.225.clone.1, s32[]{:T(128)S(6)} %select_n.270, s32[]{:T(128)} %constant.225.clone.1) | dynamic-update-slice | bytes 272388 | tf_op jit(solution)/shard_map/dynamic_update_slice | solution.py:66
  257.4 5.8 %dynamic_update_slice.100 = bf16[2,896,608]{1,2,0:T(8,128)(2,1)S(1)} dynamic-update-slice(bf16[2,896,608]{1,2,0:T(8,128)(2,1)S(1)} %dynamic_update_slice.99, bf16[2,56,608]{1,2,0:T(8,128)(2,1)} %collective-permute-done.17, s32[]{:T(128)} %constant.225.clone.1, s32[]{:T(128)S(6)} %select_n.272, s32[]{:T(128)} %constant.225.clone.1) | dynamic-update-slice | bytes 272388 | tf_op jit(solution)/shard_map/dynamic_update_slice | solution.py:69
  263.2 5.8 %dynamic_update_slice.101 = bf16[2,896,608]{1,2,0:T(8,128)(2,1)S(1)} dynamic-update-slice(bf16[2,896,608]{1,2,0:T(8,128)(2,1)S(1)} %dynamic_update_slice.100, bf16[2,56,608]{1,2,0:T(8,128)(2,1)} %collective-permute-done.18, s32[]{:T(128)} %constant.225.clone.1, s32[]{:T(128)S(6)} %select_n.274, s32[]{:T(128)} %constant.225.clone.1) | dynamic-update-slice | bytes 272388 | tf_op jit(solution)/shard_map/dynamic_update_slice | solution.py:66
  269.0 5.8 %dynamic_update_slice.102 = bf16[2,896,608]{1,2,0:T(8,128)(2,1)S(1)} dynamic-update-slice(bf16[2,896,608]{1,2,0:T(8,128)(2,1)S(1)} %dynamic_update_slice.101, bf16[2,56,608]{1,2,0:T(8,128)(2,1)} %collective-permute-done.19, s32[]{:T(128)} %constant.225.clone.1, s32[]{:T(128)S(6)} %select_n.276, s32[]{:T(128)} %constant.225.clone.1) | dynamic-update-slice | bytes 272388 | tf_op jit(solution)/shard_map/dynamic_update_slice | solution.py:69
  274.8 5.8 %dynamic_update_slice.103 = bf16[2,896,608]{1,2,0:T(8,128)(2,1)S(1)} dynamic-update-slice(bf16[2,896,608]{1,2,0:T(8,128)(2,1)S(1)} %dynamic_update_slice.102, bf16[2,56,608]{1,2,0:T(8,128)(2,1)} %collective-permute-done.20, s32[]{:T(128)} %constant.225.clone.1, s32[]{:T(128)S(6)} %select_n.278, s32[]{:T(128)} %constant.225.clone.1) | dynamic-update-slice | bytes 272388 | tf_op jit(solution)/shard_map/dynamic_update_slice | solution.py:66
  (91 shorter events, 11.5 us)
Async XLA Ops:
  0.6 72.8 %copy-start = (bf16[1,64,896]{2,1,0:T(8,128)(2,1)S(1)}, bf16[1,64,896]{2,1,0:T(8,128)(2,1)}, u32[]{:S(2)}) copy-start(bf16[1,64,896]{2,1,0:T(8,128)(2,1)} %param.9) | copy-start | bytes 344068
  2.2 121.4 %copy-start.16 = (bf16[1,4,150,64]{2,3,1,0:T(8,128)(2,1)S(1)}, bf16[1,4,150,64]{2,3,1,0:T(8,128)(2,1)}, u32[]{:S(2)}) copy-start(bf16[1,4,150,64]{2,3,1,0:T(8,128)(2,1)} %param.8) | copy-start | bytes 230404
  2.3 25.6 %collective-permute-start.2 = (bf16[2,14,608]{2,0,1:T(2,128)(2,1)S(1)}, bf16[2,14,608]{2,0,1:T(2,128)(2,1)S(1)}, u32[]{:S(2)}, u32[]{:S(2)}) collective-permute-start(bf16[2,14,608]{2,0,1:T(2,128)(2,1)S(1)} %bitcast.50), channel_id=1, source_target_pairs={{0,384},{128,0},{256,128},{384,256},{1,385},{129,1},{257,129},{385... | collective-permute-start | bytes 102152 | tf_op jit(solution)/shard_map/ppermute | solution.py:31
  15.1 14.8 %collective-permute-start.1 = (bf16[2,14,608]{2,0,1:T(2,128)(2,1)S(1)}, bf16[2,14,608]{2,0,1:T(2,128)(2,1)S(1)}, u32[]{:S(2)}, u32[]{:S(2)}) collective-permute-start(bf16[2,14,608]{2,0,1:T(2,128)(2,1)S(1)} %bitcast.51), channel_id=1, source_target_pairs={{0,256},{128,384},{256,0},{384,128},{1,257},{129,385},{257,1},{385... | collective-permute-start | bytes 102152 | tf_op jit(solution)/shard_map/ppermute | solution.py:31
  20.0 11.4 %collective-permute-start = (bf16[2,14,608]{2,0,1:T(2,128)(2,1)S(1)}, bf16[2,14,608]{2,0,1:T(2,128)(2,1)S(1)}, u32[]{:S(2)}, u32[]{:S(2)}) collective-permute-start(bf16[2,14,608]{2,0,1:T(2,128)(2,1)S(1)} %bitcast.52), channel_id=1, source_target_pairs={{0,128},{128,256},{256,384},{384,0},{1,129},{129,257},{257,385},{3... | collective-permute-start | bytes 102152 | tf_op jit(solution)/shard_map/ppermute | solution.py:31
  33.2 9.4 %copy-start.15 = (f32[2,14,608]{2,0,1:T(2,128)}, f32[2,14,608]{2,0,1:T(2,128)S(1)}, u32[]{:S(2)}) copy-start(f32[2,14,608]{2,0,1:T(2,128)S(1)} %get-tuple-element.7) | copy-start | bytes 204292
  33.4 17.7 %collective-permute-start.3 = (bf16[2,14,608]{1,2,0:T(8,128)(2,1)S(1)}, bf16[2,14,608]{1,2,0:T(8,128)(2,1)S(1)}, u32[]{:S(2)}, u32[]{:S(2)}) collective-permute-start(bf16[2,14,608]{1,2,0:T(8,128)(2,1)S(1)} %copy.16), channel_id=1, source_target_pairs={{0,8},{8,16},{16,24},{24,0},{32,40},{40,48},{48,56},{56,32},{64,72... | collective-permute-start | bytes 102152 | tf_op jit(solution)/shard_map/ppermute | solution.py:44
  36.6 18.5 %collective-permute-start.4 = (bf16[2,14,608]{1,2,0:T(8,128)(2,1)S(1)}, bf16[2,14,608]{1,2,0:T(8,128)(2,1)S(1)}, u32[]{:S(2)}, u32[]{:S(2)}) collective-permute-start(bf16[2,14,608]{1,2,0:T(8,128)(2,1)S(1)} %copy.16), channel_id=1, source_target_pairs={{0,16},{8,24},{16,0},{24,8},{32,48},{40,56},{48,32},{56,40},{64,80... | collective-permute-start | bytes 102152 | tf_op jit(solution)/shard_map/ppermute | solution.py:44
  39.2 18.4 %collective-permute-start.5 = (bf16[2,14,608]{1,2,0:T(8,128)(2,1)S(1)}, bf16[2,14,608]{1,2,0:T(8,128)(2,1)S(1)}, u32[]{:S(2)}, u32[]{:S(2)}) collective-permute-start(bf16[2,14,608]{1,2,0:T(8,128)(2,1)S(1)} %copy.16), channel_id=1, source_target_pairs={{0,24},{8,0},{16,8},{24,16},{32,56},{40,32},{48,40},{56,48},{64,88... | collective-permute-start | bytes 102152 | tf_op jit(solution)/shard_map/ppermute | solution.py:44
  61.6 10.0 %collective-permute-start.6 = (bf16[2,56,608]{1,2,0:T(8,128)(2,1)S(1)}, bf16[2,56,608]{1,2,0:T(8,128)(2,1)S(1)}, u32[]{:S(2)}, u32[]{:S(2)}) collective-permute-start(bf16[2,56,608]{1,2,0:T(8,128)(2,1)S(1)} %dynamic_update_slice.87), channel_id=1, source_target_pairs={{0,32},{8,40},{16,48},{24,56},{32,64},{40,72},{48,80},{56,88},{64,... | collective-permute-start | bytes 408584 | tf_op jit(solution)/shard_map/ppermute | solution.py:65
  63.5 27.6 %collective-permute-start.7 = (bf16[2,56,608]{1,2,0:T(8,128)(2,1)S(1)}, bf16[2,56,608]{1,2,0:T(8,128)(2,1)S(1)}, u32[]{:S(2)}, u32[]{:S(2)}) collective-permute-start(bf16[2,56,608]{1,2,0:T(8,128)(2,1)S(1)} %dynamic_update_slice.87), channel_id=1, source_target_pairs={{0,480},{8,488},{16,496},{24,504},{32,0},{40,8},{48,16},{56,24},{6... | collective-permute-start | bytes 408584 | tf_op jit(solution)/shard_map/ppermute | solution.py:68
  71.6 52.8 %copy-start.4 = (bf16[2,56,608]{1,2,0:T(8,128)(2,1)}, bf16[2,56,608]{1,2,0:T(8,128)(2,1)S(1)}, u32[]{:S(2)}) copy-start(bf16[2,56,608]{1,2,0:T(8,128)(2,1)S(1)} %collective-permute-done.6) | copy-start | bytes 408580
  71.6 24.7 %collective-permute-start.8 = (bf16[2,56,608]{1,2,0:T(8,128)(2,1)S(1)}, bf16[2,56,608]{1,2,0:T(8,128)(2,1)S(1)}, u32[]{:S(2)}, u32[]{:S(2)}) collective-permute-start(bf16[2,56,608]{1,2,0:T(8,128)(2,1)S(1)} %collective-permute-done.6), channel_id=1, source_target_pairs={{0,32},{8,40},{16,48},{24,56},{32,64},{40,72},{48,80},{56,88},{64,... | collective-permute-start | bytes 408584 | tf_op jit(solution)/shard_map/ppermute | solution.py:65
  73.6 24.6 %collective-permute-start.23 = (bf16[64,112]{1,0:T(8,128)(2,1)S(1)}, bf16[64,112]{1,0:T(8,128)(2,1)S(1)}, u32[]{:S(2)}, u32[]{:S(2)}) collective-permute-start(bf16[64,112]{1,0:T(8,128)(2,1)S(1)} %fusion.17), channel_id=1, source_target_pairs={{0,384},{128,0},{256,128},{384,256},{1,385},{129,1},{257,129},{385... | collective-permute-start | bytes 43016 | tf_op jit(solution)/shard_map/ppermute | solution.py:84
  77.9 20.4 %collective-permute-start.22 = (bf16[64,112]{1,0:T(8,128)(2,1)S(1)}, bf16[64,112]{1,0:T(8,128)(2,1)S(1)}, u32[]{:S(2)}, u32[]{:S(2)}) collective-permute-start(bf16[64,112]{1,0:T(8,128)(2,1)S(1)} %fusion.17), channel_id=1, source_target_pairs={{0,256},{128,384},{256,0},{384,128},{1,257},{129,385},{257,1},{385... | collective-permute-start | bytes 43016 | tf_op jit(solution)/shard_map/ppermute | solution.py:84
  85.5 12.8 %collective-permute-start.21 = (bf16[64,112]{1,0:T(8,128)(2,1)S(1)}, bf16[64,112]{1,0:T(8,128)(2,1)S(1)}, u32[]{:S(2)}, u32[]{:S(2)}) collective-permute-start(bf16[64,112]{1,0:T(8,128)(2,1)S(1)} %fusion.17), channel_id=1, source_target_pairs={{0,128},{128,256},{256,384},{384,0},{1,129},{129,257},{257,385},{3... | collective-permute-start | bytes 43016 | tf_op jit(solution)/shard_map/ppermute | solution.py:84
  91.1 5.1 %copy-start.5 = (bf16[2,56,608]{1,2,0:T(8,128)(2,1)}, bf16[2,56,608]{1,2,0:T(8,128)(2,1)S(1)}, u32[]{:S(2)}) copy-start(bf16[2,56,608]{1,2,0:T(8,128)(2,1)S(1)} %collective-permute-done.7) | copy-start | bytes 408580
  91.1 18.5 %collective-permute-start.9 = (bf16[2,56,608]{1,2,0:T(8,128)(2,1)S(1)}, bf16[2,56,608]{1,2,0:T(8,128)(2,1)}, u32[]{:S(2)}, u32[]{:S(2)}) collective-permute-start(bf16[2,56,608]{1,2,0:T(8,128)(2,1)S(1)} %collective-permute-done.7), channel_id=1, source_target_pairs={{0,480},{8,488},{16,496},{24,504},{32,0},{40,8},{48,16},{56,24},{6... | collective-permute-start | bytes 408584 | tf_op jit(solution)/shard_map/ppermute | solution.py:68
  96.3 13.4 %copy-start.6 = (bf16[2,56,608]{1,2,0:T(8,128)(2,1)}, bf16[2,56,608]{1,2,0:T(8,128)(2,1)S(1)}, u32[]{:S(2)}) copy-start(bf16[2,56,608]{1,2,0:T(8,128)(2,1)S(1)} %collective-permute-done.8) | copy-start | bytes 408580
  96.3 18.5 %collective-permute-start.10 = (bf16[2,56,608]{1,2,0:T(8,128)(2,1)S(1)}, bf16[2,56,608]{1,2,0:T(8,128)(2,1)}, u32[]{:S(2)}, u32[]{:S(2)}) collective-permute-start(bf16[2,56,608]{1,2,0:T(8,128)(2,1)S(1)} %collective-permute-done.8), channel_id=1, source_target_pairs={{0,32},{8,40},{16,48},{24,56},{32,64},{40,72},{48,80},{56,88},{64,... | collective-permute-start | bytes 408584 | tf_op jit(solution)/shard_map/ppermute | solution.py:65
  98.3 7.5 %collective-permute-start.24 = (bf16[4,64,112]{2,1,0:T(8,128)(2,1)S(1)}, bf16[4,64,112]{2,1,0:T(8,128)(2,1)S(1)}, u32[]{:S(2)}, u32[]{:S(2)}) collective-permute-start(bf16[4,64,112]{2,1,0:T(8,128)(2,1)S(1)} %pad_maximum_fusion), channel_id=1, source_target_pairs={{0,1},{1,2},{2,3},{3,4},{4,5},{5,6},{6,7},{7,0},{8,9},{9,10},{10,1... | collective-permute-start | bytes 172040 | tf_op jit(solution)/shard_map/ppermute | solution.py:89
  98.3 18.5 %collective-permute-start.25 = (bf16[4,64,112]{2,1,0:T(8,128)(2,1)S(1)}, bf16[4,64,112]{2,1,0:T(8,128)(2,1)S(1)}, u32[]{:S(2)}, u32[]{:S(2)}) collective-permute-start(bf16[4,64,112]{2,1,0:T(8,128)(2,1)S(1)} %pad_maximum_fusion), channel_id=1, source_target_pairs={{0,2},{1,3},{2,4},{3,5},{4,6},{5,7},{6,0},{7,1},{8,10},{9,11},{10,... | collective-permute-start | bytes 172040 | tf_op jit(solution)/shard_map/ppermute | solution.py:89
  101.7 18.3 %collective-permute-start.26 = (bf16[4,64,112]{2,1,0:T(8,128)(2,1)S(1)}, bf16[4,64,112]{2,1,0:T(8,128)(2,1)S(1)}, u32[]{:S(2)}, u32[]{:S(2)}) collective-permute-start(bf16[4,64,112]{2,1,0:T(8,128)(2,1)S(1)} %pad_maximum_fusion), channel_id=1, source_target_pairs={{0,3},{1,4},{2,5},{3,6},{4,7},{5,0},{6,1},{7,2},{8,11},{9,12},{10,... | collective-permute-start | bytes 172040 | tf_op jit(solution)/shard_map/ppermute | solution.py:89
  105.7 17.7 %collective-permute-start.27 = (bf16[4,64,112]{2,1,0:T(8,128)(2,1)S(1)}, bf16[4,64,112]{2,1,0:T(8,128)(2,1)S(1)}, u32[]{:S(2)}, u32[]{:S(2)}) collective-permute-start(bf16[4,64,112]{2,1,0:T(8,128)(2,1)S(1)} %pad_maximum_fusion), channel_id=1, source_target_pairs={{0,4},{1,5},{2,6},{3,7},{4,0},{5,1},{6,2},{7,3},{8,12},{9,13},{10,... | collective-permute-start | bytes 172040 | tf_op jit(solution)/shard_map/ppermute | solution.py:89
  109.7 47.1 %collective-permute-start.11 = (bf16[2,56,608]{1,2,0:T(8,128)(2,1)}, bf16[2,56,608]{1,2,0:T(8,128)(2,1)}, u32[]{:S(2)}, u32[]{:S(2)}) collective-permute-start(bf16[2,56,608]{1,2,0:T(8,128)(2,1)} %collective-permute-done.9), channel_id=1, source_target_pairs={{0,480},{8,488},{16,496},{24,504},{32,0},{40,8},{48,16},{56,24},{6... | collective-permute-start | bytes 408584 | tf_op jit(solution)/shard_map/ppermute | solution.py:68
  114.8 47.2 %collective-permute-start.12 = (bf16[2,56,608]{1,2,0:T(8,128)(2,1)}, bf16[2,56,608]{1,2,0:T(8,128)(2,1)}, u32[]{:S(2)}, u32[]{:S(2)}) collective-permute-start(bf16[2,56,608]{1,2,0:T(8,128)(2,1)} %collective-permute-done.10), channel_id=1, source_target_pairs={{0,32},{8,40},{16,48},{24,56},{32,64},{40,72},{48,80},{56,88},{64,... | collective-permute-start | bytes 408584 | tf_op jit(solution)/shard_map/ppermute | solution.py:65
  116.8 7.6 %copy-start.17 = (bf16[4,64,112]{2,1,0:T(8,128)(2,1)}, bf16[4,64,112]{2,1,0:T(8,128)(2,1)S(1)}, u32[]{:S(2)}) copy-start(bf16[4,64,112]{2,1,0:T(8,128)(2,1)S(1)} %collective-permute-done.25) | copy-start | bytes 172036
  116.8 16.4 %collective-permute-start.28 = (bf16[4,64,112]{2,1,0:T(8,128)(2,1)S(1)}, bf16[4,64,112]{2,1,0:T(8,128)(2,1)}, u32[]{:S(2)}, u32[]{:S(2)}) collective-permute-start(bf16[4,64,112]{2,1,0:T(8,128)(2,1)S(1)} %pad_maximum_fusion), channel_id=1, source_target_pairs={{0,5},{1,6},{2,7},{3,0},{4,1},{5,2},{6,3},{7,4},{8,13},{9,14},{10,... | collective-permute-start | bytes 172040 | tf_op jit(solution)/shard_map/ppermute | solution.py:89
  120.0 4.3 %copy-start.19 = (bf16[4,64,112]{2,1,0:T(8,128)(2,1)}, bf16[4,64,112]{2,1,0:T(8,128)(2,1)S(1)}, u32[]{:S(2)}) copy-start(bf16[4,64,112]{2,1,0:T(8,128)(2,1)S(1)} %collective-permute-done.26) | copy-start | bytes 172036
  120.0 20.8 %collective-permute-start.29 = (bf16[4,64,112]{2,1,0:T(8,128)(2,1)S(1)}, bf16[4,64,112]{2,1,0:T(8,128)(2,1)}, u32[]{:S(2)}, u32[]{:S(2)}) collective-permute-start(bf16[4,64,112]{2,1,0:T(8,128)(2,1)S(1)} %pad_maximum_fusion), channel_id=1, source_target_pairs={{0,6},{1,7},{2,0},{3,1},{4,2},{5,3},{6,4},{7,5},{8,14},{9,15},{10,... | collective-permute-start | bytes 172040 | tf_op jit(solution)/shard_map/ppermute | solution.py:89
  123.4 1.0 copy-start.20
  123.4 23.1 %collective-permute-start.30 = (bf16[4,64,112]{2,1,0:T(8,128)(2,1)S(1)}, bf16[4,64,112]{2,1,0:T(8,128)(2,1)}, u32[]{:S(2)}, u32[]{:S(2)}) collective-permute-start(bf16[4,64,112]{2,1,0:T(8,128)(2,1)S(1)} %pad_maximum_fusion), channel_id=1, source_target_pairs={{0,7},{1,0},{2,1},{3,2},{4,3},{5,4},{6,5},{7,6},{8,15},{9,8},{10,9... | collective-permute-start | bytes 172040 | tf_op jit(solution)/shard_map/ppermute | solution.py:89
  124.7 4.0 %copy-start.18 = (bf16[4,64,112]{2,1,0:T(8,128)(2,1)S(1)}, bf16[4,64,112]{2,1,0:T(8,128)(2,1)}, u32[]{:S(2)}) copy-start(bf16[4,64,112]{2,1,0:T(8,128)(2,1)} %copy-done.17) | copy-start | bytes 172036
  127.8 69.6 %copy-start.2 = (f32[150,896]{1,0:T(8,128)S(1)}, f32[150,896]{1,0:T(8,128)}, u32[]{:S(2)}) copy-start(f32[150,896]{1,0:T(8,128)} %param.12) | copy-start | bytes 1612804
  133.2 53.8 %collective-permute-start.33 = (bf16[150,64]{0,1:T(8,128)(2,1)}, bf16[150,64]{0,1:T(8,128)(2,1)S(1)}, u32[]{:S(2)}, u32[]{:S(2)}) collective-permute-start(bf16[150,64]{0,1:T(8,128)(2,1)} %get-tuple-element.15), channel_id=1, source_target_pairs={{0,384},{128,0},{256,128},{384,256},{1,385},{129,1},{257,129},{385... | collective-permute-start | bytes 57608 | tf_op jit(solution)/shard_map/ppermute | solution.py:83
  140.8 35.2 %collective-permute-start.31 = (bf16[150,64]{0,1:T(8,128)(2,1)}, bf16[150,64]{0,1:T(8,128)(2,1)S(1)}, u32[]{:S(2)}, u32[]{:S(2)}) collective-permute-start(bf16[150,64]{0,1:T(8,128)(2,1)} %get-tuple-element.14), channel_id=1, source_target_pairs={{0,128},{128,256},{256,384},{384,0},{1,129},{129,257},{257,385},{3... | collective-permute-start | bytes 57608 | tf_op jit(solution)/shard_map/ppermute | solution.py:83
  146.5 50.9 %collective-permute-start.32 = (bf16[150,64]{0,1:T(8,128)(2,1)S(1)}, bf16[150,64]{0,1:T(8,128)(2,1)S(1)}, u32[]{:S(2)}, u32[]{:S(2)}) collective-permute-start(bf16[150,64]{0,1:T(8,128)(2,1)S(1)} %get-tuple-element.13), channel_id=1, source_target_pairs={{0,256},{128,384},{256,0},{384,128},{1,257},{129,385},{257,1},{385... | collective-permute-start | bytes 57608 | tf_op jit(solution)/shard_map/ppermute | solution.py:83
  156.7 40.7 %copy-start.3 = (f32[150,896]{1,0:T(8,128)S(1)}, f32[150,896]{1,0:T(8,128)}, u32[]{:S(2)}) copy-start(f32[150,896]{1,0:T(8,128)} %param.13) | copy-start | bytes 1612804
  156.8 11.8 %collective-permute-start.13 = (bf16[2,56,608]{1,2,0:T(8,128)(2,1)}, bf16[2,56,608]{1,2,0:T(8,128)(2,1)S(1)}, u32[]{:S(2)}, u32[]{:S(2)}) collective-permute-start(bf16[2,56,608]{1,2,0:T(8,128)(2,1)} %collective-permute-done.11), channel_id=1, source_target_pairs={{0,480},{8,488},{16,496},{24,504},{32,0},{40,8},{48,16},{56,24},{6... | collective-permute-start | bytes 408584 | tf_op jit(solution)/shard_map/ppermute | solution.py:68
  162.0 12.0 %collective-permute-start.14 = (bf16[2,56,608]{1,2,0:T(8,128)(2,1)}, bf16[2,56,608]{1,2,0:T(8,128)(2,1)S(1)}, u32[]{:S(2)}, u32[]{:S(2)}) collective-permute-start(bf16[2,56,608]{1,2,0:T(8,128)(2,1)} %collective-permute-done.12), channel_id=1, source_target_pairs={{0,32},{8,40},{16,48},{24,56},{32,64},{40,72},{48,80},{56,88},{64,... | collective-permute-start | bytes 408584 | tf_op jit(solution)/shard_map/ppermute | solution.py:65
  168.6 18.4 %copy-start.7 = (bf16[2,56,608]{1,2,0:T(8,128)(2,1)}, bf16[2,56,608]{1,2,0:T(8,128)(2,1)S(1)}, u32[]{:S(2)}) copy-start(bf16[2,56,608]{1,2,0:T(8,128)(2,1)S(1)} %collective-permute-done.13) | copy-start | bytes 408580
  168.6 10.9 %collective-permute-start.15 = (bf16[2,56,608]{1,2,0:T(8,128)(2,1)S(1)}, bf16[2,56,608]{1,2,0:T(8,128)(2,1)S(1)}, u32[]{:S(2)}, u32[]{:S(2)}) collective-permute-start(bf16[2,56,608]{1,2,0:T(8,128)(2,1)S(1)} %collective-permute-done.13), channel_id=1, source_target_pairs={{0,480},{8,488},{16,496},{24,504},{32,0},{40,8},{48,16},{56,24},{6... | collective-permute-start | bytes 408584 | tf_op jit(solution)/shard_map/ppermute | solution.py:68
  174.1 12.9 %copy-start.9 = (bf16[2,56,608]{1,2,0:T(8,128)(2,1)}, bf16[2,56,608]{1,2,0:T(8,128)(2,1)S(1)}, u32[]{:S(2)}) copy-start(bf16[2,56,608]{1,2,0:T(8,128)(2,1)S(1)} %collective-permute-done.14) | copy-start | bytes 408580
  174.1 10.9 %collective-permute-start.16 = (bf16[2,56,608]{1,2,0:T(8,128)(2,1)S(1)}, bf16[2,56,608]{1,2,0:T(8,128)(2,1)S(1)}, u32[]{:S(2)}, u32[]{:S(2)}) collective-permute-start(bf16[2,56,608]{1,2,0:T(8,128)(2,1)S(1)} %collective-permute-done.14), channel_id=1, source_target_pairs={{0,32},{8,40},{16,48},{24,56},{32,64},{40,72},{48,80},{56,88},{64,... | collective-permute-start | bytes 408584 | tf_op jit(solution)/shard_map/ppermute | solution.py:65
  179.4 7.8 %copy-start.11 = (bf16[2,56,608]{1,2,0:T(8,128)(2,1)}, bf16[2,56,608]{1,2,0:T(8,128)(2,1)S(1)}, u32[]{:S(2)}) copy-start(bf16[2,56,608]{1,2,0:T(8,128)(2,1)S(1)} %collective-permute-done.15) | copy-start | bytes 408580
  179.4 10.1 %collective-permute-start.17 = (bf16[2,56,608]{1,2,0:T(8,128)(2,1)S(1)}, bf16[2,56,608]{1,2,0:T(8,128)(2,1)}, u32[]{:S(2)}, u32[]{:S(2)}) collective-permute-start(bf16[2,56,608]{1,2,0:T(8,128)(2,1)S(1)} %collective-permute-done.15), channel_id=1, source_target_pairs={{0,480},{8,488},{16,496},{24,504},{32,0},{40,8},{48,16},{56,24},{6... | collective-permute-start | bytes 408584 | tf_op jit(solution)/shard_map/ppermute | solution.py:68
  185.0 4.5 %copy-start.13 = (bf16[2,56,608]{1,2,0:T(8,128)(2,1)}, bf16[2,56,608]{1,2,0:T(8,128)(2,1)S(1)}, u32[]{:S(2)}) copy-start(bf16[2,56,608]{1,2,0:T(8,128)(2,1)S(1)} %collective-permute-done.16) | copy-start | bytes 408580
  185.1 10.2 %collective-permute-start.18 = (bf16[2,56,608]{1,2,0:T(8,128)(2,1)S(1)}, bf16[2,56,608]{1,2,0:T(8,128)(2,1)}, u32[]{:S(2)}, u32[]{:S(2)}) collective-permute-start(bf16[2,56,608]{1,2,0:T(8,128)(2,1)S(1)} %collective-permute-done.16), channel_id=1, source_target_pairs={{0,32},{8,40},{16,48},{24,56},{32,64},{40,72},{48,80},{56,88},{64,... | collective-permute-start | bytes 408584 | tf_op jit(solution)/shard_map/ppermute | solution.py:65
  189.5 79.4 %collective-permute-start.19 = (bf16[2,56,608]{1,2,0:T(8,128)(2,1)}, bf16[2,56,608]{1,2,0:T(8,128)(2,1)}, u32[]{:S(2)}, u32[]{:S(2)}) collective-permute-start(bf16[2,56,608]{1,2,0:T(8,128)(2,1)} %collective-permute-done.17), channel_id=1, source_target_pairs={{0,480},{8,488},{16,496},{24,504},{32,0},{40,8},{48,16},{56,24},{6... | collective-permute-start | bytes 408584 | tf_op jit(solution)/shard_map/ppermute | solution.py:68
  195.3 79.6 %collective-permute-start.20 = (bf16[2,56,608]{1,2,0:T(8,128)(2,1)}, bf16[2,56,608]{1,2,0:T(8,128)(2,1)}, u32[]{:S(2)}, u32[]{:S(2)}) collective-permute-start(bf16[2,56,608]{1,2,0:T(8,128)(2,1)} %collective-permute-done.18), channel_id=1, source_target_pairs={{0,32},{8,40},{16,48},{24,56},{32,64},{40,72},{48,80},{56,88},{64,... | collective-permute-start | bytes 408584 | tf_op jit(solution)/shard_map/ppermute | solution.py:65
  198.8 40.5 %copy-start.8 = (bf16[2,56,608]{1,2,0:T(8,128)(2,1)S(1)}, bf16[2,56,608]{1,2,0:T(8,128)(2,1)}, u32[]{:S(2)}) copy-start(bf16[2,56,608]{1,2,0:T(8,128)(2,1)} %copy-done.7) | copy-start | bytes 408580
  204.4 39.3 %copy-start.10 = (bf16[2,56,608]{1,2,0:T(8,128)(2,1)S(1)}, bf16[2,56,608]{1,2,0:T(8,128)(2,1)}, u32[]{:S(2)}) copy-start(bf16[2,56,608]{1,2,0:T(8,128)(2,1)} %copy-done.9) | copy-start | bytes 408580
  210.3 38.0 %copy-start.12 = (bf16[2,56,608]{1,2,0:T(8,128)(2,1)S(1)}, bf16[2,56,608]{1,2,0:T(8,128)(2,1)}, u32[]{:S(2)}) copy-start(bf16[2,56,608]{1,2,0:T(8,128)(2,1)} %copy-done.11) | copy-start | bytes 408580
  215.9 36.9 %copy-start.14 = (bf16[2,56,608]{1,2,0:T(8,128)(2,1)S(1)}, bf16[2,56,608]{1,2,0:T(8,128)(2,1)}, u32[]{:S(2)}) copy-start(bf16[2,56,608]{1,2,0:T(8,128)(2,1)} %copy-done.13) | copy-start | bytes 408580
  280.6 1.3 copy-start.1

commit v2 on v0

--- a/solution.py
+++ b/solution.py
@@ -6,26 +6,82 @@
 rate_outer = 0.7
 beta_outer = 0.9
 
+Y_SIZE = 4
+
+
+def shift_pairs(n, k):
+    return [(i, (i + k) % n) for i in range(n)]
+
 
 def on_device(
     layer_delta, emb_left, emb_right, layer_weight, layer_momentum, emb_weight, emb_momentum
 ):
+    f32 = jnp.float32
+    bf16 = jnp.bfloat16
     groups = lax.axis_size("group")
-    summed = lax.psum_scatter(
-        layer_delta.astype(jnp.float32).astype(jnp.bfloat16),
-        "group",
-        scatter_dimension=2,
-        tiled=True,
-    ).astype(jnp.float32)
-    layer_mean = summed.reshape(layer_weight.shape) / groups
+    shards = lax.axis_size("shard")
+    tensors = lax.axis_size("tensor")
+    gi = lax.axis_index("group")
+    si = lax.axis_index("shard")
+    ti = lax.axis_index("tensor")
+
+    delta = layer_delta[0]
+    nlayer = delta.size // groups
+    send_layer = jnp.moveaxis(delta, 1, 0).reshape(groups, nlayer)
+    left = emb_left[0]
+    nleft = left.size // groups
+    send_left = left.reshape(groups, nleft)
+    right = emb_right[0]
+    rank, width = right.shape
+    chunk = width // tensors
+    rchunk = lax.dynamic_slice_in_dim(right, ti * chunk, chunk, axis=1)
+    send_right = jnp.broadcast_to(rchunk.reshape(1, rank * chunk), (groups, rank * chunk))
+    send = jnp.concatenate([send_layer, send_left, send_right], axis=1)
+    recv = lax.all_to_all(send, "group", 0, 0, tiled=True)
+
+    acc = recv[:, :nlayer].astype(f32).sum(axis=0)
+    layer_mean = acc.reshape(layer_weight.shape) / groups
     new_layer_momentum = beta_outer * layer_momentum + layer_mean
     new_layer_weight = layer_weight - rate_outer * (layer_mean + beta_outer * new_layer_momentum)
-    pieces = new_layer_weight.astype(jnp.bfloat16)
-    layer_blocks = lax.all_gather(pieces, ("group", "shard"), axis=1, tiled=True)
-    terms = jnp.einsum("qnr,rd->qnd", emb_left[0], emb_right[0], preferred_element_type=jnp.float32)
-    total = lax.psum_scatter(
-        terms.astype(jnp.bfloat16), "group", scatter_dimension=0, tiled=True
-    ).astype(jnp.float32)[0]
+    piece = new_layer_weight.astype(bf16)
+
+    yi = si % Y_SIZE
+    yblk = jnp.zeros((Y_SIZE,) + piece.shape, piece.dtype)
+    yblk = lax.dynamic_update_index_in_dim(yblk, piece, yi, axis=0)
+    for k in range(1, Y_SIZE):
+        pairs = [(s, (s - s % Y_SIZE) + (s % Y_SIZE + k) % Y_SIZE) for s in range(shards)]
+        got = lax.ppermute(piece, "shard", pairs)
+        yblk = lax.dynamic_update_index_in_dim(yblk, got, (yi - k) % Y_SIZE, axis=0)
+
+    zlo_size = shards // Y_SIZE
+    nz = groups * zlo_size
+    zi = gi * zlo_size + si // Y_SIZE
+    n_all = groups * shards
+
+    def zshift(k):
+        return [(i, ((i // Y_SIZE + k) % nz) * Y_SIZE + i % Y_SIZE) for i in range(n_all)]
+
+    out = jnp.zeros((nz,) + yblk.shape, piece.dtype)
+    out = lax.dynamic_update_index_in_dim(out, yblk, zi, axis=0)
+    fwd = yblk
+    bwd = yblk
+    for step in range(1, nz // 2 + 1):
+        fwd = lax.ppermute(fwd, ("group", "shard"), zshift(1))
+        out = lax.dynamic_update_index_in_dim(out, fwd, (zi - step) % nz, axis=0)
+        if step < nz - nz // 2:
+            bwd = lax.ppermute(bwd, ("group", "shard"), zshift(-1))
+            out = lax.dynamic_update_index_in_dim(out, bwd, (zi + step) % nz, axis=0)
+    layer_blocks = jnp.moveaxis(out, 2, 0).reshape(piece.shape[0], -1, piece.shape[2])
+
+    lefts = recv[:, nlayer:nlayer + nleft].reshape((groups,) + left.shape[1:])
+    rchunks = recv[:, nlayer + nleft:].reshape(groups, rank, chunk)
+    rsend = jnp.broadcast_to(rchunks.reshape(1, -1), (tensors, rchunks.size))
+    rgot = lax.all_to_all(rsend, "tensor", 0, 0, tiled=True)
+    full = jnp.moveaxis(rgot.reshape(tensors, groups, rank, chunk), 0, 2).reshape(groups, rank, width)
+    total = jnp.zeros(emb_weight.shape, f32)
+    for g in range(groups):
+        product = jnp.dot(lefts[g], full[g], preferred_element_type=f32).astype(bf16)
+        total = total + product.astype(f32)
     emb_mean = total / groups
     new_emb_momentum = beta_outer * emb_momentum + emb_mean
     new_emb_weight = emb_weight - rate_outer * (emb_mean + beta_outer * new_emb_momentum)

time: 300 us -> 169 us (0.56)
  waiting for transfers between devices: 269 us -> 29.1 us
  starting transfers between devices: 0.12 us -> 83 us
  local copies, waits for them, and re-layouts: 10.4 us -> 40 us
  between operations: 13.8 us -> 1.22 us
  other arithmetic: 4.27 us -> 8.3 us
  matrix products: 2.39 us -> 5.63 us
    all_gather x1 -> x0, waiting for transfers between devices: 137 us -> none  [on_device(): lax.all_gather(pieces, ('group', 'shard'), axis=1, tiled=True)]
    unnamed x5 -> x0, waiting for transfers between devices: 131 us -> none
    ppermute x0 -> x18, starting transfers between devices: none -> 63.1 us  [the longest x7 30.1 us: on_device(): bwd = lax.ppermute(bwd, ('group', 'shard'), zshift(-1))]
    all_to_all x0 -> x2, starting transfers between devices: none -> 19.9 us  [the longest x1 15.1 us: on_device(): recv = lax.all_to_all(send, 'group', 0, 0, tiled=True)]
    all_to_all x0 -> x2, waiting for transfers between devices: none -> 18.7 us  [the longest x1 18.7 us: on_device(): recv = lax.all_to_all(send, 'group', 0, 0, tiled=True)]
    ppermute x0 -> x18, waiting for transfers between devices: none -> 10.4 us  [the longest x8 10.3 us: on_device(): fwd = lax.ppermute(fwd, ('group', 'shard'), zshift(1))]
    squeeze x0 -> x8, local copies, waits for them, and re-layouts: none -> 9.07 us  [the longest x4 6.89 us: on_device(): full[g]]
    slice x0 -> x6, local copies, waits for them, and re-layouts: none -> 6.86 us  [the longest x5 6.43 us: on_device(): full[g]]
  transfers between devices with their start and end apart: 3 -> 20, of which waited for: 3 -> 7; matrix products, arithmetic and copies ran while one was open for 3% -> 25% of each run, Pallas kernels for 0% -> 0%
where the time goes in v2:
time: 169 us; the launch traced here: 167 us
  starting transfers between devices  83 us (49%)
  local copies, waits for them, and re-layouts  40 us (24%)
  waiting for transfers between devices  29.1 us (17%)
  other arithmetic  8.3 us (5%)
  matrix products  5.63 us (3%)
    ppermute x7, starting transfers between devices, on_device(): bwd = lax.ppermute(bwd, ('group', 'shard'), zshift(-1))  30.1 us
    ppermute x8, starting transfers between devices, on_device(): fwd = lax.ppermute(fwd, ('group', 'shard'), zshift(1))  21.5 us
    all_to_all x1, waiting for transfers between devices, on_device(): recv = lax.all_to_all(send, 'group', 0, 0, tiled=True)  18.7 us
    all_to_all x1, starting transfers between devices, on_device(): recv = lax.all_to_all(send, 'group', 0, 0, tiled=True)  15.1 us
    unnamed x21, local copies, waits for them, and re-layouts  12.7 us
    ppermute x3, starting transfers between devices, on_device(): got = lax.ppermute(piece, 'shard', pairs)  11.6 us
    ppermute x8, waiting for transfers between devices, on_device(): fwd = lax.ppermute(fwd, ('group', 'shard'), zshift(1))  10.3 us
    squeeze x4, local copies, waits for them, and re-layouts, on_device(): full[g]  6.89 us
  transfers between devices with their start and end apart: 20, of which 7 were waited for; matrix products, arithmetic and copies ran while one was open for 25% of the time, Pallas kernels for 0%

profile of v2, /device:TPU:6, one launch (start us, length us, event | category | flops | bytes accessed | tf_op | source)
XLA Modules:
  0.0 167.3 jit_solution(11756936042481109367)
XLA Ops:
  0.7 1.1 copy.63
  1.9 0.9 copy.62
  2.8 0.3 reshape.55
  3.5 0.5 broadcast.50
  4.0 1.0 reduce.9
  5.0 0.8 reshape.64
  5.8 15.1 %all-to-all-start = ((bf16[4,2,16896]{2,1,0:T(2,128)(2,1)}), bf16[4,2,16896]{2,1,0:T(2,128)(2,1)S(1)}, u32[]{:S(2)}, u32[]{:S(2)}) async-start(bf16[4,2,16896]{2,1,0:T(2,128)(2,1)} %reshape.64), calls=%async_computation | async-start | bytes 540672 | tf_op jit(solution)/shard_map/all_to_all | solution.py:40
  20.9 18.7 %all-to-all-done = bf16[4,2,16896]{2,1,0:T(2,128)(2,1)S(1)} async-done(((bf16[4,2,16896]{2,1,0:T(2,128)(2,1)}), bf16[4,2,16896]{2,1,0:T(2,128)(2,1)S(1)}, u32[]{:S(2)}, u32[]{:S(2)}) %all-to-all-start) | async-done | bytes 270368 | tf_op jit(solution)/shard_map/all_to_all | solution.py:40
  40.4 3.5 %collective-permute-start = (bf16[2,14,608]{2,1,0:T(8,128)(2,1)S(1)}, bf16[2,14,608]{2,1,0:T(8,128)(2,1)S(1)}, u32[]{:S(2)}, u32[]{:S(2)}) collective-permute-start(bf16[2,14,608]{2,1,0:T(8,128)(2,1)S(1)} %get-tuple-element.26), channel_id=1, source_target_pairs={{0,8},{8,16},{16,24},{24,0},{32,40},{40,48},{48,56},{56,32},{64,72... | collective-permute-start | bytes 102152 | tf_op jit(solution)/shard_map/ppermute | solution.py:53
  43.9 4.8 %collective-permute-start.1 = (bf16[2,14,608]{2,1,0:T(8,128)(2,1)S(1)}, bf16[2,14,608]{2,1,0:T(8,128)(2,1)S(1)}, u32[]{:S(2)}, u32[]{:S(2)}) collective-permute-start(bf16[2,14,608]{2,1,0:T(8,128)(2,1)S(1)} %get-tuple-element.26), channel_id=1, source_target_pairs={{0,16},{8,24},{16,0},{24,8},{32,48},{40,56},{48,32},{56,40},{64,80... | collective-permute-start | bytes 102152 | tf_op jit(solution)/shard_map/ppermute | solution.py:53
  48.7 3.3 %collective-permute-start.2 = (bf16[2,14,608]{2,1,0:T(8,128)(2,1)S(1)}, bf16[2,14,608]{2,1,0:T(8,128)(2,1)S(1)}, u32[]{:S(2)}, u32[]{:S(2)}) collective-permute-start(bf16[2,14,608]{2,1,0:T(8,128)(2,1)S(1)} %get-tuple-element.26), channel_id=1, source_target_pairs={{0,24},{8,0},{16,8},{24,16},{32,56},{40,32},{48,40},{56,48},{64,88... | collective-permute-start | bytes 102152 | tf_op jit(solution)/shard_map/ppermute | solution.py:53
  52.0 0.7 copy.75
  52.7 0.7 copy.76
  53.4 0.5 broadcast_in_dim.107
  53.9 3.4 %reduce.10 = bf16[8,28672]{1,0:T(8,128)(2,1)S(1)} reduce(bf16[8,1,28672]{2,1,0:T(2,128)(2,1)S(1)} %broadcast_in_dim.107, bf16[]{:T(256)} %broadcast.50), dimensions={1}, to_apply=%broadcast_in_dim.107.reduce_sub_computation | reduce | bytes 917506 | tf_op jit(solution)/shard_map/broadcast_in_dim | solution.py:78
  57.3 1.1 reshape.66
  58.4 4.8 %all-to-all-start.1 = ((bf16[8,2,14336]{2,1,0:T(2,128)(2,1)}), bf16[8,2,14336]{2,1,0:T(2,128)(2,1)}, u32[]{:S(2)}, u32[]{:S(2)}) async-start(bf16[8,2,14336]{2,1,0:T(2,128)(2,1)} %reshape.66), calls=%async_computation.1 | async-start | bytes 917504 | tf_op jit(solution)/shard_map/all_to_all | solution.py:79
  63.3 0.4 slice_reduce_fusion.3
  63.7 0.7 squeeze.35
  64.4 0.7 squeeze.33
  65.1 0.7 squeeze.31
  66.1 5.3 %collective-permute-start.3 = (bf16[4,2,14,608]{3,1,2,0:T(2,128)(2,1)S(1)}, bf16[4,2,14,608]{3,1,2,0:T(2,128)(2,1)S(1)}, u32[]{:S(2)}, u32[]{:S(2)}) collective-permute-start(bf16[4,2,14,608]{3,1,2,0:T(2,128)(2,1)S(1)} %copy_dynamic-update-slice_fusion), channel_id=1, source_target_pairs={{0,32},{8,40},{16,48},{24,56},{32,64},{40,72},{48,80},{56,88},{64,... | collective-permute-start | bytes 408584 | tf_op jit(solution)/shard_map/ppermute | solution.py:69
  71.4 1.9 %collective-permute-start.4 = (bf16[4,2,14,608]{3,1,2,0:T(2,128)(2,1)S(1)}, bf16[4,2,14,608]{3,1,2,0:T(2,128)(2,1)S(1)}, u32[]{:S(2)}, u32[]{:S(2)}) collective-permute-start(bf16[4,2,14,608]{3,1,2,0:T(2,128)(2,1)S(1)} %copy_dynamic-update-slice_fusion), channel_id=1, source_target_pairs={{0,480},{8,488},{16,496},{24,504},{32,0},{40,8},{48,16},{56,24},{6... | collective-permute-start | bytes 408584 | tf_op jit(solution)/shard_map/ppermute | solution.py:72
  73.3 1.2 broadcast_in_dim.84
  74.7 0.5 collective-permute-done.3
  75.2 3.9 %collective-permute-start.5 = (bf16[4,2,14,608]{3,1,2,0:T(2,128)(2,1)S(1)}, bf16[4,2,14,608]{3,1,2,0:T(2,128)(2,1)}, u32[]{:S(2)}, u32[]{:S(2)}) collective-permute-start(bf16[4,2,14,608]{3,1,2,0:T(2,128)(2,1)S(1)} %collective-permute-done.3), channel_id=1, source_target_pairs={{0,32},{8,40},{16,48},{24,56},{32,64},{40,72},{48,80},{56,88},{64,... | collective-permute-start | bytes 408584 | tf_op jit(solution)/shard_map/ppermute | solution.py:69
  79.1 3.1 %collective-permute-start.6 = (bf16[4,2,14,608]{3,1,2,0:T(2,128)(2,1)S(1)}, bf16[4,2,14,608]{3,1,2,0:T(2,128)(2,1)}, u32[]{:S(2)}, u32[]{:S(2)}) collective-permute-start(bf16[4,2,14,608]{3,1,2,0:T(2,128)(2,1)S(1)} %collective-permute-done.4), channel_id=1, source_target_pairs={{0,480},{8,488},{16,496},{24,504},{32,0},{40,8},{48,16},{56,24},{6... | collective-permute-start | bytes 408584 | tf_op jit(solution)/shard_map/ppermute | solution.py:72
  82.5 1.0 collective-permute-done.5
  83.5 2.7 %collective-permute-start.7 = (bf16[4,2,14,608]{3,1,2,0:T(2,128)(2,1)}, bf16[4,2,14,608]{3,1,2,0:T(2,128)(2,1)}, u32[]{:S(2)}, u32[]{:S(2)}) collective-permute-start(bf16[4,2,14,608]{3,1,2,0:T(2,128)(2,1)} %collective-permute-done.5), channel_id=1, source_target_pairs={{0,32},{8,40},{16,48},{24,56},{32,64},{40,72},{48,80},{56,88},{64,... | collective-permute-start | bytes 408584 | tf_op jit(solution)/shard_map/ppermute | solution.py:69
  86.2 4.6 %collective-permute-start.8 = (bf16[4,2,14,608]{3,1,2,0:T(2,128)(2,1)}, bf16[4,2,14,608]{3,1,2,0:T(2,128)(2,1)}, u32[]{:S(2)}, u32[]{:S(2)}) collective-permute-start(bf16[4,2,14,608]{3,1,2,0:T(2,128)(2,1)} %collective-permute-done.6), channel_id=1, source_target_pairs={{0,480},{8,488},{16,496},{24,504},{32,0},{40,8},{48,16},{56,24},{6... | collective-permute-start | bytes 408584 | tf_op jit(solution)/shard_map/ppermute | solution.py:72
  90.7 1.0 bitcast_dynamic-update-slice_fusion.12
  91.8 1.0 bitcast_dynamic-update-slice_fusion.11
  92.8 2.2 %reshape.67 = bf16[8,1,28672]{2,1,0:T(2,128)(2,1)S(1)} reshape(bf16[8,2,14336]{2,1,0:T(2,128)(2,1)} %all-to-all-done.1) | data formatting | bytes 917504
  95.0 3.5 %reduce.1 = bf16[8,28672]{1,0:T(8,128)(2,1)} reduce(bf16[8,1,28672]{2,1,0:T(2,128)(2,1)S(1)} %reshape.67, bf16[]{:T(256)} %constant.218), dimensions={1}, to_apply=%all_to_all.15.reduce_sub_computation | reduce | bytes 917506 | tf_op jit(solution)/shard_map/all_to_all | solution.py:79
  98.5 1.7 reshape.57
  100.2 0.8 fusion.10
  101.0 0.7 copy.74
  101.7 1.7 %squeeze.36 = bf16[64,896]{1,0:T(8,128)(2,1)} reshape(bf16[1,64,8,112]{3,2,1,0:T(8,128)(2,1)} %copy.74) | data formatting | bytes 229376 | tf_op jit(solution)/shard_map/squeeze | solution.py:83
  103.4 1.6 copy.73
  105.1 1.7 %squeeze.34 = bf16[64,896]{1,0:T(8,128)(2,1)} reshape(bf16[1,64,8,112]{3,2,1,0:T(8,128)(2,1)} %copy.73) | data formatting | bytes 229376 | tf_op jit(solution)/shard_map/squeeze | solution.py:83
  106.8 1.6 copy.72
  108.4 1.7 %squeeze.32 = bf16[64,896]{1,0:T(8,128)(2,1)} reshape(bf16[1,64,8,112]{3,2,1,0:T(8,128)(2,1)} %copy.72) | data formatting | bytes 229376 | tf_op jit(solution)/shard_map/squeeze | solution.py:83
  110.2 1.6 copy.71
  111.8 1.7 %squeeze.30 = bf16[64,896]{1,0:T(8,128)(2,1)} reshape(bf16[1,64,8,112]{3,2,1,0:T(8,128)(2,1)} %copy.71) | data formatting | bytes 229376 | tf_op jit(solution)/shard_map/squeeze | solution.py:83
  113.5 1.1 fusion.7
  114.7 1.1 fusion.6
  115.8 1.1 fusion.5
  117.0 2.2 %multiply_subtract_fusion = (f32[150,896]{1,0:T(8,128)}, f32[150,896]{1,0:T(8,128)}) fusion(f32[150,896]{1,0:T(8,128)S(1)} %copy-done.1, f32[150,896]{1,0:T(8,128)S(1)} %copy-done.2, f32[150,896]{1,0:T(8,128)S(1)} %fusion.7, f32[150,896]{1,0:T(8,128)S(1)} %fusion.6, f32[150,896]{1,0:T(8,128)S(1)} %fusion.5, bf16[150,64]{1,0:T(8,128)(2,1)S(1)} %squeeze.29, ...), kind=kOutput, calls=%fused_computation.12 | convolution fusion | flops 18816000 | bytes 3897088 | tf_op jit(solution)/shard_map/dot_general | solution.py:83
  119.2 1.9 %collective-permute-start.9 = (bf16[4,2,14,608]{3,1,2,0:T(2,128)(2,1)}, bf16[4,2,14,608]{3,1,2,0:T(2,128)(2,1)S(1)}, u32[]{:S(2)}, u32[]{:S(2)}) collective-permute-start(bf16[4,2,14,608]{3,1,2,0:T(2,128)(2,1)} %collective-permute-done.7), channel_id=1, source_target_pairs={{0,32},{8,40},{16,48},{24,56},{32,64},{40,72},{48,80},{56,88},{64,... | collective-permute-start | bytes 408584 | tf_op jit(solution)/shard_map/ppermute | solution.py:69
  121.1 5.1 %collective-permute-start.10 = (bf16[4,2,14,608]{3,1,2,0:T(2,128)(2,1)}, bf16[4,2,14,608]{3,1,2,0:T(2,128)(2,1)S(1)}, u32[]{:S(2)}, u32[]{:S(2)}) collective-permute-start(bf16[4,2,14,608]{3,1,2,0:T(2,128)(2,1)} %collective-permute-done.8), channel_id=1, source_target_pairs={{0,480},{8,488},{16,496},{24,504},{32,0},{40,8},{48,16},{56,24},{6... | collective-permute-start | bytes 408584 | tf_op jit(solution)/shard_map/ppermute | solution.py:72
  126.3 1.0 bitcast_dynamic-update-slice_fusion.10
  127.3 1.0 bitcast_dynamic-update-slice_fusion.9
  128.4 1.9 %collective-permute-start.11 = (bf16[4,2,14,608]{3,1,2,0:T(2,128)(2,1)S(1)}, bf16[4,2,14,608]{3,1,2,0:T(2,128)(2,1)S(1)}, u32[]{:S(2)}, u32[]{:S(2)}) collective-permute-start(bf16[4,2,14,608]{3,1,2,0:T(2,128)(2,1)S(1)} %collective-permute-done.9), channel_id=1, source_target_pairs={{0,32},{8,40},{16,48},{24,56},{32,64},{40,72},{48,80},{56,88},{64,... | collective-permute-start | bytes 408584 | tf_op jit(solution)/shard_map/ppermute | solution.py:69
  130.3 5.1 %collective-permute-start.12 = (bf16[4,2,14,608]{3,1,2,0:T(2,128)(2,1)S(1)}, bf16[4,2,14,608]{3,1,2,0:T(2,128)(2,1)S(1)}, u32[]{:S(2)}, u32[]{:S(2)}) collective-permute-start(bf16[4,2,14,608]{3,1,2,0:T(2,128)(2,1)S(1)} %collective-permute-done.10), channel_id=1, source_target_pairs={{0,480},{8,488},{16,496},{24,504},{32,0},{40,8},{48,16},{56,24},{6... | collective-permute-start | bytes 408584 | tf_op jit(solution)/shard_map/ppermute | solution.py:72
  135.7 0.9 collective-permute-done.11
  136.6 1.9 %collective-permute-start.13 = (bf16[4,2,14,608]{3,1,2,0:T(2,128)(2,1)S(1)}, bf16[4,2,14,608]{3,1,2,0:T(2,128)(2,1)S(1)}, u32[]{:S(2)}, u32[]{:S(2)}) collective-permute-start(bf16[4,2,14,608]{3,1,2,0:T(2,128)(2,1)S(1)} %collective-permute-done.11), channel_id=1, source_target_pairs={{0,32},{8,40},{16,48},{24,56},{32,64},{40,72},{48,80},{56,88},{64,... | collective-permute-start | bytes 408584 | tf_op jit(solution)/shard_map/ppermute | solution.py:69
  138.5 5.1 %collective-permute-start.14 = (bf16[4,2,14,608]{3,1,2,0:T(2,128)(2,1)S(1)}, bf16[4,2,14,608]{3,1,2,0:T(2,128)(2,1)S(1)}, u32[]{:S(2)}, u32[]{:S(2)}) collective-permute-start(bf16[4,2,14,608]{3,1,2,0:T(2,128)(2,1)S(1)} %collective-permute-done.12), channel_id=1, source_target_pairs={{0,480},{8,488},{16,496},{24,504},{32,0},{40,8},{48,16},{56,24},{6... | collective-permute-start | bytes 408584 | tf_op jit(solution)/shard_map/ppermute | solution.py:72
  143.9 0.9 collective-permute-done.13
  144.8 1.9 %collective-permute-start.15 = (bf16[4,2,14,608]{3,1,2,0:T(2,128)(2,1)S(1)}, bf16[4,2,14,608]{3,1,2,0:T(2,128)(2,1)S(1)}, u32[]{:S(2)}, u32[]{:S(2)}) collective-permute-start(bf16[4,2,14,608]{3,1,2,0:T(2,128)(2,1)S(1)} %collective-permute-done.13), channel_id=1, source_target_pairs={{0,32},{8,40},{16,48},{24,56},{32,64},{40,72},{48,80},{56,88},{64,... | collective-permute-start | bytes 408584 | tf_op jit(solution)/shard_map/ppermute | solution.py:69
  146.7 5.1 %collective-permute-start.16 = (bf16[4,2,14,608]{3,1,2,0:T(2,128)(2,1)S(1)}, bf16[4,2,14,608]{3,1,2,0:T(2,128)(2,1)S(1)}, u32[]{:S(2)}, u32[]{:S(2)}) collective-permute-start(bf16[4,2,14,608]{3,1,2,0:T(2,128)(2,1)S(1)} %collective-permute-done.14), channel_id=1, source_target_pairs={{0,480},{8,488},{16,496},{24,504},{32,0},{40,8},{48,16},{56,24},{6... | collective-permute-start | bytes 408584 | tf_op jit(solution)/shard_map/ppermute | solution.py:72
  152.1 1.1 collective-permute-done.15
  153.2 1.9 %collective-permute-start.17 = (bf16[4,2,14,608]{3,1,2,0:T(2,128)(2,1)S(1)}, bf16[4,2,14,608]{3,1,2,0:T(2,128)(2,1)S(1)}, u32[]{:S(2)}, u32[]{:S(2)}) collective-permute-start(bf16[4,2,14,608]{3,1,2,0:T(2,128)(2,1)S(1)} %collective-permute-done.15), channel_id=1, source_target_pairs={{0,32},{8,40},{16,48},{24,56},{32,64},{40,72},{48,80},{56,88},{64,... | collective-permute-start | bytes 408584 | tf_op jit(solution)/shard_map/ppermute | solution.py:69
  155.4 6.0 %collective-permute-done.17 = bf16[4,2,14,608]{3,1,2,0:T(2,128)(2,1)S(1)} collective-permute-done((bf16[4,2,14,608]{3,1,2,0:T(2,128)(2,1)S(1)}, bf16[4,2,14,608]{3,1,2,0:T(2,128)(2,1)S(1)}, u32[]{:S(2)}, u32[]{:S(2)}) %collective-permute-start.17) | collective-permute-done | bytes 136224 | tf_op jit(solution)/shard_map/ppermute | solution.py:69
  161.5 5.7 %copy.77 = bf16[2,896,608]{1,2,0:T(8,128)(2,1)} copy(bf16[2,896,608]{2,0,1:T(2,128)(2,1)S(1)} %bitcast.67) | data formatting | bytes 4358144
  (54 shorter events, 3.1 us)
Async XLA Ops:
  0.6 2.5 %copy-start = (bf16[1,64,896]{2,1,0:T(8,128)(2,1)S(1)}, bf16[1,64,896]{2,1,0:T(8,128)(2,1)}, u32[]{:S(2)}) copy-start(bf16[1,64,896]{2,1,0:T(8,128)(2,1)} %param.9) | copy-start | bytes 344068
  3.5 36.9 %copy-start.3 = (f32[2,14,608]{2,0,1:T(2,128)S(1)}, f32[2,14,608]{2,0,1:T(2,128)}, u32[]{:S(2)}) copy-start(f32[2,14,608]{2,0,1:T(2,128)} %param.11) | copy-start | bytes 204292
  3.5 36.9 %copy-start.4 = (f32[2,14,608]{2,0,1:T(2,128)S(1)}, f32[2,14,608]{2,0,1:T(2,128)}, u32[]{:S(2)}) copy-start(f32[2,14,608]{2,0,1:T(2,128)} %param.10) | copy-start | bytes 204292
  5.8 33.8 %all-to-all-start = ((bf16[4,2,16896]{2,1,0:T(2,128)(2,1)}), bf16[4,2,16896]{2,1,0:T(2,128)(2,1)S(1)}, u32[]{:S(2)}, u32[]{:S(2)}) async-start(bf16[4,2,16896]{2,1,0:T(2,128)(2,1)} %reshape.64), calls=%async_computation | async-start | bytes 540672 | tf_op jit(solution)/shard_map/all_to_all | solution.py:40
  40.4 25.5 %collective-permute-start = (bf16[2,14,608]{2,1,0:T(8,128)(2,1)S(1)}, bf16[2,14,608]{2,1,0:T(8,128)(2,1)S(1)}, u32[]{:S(2)}, u32[]{:S(2)}) collective-permute-start(bf16[2,14,608]{2,1,0:T(8,128)(2,1)S(1)} %get-tuple-element.26), channel_id=1, source_target_pairs={{0,8},{8,16},{16,24},{24,0},{32,40},{40,48},{48,56},{56,32},{64,72... | collective-permute-start | bytes 102152 | tf_op jit(solution)/shard_map/ppermute | solution.py:53
  43.9 22.0 %collective-permute-start.1 = (bf16[2,14,608]{2,1,0:T(8,128)(2,1)S(1)}, bf16[2,14,608]{2,1,0:T(8,128)(2,1)S(1)}, u32[]{:S(2)}, u32[]{:S(2)}) collective-permute-start(bf16[2,14,608]{2,1,0:T(8,128)(2,1)S(1)} %get-tuple-element.26), channel_id=1, source_target_pairs={{0,16},{8,24},{16,0},{24,8},{32,48},{40,56},{48,32},{56,40},{64,80... | collective-permute-start | bytes 102152 | tf_op jit(solution)/shard_map/ppermute | solution.py:53
  48.7 17.3 %collective-permute-start.2 = (bf16[2,14,608]{2,1,0:T(8,128)(2,1)S(1)}, bf16[2,14,608]{2,1,0:T(8,128)(2,1)S(1)}, u32[]{:S(2)}, u32[]{:S(2)}) collective-permute-start(bf16[2,14,608]{2,1,0:T(8,128)(2,1)S(1)} %get-tuple-element.26), channel_id=1, source_target_pairs={{0,24},{8,0},{16,8},{24,16},{32,56},{40,32},{48,40},{56,48},{64,88... | collective-permute-start | bytes 102152 | tf_op jit(solution)/shard_map/ppermute | solution.py:53
  58.4 34.4 %all-to-all-start.1 = ((bf16[8,2,14336]{2,1,0:T(2,128)(2,1)}), bf16[8,2,14336]{2,1,0:T(2,128)(2,1)}, u32[]{:S(2)}, u32[]{:S(2)}) async-start(bf16[8,2,14336]{2,1,0:T(2,128)(2,1)} %reshape.66), calls=%async_computation.1 | async-start | bytes 917504 | tf_op jit(solution)/shard_map/all_to_all | solution.py:79
  66.1 9.1 %collective-permute-start.3 = (bf16[4,2,14,608]{3,1,2,0:T(2,128)(2,1)S(1)}, bf16[4,2,14,608]{3,1,2,0:T(2,128)(2,1)S(1)}, u32[]{:S(2)}, u32[]{:S(2)}) collective-permute-start(bf16[4,2,14,608]{3,1,2,0:T(2,128)(2,1)S(1)} %copy_dynamic-update-slice_fusion), channel_id=1, source_target_pairs={{0,32},{8,40},{16,48},{24,56},{32,64},{40,72},{48,80},{56,88},{64,... | collective-permute-start | bytes 408584 | tf_op jit(solution)/shard_map/ppermute | solution.py:69
  71.4 7.7 %collective-permute-start.4 = (bf16[4,2,14,608]{3,1,2,0:T(2,128)(2,1)S(1)}, bf16[4,2,14,608]{3,1,2,0:T(2,128)(2,1)S(1)}, u32[]{:S(2)}, u32[]{:S(2)}) collective-permute-start(bf16[4,2,14,608]{3,1,2,0:T(2,128)(2,1)S(1)} %copy_dynamic-update-slice_fusion), channel_id=1, source_target_pairs={{0,480},{8,488},{16,496},{24,504},{32,0},{40,8},{48,16},{56,24},{6... | collective-permute-start | bytes 408584 | tf_op jit(solution)/shard_map/ppermute | solution.py:72
  75.2 8.3 %collective-permute-start.5 = (bf16[4,2,14,608]{3,1,2,0:T(2,128)(2,1)S(1)}, bf16[4,2,14,608]{3,1,2,0:T(2,128)(2,1)}, u32[]{:S(2)}, u32[]{:S(2)}) collective-permute-start(bf16[4,2,14,608]{3,1,2,0:T(2,128)(2,1)S(1)} %collective-permute-done.3), channel_id=1, source_target_pairs={{0,32},{8,40},{16,48},{24,56},{32,64},{40,72},{48,80},{56,88},{64,... | collective-permute-start | bytes 408584 | tf_op jit(solution)/shard_map/ppermute | solution.py:69
  79.1 7.1 %collective-permute-start.6 = (bf16[4,2,14,608]{3,1,2,0:T(2,128)(2,1)S(1)}, bf16[4,2,14,608]{3,1,2,0:T(2,128)(2,1)}, u32[]{:S(2)}, u32[]{:S(2)}) collective-permute-start(bf16[4,2,14,608]{3,1,2,0:T(2,128)(2,1)S(1)} %collective-permute-done.4), channel_id=1, source_target_pairs={{0,480},{8,488},{16,496},{24,504},{32,0},{40,8},{48,16},{56,24},{6... | collective-permute-start | bytes 408584 | tf_op jit(solution)/shard_map/ppermute | solution.py:72
  83.5 35.7 %collective-permute-start.7 = (bf16[4,2,14,608]{3,1,2,0:T(2,128)(2,1)}, bf16[4,2,14,608]{3,1,2,0:T(2,128)(2,1)}, u32[]{:S(2)}, u32[]{:S(2)}) collective-permute-start(bf16[4,2,14,608]{3,1,2,0:T(2,128)(2,1)} %collective-permute-done.5), channel_id=1, source_target_pairs={{0,32},{8,40},{16,48},{24,56},{32,64},{40,72},{48,80},{56,88},{64,... | collective-permute-start | bytes 408584 | tf_op jit(solution)/shard_map/ppermute | solution.py:69
  86.2 35.0 %collective-permute-start.8 = (bf16[4,2,14,608]{3,1,2,0:T(2,128)(2,1)}, bf16[4,2,14,608]{3,1,2,0:T(2,128)(2,1)}, u32[]{:S(2)}, u32[]{:S(2)}) collective-permute-start(bf16[4,2,14,608]{3,1,2,0:T(2,128)(2,1)} %collective-permute-done.6), channel_id=1, source_target_pairs={{0,480},{8,488},{16,496},{24,504},{32,0},{40,8},{48,16},{56,24},{6... | collective-permute-start | bytes 408584 | tf_op jit(solution)/shard_map/ppermute | solution.py:72
  101.0 16.0 %copy-start.1 = (f32[150,896]{1,0:T(8,128)S(1)}, f32[150,896]{1,0:T(8,128)}, u32[]{:S(2)}) copy-start(f32[150,896]{1,0:T(8,128)} %param.12) | copy-start | bytes 1612804
  101.0 16.0 %copy-start.2 = (f32[150,896]{1,0:T(8,128)S(1)}, f32[150,896]{1,0:T(8,128)}, u32[]{:S(2)}) copy-start(f32[150,896]{1,0:T(8,128)} %param.13) | copy-start | bytes 1612804
  119.2 9.1 %collective-permute-start.9 = (bf16[4,2,14,608]{3,1,2,0:T(2,128)(2,1)}, bf16[4,2,14,608]{3,1,2,0:T(2,128)(2,1)S(1)}, u32[]{:S(2)}, u32[]{:S(2)}) collective-permute-start(bf16[4,2,14,608]{3,1,2,0:T(2,128)(2,1)} %collective-permute-done.7), channel_id=1, source_target_pairs={{0,32},{8,40},{16,48},{24,56},{32,64},{40,72},{48,80},{56,88},{64,... | collective-permute-start | bytes 408584 | tf_op jit(solution)/shard_map/ppermute | solution.py:69
  121.1 9.2 %collective-permute-start.10 = (bf16[4,2,14,608]{3,1,2,0:T(2,128)(2,1)}, bf16[4,2,14,608]{3,1,2,0:T(2,128)(2,1)S(1)}, u32[]{:S(2)}, u32[]{:S(2)}) collective-permute-start(bf16[4,2,14,608]{3,1,2,0:T(2,128)(2,1)} %collective-permute-done.8), channel_id=1, source_target_pairs={{0,480},{8,488},{16,496},{24,504},{32,0},{40,8},{48,16},{56,24},{6... | collective-permute-start | bytes 408584 | tf_op jit(solution)/shard_map/ppermute | solution.py:72
  128.4 8.2 %collective-permute-start.11 = (bf16[4,2,14,608]{3,1,2,0:T(2,128)(2,1)S(1)}, bf16[4,2,14,608]{3,1,2,0:T(2,128)(2,1)S(1)}, u32[]{:S(2)}, u32[]{:S(2)}) collective-permute-start(bf16[4,2,14,608]{3,1,2,0:T(2,128)(2,1)S(1)} %collective-permute-done.9), channel_id=1, source_target_pairs={{0,32},{8,40},{16,48},{24,56},{32,64},{40,72},{48,80},{56,88},{64,... | collective-permute-start | bytes 408584 | tf_op jit(solution)/shard_map/ppermute | solution.py:69
  130.3 8.2 %collective-permute-start.12 = (bf16[4,2,14,608]{3,1,2,0:T(2,128)(2,1)S(1)}, bf16[4,2,14,608]{3,1,2,0:T(2,128)(2,1)S(1)}, u32[]{:S(2)}, u32[]{:S(2)}) collective-permute-start(bf16[4,2,14,608]{3,1,2,0:T(2,128)(2,1)S(1)} %collective-permute-done.10), channel_id=1, source_target_pairs={{0,480},{8,488},{16,496},{24,504},{32,0},{40,8},{48,16},{56,24},{6... | collective-permute-start | bytes 408584 | tf_op jit(solution)/shard_map/ppermute | solution.py:72
  136.6 8.2 %collective-permute-start.13 = (bf16[4,2,14,608]{3,1,2,0:T(2,128)(2,1)S(1)}, bf16[4,2,14,608]{3,1,2,0:T(2,128)(2,1)S(1)}, u32[]{:S(2)}, u32[]{:S(2)}) collective-permute-start(bf16[4,2,14,608]{3,1,2,0:T(2,128)(2,1)S(1)} %collective-permute-done.11), channel_id=1, source_target_pairs={{0,32},{8,40},{16,48},{24,56},{32,64},{40,72},{48,80},{56,88},{64,... | collective-permute-start | bytes 408584 | tf_op jit(solution)/shard_map/ppermute | solution.py:69
  138.5 8.2 %collective-permute-start.14 = (bf16[4,2,14,608]{3,1,2,0:T(2,128)(2,1)S(1)}, bf16[4,2,14,608]{3,1,2,0:T(2,128)(2,1)S(1)}, u32[]{:S(2)}, u32[]{:S(2)}) collective-permute-start(bf16[4,2,14,608]{3,1,2,0:T(2,128)(2,1)S(1)} %collective-permute-done.12), channel_id=1, source_target_pairs={{0,480},{8,488},{16,496},{24,504},{32,0},{40,8},{48,16},{56,24},{6... | collective-permute-start | bytes 408584 | tf_op jit(solution)/shard_map/ppermute | solution.py:72
  144.8 8.5 %collective-permute-start.15 = (bf16[4,2,14,608]{3,1,2,0:T(2,128)(2,1)S(1)}, bf16[4,2,14,608]{3,1,2,0:T(2,128)(2,1)S(1)}, u32[]{:S(2)}, u32[]{:S(2)}) collective-permute-start(bf16[4,2,14,608]{3,1,2,0:T(2,128)(2,1)S(1)} %collective-permute-done.13), channel_id=1, source_target_pairs={{0,32},{8,40},{16,48},{24,56},{32,64},{40,72},{48,80},{56,88},{64,... | collective-permute-start | bytes 408584 | tf_op jit(solution)/shard_map/ppermute | solution.py:69
  146.7 8.6 %collective-permute-start.16 = (bf16[4,2,14,608]{3,1,2,0:T(2,128)(2,1)S(1)}, bf16[4,2,14,608]{3,1,2,0:T(2,128)(2,1)S(1)}, u32[]{:S(2)}, u32[]{:S(2)}) collective-permute-start(bf16[4,2,14,608]{3,1,2,0:T(2,128)(2,1)S(1)} %collective-permute-done.14), channel_id=1, source_target_pairs={{0,480},{8,488},{16,496},{24,504},{32,0},{40,8},{48,16},{56,24},{6... | collective-permute-start | bytes 408584 | tf_op jit(solution)/shard_map/ppermute | solution.py:72
  153.2 8.2 %collective-permute-start.17 = (bf16[4,2,14,608]{3,1,2,0:T(2,128)(2,1)S(1)}, bf16[4,2,14,608]{3,1,2,0:T(2,128)(2,1)S(1)}, u32[]{:S(2)}, u32[]{:S(2)}) collective-permute-start(bf16[4,2,14,608]{3,1,2,0:T(2,128)(2,1)S(1)} %collective-permute-done.15), channel_id=1, source_target_pairs={{0,32},{8,40},{16,48},{24,56},{32,64},{40,72},{48,80},{56,88},{64,... | collective-permute-start | bytes 408584 | tf_op jit(solution)/shard_map/ppermute | solution.py:69

commit v3 on v2

--- a/solution.py
+++ b/solution.py
@@ -33,9 +33,9 @@
     send_left = left.reshape(groups, nleft)
     right = emb_right[0]
     rank, width = right.shape
-    chunk = width // tensors
-    rchunk = lax.dynamic_slice_in_dim(right, ti * chunk, chunk, axis=1)
-    send_right = jnp.broadcast_to(rchunk.reshape(1, rank * chunk), (groups, rank * chunk))
+    chunk = rank // tensors
+    rchunk = lax.dynamic_slice_in_dim(right, ti * chunk, chunk, axis=0)
+    send_right = jnp.broadcast_to(rchunk.reshape(1, chunk * width), (groups, chunk * width))
     send = jnp.concatenate([send_layer, send_left, send_right], axis=1)
     recv = lax.all_to_all(send, "group", 0, 0, tiled=True)
 
@@ -74,10 +74,8 @@
     layer_blocks = jnp.moveaxis(out, 2, 0).reshape(piece.shape[0], -1, piece.shape[2])
 
     lefts = recv[:, nlayer:nlayer + nleft].reshape((groups,) + left.shape[1:])
-    rchunks = recv[:, nlayer + nleft:].reshape(groups, rank, chunk)
-    rsend = jnp.broadcast_to(rchunks.reshape(1, -1), (tensors, rchunks.size))
-    rgot = lax.all_to_all(rsend, "tensor", 0, 0, tiled=True)
-    full = jnp.moveaxis(rgot.reshape(tensors, groups, rank, chunk), 0, 2).reshape(groups, rank, width)
+    rchunks = recv[:, nlayer + nleft:].reshape(groups, chunk, width)
+    full = lax.all_gather(rchunks, "tensor", axis=1, tiled=True)
     total = jnp.zeros(emb_weight.shape, f32)
     for g in range(groups):
         product = jnp.dot(lefts[g], full[g], preferred_element_type=f32).astype(bf16)

time: 169 us -> 148 us (0.88)
  local copies, waits for them, and re-layouts: 40 us -> 19.3 us
  blocking collectives: 0 us -> 13.1 us
  other arithmetic: 8.3 us -> 1.36 us
  starting transfers between devices: 83 us -> 78.3 us
  matrix products: 5.63 us -> 1.98 us
  waiting for transfers between devices: 29.1 us -> 31.9 us
    all_gather x0 -> x1, blocking collectives: none -> 13.1 us  [on_device(): full = lax.all_gather(rchunks, 'tensor', axis=1, tiled=True)]
    squeeze x4 -> x0, local copies, waits for them, and re-layouts: 6.89 us -> none  [on_device(): full[g]]
    slice x5 -> x1, local copies, waits for them, and re-layouts: 6.43 us -> 0.02 us  [on_device(): rchunks = recv[:, nlayer + nleft:].reshape(groups, chunk, width)]
    all_to_all x1 -> x0, starting transfers between devices: 4.78 us -> none  [on_device(): rgot = lax.all_to_all(rsend, 'tensor', 0, 0, tiled=True)]
    dot_general x4, matrix products: 5.63 us -> 1.98 us  [on_device(): jnp.dot(lefts[g], full[g], preferred_element_type=f32).astype(bf16)]
    all_to_all x1 -> x0, other arithmetic: 3.53 us -> none  [on_device(): rgot = lax.all_to_all(rsend, 'tensor', 0, 0, tiled=True)]
    broadcast_in_dim x1 -> x0, other arithmetic: 3.41 us -> none  [on_device(): rsend = jnp.broadcast_to(rchunks.reshape(1, -1), (tensors, rchunks.size))]
    unnamed x21 -> x18, local copies, waits for them, and re-layouts: 12.7 us -> 9.4 us
  transfers between devices with their start and end apart: 20 -> 19, of which waited for: 7 -> 9; matrix products, arithmetic and copies ran while one was open for 25% -> 7% of each run, Pallas kernels for 0% -> 0%
where the time goes in v3:
time: 148 us; the launch traced here: 147 us
  starting transfers between devices  78.3 us (53%)
  waiting for transfers between devices  31.9 us (22%)
  local copies, waits for them, and re-layouts  19.3 us (13%)
  blocking collectives  13.1 us (9%)
  matrix products  1.98 us (1%)
    ppermute x7, starting transfers between devices, on_device(): bwd = lax.ppermute(bwd, ('group', 'shard'), zshift(-1))  30.4 us
    ppermute x8, starting transfers between devices, on_device(): fwd = lax.ppermute(fwd, ('group', 'shard'), zshift(1))  21.3 us
    all_to_all x1, waiting for transfers between devices, on_device(): recv = lax.all_to_all(send, 'group', 0, 0, tiled=True)  18.7 us
    all_to_all x1, starting transfers between devices, on_device(): recv = lax.all_to_all(send, 'group', 0, 0, tiled=True)  15.1 us
    ppermute x8, waiting for transfers between devices, on_device(): fwd = lax.ppermute(fwd, ('group', 'shard'), zshift(1))  13.2 us
    all_gather x1, blocking collectives, on_device(): full = lax.all_gather(rchunks, 'tensor', axis=1, tiled=True)  13.1 us
    ppermute x3, starting transfers between devices, on_device(): got = lax.ppermute(piece, 'shard', pairs)  11.6 us
    unnamed x18, local copies, waits for them, and re-layouts  9.4 us
  transfers between devices with their start and end apart: 19, of which 9 were waited for; matrix products, arithmetic and copies ran while one was open for 7% of the time, Pallas kernels for 0%

profile of v3, /device:TPU:6, one launch (start us, length us, event | category | flops | bytes accessed | tf_op | source)
XLA Modules:
  0.0 147.2 jit_solution(18048087015638535004)
XLA Ops:
  0.7 1.1 copy.55
  1.8 0.1 reshape_squeeze.3
  1.9 0.9 copy.54
  2.8 0.3 reshape.37
  3.2 0.2 maximum_bitcast_fusion
  3.4 0.5 broadcast.46
  3.9 1.0 reduce.8
  4.9 0.8 reshape.45
  5.7 15.1 %all-to-all-start = ((bf16[4,2,16896]{2,1,0:T(2,128)(2,1)}), bf16[4,2,16896]{2,1,0:T(2,128)(2,1)S(1)}, u32[]{:S(2)}, u32[]{:S(2)}) async-start(bf16[4,2,16896]{2,1,0:T(2,128)(2,1)} %reshape.45), calls=%async_computation | async-start | bytes 540672 | tf_op jit(solution)/shard_map/all_to_all | solution.py:40
  20.8 18.7 %all-to-all-done = bf16[4,2,16896]{2,1,0:T(2,128)(2,1)S(1)} async-done(((bf16[4,2,16896]{2,1,0:T(2,128)(2,1)}), bf16[4,2,16896]{2,1,0:T(2,128)(2,1)S(1)}, u32[]{:S(2)}, u32[]{:S(2)}) %all-to-all-start) | async-done | bytes 270368 | tf_op jit(solution)/shard_map/all_to_all | solution.py:40
  39.5 0.2 reshape.46
  39.8 0.1 copy.82
  39.9 0.2 convert_reduce_fusion
  40.3 3.5 %collective-permute-start = (bf16[2,14,608]{2,1,0:T(8,128)(2,1)S(1)}, bf16[2,14,608]{2,1,0:T(8,128)(2,1)}, u32[]{:S(2)}, u32[]{:S(2)}) collective-permute-start(bf16[2,14,608]{2,1,0:T(8,128)(2,1)S(1)} %get-tuple-element.26), channel_id=1, source_target_pairs={{0,8},{8,16},{16,24},{24,0},{32,40},{40,48},{48,56},{56,32},{64,72... | collective-permute-start | bytes 102152 | tf_op jit(solution)/shard_map/ppermute | solution.py:53
  43.8 4.8 %collective-permute-start.1 = (bf16[2,14,608]{2,1,0:T(8,128)(2,1)S(1)}, bf16[2,14,608]{2,1,0:T(8,128)(2,1)}, u32[]{:S(2)}, u32[]{:S(2)}) collective-permute-start(bf16[2,14,608]{2,1,0:T(8,128)(2,1)S(1)} %get-tuple-element.26), channel_id=1, source_target_pairs={{0,16},{8,24},{16,0},{24,8},{32,48},{40,56},{48,32},{56,40},{64,80... | collective-permute-start | bytes 102152 | tf_op jit(solution)/shard_map/ppermute | solution.py:53
  48.6 3.3 %collective-permute-start.2 = (bf16[2,14,608]{2,1,0:T(8,128)(2,1)S(1)}, bf16[2,14,608]{2,1,0:T(8,128)(2,1)}, u32[]{:S(2)}, u32[]{:S(2)}) collective-permute-start(bf16[2,14,608]{2,1,0:T(8,128)(2,1)S(1)} %get-tuple-element.26), channel_id=1, source_target_pairs={{0,24},{8,0},{16,8},{24,16},{32,56},{40,32},{48,40},{56,48},{64,88... | collective-permute-start | bytes 102152 | tf_op jit(solution)/shard_map/ppermute | solution.py:53
  51.9 1.0 slice_reduce_fusion.3
  53.0 13.1 %all_gather.3 = bf16[4,64,896]{2,1,0:T(8,128)(2,1)S(1)} all-gather(bf16[4,8,896]{2,1,0:T(8,128)(2,1)S(1)} %bitcast.74), channel_id=1, replica_groups=mesh['group'=4,'shard'=16,'tensor'=8] {'tensor'}, dimensions={1}, use_global_device_ids=true | all-gather | bytes 516096 | tf_op jit(solution)/shard_map/all_gather | solution.py:78
  66.2 0.2 fusion.7
  66.4 0.2 fusion.6
  66.7 0.2 fusion.5
  66.9 0.8 squeeze.29
  67.8 1.4 multiply_subtract_fusion
  69.2 0.7 copy.63
  69.9 0.7 copy.64
  70.6 0.8 copy_dynamic-update-slice_fusion.2
  71.4 0.8 copy_dynamic-update-slice_fusion.1
  72.2 0.8 copy_dynamic-update-slice_fusion
  73.1 5.3 %collective-permute-start.3 = (bf16[4,2,14,608]{3,1,2,0:T(2,128)(2,1)S(1)}, bf16[4,2,14,608]{3,1,2,0:T(2,128)(2,1)S(1)}, u32[]{:S(2)}, u32[]{:S(2)}) collective-permute-start(bf16[4,2,14,608]{3,1,2,0:T(2,128)(2,1)S(1)} %copy_dynamic-update-slice_fusion), channel_id=1, source_target_pairs={{0,32},{8,40},{16,48},{24,56},{32,64},{40,72},{48,80},{56,88},{64,... | collective-permute-start | bytes 408584 | tf_op jit(solution)/shard_map/ppermute | solution.py:69
  78.4 1.9 %collective-permute-start.4 = (bf16[4,2,14,608]{3,1,2,0:T(2,128)(2,1)S(1)}, bf16[4,2,14,608]{3,1,2,0:T(2,128)(2,1)S(1)}, u32[]{:S(2)}, u32[]{:S(2)}) collective-permute-start(bf16[4,2,14,608]{3,1,2,0:T(2,128)(2,1)S(1)} %copy_dynamic-update-slice_fusion), channel_id=1, source_target_pairs={{0,480},{8,488},{16,496},{24,504},{32,0},{40,8},{48,16},{56,24},{6... | collective-permute-start | bytes 408584 | tf_op jit(solution)/shard_map/ppermute | solution.py:72
  80.3 1.2 broadcast_in_dim.77
  81.5 0.1 bitcast_dynamic-update-slice_fusion.15
  81.7 0.7 collective-permute-done.3
  82.4 3.9 %collective-permute-start.5 = (bf16[4,2,14,608]{3,1,2,0:T(2,128)(2,1)S(1)}, bf16[4,2,14,608]{3,1,2,0:T(2,128)(2,1)S(1)}, u32[]{:S(2)}, u32[]{:S(2)}) collective-permute-start(bf16[4,2,14,608]{3,1,2,0:T(2,128)(2,1)S(1)} %collective-permute-done.3), channel_id=1, source_target_pairs={{0,32},{8,40},{16,48},{24,56},{32,64},{40,72},{48,80},{56,88},{64,... | collective-permute-start | bytes 408584 | tf_op jit(solution)/shard_map/ppermute | solution.py:69
  86.3 3.1 %collective-permute-start.6 = (bf16[4,2,14,608]{3,1,2,0:T(2,128)(2,1)S(1)}, bf16[4,2,14,608]{3,1,2,0:T(2,128)(2,1)S(1)}, u32[]{:S(2)}, u32[]{:S(2)}) collective-permute-start(bf16[4,2,14,608]{3,1,2,0:T(2,128)(2,1)S(1)} %collective-permute-done.4), channel_id=1, source_target_pairs={{0,480},{8,488},{16,496},{24,504},{32,0},{40,8},{48,16},{56,24},{6... | collective-permute-start | bytes 408584 | tf_op jit(solution)/shard_map/ppermute | solution.py:72
  89.6 0.1 bitcast_dynamic-update-slice_fusion.13
  89.7 1.1 collective-permute-done.5
  90.9 2.5 %collective-permute-start.7 = (bf16[4,2,14,608]{3,1,2,0:T(2,128)(2,1)S(1)}, bf16[4,2,14,608]{3,1,2,0:T(2,128)(2,1)S(1)}, u32[]{:S(2)}, u32[]{:S(2)}) collective-permute-start(bf16[4,2,14,608]{3,1,2,0:T(2,128)(2,1)S(1)} %collective-permute-done.5), channel_id=1, source_target_pairs={{0,32},{8,40},{16,48},{24,56},{32,64},{40,72},{48,80},{56,88},{64,... | collective-permute-start | bytes 408584 | tf_op jit(solution)/shard_map/ppermute | solution.py:69
  93.4 4.5 %collective-permute-start.8 = (bf16[4,2,14,608]{3,1,2,0:T(2,128)(2,1)S(1)}, bf16[4,2,14,608]{3,1,2,0:T(2,128)(2,1)S(1)}, u32[]{:S(2)}, u32[]{:S(2)}) collective-permute-start(bf16[4,2,14,608]{3,1,2,0:T(2,128)(2,1)S(1)} %collective-permute-done.6), channel_id=1, source_target_pairs={{0,480},{8,488},{16,496},{24,504},{32,0},{40,8},{48,16},{56,24},{6... | collective-permute-start | bytes 408584 | tf_op jit(solution)/shard_map/ppermute | solution.py:72
  97.9 0.1 bitcast_dynamic-update-slice_fusion.12
  98.2 0.9 collective-permute-done.7
  99.1 1.9 %collective-permute-start.9 = (bf16[4,2,14,608]{3,1,2,0:T(2,128)(2,1)S(1)}, bf16[4,2,14,608]{3,1,2,0:T(2,128)(2,1)S(1)}, u32[]{:S(2)}, u32[]{:S(2)}) collective-permute-start(bf16[4,2,14,608]{3,1,2,0:T(2,128)(2,1)S(1)} %collective-permute-done.7), channel_id=1, source_target_pairs={{0,32},{8,40},{16,48},{24,56},{32,64},{40,72},{48,80},{56,88},{64,... | collective-permute-start | bytes 408584 | tf_op jit(solution)/shard_map/ppermute | solution.py:69
  101.0 5.1 %collective-permute-start.10 = (bf16[4,2,14,608]{3,1,2,0:T(2,128)(2,1)S(1)}, bf16[4,2,14,608]{3,1,2,0:T(2,128)(2,1)S(1)}, u32[]{:S(2)}, u32[]{:S(2)}) collective-permute-start(bf16[4,2,14,608]{3,1,2,0:T(2,128)(2,1)S(1)} %collective-permute-done.8), channel_id=1, source_target_pairs={{0,480},{8,488},{16,496},{24,504},{32,0},{40,8},{48,16},{56,24},{6... | collective-permute-start | bytes 408584 | tf_op jit(solution)/shard_map/ppermute | solution.py:72
  106.1 0.1 bitcast_dynamic-update-slice_fusion.10
  106.3 0.1 bitcast_dynamic-update-slice_fusion.9
  106.4 0.9 collective-permute-done.9
  107.2 1.9 %collective-permute-start.11 = (bf16[4,2,14,608]{3,1,2,0:T(2,128)(2,1)S(1)}, bf16[4,2,14,608]{3,1,2,0:T(2,128)(2,1)S(1)}, u32[]{:S(2)}, u32[]{:S(2)}) collective-permute-start(bf16[4,2,14,608]{3,1,2,0:T(2,128)(2,1)S(1)} %collective-permute-done.9), channel_id=1, source_target_pairs={{0,32},{8,40},{16,48},{24,56},{32,64},{40,72},{48,80},{56,88},{64,... | collective-permute-start | bytes 408584 | tf_op jit(solution)/shard_map/ppermute | solution.py:69
  109.2 5.1 %collective-permute-start.12 = (bf16[4,2,14,608]{3,1,2,0:T(2,128)(2,1)S(1)}, bf16[4,2,14,608]{3,1,2,0:T(2,128)(2,1)S(1)}, u32[]{:S(2)}, u32[]{:S(2)}) collective-permute-start(bf16[4,2,14,608]{3,1,2,0:T(2,128)(2,1)S(1)} %collective-permute-done.10), channel_id=1, source_target_pairs={{0,480},{8,488},{16,496},{24,504},{32,0},{40,8},{48,16},{56,24},{6... | collective-permute-start | bytes 408584 | tf_op jit(solution)/shard_map/ppermute | solution.py:72
  114.3 0.1 bitcast_dynamic-update-slice_fusion.8
  114.6 0.9 collective-permute-done.11
  115.4 1.9 %collective-permute-start.13 = (bf16[4,2,14,608]{3,1,2,0:T(2,128)(2,1)S(1)}, bf16[4,2,14,608]{3,1,2,0:T(2,128)(2,1)S(1)}, u32[]{:S(2)}, u32[]{:S(2)}) collective-permute-start(bf16[4,2,14,608]{3,1,2,0:T(2,128)(2,1)S(1)} %collective-permute-done.11), channel_id=1, source_target_pairs={{0,32},{8,40},{16,48},{24,56},{32,64},{40,72},{48,80},{56,88},{64,... | collective-permute-start | bytes 408584 | tf_op jit(solution)/shard_map/ppermute | solution.py:69
  117.4 5.1 %collective-permute-start.14 = (bf16[4,2,14,608]{3,1,2,0:T(2,128)(2,1)S(1)}, bf16[4,2,14,608]{3,1,2,0:T(2,128)(2,1)S(1)}, u32[]{:S(2)}, u32[]{:S(2)}) collective-permute-start(bf16[4,2,14,608]{3,1,2,0:T(2,128)(2,1)S(1)} %collective-permute-done.12), channel_id=1, source_target_pairs={{0,480},{8,488},{16,496},{24,504},{32,0},{40,8},{48,16},{56,24},{6... | collective-permute-start | bytes 408584 | tf_op jit(solution)/shard_map/ppermute | solution.py:72
  122.5 0.1 bitcast_dynamic-update-slice_fusion.6
  122.6 0.1 bitcast_dynamic-update-slice_fusion.5
  122.8 0.9 collective-permute-done.13
  123.7 1.9 %collective-permute-start.15 = (bf16[4,2,14,608]{3,1,2,0:T(2,128)(2,1)S(1)}, bf16[4,2,14,608]{3,1,2,0:T(2,128)(2,1)S(1)}, u32[]{:S(2)}, u32[]{:S(2)}) collective-permute-start(bf16[4,2,14,608]{3,1,2,0:T(2,128)(2,1)S(1)} %collective-permute-done.13), channel_id=1, source_target_pairs={{0,32},{8,40},{16,48},{24,56},{32,64},{40,72},{48,80},{56,88},{64,... | collective-permute-start | bytes 408584 | tf_op jit(solution)/shard_map/ppermute | solution.py:69
  125.6 5.4 %collective-permute-start.16 = (bf16[4,2,14,608]{3,1,2,0:T(2,128)(2,1)S(1)}, bf16[4,2,14,608]{3,1,2,0:T(2,128)(2,1)S(1)}, u32[]{:S(2)}, u32[]{:S(2)}) collective-permute-start(bf16[4,2,14,608]{3,1,2,0:T(2,128)(2,1)S(1)} %collective-permute-done.14), channel_id=1, source_target_pairs={{0,480},{8,488},{16,496},{24,504},{32,0},{40,8},{48,16},{56,24},{6... | collective-permute-start | bytes 408584 | tf_op jit(solution)/shard_map/ppermute | solution.py:72
  131.0 0.1 bitcast_dynamic-update-slice_fusion.4
  131.2 0.1 bitcast_dynamic-update-slice_fusion.3
  131.3 1.8 %collective-permute-done.15 = bf16[4,2,14,608]{3,1,2,0:T(2,128)(2,1)S(1)} collective-permute-done((bf16[4,2,14,608]{3,1,2,0:T(2,128)(2,1)S(1)}, bf16[4,2,14,608]{3,1,2,0:T(2,128)(2,1)S(1)}, u32[]{:S(2)}, u32[]{:S(2)}) %collective-permute-start.15) | collective-permute-done | bytes 136224 | tf_op jit(solution)/shard_map/ppermute | solution.py:69
  133.1 1.9 %collective-permute-start.17 = (bf16[4,2,14,608]{3,1,2,0:T(2,128)(2,1)S(1)}, bf16[4,2,14,608]{3,1,2,0:T(2,128)(2,1)S(1)}, u32[]{:S(2)}, u32[]{:S(2)}) collective-permute-start(bf16[4,2,14,608]{3,1,2,0:T(2,128)(2,1)S(1)} %collective-permute-done.15), channel_id=1, source_target_pairs={{0,32},{8,40},{16,48},{24,56},{32,64},{40,72},{48,80},{56,88},{64,... | collective-permute-start | bytes 408584 | tf_op jit(solution)/shard_map/ppermute | solution.py:69
  135.2 0.1 bitcast_dynamic-update-slice_fusion.1
  135.3 6.0 %collective-permute-done.17 = bf16[4,2,14,608]{3,1,2,0:T(2,128)(2,1)S(1)} collective-permute-done((bf16[4,2,14,608]{3,1,2,0:T(2,128)(2,1)S(1)}, bf16[4,2,14,608]{3,1,2,0:T(2,128)(2,1)S(1)}, u32[]{:S(2)}, u32[]{:S(2)}) %collective-permute-start.17) | collective-permute-done | bytes 136224 | tf_op jit(solution)/shard_map/ppermute | solution.py:69
  141.4 5.7 %copy.65 = bf16[2,896,608]{1,2,0:T(8,128)(2,1)} copy(bf16[2,896,608]{2,0,1:T(2,128)(2,1)S(1)} %bitcast.69) | data formatting | bytes 4358144
  (38 shorter events, 1.3 us)
Async XLA Ops:
  0.6 2.5 %copy-start = (bf16[1,64,896]{2,1,0:T(8,128)(2,1)S(1)}, bf16[1,64,896]{2,1,0:T(8,128)(2,1)}, u32[]{:S(2)}) copy-start(bf16[1,64,896]{2,1,0:T(8,128)(2,1)} %param.9) | copy-start | bytes 344068
  3.4 36.9 %copy-start.3 = (f32[2,14,608]{2,0,1:T(2,128)S(1)}, f32[2,14,608]{2,0,1:T(2,128)}, u32[]{:S(2)}) copy-start(f32[2,14,608]{2,0,1:T(2,128)} %param.11) | copy-start | bytes 204292
  3.4 36.9 %copy-start.4 = (f32[2,14,608]{2,0,1:T(2,128)S(1)}, f32[2,14,608]{2,0,1:T(2,128)}, u32[]{:S(2)}) copy-start(f32[2,14,608]{2,0,1:T(2,128)} %param.10) | copy-start | bytes 204292
  5.7 33.8 %all-to-all-start = ((bf16[4,2,16896]{2,1,0:T(2,128)(2,1)}), bf16[4,2,16896]{2,1,0:T(2,128)(2,1)S(1)}, u32[]{:S(2)}, u32[]{:S(2)}) async-start(bf16[4,2,16896]{2,1,0:T(2,128)(2,1)} %reshape.45), calls=%async_computation | async-start | bytes 540672 | tf_op jit(solution)/shard_map/all_to_all | solution.py:40
  39.9 27.8 %copy-start.1 = (f32[150,896]{1,0:T(8,128)S(1)}, f32[150,896]{1,0:T(8,128)}, u32[]{:S(2)}) copy-start(f32[150,896]{1,0:T(8,128)} %param.12) | copy-start | bytes 1612804
  39.9 27.8 %copy-start.2 = (f32[150,896]{1,0:T(8,128)S(1)}, f32[150,896]{1,0:T(8,128)}, u32[]{:S(2)}) copy-start(f32[150,896]{1,0:T(8,128)} %param.13) | copy-start | bytes 1612804
  40.3 30.3 %collective-permute-start = (bf16[2,14,608]{2,1,0:T(8,128)(2,1)S(1)}, bf16[2,14,608]{2,1,0:T(8,128)(2,1)}, u32[]{:S(2)}, u32[]{:S(2)}) collective-permute-start(bf16[2,14,608]{2,1,0:T(8,128)(2,1)S(1)} %get-tuple-element.26), channel_id=1, source_target_pairs={{0,8},{8,16},{16,24},{24,0},{32,40},{40,48},{48,56},{56,32},{64,72... | collective-permute-start | bytes 102152 | tf_op jit(solution)/shard_map/ppermute | solution.py:53
  43.8 27.6 %collective-permute-start.1 = (bf16[2,14,608]{2,1,0:T(8,128)(2,1)S(1)}, bf16[2,14,608]{2,1,0:T(8,128)(2,1)}, u32[]{:S(2)}, u32[]{:S(2)}) collective-permute-start(bf16[2,14,608]{2,1,0:T(8,128)(2,1)S(1)} %get-tuple-element.26), channel_id=1, source_target_pairs={{0,16},{8,24},{16,0},{24,8},{32,48},{40,56},{48,32},{56,40},{64,80... | collective-permute-start | bytes 102152 | tf_op jit(solution)/shard_map/ppermute | solution.py:53
  48.6 23.6 %collective-permute-start.2 = (bf16[2,14,608]{2,1,0:T(8,128)(2,1)S(1)}, bf16[2,14,608]{2,1,0:T(8,128)(2,1)}, u32[]{:S(2)}, u32[]{:S(2)}) collective-permute-start(bf16[2,14,608]{2,1,0:T(8,128)(2,1)S(1)} %get-tuple-element.26), channel_id=1, source_target_pairs={{0,24},{8,0},{16,8},{24,16},{32,56},{40,32},{48,40},{56,48},{64,88... | collective-permute-start | bytes 102152 | tf_op jit(solution)/shard_map/ppermute | solution.py:53
  73.1 9.3 %collective-permute-start.3 = (bf16[4,2,14,608]{3,1,2,0:T(2,128)(2,1)S(1)}, bf16[4,2,14,608]{3,1,2,0:T(2,128)(2,1)S(1)}, u32[]{:S(2)}, u32[]{:S(2)}) collective-permute-start(bf16[4,2,14,608]{3,1,2,0:T(2,128)(2,1)S(1)} %copy_dynamic-update-slice_fusion), channel_id=1, source_target_pairs={{0,32},{8,40},{16,48},{24,56},{32,64},{40,72},{48,80},{56,88},{64,... | collective-permute-start | bytes 408584 | tf_op jit(solution)/shard_map/ppermute | solution.py:69
  78.4 7.9 %collective-permute-start.4 = (bf16[4,2,14,608]{3,1,2,0:T(2,128)(2,1)S(1)}, bf16[4,2,14,608]{3,1,2,0:T(2,128)(2,1)S(1)}, u32[]{:S(2)}, u32[]{:S(2)}) collective-permute-start(bf16[4,2,14,608]{3,1,2,0:T(2,128)(2,1)S(1)} %copy_dynamic-update-slice_fusion), channel_id=1, source_target_pairs={{0,480},{8,488},{16,496},{24,504},{32,0},{40,8},{48,16},{56,24},{6... | collective-permute-start | bytes 408584 | tf_op jit(solution)/shard_map/ppermute | solution.py:72
  82.4 8.5 %collective-permute-start.5 = (bf16[4,2,14,608]{3,1,2,0:T(2,128)(2,1)S(1)}, bf16[4,2,14,608]{3,1,2,0:T(2,128)(2,1)S(1)}, u32[]{:S(2)}, u32[]{:S(2)}) collective-permute-start(bf16[4,2,14,608]{3,1,2,0:T(2,128)(2,1)S(1)} %collective-permute-done.3), channel_id=1, source_target_pairs={{0,32},{8,40},{16,48},{24,56},{32,64},{40,72},{48,80},{56,88},{64,... | collective-permute-start | bytes 408584 | tf_op jit(solution)/shard_map/ppermute | solution.py:69
  86.3 7.0 %collective-permute-start.6 = (bf16[4,2,14,608]{3,1,2,0:T(2,128)(2,1)S(1)}, bf16[4,2,14,608]{3,1,2,0:T(2,128)(2,1)S(1)}, u32[]{:S(2)}, u32[]{:S(2)}) collective-permute-start(bf16[4,2,14,608]{3,1,2,0:T(2,128)(2,1)S(1)} %collective-permute-done.4), channel_id=1, source_target_pairs={{0,480},{8,488},{16,496},{24,504},{32,0},{40,8},{48,16},{56,24},{6... | collective-permute-start | bytes 408584 | tf_op jit(solution)/shard_map/ppermute | solution.py:72
  90.9 8.2 %collective-permute-start.7 = (bf16[4,2,14,608]{3,1,2,0:T(2,128)(2,1)S(1)}, bf16[4,2,14,608]{3,1,2,0:T(2,128)(2,1)S(1)}, u32[]{:S(2)}, u32[]{:S(2)}) collective-permute-start(bf16[4,2,14,608]{3,1,2,0:T(2,128)(2,1)S(1)} %collective-permute-done.5), channel_id=1, source_target_pairs={{0,32},{8,40},{16,48},{24,56},{32,64},{40,72},{48,80},{56,88},{64,... | collective-permute-start | bytes 408584 | tf_op jit(solution)/shard_map/ppermute | solution.py:69
  93.4 7.6 %collective-permute-start.8 = (bf16[4,2,14,608]{3,1,2,0:T(2,128)(2,1)S(1)}, bf16[4,2,14,608]{3,1,2,0:T(2,128)(2,1)S(1)}, u32[]{:S(2)}, u32[]{:S(2)}) collective-permute-start(bf16[4,2,14,608]{3,1,2,0:T(2,128)(2,1)S(1)} %collective-permute-done.6), channel_id=1, source_target_pairs={{0,480},{8,488},{16,496},{24,504},{32,0},{40,8},{48,16},{56,24},{6... | collective-permute-start | bytes 408584 | tf_op jit(solution)/shard_map/ppermute | solution.py:72
  99.1 8.2 %collective-permute-start.9 = (bf16[4,2,14,608]{3,1,2,0:T(2,128)(2,1)S(1)}, bf16[4,2,14,608]{3,1,2,0:T(2,128)(2,1)S(1)}, u32[]{:S(2)}, u32[]{:S(2)}) collective-permute-start(bf16[4,2,14,608]{3,1,2,0:T(2,128)(2,1)S(1)} %collective-permute-done.7), channel_id=1, source_target_pairs={{0,32},{8,40},{16,48},{24,56},{32,64},{40,72},{48,80},{56,88},{64,... | collective-permute-start | bytes 408584 | tf_op jit(solution)/shard_map/ppermute | solution.py:69
  101.0 8.2 %collective-permute-start.10 = (bf16[4,2,14,608]{3,1,2,0:T(2,128)(2,1)S(1)}, bf16[4,2,14,608]{3,1,2,0:T(2,128)(2,1)S(1)}, u32[]{:S(2)}, u32[]{:S(2)}) collective-permute-start(bf16[4,2,14,608]{3,1,2,0:T(2,128)(2,1)S(1)} %collective-permute-done.8), channel_id=1, source_target_pairs={{0,480},{8,488},{16,496},{24,504},{32,0},{40,8},{48,16},{56,24},{6... | collective-permute-start | bytes 408584 | tf_op jit(solution)/shard_map/ppermute | solution.py:72
  107.2 8.2 %collective-permute-start.11 = (bf16[4,2,14,608]{3,1,2,0:T(2,128)(2,1)S(1)}, bf16[4,2,14,608]{3,1,2,0:T(2,128)(2,1)S(1)}, u32[]{:S(2)}, u32[]{:S(2)}) collective-permute-start(bf16[4,2,14,608]{3,1,2,0:T(2,128)(2,1)S(1)} %collective-permute-done.9), channel_id=1, source_target_pairs={{0,32},{8,40},{16,48},{24,56},{32,64},{40,72},{48,80},{56,88},{64,... | collective-permute-start | bytes 408584 | tf_op jit(solution)/shard_map/ppermute | solution.py:69
  109.2 8.2 %collective-permute-start.12 = (bf16[4,2,14,608]{3,1,2,0:T(2,128)(2,1)S(1)}, bf16[4,2,14,608]{3,1,2,0:T(2,128)(2,1)S(1)}, u32[]{:S(2)}, u32[]{:S(2)}) collective-permute-start(bf16[4,2,14,608]{3,1,2,0:T(2,128)(2,1)S(1)} %collective-permute-done.10), channel_id=1, source_target_pairs={{0,480},{8,488},{16,496},{24,504},{32,0},{40,8},{48,16},{56,24},{6... | collective-permute-start | bytes 408584 | tf_op jit(solution)/shard_map/ppermute | solution.py:72
  115.4 8.3 %collective-permute-start.13 = (bf16[4,2,14,608]{3,1,2,0:T(2,128)(2,1)S(1)}, bf16[4,2,14,608]{3,1,2,0:T(2,128)(2,1)S(1)}, u32[]{:S(2)}, u32[]{:S(2)}) collective-permute-start(bf16[4,2,14,608]{3,1,2,0:T(2,128)(2,1)S(1)} %collective-permute-done.11), channel_id=1, source_target_pairs={{0,32},{8,40},{16,48},{24,56},{32,64},{40,72},{48,80},{56,88},{64,... | collective-permute-start | bytes 408584 | tf_op jit(solution)/shard_map/ppermute | solution.py:69
  117.4 8.2 %collective-permute-start.14 = (bf16[4,2,14,608]{3,1,2,0:T(2,128)(2,1)S(1)}, bf16[4,2,14,608]{3,1,2,0:T(2,128)(2,1)S(1)}, u32[]{:S(2)}, u32[]{:S(2)}) collective-permute-start(bf16[4,2,14,608]{3,1,2,0:T(2,128)(2,1)S(1)} %collective-permute-done.12), channel_id=1, source_target_pairs={{0,480},{8,488},{16,496},{24,504},{32,0},{40,8},{48,16},{56,24},{6... | collective-permute-start | bytes 408584 | tf_op jit(solution)/shard_map/ppermute | solution.py:72
  123.7 9.4 %collective-permute-start.15 = (bf16[4,2,14,608]{3,1,2,0:T(2,128)(2,1)S(1)}, bf16[4,2,14,608]{3,1,2,0:T(2,128)(2,1)S(1)}, u32[]{:S(2)}, u32[]{:S(2)}) collective-permute-start(bf16[4,2,14,608]{3,1,2,0:T(2,128)(2,1)S(1)} %collective-permute-done.13), channel_id=1, source_target_pairs={{0,32},{8,40},{16,48},{24,56},{32,64},{40,72},{48,80},{56,88},{64,... | collective-permute-start | bytes 408584 | tf_op jit(solution)/shard_map/ppermute | solution.py:69
  125.6 9.5 %collective-permute-start.16 = (bf16[4,2,14,608]{3,1,2,0:T(2,128)(2,1)S(1)}, bf16[4,2,14,608]{3,1,2,0:T(2,128)(2,1)S(1)}, u32[]{:S(2)}, u32[]{:S(2)}) collective-permute-start(bf16[4,2,14,608]{3,1,2,0:T(2,128)(2,1)S(1)} %collective-permute-done.14), channel_id=1, source_target_pairs={{0,480},{8,488},{16,496},{24,504},{32,0},{40,8},{48,16},{56,24},{6... | collective-permute-start | bytes 408584 | tf_op jit(solution)/shard_map/ppermute | solution.py:72
  133.1 8.2 %collective-permute-start.17 = (bf16[4,2,14,608]{3,1,2,0:T(2,128)(2,1)S(1)}, bf16[4,2,14,608]{3,1,2,0:T(2,128)(2,1)S(1)}, u32[]{:S(2)}, u32[]{:S(2)}) collective-permute-start(bf16[4,2,14,608]{3,1,2,0:T(2,128)(2,1)S(1)} %collective-permute-done.15), channel_id=1, source_target_pairs={{0,32},{8,40},{16,48},{24,56},{32,64},{40,72},{48,80},{56,88},{64,... | collective-permute-start | bytes 408584 | tf_op jit(solution)/shard_map/ppermute | solution.py:69

commit v4 on v3

--- a/solution.py
+++ b/solution.py
@@ -31,12 +31,8 @@
     left = emb_left[0]
     nleft = left.size // groups
     send_left = left.reshape(groups, nleft)
-    right = emb_right[0]
-    rank, width = right.shape
-    chunk = rank // tensors
-    rchunk = lax.dynamic_slice_in_dim(right, ti * chunk, chunk, axis=0)
-    send_right = jnp.broadcast_to(rchunk.reshape(1, chunk * width), (groups, chunk * width))
-    send = jnp.concatenate([send_layer, send_left, send_right], axis=1)
+    rights = lax.all_gather(emb_right, "group", axis=0, tiled=True)
+    send = jnp.concatenate([send_layer, send_left], axis=1)
     recv = lax.all_to_all(send, "group", 0, 0, tiled=True)
 
     acc = recv[:, :nlayer].astype(f32).sum(axis=0)
@@ -74,11 +70,9 @@
     layer_blocks = jnp.moveaxis(out, 2, 0).reshape(piece.shape[0], -1, piece.shape[2])
 
     lefts = recv[:, nlayer:nlayer + nleft].reshape((groups,) + left.shape[1:])
-    rchunks = recv[:, nlayer + nleft:].reshape(groups, chunk, width)
-    full = lax.all_gather(rchunks, "tensor", axis=1, tiled=True)
     total = jnp.zeros(emb_weight.shape, f32)
     for g in range(groups):
-        product = jnp.dot(lefts[g], full[g], preferred_element_type=f32).astype(bf16)
+        product = jnp.dot(lefts[g], rights[g], preferred_element_type=f32).astype(bf16)
         total = total + product.astype(f32)
     emb_mean = total / groups
     new_emb_momentum = beta_outer * emb_momentum + emb_mean

time: 148 us -> 147 us (level)
  waiting for transfers between devices: 31.9 us -> 12.6 us
  blocking collectives: 13.1 us -> 32.1 us
  local copies, waits for them, and re-layouts: 19.3 us -> 16.4 us
  starting transfers between devices: 78.3 us -> 80.7 us
    all_gather x1, blocking collectives: 13.1 us -> 32.1 us  [on_device(): rights = lax.all_gather(emb_right, 'group', axis=0, tiled=True)]
    all_to_all x1, waiting for transfers between devices: 18.7 us -> 0.01 us  [on_device(): recv = lax.all_to_all(send, 'group', 0, 0, tiled=True)]
    ppermute x7, starting transfers between devices: 30.4 us -> 35.9 us  [on_device(): bwd = lax.ppermute(bwd, ('group', 'shard'), zshift(-1))]
    ppermute x8, starting transfers between devices: 21.3 us -> 18.2 us  [on_device(): fwd = lax.ppermute(fwd, ('group', 'shard'), zshift(1))]
    dynamic_update_slice x3, local copies, waits for them, and re-layouts: 2.46 us -> 0.9 us  [on_device(): yblk = lax.dynamic_update_index_in_dim(yblk, got, (yi - k) % Y_SIZE, axis=0)]
    unnamed x18 -> x17, local copies, waits for them, and re-layouts: 9.4 us -> 9.4 us
  transfers between devices with their start and end apart: 19 -> 19, of which waited for: 9 -> 7; matrix products, arithmetic and copies ran while one was open for 7% -> 6% of each run, Pallas kernels for 0% -> 0%
where the time goes in v4:
time: 147 us; the launch traced here: 146 us
  starting transfers between devices  80.7 us (55%)
  blocking collectives  32.1 us (22%)
  local copies, waits for them, and re-layouts  16.4 us (11%)
  waiting for transfers between devices  12.6 us (9%)
  matrix products  1.97 us (1%)
    ppermute x7, starting transfers between devices, on_device(): bwd = lax.ppermute(bwd, ('group', 'shard'), zshift(-1))  35.9 us
    all_gather x1, blocking collectives, on_device(): rights = lax.all_gather(emb_right, 'group', axis=0, tiled=True)  32.1 us
    ppermute x8, starting transfers between devices, on_device(): fwd = lax.ppermute(fwd, ('group', 'shard'), zshift(1))  18.2 us
    all_to_all x1, starting transfers between devices, on_device(): recv = lax.all_to_all(send, 'group', 0, 0, tiled=True)  15.1 us
    ppermute x8, waiting for transfers between devices, on_device(): fwd = lax.ppermute(fwd, ('group', 'shard'), zshift(1))  12.5 us
    ppermute x3, starting transfers between devices, on_device(): got = lax.ppermute(piece, 'shard', pairs)  11.6 us
    unnamed x17, local copies, waits for them, and re-layouts  9.4 us
  transfers between devices with their start and end apart: 19, of which 7 were waited for; matrix products, arithmetic and copies ran while one was open for 6% of the time, Pallas kernels for 0%

profile of v4, /device:TPU:6, one launch (start us, length us, event | category | flops | bytes accessed | tf_op | source)
XLA Modules:
  0.0 146.1 jit_solution(17755182659849023928)
XLA Ops:
  0.6 1.1 copy.55
  1.7 0.1 reshape_squeeze.3
  1.9 0.9 copy.54
  2.8 0.3 reshape.30
  3.2 0.5 broadcast.44
  3.8 0.9 reduce.8
  4.7 0.8 reshape.36
  5.5 15.1 %all-to-all-start = ((bf16[4,2,13312]{2,1,0:T(2,128)(2,1)}), bf16[4,2,13312]{2,1,0:T(2,128)(2,1)S(1)}, u32[]{:S(2)}, u32[]{:S(2)}) async-start(bf16[4,2,13312]{2,1,0:T(2,128)(2,1)} %reshape.36), calls=%async_computation | async-start | bytes 425984 | tf_op jit(solution)/shard_map/all_to_all | solution.py:36
  20.6 32.1 %all_gather.3 = bf16[4,64,896]{2,1,0:T(8,128)(2,1)S(1)} all-gather(bf16[1,64,896]{2,1,0:T(8,128)(2,1)S(1)} %copy-done.2), channel_id=1, replica_groups=mesh['group'=4,'shard'=16,'tensor'=8] {'group'}, dimensions={0}, use_global_device_ids=true | all-gather | bytes 573440 | tf_op jit(solution)/shard_map/all_gather | solution.py:34
  52.7 0.2 reshape.37
  52.9 0.2 copy.80
  53.1 0.2 convert_reduce_fusion
  53.3 0.1 div.24
  53.4 3.5 %collective-permute-start = (bf16[2,14,608]{2,1,0:T(8,128)(2,1)S(1)}, bf16[2,14,608]{2,1,0:T(8,128)(2,1)}, u32[]{:S(2)}, u32[]{:S(2)}) collective-permute-start(bf16[2,14,608]{2,1,0:T(8,128)(2,1)S(1)} %get-tuple-element.26), channel_id=1, source_target_pairs={{0,8},{8,16},{16,24},{24,0},{32,40},{40,48},{48,56},{56,32},{64,72... | collective-permute-start | bytes 102152 | tf_op jit(solution)/shard_map/ppermute | solution.py:49
  56.9 4.8 %collective-permute-start.1 = (bf16[2,14,608]{2,1,0:T(8,128)(2,1)S(1)}, bf16[2,14,608]{2,1,0:T(8,128)(2,1)S(1)}, u32[]{:S(2)}, u32[]{:S(2)}) collective-permute-start(bf16[2,14,608]{2,1,0:T(8,128)(2,1)S(1)} %get-tuple-element.26), channel_id=1, source_target_pairs={{0,16},{8,24},{16,0},{24,8},{32,48},{40,56},{48,32},{56,40},{64,80... | collective-permute-start | bytes 102152 | tf_op jit(solution)/shard_map/ppermute | solution.py:49
  61.7 3.3 %collective-permute-start.2 = (bf16[2,14,608]{2,1,0:T(8,128)(2,1)S(1)}, bf16[2,14,608]{2,1,0:T(8,128)(2,1)S(1)}, u32[]{:S(2)}, u32[]{:S(2)}) collective-permute-start(bf16[2,14,608]{2,1,0:T(8,128)(2,1)S(1)} %get-tuple-element.26), channel_id=1, source_target_pairs={{0,24},{8,0},{16,8},{24,16},{32,56},{40,32},{48,40},{56,48},{64,88... | collective-permute-start | bytes 102152 | tf_op jit(solution)/shard_map/ppermute | solution.py:49
  65.0 0.4 slice_reduce_fusion.3
  65.6 0.2 fusion.7
  65.8 0.2 fusion.6
  66.1 0.2 fusion.5
  66.5 1.4 multiply_subtract_fusion
  67.9 0.7 copy.63
  68.6 0.7 copy.64
  69.3 0.8 copy_dynamic-update-slice_fusion.2
  70.2 4.9 %collective-permute-start.3 = (bf16[4,2,14,608]{3,1,2,0:T(2,128)(2,1)S(1)}, bf16[4,2,14,608]{3,1,2,0:T(2,128)(2,1)S(1)}, u32[]{:S(2)}, u32[]{:S(2)}) collective-permute-start(bf16[4,2,14,608]{3,1,2,0:T(2,128)(2,1)S(1)} %copy_dynamic-update-slice_fusion), channel_id=1, source_target_pairs={{0,32},{8,40},{16,48},{24,56},{32,64},{40,72},{48,80},{56,88},{64,... | collective-permute-start | bytes 408584 | tf_op jit(solution)/shard_map/ppermute | solution.py:65
  75.1 4.1 %collective-permute-start.4 = (bf16[4,2,14,608]{3,1,2,0:T(2,128)(2,1)S(1)}, bf16[4,2,14,608]{3,1,2,0:T(2,128)(2,1)S(1)}, u32[]{:S(2)}, u32[]{:S(2)}) collective-permute-start(bf16[4,2,14,608]{3,1,2,0:T(2,128)(2,1)S(1)} %copy_dynamic-update-slice_fusion), channel_id=1, source_target_pairs={{0,480},{8,488},{16,496},{24,504},{32,0},{40,8},{48,16},{56,24},{6... | collective-permute-start | bytes 408584 | tf_op jit(solution)/shard_map/ppermute | solution.py:68
  79.2 1.2 broadcast_in_dim.68
  80.4 0.1 bitcast_dynamic-update-slice_fusion.15
  80.6 1.9 %collective-permute-start.5 = (bf16[4,2,14,608]{3,1,2,0:T(2,128)(2,1)S(1)}, bf16[4,2,14,608]{3,1,2,0:T(2,128)(2,1)S(1)}, u32[]{:S(2)}, u32[]{:S(2)}) collective-permute-start(bf16[4,2,14,608]{3,1,2,0:T(2,128)(2,1)S(1)} %collective-permute-done.3), channel_id=1, source_target_pairs={{0,32},{8,40},{16,48},{24,56},{32,64},{40,72},{48,80},{56,88},{64,... | collective-permute-start | bytes 408584 | tf_op jit(solution)/shard_map/ppermute | solution.py:65
  82.5 5.1 %collective-permute-start.6 = (bf16[4,2,14,608]{3,1,2,0:T(2,128)(2,1)S(1)}, bf16[4,2,14,608]{3,1,2,0:T(2,128)(2,1)S(1)}, u32[]{:S(2)}, u32[]{:S(2)}) collective-permute-start(bf16[4,2,14,608]{3,1,2,0:T(2,128)(2,1)S(1)} %collective-permute-done.4), channel_id=1, source_target_pairs={{0,480},{8,488},{16,496},{24,504},{32,0},{40,8},{48,16},{56,24},{6... | collective-permute-start | bytes 408584 | tf_op jit(solution)/shard_map/ppermute | solution.py:68
  87.7 0.1 bitcast_dynamic-update-slice_fusion.14
  87.8 0.1 bitcast_dynamic-update-slice_fusion.13
  87.9 0.9 collective-permute-done.5
  88.8 1.9 %collective-permute-start.7 = (bf16[4,2,14,608]{3,1,2,0:T(2,128)(2,1)S(1)}, bf16[4,2,14,608]{3,1,2,0:T(2,128)(2,1)S(1)}, u32[]{:S(2)}, u32[]{:S(2)}) collective-permute-start(bf16[4,2,14,608]{3,1,2,0:T(2,128)(2,1)S(1)} %collective-permute-done.5), channel_id=1, source_target_pairs={{0,32},{8,40},{16,48},{24,56},{32,64},{40,72},{48,80},{56,88},{64,... | collective-permute-start | bytes 408584 | tf_op jit(solution)/shard_map/ppermute | solution.py:65
  90.7 5.1 %collective-permute-start.8 = (bf16[4,2,14,608]{3,1,2,0:T(2,128)(2,1)S(1)}, bf16[4,2,14,608]{3,1,2,0:T(2,128)(2,1)S(1)}, u32[]{:S(2)}, u32[]{:S(2)}) collective-permute-start(bf16[4,2,14,608]{3,1,2,0:T(2,128)(2,1)S(1)} %collective-permute-done.6), channel_id=1, source_target_pairs={{0,480},{8,488},{16,496},{24,504},{32,0},{40,8},{48,16},{56,24},{6... | collective-permute-start | bytes 408584 | tf_op jit(solution)/shard_map/ppermute | solution.py:68
  95.8 0.1 bitcast_dynamic-update-slice_fusion.12
  96.0 0.1 bitcast_dynamic-update-slice_fusion.11
  96.1 1.1 collective-permute-done.7
  97.2 1.9 %collective-permute-start.9 = (bf16[4,2,14,608]{3,1,2,0:T(2,128)(2,1)S(1)}, bf16[4,2,14,608]{3,1,2,0:T(2,128)(2,1)S(1)}, u32[]{:S(2)}, u32[]{:S(2)}) collective-permute-start(bf16[4,2,14,608]{3,1,2,0:T(2,128)(2,1)S(1)} %collective-permute-done.7), channel_id=1, source_target_pairs={{0,32},{8,40},{16,48},{24,56},{32,64},{40,72},{48,80},{56,88},{64,... | collective-permute-start | bytes 408584 | tf_op jit(solution)/shard_map/ppermute | solution.py:65
  99.1 5.4 %collective-permute-start.10 = (bf16[4,2,14,608]{3,1,2,0:T(2,128)(2,1)S(1)}, bf16[4,2,14,608]{3,1,2,0:T(2,128)(2,1)S(1)}, u32[]{:S(2)}, u32[]{:S(2)}) collective-permute-start(bf16[4,2,14,608]{3,1,2,0:T(2,128)(2,1)S(1)} %collective-permute-done.8), channel_id=1, source_target_pairs={{0,480},{8,488},{16,496},{24,504},{32,0},{40,8},{48,16},{56,24},{6... | collective-permute-start | bytes 408584 | tf_op jit(solution)/shard_map/ppermute | solution.py:68
  104.6 0.1 bitcast_dynamic-update-slice_fusion.10
  104.7 0.1 bitcast_dynamic-update-slice_fusion.9
  104.8 2.0 %collective-permute-done.9 = bf16[4,2,14,608]{3,1,2,0:T(2,128)(2,1)S(1)} collective-permute-done((bf16[4,2,14,608]{3,1,2,0:T(2,128)(2,1)S(1)}, bf16[4,2,14,608]{3,1,2,0:T(2,128)(2,1)S(1)}, u32[]{:S(2)}, u32[]{:S(2)}) %collective-permute-start.9) | collective-permute-done | bytes 136224 | tf_op jit(solution)/shard_map/ppermute | solution.py:65
  106.8 1.9 %collective-permute-start.11 = (bf16[4,2,14,608]{3,1,2,0:T(2,128)(2,1)S(1)}, bf16[4,2,14,608]{3,1,2,0:T(2,128)(2,1)S(1)}, u32[]{:S(2)}, u32[]{:S(2)}) collective-permute-start(bf16[4,2,14,608]{3,1,2,0:T(2,128)(2,1)S(1)} %collective-permute-done.9), channel_id=1, source_target_pairs={{0,32},{8,40},{16,48},{24,56},{32,64},{40,72},{48,80},{56,88},{64,... | collective-permute-start | bytes 408584 | tf_op jit(solution)/shard_map/ppermute | solution.py:65
  108.7 5.4 %collective-permute-start.12 = (bf16[4,2,14,608]{3,1,2,0:T(2,128)(2,1)S(1)}, bf16[4,2,14,608]{3,1,2,0:T(2,128)(2,1)S(1)}, u32[]{:S(2)}, u32[]{:S(2)}) collective-permute-start(bf16[4,2,14,608]{3,1,2,0:T(2,128)(2,1)S(1)} %collective-permute-done.10), channel_id=1, source_target_pairs={{0,480},{8,488},{16,496},{24,504},{32,0},{40,8},{48,16},{56,24},{6... | collective-permute-start | bytes 408584 | tf_op jit(solution)/shard_map/ppermute | solution.py:68
  114.2 0.1 bitcast_dynamic-update-slice_fusion.8
  114.3 0.1 bitcast_dynamic-update-slice_fusion.7
  114.4 1.2 collective-permute-done.11
  115.7 1.9 %collective-permute-start.13 = (bf16[4,2,14,608]{3,1,2,0:T(2,128)(2,1)S(1)}, bf16[4,2,14,608]{3,1,2,0:T(2,128)(2,1)S(1)}, u32[]{:S(2)}, u32[]{:S(2)}) collective-permute-start(bf16[4,2,14,608]{3,1,2,0:T(2,128)(2,1)S(1)} %collective-permute-done.11), channel_id=1, source_target_pairs={{0,32},{8,40},{16,48},{24,56},{32,64},{40,72},{48,80},{56,88},{64,... | collective-permute-start | bytes 408584 | tf_op jit(solution)/shard_map/ppermute | solution.py:65
  117.6 5.3 %collective-permute-start.14 = (bf16[4,2,14,608]{3,1,2,0:T(2,128)(2,1)S(1)}, bf16[4,2,14,608]{3,1,2,0:T(2,128)(2,1)S(1)}, u32[]{:S(2)}, u32[]{:S(2)}) collective-permute-start(bf16[4,2,14,608]{3,1,2,0:T(2,128)(2,1)S(1)} %collective-permute-done.12), channel_id=1, source_target_pairs={{0,480},{8,488},{16,496},{24,504},{32,0},{40,8},{48,16},{56,24},{6... | collective-permute-start | bytes 408584 | tf_op jit(solution)/shard_map/ppermute | solution.py:68
  122.9 0.1 bitcast_dynamic-update-slice_fusion.6
  123.0 0.1 bitcast_dynamic-update-slice_fusion.5
  123.2 0.7 collective-permute-done.13
  123.8 1.9 %collective-permute-start.15 = (bf16[4,2,14,608]{3,1,2,0:T(2,128)(2,1)S(1)}, bf16[4,2,14,608]{3,1,2,0:T(2,128)(2,1)S(1)}, u32[]{:S(2)}, u32[]{:S(2)}) collective-permute-start(bf16[4,2,14,608]{3,1,2,0:T(2,128)(2,1)S(1)} %collective-permute-done.13), channel_id=1, source_target_pairs={{0,32},{8,40},{16,48},{24,56},{32,64},{40,72},{48,80},{56,88},{64,... | collective-permute-start | bytes 408584 | tf_op jit(solution)/shard_map/ppermute | solution.py:65
  125.8 5.3 %collective-permute-start.16 = (bf16[4,2,14,608]{3,1,2,0:T(2,128)(2,1)S(1)}, bf16[4,2,14,608]{3,1,2,0:T(2,128)(2,1)S(1)}, u32[]{:S(2)}, u32[]{:S(2)}) collective-permute-start(bf16[4,2,14,608]{3,1,2,0:T(2,128)(2,1)S(1)} %collective-permute-done.14), channel_id=1, source_target_pairs={{0,480},{8,488},{16,496},{24,504},{32,0},{40,8},{48,16},{56,24},{6... | collective-permute-start | bytes 408584 | tf_op jit(solution)/shard_map/ppermute | solution.py:68
  131.1 0.1 bitcast_dynamic-update-slice_fusion.4
  131.2 0.1 bitcast_dynamic-update-slice_fusion.3
  131.4 0.7 collective-permute-done.15
  132.0 1.9 %collective-permute-start.17 = (bf16[4,2,14,608]{3,1,2,0:T(2,128)(2,1)S(1)}, bf16[4,2,14,608]{3,1,2,0:T(2,128)(2,1)S(1)}, u32[]{:S(2)}, u32[]{:S(2)}) collective-permute-start(bf16[4,2,14,608]{3,1,2,0:T(2,128)(2,1)S(1)} %collective-permute-done.15), channel_id=1, source_target_pairs={{0,32},{8,40},{16,48},{24,56},{32,64},{40,72},{48,80},{56,88},{64,... | collective-permute-start | bytes 408584 | tf_op jit(solution)/shard_map/ppermute | solution.py:65
  134.0 0.1 bitcast_dynamic-update-slice_fusion.2
  134.1 0.1 bitcast_dynamic-update-slice_fusion.1
  134.2 6.0 %collective-permute-done.17 = bf16[4,2,14,608]{3,1,2,0:T(2,128)(2,1)S(1)} collective-permute-done((bf16[4,2,14,608]{3,1,2,0:T(2,128)(2,1)S(1)}, bf16[4,2,14,608]{3,1,2,0:T(2,128)(2,1)S(1)}, u32[]{:S(2)}, u32[]{:S(2)}) %collective-permute-start.17) | collective-permute-done | bytes 136224 | tf_op jit(solution)/shard_map/ppermute | solution.py:65
  140.2 0.1 bitcast_dynamic-update-slice_fusion
  140.4 5.7 %copy.65 = bf16[2,896,608]{1,2,0:T(8,128)(2,1)} copy(bf16[2,896,608]{2,0,1:T(2,128)(2,1)S(1)} %bitcast.65) | data formatting | bytes 4358144
  (33 shorter events, 0.7 us)
Async XLA Ops:
  0.6 19.9 %copy-start.2 = (bf16[1,64,896]{2,1,0:T(8,128)(2,1)S(1)}, bf16[1,64,896]{2,1,0:T(8,128)(2,1)}, u32[]{:S(2)}) copy-start(bf16[1,64,896]{2,1,0:T(8,128)(2,1)} %param.9) | copy-start | bytes 344068
  3.1 50.3 %copy-start.3 = (f32[2,14,608]{2,0,1:T(2,128)S(1)}, f32[2,14,608]{2,0,1:T(2,128)}, u32[]{:S(2)}) copy-start(f32[2,14,608]{2,0,1:T(2,128)} %param.11) | copy-start | bytes 204292
  3.1 50.3 %copy-start.4 = (f32[2,14,608]{2,0,1:T(2,128)S(1)}, f32[2,14,608]{2,0,1:T(2,128)}, u32[]{:S(2)}) copy-start(f32[2,14,608]{2,0,1:T(2,128)} %param.10) | copy-start | bytes 204292
  5.5 47.2 %all-to-all-start = ((bf16[4,2,13312]{2,1,0:T(2,128)(2,1)}), bf16[4,2,13312]{2,1,0:T(2,128)(2,1)S(1)}, u32[]{:S(2)}, u32[]{:S(2)}) async-start(bf16[4,2,13312]{2,1,0:T(2,128)(2,1)} %reshape.36), calls=%async_computation | async-start | bytes 425984 | tf_op jit(solution)/shard_map/all_to_all | solution.py:36
  52.7 13.8 %copy-start = (f32[150,896]{1,0:T(8,128)S(1)}, f32[150,896]{1,0:T(8,128)}, u32[]{:S(2)}) copy-start(f32[150,896]{1,0:T(8,128)} %param.12) | copy-start | bytes 1612804
  52.7 13.8 %copy-start.1 = (f32[150,896]{1,0:T(8,128)S(1)}, f32[150,896]{1,0:T(8,128)}, u32[]{:S(2)}) copy-start(f32[150,896]{1,0:T(8,128)} %param.13) | copy-start | bytes 1612804
  53.4 15.8 %collective-permute-start = (bf16[2,14,608]{2,1,0:T(8,128)(2,1)S(1)}, bf16[2,14,608]{2,1,0:T(8,128)(2,1)}, u32[]{:S(2)}, u32[]{:S(2)}) collective-permute-start(bf16[2,14,608]{2,1,0:T(8,128)(2,1)S(1)} %get-tuple-element.26), channel_id=1, source_target_pairs={{0,8},{8,16},{16,24},{24,0},{32,40},{40,48},{48,56},{56,32},{64,72... | collective-permute-start | bytes 102152 | tf_op jit(solution)/shard_map/ppermute | solution.py:49
  56.9 13.2 %collective-permute-start.1 = (bf16[2,14,608]{2,1,0:T(8,128)(2,1)S(1)}, bf16[2,14,608]{2,1,0:T(8,128)(2,1)S(1)}, u32[]{:S(2)}, u32[]{:S(2)}) collective-permute-start(bf16[2,14,608]{2,1,0:T(8,128)(2,1)S(1)} %get-tuple-element.26), channel_id=1, source_target_pairs={{0,16},{8,24},{16,0},{24,8},{32,48},{40,56},{48,32},{56,40},{64,80... | collective-permute-start | bytes 102152 | tf_op jit(solution)/shard_map/ppermute | solution.py:49
  61.7 8.4 %collective-permute-start.2 = (bf16[2,14,608]{2,1,0:T(8,128)(2,1)S(1)}, bf16[2,14,608]{2,1,0:T(8,128)(2,1)S(1)}, u32[]{:S(2)}, u32[]{:S(2)}) collective-permute-start(bf16[2,14,608]{2,1,0:T(8,128)(2,1)S(1)} %get-tuple-element.26), channel_id=1, source_target_pairs={{0,24},{8,0},{16,8},{24,16},{32,56},{40,32},{48,40},{56,48},{64,88... | collective-permute-start | bytes 102152 | tf_op jit(solution)/shard_map/ppermute | solution.py:49
  70.2 10.4 %collective-permute-start.3 = (bf16[4,2,14,608]{3,1,2,0:T(2,128)(2,1)S(1)}, bf16[4,2,14,608]{3,1,2,0:T(2,128)(2,1)S(1)}, u32[]{:S(2)}, u32[]{:S(2)}) collective-permute-start(bf16[4,2,14,608]{3,1,2,0:T(2,128)(2,1)S(1)} %copy_dynamic-update-slice_fusion), channel_id=1, source_target_pairs={{0,32},{8,40},{16,48},{24,56},{32,64},{40,72},{48,80},{56,88},{64,... | collective-permute-start | bytes 408584 | tf_op jit(solution)/shard_map/ppermute | solution.py:65
  75.1 7.4 %collective-permute-start.4 = (bf16[4,2,14,608]{3,1,2,0:T(2,128)(2,1)S(1)}, bf16[4,2,14,608]{3,1,2,0:T(2,128)(2,1)S(1)}, u32[]{:S(2)}, u32[]{:S(2)}) collective-permute-start(bf16[4,2,14,608]{3,1,2,0:T(2,128)(2,1)S(1)} %copy_dynamic-update-slice_fusion), channel_id=1, source_target_pairs={{0,480},{8,488},{16,496},{24,504},{32,0},{40,8},{48,16},{56,24},{6... | collective-permute-start | bytes 408584 | tf_op jit(solution)/shard_map/ppermute | solution.py:68
  80.6 8.2 %collective-permute-start.5 = (bf16[4,2,14,608]{3,1,2,0:T(2,128)(2,1)S(1)}, bf16[4,2,14,608]{3,1,2,0:T(2,128)(2,1)S(1)}, u32[]{:S(2)}, u32[]{:S(2)}) collective-permute-start(bf16[4,2,14,608]{3,1,2,0:T(2,128)(2,1)S(1)} %collective-permute-done.3), channel_id=1, source_target_pairs={{0,32},{8,40},{16,48},{24,56},{32,64},{40,72},{48,80},{56,88},{64,... | collective-permute-start | bytes 408584 | tf_op jit(solution)/shard_map/ppermute | solution.py:65
  82.5 8.2 %collective-permute-start.6 = (bf16[4,2,14,608]{3,1,2,0:T(2,128)(2,1)S(1)}, bf16[4,2,14,608]{3,1,2,0:T(2,128)(2,1)S(1)}, u32[]{:S(2)}, u32[]{:S(2)}) collective-permute-start(bf16[4,2,14,608]{3,1,2,0:T(2,128)(2,1)S(1)} %collective-permute-done.4), channel_id=1, source_target_pairs={{0,480},{8,488},{16,496},{24,504},{32,0},{40,8},{48,16},{56,24},{6... | collective-permute-start | bytes 408584 | tf_op jit(solution)/shard_map/ppermute | solution.py:68
  88.8 8.4 %collective-permute-start.7 = (bf16[4,2,14,608]{3,1,2,0:T(2,128)(2,1)S(1)}, bf16[4,2,14,608]{3,1,2,0:T(2,128)(2,1)S(1)}, u32[]{:S(2)}, u32[]{:S(2)}) collective-permute-start(bf16[4,2,14,608]{3,1,2,0:T(2,128)(2,1)S(1)} %collective-permute-done.5), channel_id=1, source_target_pairs={{0,32},{8,40},{16,48},{24,56},{32,64},{40,72},{48,80},{56,88},{64,... | collective-permute-start | bytes 408584 | tf_op jit(solution)/shard_map/ppermute | solution.py:65
  90.7 8.4 %collective-permute-start.8 = (bf16[4,2,14,608]{3,1,2,0:T(2,128)(2,1)S(1)}, bf16[4,2,14,608]{3,1,2,0:T(2,128)(2,1)S(1)}, u32[]{:S(2)}, u32[]{:S(2)}) collective-permute-start(bf16[4,2,14,608]{3,1,2,0:T(2,128)(2,1)S(1)} %collective-permute-done.6), channel_id=1, source_target_pairs={{0,480},{8,488},{16,496},{24,504},{32,0},{40,8},{48,16},{56,24},{6... | collective-permute-start | bytes 408584 | tf_op jit(solution)/shard_map/ppermute | solution.py:68
  97.2 9.6 %collective-permute-start.9 = (bf16[4,2,14,608]{3,1,2,0:T(2,128)(2,1)S(1)}, bf16[4,2,14,608]{3,1,2,0:T(2,128)(2,1)S(1)}, u32[]{:S(2)}, u32[]{:S(2)}) collective-permute-start(bf16[4,2,14,608]{3,1,2,0:T(2,128)(2,1)S(1)} %collective-permute-done.7), channel_id=1, source_target_pairs={{0,32},{8,40},{16,48},{24,56},{32,64},{40,72},{48,80},{56,88},{64,... | collective-permute-start | bytes 408584 | tf_op jit(solution)/shard_map/ppermute | solution.py:65
  99.1 9.6 %collective-permute-start.10 = (bf16[4,2,14,608]{3,1,2,0:T(2,128)(2,1)S(1)}, bf16[4,2,14,608]{3,1,2,0:T(2,128)(2,1)S(1)}, u32[]{:S(2)}, u32[]{:S(2)}) collective-permute-start(bf16[4,2,14,608]{3,1,2,0:T(2,128)(2,1)S(1)} %collective-permute-done.8), channel_id=1, source_target_pairs={{0,480},{8,488},{16,496},{24,504},{32,0},{40,8},{48,16},{56,24},{6... | collective-permute-start | bytes 408584 | tf_op jit(solution)/shard_map/ppermute | solution.py:68
  106.8 8.9 %collective-permute-start.11 = (bf16[4,2,14,608]{3,1,2,0:T(2,128)(2,1)S(1)}, bf16[4,2,14,608]{3,1,2,0:T(2,128)(2,1)S(1)}, u32[]{:S(2)}, u32[]{:S(2)}) collective-permute-start(bf16[4,2,14,608]{3,1,2,0:T(2,128)(2,1)S(1)} %collective-permute-done.9), channel_id=1, source_target_pairs={{0,32},{8,40},{16,48},{24,56},{32,64},{40,72},{48,80},{56,88},{64,... | collective-permute-start | bytes 408584 | tf_op jit(solution)/shard_map/ppermute | solution.py:65
  108.7 8.9 %collective-permute-start.12 = (bf16[4,2,14,608]{3,1,2,0:T(2,128)(2,1)S(1)}, bf16[4,2,14,608]{3,1,2,0:T(2,128)(2,1)S(1)}, u32[]{:S(2)}, u32[]{:S(2)}) collective-permute-start(bf16[4,2,14,608]{3,1,2,0:T(2,128)(2,1)S(1)} %collective-permute-done.10), channel_id=1, source_target_pairs={{0,480},{8,488},{16,496},{24,504},{32,0},{40,8},{48,16},{56,24},{6... | collective-permute-start | bytes 408584 | tf_op jit(solution)/shard_map/ppermute | solution.py:68
  115.7 8.2 %collective-permute-start.13 = (bf16[4,2,14,608]{3,1,2,0:T(2,128)(2,1)S(1)}, bf16[4,2,14,608]{3,1,2,0:T(2,128)(2,1)S(1)}, u32[]{:S(2)}, u32[]{:S(2)}) collective-permute-start(bf16[4,2,14,608]{3,1,2,0:T(2,128)(2,1)S(1)} %collective-permute-done.11), channel_id=1, source_target_pairs={{0,32},{8,40},{16,48},{24,56},{32,64},{40,72},{48,80},{56,88},{64,... | collective-permute-start | bytes 408584 | tf_op jit(solution)/shard_map/ppermute | solution.py:65
  117.6 8.2 %collective-permute-start.14 = (bf16[4,2,14,608]{3,1,2,0:T(2,128)(2,1)S(1)}, bf16[4,2,14,608]{3,1,2,0:T(2,128)(2,1)S(1)}, u32[]{:S(2)}, u32[]{:S(2)}) collective-permute-start(bf16[4,2,14,608]{3,1,2,0:T(2,128)(2,1)S(1)} %collective-permute-done.12), channel_id=1, source_target_pairs={{0,480},{8,488},{16,496},{24,504},{32,0},{40,8},{48,16},{56,24},{6... | collective-permute-start | bytes 408584 | tf_op jit(solution)/shard_map/ppermute | solution.py:68
  123.8 8.2 %collective-permute-start.15 = (bf16[4,2,14,608]{3,1,2,0:T(2,128)(2,1)S(1)}, bf16[4,2,14,608]{3,1,2,0:T(2,128)(2,1)S(1)}, u32[]{:S(2)}, u32[]{:S(2)}) collective-permute-start(bf16[4,2,14,608]{3,1,2,0:T(2,128)(2,1)S(1)} %collective-permute-done.13), channel_id=1, source_target_pairs={{0,32},{8,40},{16,48},{24,56},{32,64},{40,72},{48,80},{56,88},{64,... | collective-permute-start | bytes 408584 | tf_op jit(solution)/shard_map/ppermute | solution.py:65
  125.8 8.3 %collective-permute-start.16 = (bf16[4,2,14,608]{3,1,2,0:T(2,128)(2,1)S(1)}, bf16[4,2,14,608]{3,1,2,0:T(2,128)(2,1)S(1)}, u32[]{:S(2)}, u32[]{:S(2)}) collective-permute-start(bf16[4,2,14,608]{3,1,2,0:T(2,128)(2,1)S(1)} %collective-permute-done.14), channel_id=1, source_target_pairs={{0,480},{8,488},{16,496},{24,504},{32,0},{40,8},{48,16},{56,24},{6... | collective-permute-start | bytes 408584 | tf_op jit(solution)/shard_map/ppermute | solution.py:68
  132.0 8.2 %collective-permute-start.17 = (bf16[4,2,14,608]{3,1,2,0:T(2,128)(2,1)S(1)}, bf16[4,2,14,608]{3,1,2,0:T(2,128)(2,1)S(1)}, u32[]{:S(2)}, u32[]{:S(2)}) collective-permute-start(bf16[4,2,14,608]{3,1,2,0:T(2,128)(2,1)S(1)} %collective-permute-done.15), channel_id=1, source_target_pairs={{0,32},{8,40},{16,48},{24,56},{32,64},{40,72},{48,80},{56,88},{64,... | collective-permute-start | bytes 408584 | tf_op jit(solution)/shard_map/ppermute | solution.py:65

commit v5 on v3

--- a/solution.py
+++ b/solution.py
@@ -7,6 +7,8 @@
 beta_outer = 0.9
 
 Y_SIZE = 4
+OFFLOAD_MIN_BYTES = 1 << 20
+LANES = 128
 
 
 def shift_pairs(n, k):
@@ -75,10 +77,12 @@
 
     lefts = recv[:, nlayer:nlayer + nleft].reshape((groups,) + left.shape[1:])
     rchunks = recv[:, nlayer + nleft:].reshape(groups, chunk, width)
-    full = lax.all_gather(rchunks, "tensor", axis=1, tiled=True)
+    padded = -(-OFFLOAD_MIN_BYTES // (groups * rank * 2 * LANES)) * LANES
+    rchunks = jnp.pad(rchunks, ((0, 0), (0, 0), (0, max(padded - width, 0))))
+    rights = lax.all_gather(rchunks, "tensor", axis=1, tiled=True)[:, :, :width]
     total = jnp.zeros(emb_weight.shape, f32)
     for g in range(groups):
-        product = jnp.dot(lefts[g], full[g], preferred_element_type=f32).astype(bf16)
+        product = jnp.dot(lefts[g], rights[g], preferred_element_type=f32).astype(bf16)
         total = total + product.astype(f32)
     emb_mean = total / groups
     new_emb_momentum = beta_outer * emb_momentum + emb_mean

time: 148 us -> 151 us (1.020)
  between operations: 1.2 us -> 14.6 us
  blocking collectives: 13.1 us -> 0 us
  matrix products: 1.98 us -> 5.63 us
    all_gather x1 -> x0, blocking collectives: 13.1 us -> none  [on_device(): full = lax.all_gather(rchunks, 'tensor', axis=1, tiled=True)]
    dot_general x4, matrix products: 1.98 us -> 5.63 us  [on_device(): jnp.dot(lefts[g], rights[g], preferred_element_type=f32).astype(bf16)]
    dynamic_update_slice x3, local copies, waits for them, and re-layouts: 2.46 us -> 0.13 us  [on_device(): yblk = lax.dynamic_update_index_in_dim(yblk, got, (yi - k) % Y_SIZE, axis=0)]
  transfers between devices with their start and end apart: 19 -> 20, of which waited for: 9 -> 8; matrix products, arithmetic and copies ran while one was open for 7% -> 9% of each run, Pallas kernels for 0% -> 0%
where the time goes in v5:
time: 151 us; the launch traced here: 150 us
  starting transfers between devices  78.3 us (52%)
  waiting for transfers between devices  32 us (21%)
  local copies, waits for them, and re-layouts  18.2 us (12%)
  between operations  14.6 us (10%)
  matrix products  5.63 us (4%)
    ppermute x7, starting transfers between devices, on_device(): bwd = lax.ppermute(bwd, ('group', 'shard'), zshift(-1))  30.2 us
    ppermute x8, starting transfers between devices, on_device(): fwd = lax.ppermute(fwd, ('group', 'shard'), zshift(1))  21.5 us
    all_to_all x1, waiting for transfers between devices, on_device(): recv = lax.all_to_all(send, 'group', 0, 0, tiled=True)  18.7 us
    all_to_all x1, starting transfers between devices, on_device(): recv = lax.all_to_all(send, 'group', 0, 0, tiled=True)  15.1 us
    ppermute x8, waiting for transfers between devices, on_device(): fwd = lax.ppermute(fwd, ('group', 'shard'), zshift(1))  13.2 us
    ppermute x3, starting transfers between devices, on_device(): got = lax.ppermute(piece, 'shard', pairs)  11.6 us
    unnamed x18, local copies, waits for them, and re-layouts  9.4 us
    dot_general x4, matrix products, on_device(): jnp.dot(lefts[g], rights[g], preferred_element_type=f32).astype(bf16)  5.63 us
  transfers between devices with their start and end apart: 20, of which 8 were waited for; matrix products, arithmetic and copies ran while one was open for 9% of the time, Pallas kernels for 0%

profile of v5, /device:TPU:6, one launch (start us, length us, event | category | flops | bytes accessed | tf_op | source)
XLA Modules:
  0.0 150.1 jit_solution(1501636137274168463)
XLA Ops:
  7.2 1.1 copy.55
  8.3 0.1 reshape_squeeze.3
  8.4 0.9 copy.54
  9.4 0.3 reshape.37
  9.8 0.2 maximum_bitcast_fusion
  9.9 0.5 broadcast.48
  10.5 1.0 reduce.8
  11.4 0.8 reshape.45
  12.3 15.1 %all-to-all-start = ((bf16[4,2,16896]{2,1,0:T(2,128)(2,1)}), bf16[4,2,16896]{2,1,0:T(2,128)(2,1)S(1)}, u32[]{:S(2)}, u32[]{:S(2)}) async-start(bf16[4,2,16896]{2,1,0:T(2,128)(2,1)} %reshape.45), calls=%async_computation | async-start | bytes 540672 | tf_op jit(solution)/shard_map/all_to_all | solution.py:42
  27.3 18.7 %all-to-all-done = bf16[4,2,16896]{2,1,0:T(2,128)(2,1)S(1)} async-done(((bf16[4,2,16896]{2,1,0:T(2,128)(2,1)}), bf16[4,2,16896]{2,1,0:T(2,128)(2,1)S(1)}, u32[]{:S(2)}, u32[]{:S(2)}) %all-to-all-start) | async-done | bytes 270368 | tf_op jit(solution)/shard_map/all_to_all | solution.py:42
  46.1 0.2 reshape.46
  46.3 0.1 copy.82
  46.5 0.2 convert_reduce_fusion
  46.8 3.5 %collective-permute-start = (bf16[2,14,608]{2,1,0:T(8,128)(2,1)S(1)}, bf16[2,14,608]{2,1,0:T(8,128)(2,1)S(1)}, u32[]{:S(2)}, u32[]{:S(2)}) collective-permute-start(bf16[2,14,608]{2,1,0:T(8,128)(2,1)S(1)} %get-tuple-element.26), channel_id=1, source_target_pairs={{0,8},{8,16},{16,24},{24,0},{32,40},{40,48},{48,56},{56,32},{64,72... | collective-permute-start | bytes 102152 | tf_op jit(solution)/shard_map/ppermute | solution.py:55
  50.3 4.8 %collective-permute-start.1 = (bf16[2,14,608]{2,1,0:T(8,128)(2,1)S(1)}, bf16[2,14,608]{2,1,0:T(8,128)(2,1)S(1)}, u32[]{:S(2)}, u32[]{:S(2)}) collective-permute-start(bf16[2,14,608]{2,1,0:T(8,128)(2,1)S(1)} %get-tuple-element.26), channel_id=1, source_target_pairs={{0,16},{8,24},{16,0},{24,8},{32,48},{40,56},{48,32},{56,40},{64,80... | collective-permute-start | bytes 102152 | tf_op jit(solution)/shard_map/ppermute | solution.py:55
  55.1 3.3 %collective-permute-start.2 = (bf16[2,14,608]{2,1,0:T(8,128)(2,1)S(1)}, bf16[2,14,608]{2,1,0:T(8,128)(2,1)S(1)}, u32[]{:S(2)}, u32[]{:S(2)}) collective-permute-start(bf16[2,14,608]{2,1,0:T(8,128)(2,1)S(1)} %get-tuple-element.26), channel_id=1, source_target_pairs={{0,24},{8,0},{16,8},{24,16},{32,56},{40,32},{48,40},{56,48},{64,88... | collective-permute-start | bytes 102152 | tf_op jit(solution)/shard_map/ppermute | solution.py:55
  58.4 0.7 copy.63
  59.1 0.7 copy.64
  59.8 0.7 pad.4
  60.6 0.4 slice_reduce_fusion.3
  61.0 0.7 squeeze.35
  61.7 0.7 squeeze.33
  62.4 0.7 squeeze.31
  63.4 5.3 %collective-permute-start.3 = (bf16[4,2,14,608]{3,1,2,0:T(2,128)(2,1)S(1)}, bf16[4,2,14,608]{3,1,2,0:T(2,128)(2,1)S(1)}, u32[]{:S(2)}, u32[]{:S(2)}) collective-permute-start(bf16[4,2,14,608]{3,1,2,0:T(2,128)(2,1)S(1)} %copy_dynamic-update-slice_fusion), channel_id=1, source_target_pairs={{0,32},{8,40},{16,48},{24,56},{32,64},{40,72},{48,80},{56,88},{64,... | collective-permute-start | bytes 408584 | tf_op jit(solution)/shard_map/ppermute | solution.py:71
  68.7 1.9 %collective-permute-start.4 = (bf16[4,2,14,608]{3,1,2,0:T(2,128)(2,1)S(1)}, bf16[4,2,14,608]{3,1,2,0:T(2,128)(2,1)S(1)}, u32[]{:S(2)}, u32[]{:S(2)}) collective-permute-start(bf16[4,2,14,608]{3,1,2,0:T(2,128)(2,1)S(1)} %copy_dynamic-update-slice_fusion), channel_id=1, source_target_pairs={{0,480},{8,488},{16,496},{24,504},{32,0},{40,8},{48,16},{56,24},{6... | collective-permute-start | bytes 408584 | tf_op jit(solution)/shard_map/ppermute | solution.py:74
  70.7 1.2 broadcast_in_dim.77
  71.9 0.1 bitcast_dynamic-update-slice_fusion.15
  72.0 3.9 %collective-permute-start.5 = (bf16[4,2,14,608]{3,1,2,0:T(2,128)(2,1)S(1)}, bf16[4,2,14,608]{3,1,2,0:T(2,128)(2,1)S(1)}, u32[]{:S(2)}, u32[]{:S(2)}) collective-permute-start(bf16[4,2,14,608]{3,1,2,0:T(2,128)(2,1)S(1)} %collective-permute-done.3), channel_id=1, source_target_pairs={{0,32},{8,40},{16,48},{24,56},{32,64},{40,72},{48,80},{56,88},{64,... | collective-permute-start | bytes 408584 | tf_op jit(solution)/shard_map/ppermute | solution.py:71
  75.9 3.1 %collective-permute-start.6 = (bf16[4,2,14,608]{3,1,2,0:T(2,128)(2,1)S(1)}, bf16[4,2,14,608]{3,1,2,0:T(2,128)(2,1)S(1)}, u32[]{:S(2)}, u32[]{:S(2)}) collective-permute-start(bf16[4,2,14,608]{3,1,2,0:T(2,128)(2,1)S(1)} %collective-permute-done.4), channel_id=1, source_target_pairs={{0,480},{8,488},{16,496},{24,504},{32,0},{40,8},{48,16},{56,24},{6... | collective-permute-start | bytes 408584 | tf_op jit(solution)/shard_map/ppermute | solution.py:74
  79.1 0.1 bitcast_dynamic-update-slice_fusion.14
  79.2 0.1 bitcast_dynamic-update-slice_fusion.13
  79.3 0.9 collective-permute-done.5
  80.2 2.7 %collective-permute-start.7 = (bf16[4,2,14,608]{3,1,2,0:T(2,128)(2,1)S(1)}, bf16[4,2,14,608]{3,1,2,0:T(2,128)(2,1)S(1)}, u32[]{:S(2)}, u32[]{:S(2)}) collective-permute-start(bf16[4,2,14,608]{3,1,2,0:T(2,128)(2,1)S(1)} %collective-permute-done.5), channel_id=1, source_target_pairs={{0,32},{8,40},{16,48},{24,56},{32,64},{40,72},{48,80},{56,88},{64,... | collective-permute-start | bytes 408584 | tf_op jit(solution)/shard_map/ppermute | solution.py:71
  82.9 4.3 %collective-permute-start.8 = (bf16[4,2,14,608]{3,1,2,0:T(2,128)(2,1)S(1)}, bf16[4,2,14,608]{3,1,2,0:T(2,128)(2,1)S(1)}, u32[]{:S(2)}, u32[]{:S(2)}) collective-permute-start(bf16[4,2,14,608]{3,1,2,0:T(2,128)(2,1)S(1)} %collective-permute-done.6), channel_id=1, source_target_pairs={{0,480},{8,488},{16,496},{24,504},{32,0},{40,8},{48,16},{56,24},{6... | collective-permute-start | bytes 408584 | tf_op jit(solution)/shard_map/ppermute | solution.py:74
  87.3 0.1 bitcast_dynamic-update-slice_fusion.12
  87.5 0.9 collective-permute-done.7
  88.4 1.9 %collective-permute-start.9 = (bf16[4,2,14,608]{3,1,2,0:T(2,128)(2,1)S(1)}, bf16[4,2,14,608]{3,1,2,0:T(2,128)(2,1)S(1)}, u32[]{:S(2)}, u32[]{:S(2)}) collective-permute-start(bf16[4,2,14,608]{3,1,2,0:T(2,128)(2,1)S(1)} %collective-permute-done.7), channel_id=1, source_target_pairs={{0,32},{8,40},{16,48},{24,56},{32,64},{40,72},{48,80},{56,88},{64,... | collective-permute-start | bytes 408584 | tf_op jit(solution)/shard_map/ppermute | solution.py:71
  90.3 5.1 %collective-permute-start.10 = (bf16[4,2,14,608]{3,1,2,0:T(2,128)(2,1)S(1)}, bf16[4,2,14,608]{3,1,2,0:T(2,128)(2,1)S(1)}, u32[]{:S(2)}, u32[]{:S(2)}) collective-permute-start(bf16[4,2,14,608]{3,1,2,0:T(2,128)(2,1)S(1)} %collective-permute-done.8), channel_id=1, source_target_pairs={{0,480},{8,488},{16,496},{24,504},{32,0},{40,8},{48,16},{56,24},{6... | collective-permute-start | bytes 408584 | tf_op jit(solution)/shard_map/ppermute | solution.py:74
  95.5 0.1 bitcast_dynamic-update-slice_fusion.10
  95.6 0.1 bitcast_dynamic-update-slice_fusion.9
  95.7 1.6 %collective-permute-done.9 = bf16[4,2,14,608]{3,1,2,0:T(2,128)(2,1)S(1)} collective-permute-done((bf16[4,2,14,608]{3,1,2,0:T(2,128)(2,1)S(1)}, bf16[4,2,14,608]{3,1,2,0:T(2,128)(2,1)S(1)}, u32[]{:S(2)}, u32[]{:S(2)}) %collective-permute-start.9) | collective-permute-done | bytes 136224 | tf_op jit(solution)/shard_map/ppermute | solution.py:71
  97.3 1.9 %collective-permute-start.11 = (bf16[4,2,14,608]{3,1,2,0:T(2,128)(2,1)S(1)}, bf16[4,2,14,608]{3,1,2,0:T(2,128)(2,1)S(1)}, u32[]{:S(2)}, u32[]{:S(2)}) collective-permute-start(bf16[4,2,14,608]{3,1,2,0:T(2,128)(2,1)S(1)} %collective-permute-done.9), channel_id=1, source_target_pairs={{0,32},{8,40},{16,48},{24,56},{32,64},{40,72},{48,80},{56,88},{64,... | collective-permute-start | bytes 408584 | tf_op jit(solution)/shard_map/ppermute | solution.py:71
  99.2 5.4 %collective-permute-start.12 = (bf16[4,2,14,608]{3,1,2,0:T(2,128)(2,1)S(1)}, bf16[4,2,14,608]{3,1,2,0:T(2,128)(2,1)S(1)}, u32[]{:S(2)}, u32[]{:S(2)}) collective-permute-start(bf16[4,2,14,608]{3,1,2,0:T(2,128)(2,1)S(1)} %collective-permute-done.10), channel_id=1, source_target_pairs={{0,480},{8,488},{16,496},{24,504},{32,0},{40,8},{48,16},{56,24},{6... | collective-permute-start | bytes 408584 | tf_op jit(solution)/shard_map/ppermute | solution.py:74
  104.6 0.1 bitcast_dynamic-update-slice_fusion.8
  104.8 0.1 bitcast_dynamic-update-slice_fusion.7
  104.9 1.8 %collective-permute-done.11 = bf16[4,2,14,608]{3,1,2,0:T(2,128)(2,1)S(1)} collective-permute-done((bf16[4,2,14,608]{3,1,2,0:T(2,128)(2,1)S(1)}, bf16[4,2,14,608]{3,1,2,0:T(2,128)(2,1)S(1)}, u32[]{:S(2)}, u32[]{:S(2)}) %collective-permute-start.11) | collective-permute-done | bytes 136224 | tf_op jit(solution)/shard_map/ppermute | solution.py:71
  106.7 1.9 %collective-permute-start.13 = (bf16[4,2,14,608]{3,1,2,0:T(2,128)(2,1)S(1)}, bf16[4,2,14,608]{3,1,2,0:T(2,128)(2,1)S(1)}, u32[]{:S(2)}, u32[]{:S(2)}) collective-permute-start(bf16[4,2,14,608]{3,1,2,0:T(2,128)(2,1)S(1)} %collective-permute-done.11), channel_id=1, source_target_pairs={{0,32},{8,40},{16,48},{24,56},{32,64},{40,72},{48,80},{56,88},{64,... | collective-permute-start | bytes 408584 | tf_op jit(solution)/shard_map/ppermute | solution.py:71
  108.6 5.1 %collective-permute-start.14 = (bf16[4,2,14,608]{3,1,2,0:T(2,128)(2,1)S(1)}, bf16[4,2,14,608]{3,1,2,0:T(2,128)(2,1)S(1)}, u32[]{:S(2)}, u32[]{:S(2)}) collective-permute-start(bf16[4,2,14,608]{3,1,2,0:T(2,128)(2,1)S(1)} %collective-permute-done.12), channel_id=1, source_target_pairs={{0,480},{8,488},{16,496},{24,504},{32,0},{40,8},{48,16},{56,24},{6... | collective-permute-start | bytes 408584 | tf_op jit(solution)/shard_map/ppermute | solution.py:74
  113.8 0.1 bitcast_dynamic-update-slice_fusion.6
  113.9 0.1 bitcast_dynamic-update-slice_fusion.5
  114.0 1.2 collective-permute-done.13
  115.3 1.9 %collective-permute-start.15 = (bf16[4,2,14,608]{3,1,2,0:T(2,128)(2,1)S(1)}, bf16[4,2,14,608]{3,1,2,0:T(2,128)(2,1)S(1)}, u32[]{:S(2)}, u32[]{:S(2)}) collective-permute-start(bf16[4,2,14,608]{3,1,2,0:T(2,128)(2,1)S(1)} %collective-permute-done.13), channel_id=1, source_target_pairs={{0,32},{8,40},{16,48},{24,56},{32,64},{40,72},{48,80},{56,88},{64,... | collective-permute-start | bytes 408584 | tf_op jit(solution)/shard_map/ppermute | solution.py:71
  117.2 5.1 %collective-permute-start.16 = (bf16[4,2,14,608]{3,1,2,0:T(2,128)(2,1)S(1)}, bf16[4,2,14,608]{3,1,2,0:T(2,128)(2,1)S(1)}, u32[]{:S(2)}, u32[]{:S(2)}) collective-permute-start(bf16[4,2,14,608]{3,1,2,0:T(2,128)(2,1)S(1)} %collective-permute-done.14), channel_id=1, source_target_pairs={{0,480},{8,488},{16,496},{24,504},{32,0},{40,8},{48,16},{56,24},{6... | collective-permute-start | bytes 408584 | tf_op jit(solution)/shard_map/ppermute | solution.py:74
  122.3 0.1 bitcast_dynamic-update-slice_fusion.4
  122.6 0.9 collective-permute-done.15
  123.5 1.9 %collective-permute-start.17 = (bf16[4,2,14,608]{3,1,2,0:T(2,128)(2,1)S(1)}, bf16[4,2,14,608]{3,1,2,0:T(2,128)(2,1)S(1)}, u32[]{:S(2)}, u32[]{:S(2)}) collective-permute-start(bf16[4,2,14,608]{3,1,2,0:T(2,128)(2,1)S(1)} %collective-permute-done.15), channel_id=1, source_target_pairs={{0,32},{8,40},{16,48},{24,56},{32,64},{40,72},{48,80},{56,88},{64,... | collective-permute-start | bytes 408584 | tf_op jit(solution)/shard_map/ppermute | solution.py:71
  125.4 0.1 bitcast_dynamic-update-slice_fusion.2
  125.5 0.1 bitcast_dynamic-update-slice_fusion.1
  125.7 6.0 %collective-permute-done.17 = bf16[4,2,14,608]{3,1,2,0:T(2,128)(2,1)S(1)} collective-permute-done((bf16[4,2,14,608]{3,1,2,0:T(2,128)(2,1)S(1)}, bf16[4,2,14,608]{3,1,2,0:T(2,128)(2,1)S(1)}, u32[]{:S(2)}, u32[]{:S(2)}) %collective-permute-start.17) | collective-permute-done | bytes 136224 | tf_op jit(solution)/shard_map/ppermute | solution.py:71
  131.8 5.7 %copy.65 = bf16[2,896,608]{1,2,0:T(8,128)(2,1)} copy(bf16[2,896,608]{2,0,1:T(2,128)(2,1)S(1)} %bitcast.69) | data formatting | bytes 4358144
  137.6 1.1 fusion.7
  138.7 1.1 fusion.6
  139.8 1.1 fusion.5
  141.0 2.3 %multiply_subtract_fusion = (f32[150,896]{1,0:T(8,128)}, f32[150,896]{1,0:T(8,128)}) fusion(f32[150,896]{1,0:T(8,128)S(1)} %copy-done.1, f32[150,896]{1,0:T(8,128)S(1)} %copy-done.2, f32[150,896]{1,0:T(8,128)S(1)} %fusion.7, f32[150,896]{1,0:T(8,128)S(1)} %fusion.6, f32[150,896]{1,0:T(8,128)S(1)} %fusion.5, bf16[150,64]{1,0:T(8,128)(2,1)S(1)} %squeeze.29, ...), kind=kOutput, calls=%fused_computation.12 | convolution fusion | flops 18816000 | bytes 3897088 | tf_op jit(solution)/shard_map/dot_general | solution.py:85
  (41 shorter events, 1.0 us)
Async XLA Ops:
  7.2 2.5 %copy-start = (bf16[1,64,896]{2,1,0:T(8,128)(2,1)S(1)}, bf16[1,64,896]{2,1,0:T(8,128)(2,1)}, u32[]{:S(2)}) copy-start(bf16[1,64,896]{2,1,0:T(8,128)(2,1)} %param.9) | copy-start | bytes 344068
  9.9 36.9 %copy-start.3 = (f32[2,14,608]{2,0,1:T(2,128)S(1)}, f32[2,14,608]{2,0,1:T(2,128)}, u32[]{:S(2)}) copy-start(f32[2,14,608]{2,0,1:T(2,128)} %param.11) | copy-start | bytes 204292
  9.9 36.9 %copy-start.4 = (f32[2,14,608]{2,0,1:T(2,128)S(1)}, f32[2,14,608]{2,0,1:T(2,128)}, u32[]{:S(2)}) copy-start(f32[2,14,608]{2,0,1:T(2,128)} %param.10) | copy-start | bytes 204292
  12.3 33.8 %all-to-all-start = ((bf16[4,2,16896]{2,1,0:T(2,128)(2,1)}), bf16[4,2,16896]{2,1,0:T(2,128)(2,1)S(1)}, u32[]{:S(2)}, u32[]{:S(2)}) async-start(bf16[4,2,16896]{2,1,0:T(2,128)(2,1)} %reshape.45), calls=%async_computation | async-start | bytes 540672 | tf_op jit(solution)/shard_map/all_to_all | solution.py:42
  27.3 110.2 %all-gather.2.cloned.1.call-start = ((), (), s32[]{:S(2)}) async-start(), calls=%async_computation.1 | async-start | bytes 1179648 | tf_op jit(solution)/shard_map/all_gather | solution.py:82
  46.8 16.4 %collective-permute-start = (bf16[2,14,608]{2,1,0:T(8,128)(2,1)S(1)}, bf16[2,14,608]{2,1,0:T(8,128)(2,1)S(1)}, u32[]{:S(2)}, u32[]{:S(2)}) collective-permute-start(bf16[2,14,608]{2,1,0:T(8,128)(2,1)S(1)} %get-tuple-element.26), channel_id=1, source_target_pairs={{0,8},{8,16},{16,24},{24,0},{32,40},{40,48},{48,56},{56,32},{64,72... | collective-permute-start | bytes 102152 | tf_op jit(solution)/shard_map/ppermute | solution.py:55
  50.3 13.0 %collective-permute-start.1 = (bf16[2,14,608]{2,1,0:T(8,128)(2,1)S(1)}, bf16[2,14,608]{2,1,0:T(8,128)(2,1)S(1)}, u32[]{:S(2)}, u32[]{:S(2)}) collective-permute-start(bf16[2,14,608]{2,1,0:T(8,128)(2,1)S(1)} %get-tuple-element.26), channel_id=1, source_target_pairs={{0,16},{8,24},{16,0},{24,8},{32,48},{40,56},{48,32},{56,40},{64,80... | collective-permute-start | bytes 102152 | tf_op jit(solution)/shard_map/ppermute | solution.py:55
  55.1 8.2 %collective-permute-start.2 = (bf16[2,14,608]{2,1,0:T(8,128)(2,1)S(1)}, bf16[2,14,608]{2,1,0:T(8,128)(2,1)S(1)}, u32[]{:S(2)}, u32[]{:S(2)}) collective-permute-start(bf16[2,14,608]{2,1,0:T(8,128)(2,1)S(1)} %get-tuple-element.26), channel_id=1, source_target_pairs={{0,24},{8,0},{16,8},{24,16},{32,56},{40,32},{48,40},{56,48},{64,88... | collective-permute-start | bytes 102152 | tf_op jit(solution)/shard_map/ppermute | solution.py:55
  63.4 8.6 %collective-permute-start.3 = (bf16[4,2,14,608]{3,1,2,0:T(2,128)(2,1)S(1)}, bf16[4,2,14,608]{3,1,2,0:T(2,128)(2,1)S(1)}, u32[]{:S(2)}, u32[]{:S(2)}) collective-permute-start(bf16[4,2,14,608]{3,1,2,0:T(2,128)(2,1)S(1)} %copy_dynamic-update-slice_fusion), channel_id=1, source_target_pairs={{0,32},{8,40},{16,48},{24,56},{32,64},{40,72},{48,80},{56,88},{64,... | collective-permute-start | bytes 408584 | tf_op jit(solution)/shard_map/ppermute | solution.py:71
  68.7 7.2 %collective-permute-start.4 = (bf16[4,2,14,608]{3,1,2,0:T(2,128)(2,1)S(1)}, bf16[4,2,14,608]{3,1,2,0:T(2,128)(2,1)S(1)}, u32[]{:S(2)}, u32[]{:S(2)}) collective-permute-start(bf16[4,2,14,608]{3,1,2,0:T(2,128)(2,1)S(1)} %copy_dynamic-update-slice_fusion), channel_id=1, source_target_pairs={{0,480},{8,488},{16,496},{24,504},{32,0},{40,8},{48,16},{56,24},{6... | collective-permute-start | bytes 408584 | tf_op jit(solution)/shard_map/ppermute | solution.py:74
  72.0 8.2 %collective-permute-start.5 = (bf16[4,2,14,608]{3,1,2,0:T(2,128)(2,1)S(1)}, bf16[4,2,14,608]{3,1,2,0:T(2,128)(2,1)S(1)}, u32[]{:S(2)}, u32[]{:S(2)}) collective-permute-start(bf16[4,2,14,608]{3,1,2,0:T(2,128)(2,1)S(1)} %collective-permute-done.3), channel_id=1, source_target_pairs={{0,32},{8,40},{16,48},{24,56},{32,64},{40,72},{48,80},{56,88},{64,... | collective-permute-start | bytes 408584 | tf_op jit(solution)/shard_map/ppermute | solution.py:71
  75.9 7.0 %collective-permute-start.6 = (bf16[4,2,14,608]{3,1,2,0:T(2,128)(2,1)S(1)}, bf16[4,2,14,608]{3,1,2,0:T(2,128)(2,1)S(1)}, u32[]{:S(2)}, u32[]{:S(2)}) collective-permute-start(bf16[4,2,14,608]{3,1,2,0:T(2,128)(2,1)S(1)} %collective-permute-done.4), channel_id=1, source_target_pairs={{0,480},{8,488},{16,496},{24,504},{32,0},{40,8},{48,16},{56,24},{6... | collective-permute-start | bytes 408584 | tf_op jit(solution)/shard_map/ppermute | solution.py:74
  80.2 8.2 %collective-permute-start.7 = (bf16[4,2,14,608]{3,1,2,0:T(2,128)(2,1)S(1)}, bf16[4,2,14,608]{3,1,2,0:T(2,128)(2,1)S(1)}, u32[]{:S(2)}, u32[]{:S(2)}) collective-permute-start(bf16[4,2,14,608]{3,1,2,0:T(2,128)(2,1)S(1)} %collective-permute-done.5), channel_id=1, source_target_pairs={{0,32},{8,40},{16,48},{24,56},{32,64},{40,72},{48,80},{56,88},{64,... | collective-permute-start | bytes 408584 | tf_op jit(solution)/shard_map/ppermute | solution.py:71
  82.9 7.4 %collective-permute-start.8 = (bf16[4,2,14,608]{3,1,2,0:T(2,128)(2,1)S(1)}, bf16[4,2,14,608]{3,1,2,0:T(2,128)(2,1)S(1)}, u32[]{:S(2)}, u32[]{:S(2)}) collective-permute-start(bf16[4,2,14,608]{3,1,2,0:T(2,128)(2,1)S(1)} %collective-permute-done.6), channel_id=1, source_target_pairs={{0,480},{8,488},{16,496},{24,504},{32,0},{40,8},{48,16},{56,24},{6... | collective-permute-start | bytes 408584 | tf_op jit(solution)/shard_map/ppermute | solution.py:74
  88.4 8.9 %collective-permute-start.9 = (bf16[4,2,14,608]{3,1,2,0:T(2,128)(2,1)S(1)}, bf16[4,2,14,608]{3,1,2,0:T(2,128)(2,1)S(1)}, u32[]{:S(2)}, u32[]{:S(2)}) collective-permute-start(bf16[4,2,14,608]{3,1,2,0:T(2,128)(2,1)S(1)} %collective-permute-done.7), channel_id=1, source_target_pairs={{0,32},{8,40},{16,48},{24,56},{32,64},{40,72},{48,80},{56,88},{64,... | collective-permute-start | bytes 408584 | tf_op jit(solution)/shard_map/ppermute | solution.py:71
  90.3 8.9 %collective-permute-start.10 = (bf16[4,2,14,608]{3,1,2,0:T(2,128)(2,1)S(1)}, bf16[4,2,14,608]{3,1,2,0:T(2,128)(2,1)S(1)}, u32[]{:S(2)}, u32[]{:S(2)}) collective-permute-start(bf16[4,2,14,608]{3,1,2,0:T(2,128)(2,1)S(1)} %collective-permute-done.8), channel_id=1, source_target_pairs={{0,480},{8,488},{16,496},{24,504},{32,0},{40,8},{48,16},{56,24},{6... | collective-permute-start | bytes 408584 | tf_op jit(solution)/shard_map/ppermute | solution.py:74
  97.3 9.4 %collective-permute-start.11 = (bf16[4,2,14,608]{3,1,2,0:T(2,128)(2,1)S(1)}, bf16[4,2,14,608]{3,1,2,0:T(2,128)(2,1)S(1)}, u32[]{:S(2)}, u32[]{:S(2)}) collective-permute-start(bf16[4,2,14,608]{3,1,2,0:T(2,128)(2,1)S(1)} %collective-permute-done.9), channel_id=1, source_target_pairs={{0,32},{8,40},{16,48},{24,56},{32,64},{40,72},{48,80},{56,88},{64,... | collective-permute-start | bytes 408584 | tf_op jit(solution)/shard_map/ppermute | solution.py:71
  99.2 9.4 %collective-permute-start.12 = (bf16[4,2,14,608]{3,1,2,0:T(2,128)(2,1)S(1)}, bf16[4,2,14,608]{3,1,2,0:T(2,128)(2,1)S(1)}, u32[]{:S(2)}, u32[]{:S(2)}) collective-permute-start(bf16[4,2,14,608]{3,1,2,0:T(2,128)(2,1)S(1)} %collective-permute-done.10), channel_id=1, source_target_pairs={{0,480},{8,488},{16,496},{24,504},{32,0},{40,8},{48,16},{56,24},{6... | collective-permute-start | bytes 408584 | tf_op jit(solution)/shard_map/ppermute | solution.py:74
  106.7 8.6 %collective-permute-start.13 = (bf16[4,2,14,608]{3,1,2,0:T(2,128)(2,1)S(1)}, bf16[4,2,14,608]{3,1,2,0:T(2,128)(2,1)S(1)}, u32[]{:S(2)}, u32[]{:S(2)}) collective-permute-start(bf16[4,2,14,608]{3,1,2,0:T(2,128)(2,1)S(1)} %collective-permute-done.11), channel_id=1, source_target_pairs={{0,32},{8,40},{16,48},{24,56},{32,64},{40,72},{48,80},{56,88},{64,... | collective-permute-start | bytes 408584 | tf_op jit(solution)/shard_map/ppermute | solution.py:71
  108.6 8.6 %collective-permute-start.14 = (bf16[4,2,14,608]{3,1,2,0:T(2,128)(2,1)S(1)}, bf16[4,2,14,608]{3,1,2,0:T(2,128)(2,1)S(1)}, u32[]{:S(2)}, u32[]{:S(2)}) collective-permute-start(bf16[4,2,14,608]{3,1,2,0:T(2,128)(2,1)S(1)} %collective-permute-done.12), channel_id=1, source_target_pairs={{0,480},{8,488},{16,496},{24,504},{32,0},{40,8},{48,16},{56,24},{6... | collective-permute-start | bytes 408584 | tf_op jit(solution)/shard_map/ppermute | solution.py:74
  115.3 8.2 %collective-permute-start.15 = (bf16[4,2,14,608]{3,1,2,0:T(2,128)(2,1)S(1)}, bf16[4,2,14,608]{3,1,2,0:T(2,128)(2,1)S(1)}, u32[]{:S(2)}, u32[]{:S(2)}) collective-permute-start(bf16[4,2,14,608]{3,1,2,0:T(2,128)(2,1)S(1)} %collective-permute-done.13), channel_id=1, source_target_pairs={{0,32},{8,40},{16,48},{24,56},{32,64},{40,72},{48,80},{56,88},{64,... | collective-permute-start | bytes 408584 | tf_op jit(solution)/shard_map/ppermute | solution.py:71
  117.2 8.3 %collective-permute-start.16 = (bf16[4,2,14,608]{3,1,2,0:T(2,128)(2,1)S(1)}, bf16[4,2,14,608]{3,1,2,0:T(2,128)(2,1)S(1)}, u32[]{:S(2)}, u32[]{:S(2)}) collective-permute-start(bf16[4,2,14,608]{3,1,2,0:T(2,128)(2,1)S(1)} %collective-permute-done.14), channel_id=1, source_target_pairs={{0,480},{8,488},{16,496},{24,504},{32,0},{40,8},{48,16},{56,24},{6... | collective-permute-start | bytes 408584 | tf_op jit(solution)/shard_map/ppermute | solution.py:74
  123.5 8.2 %collective-permute-start.17 = (bf16[4,2,14,608]{3,1,2,0:T(2,128)(2,1)S(1)}, bf16[4,2,14,608]{3,1,2,0:T(2,128)(2,1)S(1)}, u32[]{:S(2)}, u32[]{:S(2)}) collective-permute-start(bf16[4,2,14,608]{3,1,2,0:T(2,128)(2,1)S(1)} %collective-permute-done.15), channel_id=1, source_target_pairs={{0,32},{8,40},{16,48},{24,56},{32,64},{40,72},{48,80},{56,88},{64,... | collective-permute-start | bytes 408584 | tf_op jit(solution)/shard_map/ppermute | solution.py:71
  131.8 9.2 %copy-start.1 = (f32[150,896]{1,0:T(8,128)S(1)}, f32[150,896]{1,0:T(8,128)}, u32[]{:S(2)}) copy-start(f32[150,896]{1,0:T(8,128)} %param.12) | copy-start | bytes 1612804
  131.8 9.2 %copy-start.2 = (f32[150,896]{1,0:T(8,128)S(1)}, f32[150,896]{1,0:T(8,128)}, u32[]{:S(2)}) copy-start(f32[150,896]{1,0:T(8,128)} %param.13) | copy-start | bytes 1612804
Sparse Core Ops, SparseCore 0:
  60.6 22.2 all-gather.1

commit v6 on v4

--- a/solution.py
+++ b/solution.py
@@ -41,32 +41,49 @@
     new_layer_weight = layer_weight - rate_outer * (layer_mean + beta_outer * new_layer_momentum)
     piece = new_layer_weight.astype(bf16)
 
+    sgn = 1 - 2 * (ti % 2)
+    n_st = shards * tensors
+
+    def yshift(k):
+        pairs = []
+        for i in range(n_st):
+            s, t = i // tensors, i % tensors
+            d = k if t % 2 == 0 else -k
+            pairs.append((i, ((s - s % Y_SIZE) + (s % Y_SIZE + d) % Y_SIZE) * tensors + t))
+        return pairs
+
     yi = si % Y_SIZE
     yblk = jnp.zeros((Y_SIZE,) + piece.shape, piece.dtype)
     yblk = lax.dynamic_update_index_in_dim(yblk, piece, yi, axis=0)
-    for k in range(1, Y_SIZE):
-        pairs = [(s, (s - s % Y_SIZE) + (s % Y_SIZE + k) % Y_SIZE) for s in range(shards)]
-        got = lax.ppermute(piece, "shard", pairs)
-        yblk = lax.dynamic_update_index_in_dim(yblk, got, (yi - k) % Y_SIZE, axis=0)
+    for k in (1, -1, 2):
+        got = lax.ppermute(piece, ("shard", "tensor"), yshift(k))
+        yblk = lax.dynamic_update_index_in_dim(yblk, got, (yi - k * sgn) % Y_SIZE, axis=0)
 
     zlo_size = shards // Y_SIZE
     nz = groups * zlo_size
     zi = gi * zlo_size + si // Y_SIZE
-    n_all = groups * shards
+    n_all = groups * shards * tensors
 
     def zshift(k):
-        return [(i, ((i // Y_SIZE + k) % nz) * Y_SIZE + i % Y_SIZE) for i in range(n_all)]
+        pairs = []
+        for i in range(n_all):
+            gs, t = i // tensors, i % tensors
+            z, y = gs // Y_SIZE, gs % Y_SIZE
+            d = k if t % 2 == 0 else -k
+            pairs.append((i, (((z + d) % nz) * Y_SIZE + y) * tensors + t))
+        return pairs
 
     out = jnp.zeros((nz,) + yblk.shape, piece.dtype)
     out = lax.dynamic_update_index_in_dim(out, yblk, zi, axis=0)
     fwd = yblk
     bwd = yblk
+    axes = ("group", "shard", "tensor")
     for step in range(1, nz // 2 + 1):
-        fwd = lax.ppermute(fwd, ("group", "shard"), zshift(1))
-        out = lax.dynamic_update_index_in_dim(out, fwd, (zi - step) % nz, axis=0)
+        fwd = lax.ppermute(fwd, axes, zshift(1))
+        out = lax.dynamic_update_index_in_dim(out, fwd, (zi - step * sgn) % nz, axis=0)
         if step < nz - nz // 2:
-            bwd = lax.ppermute(bwd, ("group", "shard"), zshift(-1))
-            out = lax.dynamic_update_index_in_dim(out, bwd, (zi + step) % nz, axis=0)
+            bwd = lax.ppermute(bwd, axes, zshift(-1))
+            out = lax.dynamic_update_index_in_dim(out, bwd, (zi + step * sgn) % nz, axis=0)
     layer_blocks = jnp.moveaxis(out, 2, 0).reshape(piece.shape[0], -1, piece.shape[2])
 
     lefts = recv[:, nlayer:nlayer + nleft].reshape((groups,) + left.shape[1:])

time: 147 us -> 144 us (0.980)
  waiting for transfers between devices: 12.6 us -> 10.2 us
    ppermute x18, waiting for transfers between devices: 12.6 us -> 10.2 us  [the longest x8 7.75 us: on_device(): fwd = lax.ppermute(fwd, axes, zshift(1))]
  transfers between devices with their start and end apart: 19 -> 19, of which waited for: 7 -> 13; matrix products, arithmetic and copies ran while one was open for 6% -> 6% of each run, Pallas kernels for 0% -> 0%
where the time goes in v6:
time: 144 us
  starting transfers between devices  80.7 us (56%)
  blocking collectives  32.1 us (22%)
  local copies, waits for them, and re-layouts  16.3 us (11%)
  waiting for transfers between devices  10.2 us (7%)
  matrix products  1.98 us (1%)
    ppermute x7, starting transfers between devices, on_device(): bwd = lax.ppermute(bwd, axes, zshift(-1))  36.4 us
    all_gather x1, blocking collectives, on_device(): rights = lax.all_gather(emb_right, 'group', axis=0, tiled=True)  32.1 us
    ppermute x8, starting transfers between devices, on_device(): fwd = lax.ppermute(fwd, axes, zshift(1))  18.3 us
    all_to_all x1, starting transfers between devices, on_device(): recv = lax.all_to_all(send, 'group', 0, 0, tiled=True)  15.1 us
    ppermute x3, starting transfers between devices, on_device(): got = lax.ppermute(piece, ('shard', 'tensor'), yshift(k))  10.9 us
    unnamed x17, local copies, waits for them, and re-layouts  9.4 us
    ppermute x8, waiting for transfers between devices, on_device(): fwd = lax.ppermute(fwd, axes, zshift(1))  7.75 us
  transfers between devices with their start and end apart: 19, of which 13 were waited for; matrix products, arithmetic and copies ran while one was open for 6% of the time, Pallas kernels for 0%

profile of v6, /device:TPU:6, one launch (start us, length us, event | category | flops | bytes accessed | tf_op | source)
XLA Modules:
  0.0 143.6 jit_solution(11150271059879356122)
XLA Ops:
  0.6 1.1 copy.55
  1.7 0.1 reshape_squeeze.3
  1.9 0.9 copy.54
  2.8 0.3 reshape.30
  3.2 0.5 broadcast.45
  3.8 0.9 reduce.8
  4.7 0.8 reshape.36
  5.5 15.1 %all-to-all-start = ((bf16[4,2,13312]{2,1,0:T(2,128)(2,1)}), bf16[4,2,13312]{2,1,0:T(2,128)(2,1)S(1)}, u32[]{:S(2)}, u32[]{:S(2)}) async-start(bf16[4,2,13312]{2,1,0:T(2,128)(2,1)} %reshape.36), calls=%async_computation | async-start | bytes 425984 | tf_op jit(solution)/shard_map/all_to_all | solution.py:36
  20.6 32.1 %all_gather.3 = bf16[4,64,896]{2,1,0:T(8,128)(2,1)S(1)} all-gather(bf16[1,64,896]{2,1,0:T(8,128)(2,1)S(1)} %copy-done.2), channel_id=1, replica_groups=mesh['group'=4,'shard'=16,'tensor'=8] {'group'}, dimensions={0}, use_global_device_ids=true | all-gather | bytes 573440 | tf_op jit(solution)/shard_map/all_gather | solution.py:34
  52.7 0.2 reshape.37
  52.9 0.2 copy.80
  53.1 0.2 convert_reduce_fusion
  53.4 3.5 %collective-permute-start = (bf16[2,14,608]{2,1,0:T(8,128)(2,1)S(1)}, bf16[2,14,608]{2,1,0:T(8,128)(2,1)}, u32[]{:S(2)}, u32[]{:S(2)}) collective-permute-start(bf16[2,14,608]{2,1,0:T(8,128)(2,1)S(1)} %get-tuple-element.26), channel_id=1, source_target_pairs={{0,8},{1,25},{2,10},{3,27},{4,12},{5,29},{6,14},{7,31},{8,16},{9,1... | collective-permute-start | bytes 102152 | tf_op jit(solution)/shard_map/ppermute | solution.py:59
  56.9 3.6 %collective-permute-start.1 = (bf16[2,14,608]{2,1,0:T(8,128)(2,1)S(1)}, bf16[2,14,608]{2,1,0:T(8,128)(2,1)S(1)}, u32[]{:S(2)}, u32[]{:S(2)}) collective-permute-start(bf16[2,14,608]{2,1,0:T(8,128)(2,1)S(1)} %get-tuple-element.26), channel_id=1, source_target_pairs={{0,24},{1,9},{2,26},{3,11},{4,28},{5,13},{6,30},{7,15},{8,0},{9,17... | collective-permute-start | bytes 102152 | tf_op jit(solution)/shard_map/ppermute | solution.py:59
  60.5 3.9 %collective-permute-start.2 = (bf16[2,14,608]{2,1,0:T(8,128)(2,1)S(1)}, bf16[2,14,608]{2,1,0:T(8,128)(2,1)S(1)}, u32[]{:S(2)}, u32[]{:S(2)}) collective-permute-start(bf16[2,14,608]{2,1,0:T(8,128)(2,1)S(1)} %get-tuple-element.26), channel_id=1, source_target_pairs={{0,16},{1,17},{2,18},{3,19},{4,20},{5,21},{6,22},{7,23},{8,24},{9,... | collective-permute-start | bytes 102152 | tf_op jit(solution)/shard_map/ppermute | solution.py:59
  64.4 0.4 slice_reduce_fusion.3
  65.0 0.2 fusion.7
  65.2 0.2 fusion.6
  65.5 0.2 fusion.5
  65.9 1.4 multiply_subtract_fusion
  67.3 0.7 copy.63
  68.0 0.7 copy.64
  68.7 0.8 copy_dynamic-update-slice_fusion.2
  69.6 4.9 %collective-permute-start.3 = (bf16[4,2,14,608]{3,1,2,0:T(2,128)(2,1)S(1)}, bf16[4,2,14,608]{3,1,2,0:T(2,128)(2,1)S(1)}, u32[]{:S(2)}, u32[]{:S(2)}) collective-permute-start(bf16[4,2,14,608]{3,1,2,0:T(2,128)(2,1)S(1)} %copy_dynamic-update-slice_fusion), channel_id=1, source_target_pairs={{0,32},{1,481},{2,34},{3,483},{4,36},{5,485},{6,38},{7,487},{8,40}... | collective-permute-start | bytes 408584 | tf_op jit(solution)/shard_map/ppermute | solution.py:82
  74.5 4.1 %collective-permute-start.4 = (bf16[4,2,14,608]{3,1,2,0:T(2,128)(2,1)S(1)}, bf16[4,2,14,608]{3,1,2,0:T(2,128)(2,1)S(1)}, u32[]{:S(2)}, u32[]{:S(2)}) collective-permute-start(bf16[4,2,14,608]{3,1,2,0:T(2,128)(2,1)S(1)} %copy_dynamic-update-slice_fusion), channel_id=1, source_target_pairs={{0,480},{1,33},{2,482},{3,35},{4,484},{5,37},{6,486},{7,39},{8,488... | collective-permute-start | bytes 408584 | tf_op jit(solution)/shard_map/ppermute | solution.py:85
  78.6 1.2 broadcast_in_dim.68
  79.8 0.1 bitcast_dynamic-update-slice_fusion.15
  80.0 1.9 %collective-permute-start.5 = (bf16[4,2,14,608]{3,1,2,0:T(2,128)(2,1)S(1)}, bf16[4,2,14,608]{3,1,2,0:T(2,128)(2,1)S(1)}, u32[]{:S(2)}, u32[]{:S(2)}) collective-permute-start(bf16[4,2,14,608]{3,1,2,0:T(2,128)(2,1)S(1)} %collective-permute-done.3), channel_id=1, source_target_pairs={{0,32},{1,481},{2,34},{3,483},{4,36},{5,485},{6,38},{7,487},{8,40}... | collective-permute-start | bytes 408584 | tf_op jit(solution)/shard_map/ppermute | solution.py:82
  81.9 1.0 collective-permute-done.4
  82.9 4.7 %collective-permute-start.6 = (bf16[4,2,14,608]{3,1,2,0:T(2,128)(2,1)S(1)}, bf16[4,2,14,608]{3,1,2,0:T(2,128)(2,1)S(1)}, u32[]{:S(2)}, u32[]{:S(2)}) collective-permute-start(bf16[4,2,14,608]{3,1,2,0:T(2,128)(2,1)S(1)} %collective-permute-done.4), channel_id=1, source_target_pairs={{0,480},{1,33},{2,482},{3,35},{4,484},{5,37},{6,486},{7,39},{8,488... | collective-permute-start | bytes 408584 | tf_op jit(solution)/shard_map/ppermute | solution.py:85
  87.6 0.1 bitcast_dynamic-update-slice_fusion.14
  87.7 0.1 bitcast_dynamic-update-slice_fusion.13
  87.8 0.3 collective-permute-done.5
  88.2 1.9 %collective-permute-start.7 = (bf16[4,2,14,608]{3,1,2,0:T(2,128)(2,1)S(1)}, bf16[4,2,14,608]{3,1,2,0:T(2,128)(2,1)S(1)}, u32[]{:S(2)}, u32[]{:S(2)}) collective-permute-start(bf16[4,2,14,608]{3,1,2,0:T(2,128)(2,1)S(1)} %collective-permute-done.5), channel_id=1, source_target_pairs={{0,32},{1,481},{2,34},{3,483},{4,36},{5,485},{6,38},{7,487},{8,40}... | collective-permute-start | bytes 408584 | tf_op jit(solution)/shard_map/ppermute | solution.py:82
  90.1 0.4 collective-permute-done.6
  90.5 5.3 %collective-permute-start.8 = (bf16[4,2,14,608]{3,1,2,0:T(2,128)(2,1)S(1)}, bf16[4,2,14,608]{3,1,2,0:T(2,128)(2,1)S(1)}, u32[]{:S(2)}, u32[]{:S(2)}) collective-permute-start(bf16[4,2,14,608]{3,1,2,0:T(2,128)(2,1)S(1)} %collective-permute-done.6), channel_id=1, source_target_pairs={{0,480},{1,33},{2,482},{3,35},{4,484},{5,37},{6,486},{7,39},{8,488... | collective-permute-start | bytes 408584 | tf_op jit(solution)/shard_map/ppermute | solution.py:85
  95.8 0.1 bitcast_dynamic-update-slice_fusion.12
  95.9 0.1 bitcast_dynamic-update-slice_fusion.11
  96.0 0.3 collective-permute-done.7
  96.4 1.9 %collective-permute-start.9 = (bf16[4,2,14,608]{3,1,2,0:T(2,128)(2,1)S(1)}, bf16[4,2,14,608]{3,1,2,0:T(2,128)(2,1)S(1)}, u32[]{:S(2)}, u32[]{:S(2)}) collective-permute-start(bf16[4,2,14,608]{3,1,2,0:T(2,128)(2,1)S(1)} %collective-permute-done.7), channel_id=1, source_target_pairs={{0,32},{1,481},{2,34},{3,483},{4,36},{5,485},{6,38},{7,487},{8,40}... | collective-permute-start | bytes 408584 | tf_op jit(solution)/shard_map/ppermute | solution.py:82
  98.4 5.6 %collective-permute-start.10 = (bf16[4,2,14,608]{3,1,2,0:T(2,128)(2,1)S(1)}, bf16[4,2,14,608]{3,1,2,0:T(2,128)(2,1)S(1)}, u32[]{:S(2)}, u32[]{:S(2)}) collective-permute-start(bf16[4,2,14,608]{3,1,2,0:T(2,128)(2,1)S(1)} %collective-permute-done.8), channel_id=1, source_target_pairs={{0,480},{1,33},{2,482},{3,35},{4,484},{5,37},{6,486},{7,39},{8,488... | collective-permute-start | bytes 408584 | tf_op jit(solution)/shard_map/ppermute | solution.py:85
  104.0 0.1 bitcast_dynamic-update-slice_fusion.10
  104.1 0.1 bitcast_dynamic-update-slice_fusion.9
  104.2 0.3 collective-permute-done.9
  104.6 1.9 %collective-permute-start.11 = (bf16[4,2,14,608]{3,1,2,0:T(2,128)(2,1)S(1)}, bf16[4,2,14,608]{3,1,2,0:T(2,128)(2,1)S(1)}, u32[]{:S(2)}, u32[]{:S(2)}) collective-permute-start(bf16[4,2,14,608]{3,1,2,0:T(2,128)(2,1)S(1)} %collective-permute-done.9), channel_id=1, source_target_pairs={{0,32},{1,481},{2,34},{3,483},{4,36},{5,485},{6,38},{7,487},{8,40}... | collective-permute-start | bytes 408584 | tf_op jit(solution)/shard_map/ppermute | solution.py:82
  106.6 5.6 %collective-permute-start.12 = (bf16[4,2,14,608]{3,1,2,0:T(2,128)(2,1)S(1)}, bf16[4,2,14,608]{3,1,2,0:T(2,128)(2,1)S(1)}, u32[]{:S(2)}, u32[]{:S(2)}) collective-permute-start(bf16[4,2,14,608]{3,1,2,0:T(2,128)(2,1)S(1)} %collective-permute-done.10), channel_id=1, source_target_pairs={{0,480},{1,33},{2,482},{3,35},{4,484},{5,37},{6,486},{7,39},{8,488... | collective-permute-start | bytes 408584 | tf_op jit(solution)/shard_map/ppermute | solution.py:85
  112.2 0.1 bitcast_dynamic-update-slice_fusion.8
  112.3 0.1 bitcast_dynamic-update-slice_fusion.7
  112.4 0.3 collective-permute-done.11
  112.7 1.9 %collective-permute-start.13 = (bf16[4,2,14,608]{3,1,2,0:T(2,128)(2,1)S(1)}, bf16[4,2,14,608]{3,1,2,0:T(2,128)(2,1)S(1)}, u32[]{:S(2)}, u32[]{:S(2)}) collective-permute-start(bf16[4,2,14,608]{3,1,2,0:T(2,128)(2,1)S(1)} %collective-permute-done.11), channel_id=1, source_target_pairs={{0,32},{1,481},{2,34},{3,483},{4,36},{5,485},{6,38},{7,487},{8,40}... | collective-permute-start | bytes 408584 | tf_op jit(solution)/shard_map/ppermute | solution.py:82
  114.8 5.6 %collective-permute-start.14 = (bf16[4,2,14,608]{3,1,2,0:T(2,128)(2,1)S(1)}, bf16[4,2,14,608]{3,1,2,0:T(2,128)(2,1)S(1)}, u32[]{:S(2)}, u32[]{:S(2)}) collective-permute-start(bf16[4,2,14,608]{3,1,2,0:T(2,128)(2,1)S(1)} %collective-permute-done.12), channel_id=1, source_target_pairs={{0,480},{1,33},{2,482},{3,35},{4,484},{5,37},{6,486},{7,39},{8,488... | collective-permute-start | bytes 408584 | tf_op jit(solution)/shard_map/ppermute | solution.py:85
  120.4 0.1 bitcast_dynamic-update-slice_fusion.6
  120.5 0.1 bitcast_dynamic-update-slice_fusion.5
  120.6 0.7 collective-permute-done.13
  121.3 1.9 %collective-permute-start.15 = (bf16[4,2,14,608]{3,1,2,0:T(2,128)(2,1)S(1)}, bf16[4,2,14,608]{3,1,2,0:T(2,128)(2,1)S(1)}, u32[]{:S(2)}, u32[]{:S(2)}) collective-permute-start(bf16[4,2,14,608]{3,1,2,0:T(2,128)(2,1)S(1)} %collective-permute-done.13), channel_id=1, source_target_pairs={{0,32},{1,481},{2,34},{3,483},{4,36},{5,485},{6,38},{7,487},{8,40}... | collective-permute-start | bytes 408584 | tf_op jit(solution)/shard_map/ppermute | solution.py:82
  123.3 0.4 collective-permute-done.14
  123.7 5.6 %collective-permute-start.16 = (bf16[4,2,14,608]{3,1,2,0:T(2,128)(2,1)S(1)}, bf16[4,2,14,608]{3,1,2,0:T(2,128)(2,1)S(1)}, u32[]{:S(2)}, u32[]{:S(2)}) collective-permute-start(bf16[4,2,14,608]{3,1,2,0:T(2,128)(2,1)S(1)} %collective-permute-done.14), channel_id=1, source_target_pairs={{0,480},{1,33},{2,482},{3,35},{4,484},{5,37},{6,486},{7,39},{8,488... | collective-permute-start | bytes 408584 | tf_op jit(solution)/shard_map/ppermute | solution.py:85
  129.3 0.1 bitcast_dynamic-update-slice_fusion.4
  129.4 0.1 bitcast_dynamic-update-slice_fusion.3
  129.5 1.9 %collective-permute-start.17 = (bf16[4,2,14,608]{3,1,2,0:T(2,128)(2,1)S(1)}, bf16[4,2,14,608]{3,1,2,0:T(2,128)(2,1)S(1)}, u32[]{:S(2)}, u32[]{:S(2)}) collective-permute-start(bf16[4,2,14,608]{3,1,2,0:T(2,128)(2,1)S(1)} %collective-permute-done.15), channel_id=1, source_target_pairs={{0,32},{1,481},{2,34},{3,483},{4,36},{5,485},{6,38},{7,487},{8,40}... | collective-permute-start | bytes 408584 | tf_op jit(solution)/shard_map/ppermute | solution.py:82
  131.5 0.1 bitcast_dynamic-update-slice_fusion.2
  131.6 0.3 collective-permute-done.16
  132.0 5.7 %collective-permute-done.17 = bf16[4,2,14,608]{3,1,2,0:T(2,128)(2,1)S(1)} collective-permute-done((bf16[4,2,14,608]{3,1,2,0:T(2,128)(2,1)S(1)}, bf16[4,2,14,608]{3,1,2,0:T(2,128)(2,1)S(1)}, u32[]{:S(2)}, u32[]{:S(2)}) %collective-permute-start.17) | collective-permute-done | bytes 136224 | tf_op jit(solution)/shard_map/ppermute | solution.py:82
  137.9 5.7 %copy.65 = bf16[2,896,608]{1,2,0:T(8,128)(2,1)} copy(bf16[2,896,608]{2,0,1:T(2,128)(2,1)S(1)} %bitcast.65) | data formatting | bytes 4358144
  (33 shorter events, 1.4 us)
Async XLA Ops:
  0.6 19.9 %copy-start.2 = (bf16[1,64,896]{2,1,0:T(8,128)(2,1)S(1)}, bf16[1,64,896]{2,1,0:T(8,128)(2,1)}, u32[]{:S(2)}) copy-start(bf16[1,64,896]{2,1,0:T(8,128)(2,1)} %param.9) | copy-start | bytes 344068
  3.1 50.3 %copy-start.3 = (f32[2,14,608]{2,0,1:T(2,128)S(1)}, f32[2,14,608]{2,0,1:T(2,128)}, u32[]{:S(2)}) copy-start(f32[2,14,608]{2,0,1:T(2,128)} %param.11) | copy-start | bytes 204292
  3.1 50.3 %copy-start.4 = (f32[2,14,608]{2,0,1:T(2,128)S(1)}, f32[2,14,608]{2,0,1:T(2,128)}, u32[]{:S(2)}) copy-start(f32[2,14,608]{2,0,1:T(2,128)} %param.10) | copy-start | bytes 204292
  5.5 47.2 %all-to-all-start = ((bf16[4,2,13312]{2,1,0:T(2,128)(2,1)}), bf16[4,2,13312]{2,1,0:T(2,128)(2,1)S(1)}, u32[]{:S(2)}, u32[]{:S(2)}) async-start(bf16[4,2,13312]{2,1,0:T(2,128)(2,1)} %reshape.36), calls=%async_computation | async-start | bytes 425984 | tf_op jit(solution)/shard_map/all_to_all | solution.py:36
  52.7 13.2 %copy-start = (f32[150,896]{1,0:T(8,128)S(1)}, f32[150,896]{1,0:T(8,128)}, u32[]{:S(2)}) copy-start(f32[150,896]{1,0:T(8,128)} %param.12) | copy-start | bytes 1612804
  52.7 13.2 %copy-start.1 = (f32[150,896]{1,0:T(8,128)S(1)}, f32[150,896]{1,0:T(8,128)}, u32[]{:S(2)}) copy-start(f32[150,896]{1,0:T(8,128)} %param.13) | copy-start | bytes 1612804
  53.4 15.2 %collective-permute-start = (bf16[2,14,608]{2,1,0:T(8,128)(2,1)S(1)}, bf16[2,14,608]{2,1,0:T(8,128)(2,1)}, u32[]{:S(2)}, u32[]{:S(2)}) collective-permute-start(bf16[2,14,608]{2,1,0:T(8,128)(2,1)S(1)} %get-tuple-element.26), channel_id=1, source_target_pairs={{0,8},{1,25},{2,10},{3,27},{4,12},{5,29},{6,14},{7,31},{8,16},{9,1... | collective-permute-start | bytes 102152 | tf_op jit(solution)/shard_map/ppermute | solution.py:59
  56.9 12.6 %collective-permute-start.1 = (bf16[2,14,608]{2,1,0:T(8,128)(2,1)S(1)}, bf16[2,14,608]{2,1,0:T(8,128)(2,1)S(1)}, u32[]{:S(2)}, u32[]{:S(2)}) collective-permute-start(bf16[2,14,608]{2,1,0:T(8,128)(2,1)S(1)} %get-tuple-element.26), channel_id=1, source_target_pairs={{0,24},{1,9},{2,26},{3,11},{4,28},{5,13},{6,30},{7,15},{8,0},{9,17... | collective-permute-start | bytes 102152 | tf_op jit(solution)/shard_map/ppermute | solution.py:59
  60.5 9.1 %collective-permute-start.2 = (bf16[2,14,608]{2,1,0:T(8,128)(2,1)S(1)}, bf16[2,14,608]{2,1,0:T(8,128)(2,1)S(1)}, u32[]{:S(2)}, u32[]{:S(2)}) collective-permute-start(bf16[2,14,608]{2,1,0:T(8,128)(2,1)S(1)} %get-tuple-element.26), channel_id=1, source_target_pairs={{0,16},{1,17},{2,18},{3,19},{4,20},{5,21},{6,22},{7,23},{8,24},{9,... | collective-permute-start | bytes 102152 | tf_op jit(solution)/shard_map/ppermute | solution.py:59
  69.6 10.3 %collective-permute-start.3 = (bf16[4,2,14,608]{3,1,2,0:T(2,128)(2,1)S(1)}, bf16[4,2,14,608]{3,1,2,0:T(2,128)(2,1)S(1)}, u32[]{:S(2)}, u32[]{:S(2)}) collective-permute-start(bf16[4,2,14,608]{3,1,2,0:T(2,128)(2,1)S(1)} %copy_dynamic-update-slice_fusion), channel_id=1, source_target_pairs={{0,32},{1,481},{2,34},{3,483},{4,36},{5,485},{6,38},{7,487},{8,40}... | collective-permute-start | bytes 408584 | tf_op jit(solution)/shard_map/ppermute | solution.py:82
  74.5 8.4 %collective-permute-start.4 = (bf16[4,2,14,608]{3,1,2,0:T(2,128)(2,1)S(1)}, bf16[4,2,14,608]{3,1,2,0:T(2,128)(2,1)S(1)}, u32[]{:S(2)}, u32[]{:S(2)}) collective-permute-start(bf16[4,2,14,608]{3,1,2,0:T(2,128)(2,1)S(1)} %copy_dynamic-update-slice_fusion), channel_id=1, source_target_pairs={{0,480},{1,33},{2,482},{3,35},{4,484},{5,37},{6,486},{7,39},{8,488... | collective-permute-start | bytes 408584 | tf_op jit(solution)/shard_map/ppermute | solution.py:85
  80.0 8.2 %collective-permute-start.5 = (bf16[4,2,14,608]{3,1,2,0:T(2,128)(2,1)S(1)}, bf16[4,2,14,608]{3,1,2,0:T(2,128)(2,1)S(1)}, u32[]{:S(2)}, u32[]{:S(2)}) collective-permute-start(bf16[4,2,14,608]{3,1,2,0:T(2,128)(2,1)S(1)} %collective-permute-done.3), channel_id=1, source_target_pairs={{0,32},{1,481},{2,34},{3,483},{4,36},{5,485},{6,38},{7,487},{8,40}... | collective-permute-start | bytes 408584 | tf_op jit(solution)/shard_map/ppermute | solution.py:82
  82.9 7.5 %collective-permute-start.6 = (bf16[4,2,14,608]{3,1,2,0:T(2,128)(2,1)S(1)}, bf16[4,2,14,608]{3,1,2,0:T(2,128)(2,1)S(1)}, u32[]{:S(2)}, u32[]{:S(2)}) collective-permute-start(bf16[4,2,14,608]{3,1,2,0:T(2,128)(2,1)S(1)} %collective-permute-done.4), channel_id=1, source_target_pairs={{0,480},{1,33},{2,482},{3,35},{4,484},{5,37},{6,486},{7,39},{8,488... | collective-permute-start | bytes 408584 | tf_op jit(solution)/shard_map/ppermute | solution.py:85
  88.2 8.2 %collective-permute-start.7 = (bf16[4,2,14,608]{3,1,2,0:T(2,128)(2,1)S(1)}, bf16[4,2,14,608]{3,1,2,0:T(2,128)(2,1)S(1)}, u32[]{:S(2)}, u32[]{:S(2)}) collective-permute-start(bf16[4,2,14,608]{3,1,2,0:T(2,128)(2,1)S(1)} %collective-permute-done.5), channel_id=1, source_target_pairs={{0,32},{1,481},{2,34},{3,483},{4,36},{5,485},{6,38},{7,487},{8,40}... | collective-permute-start | bytes 408584 | tf_op jit(solution)/shard_map/ppermute | solution.py:82
  90.5 7.9 %collective-permute-start.8 = (bf16[4,2,14,608]{3,1,2,0:T(2,128)(2,1)S(1)}, bf16[4,2,14,608]{3,1,2,0:T(2,128)(2,1)S(1)}, u32[]{:S(2)}, u32[]{:S(2)}) collective-permute-start(bf16[4,2,14,608]{3,1,2,0:T(2,128)(2,1)S(1)} %collective-permute-done.6), channel_id=1, source_target_pairs={{0,480},{1,33},{2,482},{3,35},{4,484},{5,37},{6,486},{7,39},{8,488... | collective-permute-start | bytes 408584 | tf_op jit(solution)/shard_map/ppermute | solution.py:85
  96.4 8.2 %collective-permute-start.9 = (bf16[4,2,14,608]{3,1,2,0:T(2,128)(2,1)S(1)}, bf16[4,2,14,608]{3,1,2,0:T(2,128)(2,1)S(1)}, u32[]{:S(2)}, u32[]{:S(2)}) collective-permute-start(bf16[4,2,14,608]{3,1,2,0:T(2,128)(2,1)S(1)} %collective-permute-done.7), channel_id=1, source_target_pairs={{0,32},{1,481},{2,34},{3,483},{4,36},{5,485},{6,38},{7,487},{8,40}... | collective-permute-start | bytes 408584 | tf_op jit(solution)/shard_map/ppermute | solution.py:82
  98.4 8.2 %collective-permute-start.10 = (bf16[4,2,14,608]{3,1,2,0:T(2,128)(2,1)S(1)}, bf16[4,2,14,608]{3,1,2,0:T(2,128)(2,1)S(1)}, u32[]{:S(2)}, u32[]{:S(2)}) collective-permute-start(bf16[4,2,14,608]{3,1,2,0:T(2,128)(2,1)S(1)} %collective-permute-done.8), channel_id=1, source_target_pairs={{0,480},{1,33},{2,482},{3,35},{4,484},{5,37},{6,486},{7,39},{8,488... | collective-permute-start | bytes 408584 | tf_op jit(solution)/shard_map/ppermute | solution.py:85
  104.6 8.2 %collective-permute-start.11 = (bf16[4,2,14,608]{3,1,2,0:T(2,128)(2,1)S(1)}, bf16[4,2,14,608]{3,1,2,0:T(2,128)(2,1)S(1)}, u32[]{:S(2)}, u32[]{:S(2)}) collective-permute-start(bf16[4,2,14,608]{3,1,2,0:T(2,128)(2,1)S(1)} %collective-permute-done.9), channel_id=1, source_target_pairs={{0,32},{1,481},{2,34},{3,483},{4,36},{5,485},{6,38},{7,487},{8,40}... | collective-permute-start | bytes 408584 | tf_op jit(solution)/shard_map/ppermute | solution.py:82
  106.6 8.2 %collective-permute-start.12 = (bf16[4,2,14,608]{3,1,2,0:T(2,128)(2,1)S(1)}, bf16[4,2,14,608]{3,1,2,0:T(2,128)(2,1)S(1)}, u32[]{:S(2)}, u32[]{:S(2)}) collective-permute-start(bf16[4,2,14,608]{3,1,2,0:T(2,128)(2,1)S(1)} %collective-permute-done.10), channel_id=1, source_target_pairs={{0,480},{1,33},{2,482},{3,35},{4,484},{5,37},{6,486},{7,39},{8,488... | collective-permute-start | bytes 408584 | tf_op jit(solution)/shard_map/ppermute | solution.py:85
  112.7 8.6 %collective-permute-start.13 = (bf16[4,2,14,608]{3,1,2,0:T(2,128)(2,1)S(1)}, bf16[4,2,14,608]{3,1,2,0:T(2,128)(2,1)S(1)}, u32[]{:S(2)}, u32[]{:S(2)}) collective-permute-start(bf16[4,2,14,608]{3,1,2,0:T(2,128)(2,1)S(1)} %collective-permute-done.11), channel_id=1, source_target_pairs={{0,32},{1,481},{2,34},{3,483},{4,36},{5,485},{6,38},{7,487},{8,40}... | collective-permute-start | bytes 408584 | tf_op jit(solution)/shard_map/ppermute | solution.py:82
  114.8 8.9 %collective-permute-start.14 = (bf16[4,2,14,608]{3,1,2,0:T(2,128)(2,1)S(1)}, bf16[4,2,14,608]{3,1,2,0:T(2,128)(2,1)S(1)}, u32[]{:S(2)}, u32[]{:S(2)}) collective-permute-start(bf16[4,2,14,608]{3,1,2,0:T(2,128)(2,1)S(1)} %collective-permute-done.12), channel_id=1, source_target_pairs={{0,480},{1,33},{2,482},{3,35},{4,484},{5,37},{6,486},{7,39},{8,488... | collective-permute-start | bytes 408584 | tf_op jit(solution)/shard_map/ppermute | solution.py:85
  121.3 8.2 %collective-permute-start.15 = (bf16[4,2,14,608]{3,1,2,0:T(2,128)(2,1)S(1)}, bf16[4,2,14,608]{3,1,2,0:T(2,128)(2,1)S(1)}, u32[]{:S(2)}, u32[]{:S(2)}) collective-permute-start(bf16[4,2,14,608]{3,1,2,0:T(2,128)(2,1)S(1)} %collective-permute-done.13), channel_id=1, source_target_pairs={{0,32},{1,481},{2,34},{3,483},{4,36},{5,485},{6,38},{7,487},{8,40}... | collective-permute-start | bytes 408584 | tf_op jit(solution)/shard_map/ppermute | solution.py:82
  123.7 8.2 %collective-permute-start.16 = (bf16[4,2,14,608]{3,1,2,0:T(2,128)(2,1)S(1)}, bf16[4,2,14,608]{3,1,2,0:T(2,128)(2,1)S(1)}, u32[]{:S(2)}, u32[]{:S(2)}) collective-permute-start(bf16[4,2,14,608]{3,1,2,0:T(2,128)(2,1)S(1)} %collective-permute-done.14), channel_id=1, source_target_pairs={{0,480},{1,33},{2,482},{3,35},{4,484},{5,37},{6,486},{7,39},{8,488... | collective-permute-start | bytes 408584 | tf_op jit(solution)/shard_map/ppermute | solution.py:85
  129.5 8.2 %collective-permute-start.17 = (bf16[4,2,14,608]{3,1,2,0:T(2,128)(2,1)S(1)}, bf16[4,2,14,608]{3,1,2,0:T(2,128)(2,1)S(1)}, u32[]{:S(2)}, u32[]{:S(2)}) collective-permute-start(bf16[4,2,14,608]{3,1,2,0:T(2,128)(2,1)S(1)} %collective-permute-done.15), channel_id=1, source_target_pairs={{0,32},{1,481},{2,34},{3,483},{4,36},{5,485},{6,38},{7,487},{8,40}... | collective-permute-start | bytes 408584 | tf_op jit(solution)/shard_map/ppermute | solution.py:82

commit v7 on v6

--- a/solution.py
+++ b/solution.py
@@ -31,8 +31,12 @@
     left = emb_left[0]
     nleft = left.size // groups
     send_left = left.reshape(groups, nleft)
-    rights = lax.all_gather(emb_right, "group", axis=0, tiled=True)
-    send = jnp.concatenate([send_layer, send_left], axis=1)
+    right = emb_right[0]
+    rank, width = right.shape
+    rrows = rank // Y_SIZE
+    ry = lax.dynamic_slice_in_dim(right, (si % Y_SIZE) * rrows, rrows, axis=0)
+    send_right = jnp.broadcast_to(ry.reshape(1, rrows * width), (groups, rrows * width))
+    send = jnp.concatenate([send_layer, send_left, send_right], axis=1)
     recv = lax.all_to_all(send, "group", 0, 0, tiled=True)
 
     acc = recv[:, :nlayer].astype(f32).sum(axis=0)
@@ -53,11 +57,19 @@
         return pairs
 
     yi = si % Y_SIZE
+    rgot = recv[:, nlayer + nleft:]
+    npiece = piece.size
+    payload = jnp.concatenate([piece.reshape(1, npiece), rgot.reshape(1, -1)], axis=1)
     yblk = jnp.zeros((Y_SIZE,) + piece.shape, piece.dtype)
     yblk = lax.dynamic_update_index_in_dim(yblk, piece, yi, axis=0)
+    rights = jnp.zeros((groups, rank, width), rgot.dtype)
+    rights = lax.dynamic_update_slice_in_dim(rights, rgot.reshape(groups, rrows, width), yi * rrows, axis=1)
     for k in (1, -1, 2):
-        got = lax.ppermute(piece, ("shard", "tensor"), yshift(k))
-        yblk = lax.dynamic_update_index_in_dim(yblk, got, (yi - k * sgn) % Y_SIZE, axis=0)
+        got = lax.ppermute(payload, ("shard", "tensor"), yshift(k))
+        src = (yi - k * sgn) % Y_SIZE
+        yblk = lax.dynamic_update_index_in_dim(yblk, got[0, :npiece].reshape(piece.shape), src, axis=0)
+        rpart = got[0, npiece:].reshape(groups, rrows, width)
+        rights = lax.dynamic_update_slice_in_dim(rights, rpart, src * rrows, axis=1)
 
     zlo_size = shards // Y_SIZE
     nz = groups * zlo_size

time: 144 us -> 145 us (level)
  blocking collectives: 32.1 us -> 0 us
  waiting for transfers between devices: 10.2 us -> 37.8 us
  local copies, waits for them, and re-layouts: 16.3 us -> 21.3 us
    all_gather x1 -> x0, blocking collectives: 32.1 us -> none  [on_device(): rights = lax.all_gather(emb_right, 'group', axis=0, tiled=True)]
    all_to_all x1, waiting for transfers between devices: 0.01 us -> 19.1 us  [on_device(): recv = lax.all_to_all(send, 'group', 0, 0, tiled=True)]
    ppermute x7, starting transfers between devices: 36.4 us -> 28.2 us  [on_device(): bwd = lax.ppermute(bwd, axes, zshift(-1))]
    ppermute x8, starting transfers between devices: 18.3 us -> 26.1 us  [on_device(): fwd = lax.ppermute(fwd, axes, zshift(1))]
    ppermute x3, waiting for transfers between devices: 0.01 us -> 5.55 us  [on_device(): got = lax.ppermute(payload, ('shard', 'tensor'), yshift(k))]
    ppermute x8, waiting for transfers between devices: 7.75 us -> 13.1 us  [on_device(): fwd = lax.ppermute(fwd, axes, zshift(1))]
    slice x0 -> x7, local copies, waits for them, and re-layouts: none -> 2.59 us  [the longest x3 1.95 us: on_device(): rpart = got[0, npiece:].reshape(groups, rrows, width)]
    ppermute x7, waiting for transfers between devices: 2.42 us -> 0.06 us  [on_device(): bwd = lax.ppermute(bwd, axes, zshift(-1))]
  transfers between devices with their start and end apart: 19 -> 19, of which waited for: 13 -> 10; matrix products, arithmetic and copies ran while one was open for 6% -> 7% of each run, Pallas kernels for 0% -> 0%
where the time goes in v7:
time: 145 us; the launch traced here: 144 us
  starting transfers between devices  80.3 us (55%)
  waiting for transfers between devices  37.8 us (26%)
  local copies, waits for them, and re-layouts  21.3 us (15%)
  matrix products  1.97 us (1%)
  other arithmetic  1.46 us (1%)
    ppermute x7, starting transfers between devices, on_device(): bwd = lax.ppermute(bwd, axes, zshift(-1))  28.2 us
    ppermute x8, starting transfers between devices, on_device(): fwd = lax.ppermute(fwd, axes, zshift(1))  26.1 us
    all_to_all x1, waiting for transfers between devices, on_device(): recv = lax.all_to_all(send, 'group', 0, 0, tiled=True)  19.1 us
    all_to_all x1, starting transfers between devices, on_device(): recv = lax.all_to_all(send, 'group', 0, 0, tiled=True)  15.1 us
    ppermute x8, waiting for transfers between devices, on_device(): fwd = lax.ppermute(fwd, axes, zshift(1))  13.1 us
    unnamed x19, local copies, waits for them, and re-layouts  11.1 us
    ppermute x3, starting transfers between devices, on_device(): got = lax.ppermute(payload, ('shard', 'tensor'), yshift(k))  10.9 us
    ppermute x3, waiting for transfers between devices, on_device(): got = lax.ppermute(payload, ('shard', 'tensor'), yshift(k))  5.55 us
  transfers between devices with their start and end apart: 19, of which 10 were waited for; matrix products, arithmetic and copies ran while one was open for 7% of the time, Pallas kernels for 0%

profile of v7, /device:TPU:6, one launch (start us, length us, event | category | flops | bytes accessed | tf_op | source)
XLA Modules:
  0.0 144.1 jit_solution(17905553125352851995)
XLA Ops:
  0.7 0.9 copy-done
  1.6 0.9 copy.51
  2.5 0.3 reshape.46
  2.8 1.1 copy.52
  3.9 0.1 reshape_squeeze.15
  4.1 0.2 maximum_bitcast_fusion
  4.2 0.5 broadcast.53
  4.7 1.1 reduce.20
  5.8 1.1 reshape.62
  6.9 15.1 %all-to-all-start = ((bf16[4,2,20480]{2,1,0:T(2,128)(2,1)}), bf16[4,2,20480]{2,1,0:T(2,128)(2,1)S(1)}, u32[]{:S(2)}, u32[]{:S(2)}) async-start(bf16[4,2,20480]{2,1,0:T(2,128)(2,1)} %reshape.62), calls=%async_computation | async-start | bytes 655360 | tf_op jit(solution)/shard_map/all_to_all | solution.py:40
  22.0 19.1 %all-to-all-done = bf16[4,2,20480]{2,1,0:T(2,128)(2,1)S(1)} async-done(((bf16[4,2,20480]{2,1,0:T(2,128)(2,1)}), bf16[4,2,20480]{2,1,0:T(2,128)(2,1)S(1)}, u32[]{:S(2)}, u32[]{:S(2)}) %all-to-all-start) | async-done | bytes 327712 | tf_op jit(solution)/shard_map/all_to_all | solution.py:40
  41.1 0.3 reshape.63
  41.4 0.4 copy.80
  41.8 0.2 convert_reduce_fusion
  42.3 0.2 reshape.47
  42.5 0.2 copy.64
  42.7 0.3 constant_dynamic-update-slice_fusion.3
  43.0 3.5 %collective-permute-start = (bf16[1,74368]{1,0:T(2,128)(2,1)S(1)}, bf16[1,74368]{1,0:T(2,128)(2,1)S(1)}, u32[]{:S(2)}, u32[]{:S(2)}) collective-permute-start(bf16[1,74368]{1,0:T(2,128)(2,1)S(1)} %constant_dynamic-update-slice_fusion.3), channel_id=1, source_target_pairs={{0,8},{1,25},{2,10},{3,27},{4,12},{5,29},{6,14},{7,31},{8,16},{9,1... | collective-permute-start | bytes 446216 | tf_op jit(solution)/shard_map/ppermute | solution.py:68
  46.5 3.6 %collective-permute-start.1 = (bf16[1,74368]{1,0:T(2,128)(2,1)S(1)}, bf16[1,74368]{1,0:T(2,128)(2,1)S(1)}, u32[]{:S(2)}, u32[]{:S(2)}) collective-permute-start(bf16[1,74368]{1,0:T(2,128)(2,1)S(1)} %constant_dynamic-update-slice_fusion.3), channel_id=1, source_target_pairs={{0,24},{1,9},{2,26},{3,11},{4,28},{5,13},{6,30},{7,15},{8,0},{9,17... | collective-permute-start | bytes 446216 | tf_op jit(solution)/shard_map/ppermute | solution.py:68
  50.1 3.9 %collective-permute-start.2 = (bf16[1,74368]{1,0:T(2,128)(2,1)S(1)}, bf16[1,74368]{1,0:T(2,128)(2,1)S(1)}, u32[]{:S(2)}, u32[]{:S(2)}) collective-permute-start(bf16[1,74368]{1,0:T(2,128)(2,1)S(1)} %constant_dynamic-update-slice_fusion.3), channel_id=1, source_target_pairs={{0,16},{1,17},{2,18},{3,19},{4,20},{5,21},{6,22},{7,23},{8,24},{9,... | collective-permute-start | bytes 446216 | tf_op jit(solution)/shard_map/ppermute | solution.py:68
  54.2 0.4 slice_reduce_fusion.9
  54.9 0.7 copy.60
  55.6 0.7 copy.61
  56.3 0.2 slice_reduce_fusion.5
  56.6 0.4 collective-permute-done.1
  57.0 0.2 slice_reduce_fusion.4
  57.3 5.2 %collective-permute-done.2 = bf16[1,74368]{1,0:T(2,128)(2,1)S(1)} collective-permute-done((bf16[1,74368]{1,0:T(2,128)(2,1)S(1)}, bf16[1,74368]{1,0:T(2,128)(2,1)S(1)}, u32[]{:S(2)}, u32[]{:S(2)}) %collective-permute-start.2) | collective-permute-done | bytes 148768 | tf_op jit(solution)/shard_map/ppermute | solution.py:68
  62.5 0.2 slice_reduce_fusion.3
  63.0 8.2 %collective-permute-start.3 = (bf16[4,2,14,608]{3,1,2,0:T(2,128)(2,1)S(1)}, bf16[4,2,14,608]{3,1,2,0:T(2,128)(2,1)S(1)}, u32[]{:S(2)}, u32[]{:S(2)}) collective-permute-start(bf16[4,2,14,608]{3,1,2,0:T(2,128)(2,1)S(1)} %copy_dynamic-update-slice_fusion), channel_id=1, source_target_pairs={{0,32},{1,481},{2,34},{3,483},{4,36},{5,485},{6,38},{7,487},{8,40}... | collective-permute-start | bytes 408584 | tf_op jit(solution)/shard_map/ppermute | solution.py:94
  71.2 1.9 %collective-permute-start.4 = (bf16[4,2,14,608]{3,1,2,0:T(2,128)(2,1)S(1)}, bf16[4,2,14,608]{3,1,2,0:T(2,128)(2,1)S(1)}, u32[]{:S(2)}, u32[]{:S(2)}) collective-permute-start(bf16[4,2,14,608]{3,1,2,0:T(2,128)(2,1)S(1)} %copy_dynamic-update-slice_fusion), channel_id=1, source_target_pairs={{0,480},{1,33},{2,482},{3,35},{4,484},{5,37},{6,486},{7,39},{8,488... | collective-permute-start | bytes 408584 | tf_op jit(solution)/shard_map/ppermute | solution.py:97
  73.1 0.7 slice_reduce_fusion.2
  73.8 0.1 reshape_squeeze.16
  73.9 0.7 slice_reduce_fusion.1
  74.6 0.1 reshape_squeeze.17
  74.7 0.7 slice_reduce_fusion
  75.4 0.1 reshape_squeeze.18
  75.6 0.2 fusion.5
  75.8 0.2 fusion.6
  76.0 0.2 fusion.7
  76.3 1.3 multiply_subtract_fusion
  77.6 1.2 broadcast_in_dim.80
  78.9 3.9 %collective-permute-start.5 = (bf16[4,2,14,608]{3,1,2,0:T(2,128)(2,1)S(1)}, bf16[4,2,14,608]{3,1,2,0:T(2,128)(2,1)S(1)}, u32[]{:S(2)}, u32[]{:S(2)}) collective-permute-start(bf16[4,2,14,608]{3,1,2,0:T(2,128)(2,1)S(1)} %collective-permute-done.3), channel_id=1, source_target_pairs={{0,32},{1,481},{2,34},{3,483},{4,36},{5,485},{6,38},{7,487},{8,40}... | collective-permute-start | bytes 408584 | tf_op jit(solution)/shard_map/ppermute | solution.py:94
  82.9 3.1 %collective-permute-start.6 = (bf16[4,2,14,608]{3,1,2,0:T(2,128)(2,1)S(1)}, bf16[4,2,14,608]{3,1,2,0:T(2,128)(2,1)S(1)}, u32[]{:S(2)}, u32[]{:S(2)}) collective-permute-start(bf16[4,2,14,608]{3,1,2,0:T(2,128)(2,1)S(1)} %collective-permute-done.4), channel_id=1, source_target_pairs={{0,480},{1,33},{2,482},{3,35},{4,484},{5,37},{6,486},{7,39},{8,488... | collective-permute-start | bytes 408584 | tf_op jit(solution)/shard_map/ppermute | solution.py:97
  86.3 0.9 collective-permute-done.5
  87.1 3.2 %collective-permute-start.7 = (bf16[4,2,14,608]{3,1,2,0:T(2,128)(2,1)S(1)}, bf16[4,2,14,608]{3,1,2,0:T(2,128)(2,1)S(1)}, u32[]{:S(2)}, u32[]{:S(2)}) collective-permute-start(bf16[4,2,14,608]{3,1,2,0:T(2,128)(2,1)S(1)} %collective-permute-done.5), channel_id=1, source_target_pairs={{0,32},{1,481},{2,34},{3,483},{4,36},{5,485},{6,38},{7,487},{8,40}... | collective-permute-start | bytes 408584 | tf_op jit(solution)/shard_map/ppermute | solution.py:94
  90.4 3.8 %collective-permute-start.8 = (bf16[4,2,14,608]{3,1,2,0:T(2,128)(2,1)S(1)}, bf16[4,2,14,608]{3,1,2,0:T(2,128)(2,1)S(1)}, u32[]{:S(2)}, u32[]{:S(2)}) collective-permute-start(bf16[4,2,14,608]{3,1,2,0:T(2,128)(2,1)S(1)} %collective-permute-done.6), channel_id=1, source_target_pairs={{0,480},{1,33},{2,482},{3,35},{4,484},{5,37},{6,486},{7,39},{8,488... | collective-permute-start | bytes 408584 | tf_op jit(solution)/shard_map/ppermute | solution.py:97
  94.2 0.1 bitcast_dynamic-update-slice_fusion.12
  94.5 0.9 collective-permute-done.7
  95.3 3.1 %collective-permute-start.9 = (bf16[4,2,14,608]{3,1,2,0:T(2,128)(2,1)S(1)}, bf16[4,2,14,608]{3,1,2,0:T(2,128)(2,1)S(1)}, u32[]{:S(2)}, u32[]{:S(2)}) collective-permute-start(bf16[4,2,14,608]{3,1,2,0:T(2,128)(2,1)S(1)} %collective-permute-done.7), channel_id=1, source_target_pairs={{0,32},{1,481},{2,34},{3,483},{4,36},{5,485},{6,38},{7,487},{8,40}... | collective-permute-start | bytes 408584 | tf_op jit(solution)/shard_map/ppermute | solution.py:94
  98.5 3.9 %collective-permute-start.10 = (bf16[4,2,14,608]{3,1,2,0:T(2,128)(2,1)S(1)}, bf16[4,2,14,608]{3,1,2,0:T(2,128)(2,1)S(1)}, u32[]{:S(2)}, u32[]{:S(2)}) collective-permute-start(bf16[4,2,14,608]{3,1,2,0:T(2,128)(2,1)S(1)} %collective-permute-done.8), channel_id=1, source_target_pairs={{0,480},{1,33},{2,482},{3,35},{4,484},{5,37},{6,486},{7,39},{8,488... | collective-permute-start | bytes 408584 | tf_op jit(solution)/shard_map/ppermute | solution.py:97
  102.4 0.1 bitcast_dynamic-update-slice_fusion.10
  102.7 2.0 %collective-permute-done.9 = bf16[4,2,14,608]{3,1,2,0:T(2,128)(2,1)S(1)} collective-permute-done((bf16[4,2,14,608]{3,1,2,0:T(2,128)(2,1)S(1)}, bf16[4,2,14,608]{3,1,2,0:T(2,128)(2,1)S(1)}, u32[]{:S(2)}, u32[]{:S(2)}) %collective-permute-start.9) | collective-permute-done | bytes 136224 | tf_op jit(solution)/shard_map/ppermute | solution.py:94
  104.7 1.9 %collective-permute-start.11 = (bf16[4,2,14,608]{3,1,2,0:T(2,128)(2,1)S(1)}, bf16[4,2,14,608]{3,1,2,0:T(2,128)(2,1)S(1)}, u32[]{:S(2)}, u32[]{:S(2)}) collective-permute-start(bf16[4,2,14,608]{3,1,2,0:T(2,128)(2,1)S(1)} %collective-permute-done.9), channel_id=1, source_target_pairs={{0,32},{1,481},{2,34},{3,483},{4,36},{5,485},{6,38},{7,487},{8,40}... | collective-permute-start | bytes 408584 | tf_op jit(solution)/shard_map/ppermute | solution.py:94
  106.6 5.1 %collective-permute-start.12 = (bf16[4,2,14,608]{3,1,2,0:T(2,128)(2,1)S(1)}, bf16[4,2,14,608]{3,1,2,0:T(2,128)(2,1)S(1)}, u32[]{:S(2)}, u32[]{:S(2)}) collective-permute-start(bf16[4,2,14,608]{3,1,2,0:T(2,128)(2,1)S(1)} %collective-permute-done.10), channel_id=1, source_target_pairs={{0,480},{1,33},{2,482},{3,35},{4,484},{5,37},{6,486},{7,39},{8,488... | collective-permute-start | bytes 408584 | tf_op jit(solution)/shard_map/ppermute | solution.py:97
  112.0 1.7 %collective-permute-done.11 = bf16[4,2,14,608]{3,1,2,0:T(2,128)(2,1)S(1)} collective-permute-done((bf16[4,2,14,608]{3,1,2,0:T(2,128)(2,1)S(1)}, bf16[4,2,14,608]{3,1,2,0:T(2,128)(2,1)S(1)}, u32[]{:S(2)}, u32[]{:S(2)}) %collective-permute-start.11) | collective-permute-done | bytes 136224 | tf_op jit(solution)/shard_map/ppermute | solution.py:94
  113.6 1.9 %collective-permute-start.13 = (bf16[4,2,14,608]{3,1,2,0:T(2,128)(2,1)S(1)}, bf16[4,2,14,608]{3,1,2,0:T(2,128)(2,1)S(1)}, u32[]{:S(2)}, u32[]{:S(2)}) collective-permute-start(bf16[4,2,14,608]{3,1,2,0:T(2,128)(2,1)S(1)} %collective-permute-done.11), channel_id=1, source_target_pairs={{0,32},{1,481},{2,34},{3,483},{4,36},{5,485},{6,38},{7,487},{8,40}... | collective-permute-start | bytes 408584 | tf_op jit(solution)/shard_map/ppermute | solution.py:94
  115.6 5.1 %collective-permute-start.14 = (bf16[4,2,14,608]{3,1,2,0:T(2,128)(2,1)S(1)}, bf16[4,2,14,608]{3,1,2,0:T(2,128)(2,1)S(1)}, u32[]{:S(2)}, u32[]{:S(2)}) collective-permute-start(bf16[4,2,14,608]{3,1,2,0:T(2,128)(2,1)S(1)} %collective-permute-done.12), channel_id=1, source_target_pairs={{0,480},{1,33},{2,482},{3,35},{4,484},{5,37},{6,486},{7,39},{8,488... | collective-permute-start | bytes 408584 | tf_op jit(solution)/shard_map/ppermute | solution.py:97
  121.0 0.9 collective-permute-done.13
  121.8 1.9 %collective-permute-start.15 = (bf16[4,2,14,608]{3,1,2,0:T(2,128)(2,1)S(1)}, bf16[4,2,14,608]{3,1,2,0:T(2,128)(2,1)S(1)}, u32[]{:S(2)}, u32[]{:S(2)}) collective-permute-start(bf16[4,2,14,608]{3,1,2,0:T(2,128)(2,1)S(1)} %collective-permute-done.13), channel_id=1, source_target_pairs={{0,32},{1,481},{2,34},{3,483},{4,36},{5,485},{6,38},{7,487},{8,40}... | collective-permute-start | bytes 408584 | tf_op jit(solution)/shard_map/ppermute | solution.py:94
  123.8 5.1 %collective-permute-start.16 = (bf16[4,2,14,608]{3,1,2,0:T(2,128)(2,1)S(1)}, bf16[4,2,14,608]{3,1,2,0:T(2,128)(2,1)S(1)}, u32[]{:S(2)}, u32[]{:S(2)}) collective-permute-start(bf16[4,2,14,608]{3,1,2,0:T(2,128)(2,1)S(1)} %collective-permute-done.14), channel_id=1, source_target_pairs={{0,480},{1,33},{2,482},{3,35},{4,484},{5,37},{6,486},{7,39},{8,488... | collective-permute-start | bytes 408584 | tf_op jit(solution)/shard_map/ppermute | solution.py:97
  129.2 0.9 collective-permute-done.15
  130.0 1.9 %collective-permute-start.17 = (bf16[4,2,14,608]{3,1,2,0:T(2,128)(2,1)S(1)}, bf16[4,2,14,608]{3,1,2,0:T(2,128)(2,1)S(1)}, u32[]{:S(2)}, u32[]{:S(2)}) collective-permute-start(bf16[4,2,14,608]{3,1,2,0:T(2,128)(2,1)S(1)} %collective-permute-done.15), channel_id=1, source_target_pairs={{0,32},{1,481},{2,34},{3,483},{4,36},{5,485},{6,38},{7,487},{8,40}... | collective-permute-start | bytes 408584 | tf_op jit(solution)/shard_map/ppermute | solution.py:94
  132.2 6.0 %collective-permute-done.17 = bf16[4,2,14,608]{3,1,2,0:T(2,128)(2,1)S(1)} collective-permute-done((bf16[4,2,14,608]{3,1,2,0:T(2,128)(2,1)S(1)}, bf16[4,2,14,608]{3,1,2,0:T(2,128)(2,1)S(1)}, u32[]{:S(2)}, u32[]{:S(2)}) %collective-permute-start.17) | collective-permute-done | bytes 136224 | tf_op jit(solution)/shard_map/ppermute | solution.py:94
  138.3 5.7 %copy.62 = bf16[2,896,608]{1,2,0:T(8,128)(2,1)} copy(bf16[2,896,608]{2,0,1:T(2,128)(2,1)S(1)} %bitcast.69) | data formatting | bytes 4358144
  (57 shorter events, 3.3 us)
Async XLA Ops:
  0.6 0.9 copy-start
  5.8 36.4 %copy-start.3 = (f32[2,14,608]{2,0,1:T(2,128)S(1)}, f32[2,14,608]{2,0,1:T(2,128)}, u32[]{:S(2)}) copy-start(f32[2,14,608]{2,0,1:T(2,128)} %param.11) | copy-start | bytes 204292
  5.8 36.4 %copy-start.4 = (f32[2,14,608]{2,0,1:T(2,128)S(1)}, f32[2,14,608]{2,0,1:T(2,128)}, u32[]{:S(2)}) copy-start(f32[2,14,608]{2,0,1:T(2,128)} %param.10) | copy-start | bytes 204292
  6.9 34.2 %all-to-all-start = ((bf16[4,2,20480]{2,1,0:T(2,128)(2,1)}), bf16[4,2,20480]{2,1,0:T(2,128)(2,1)S(1)}, u32[]{:S(2)}, u32[]{:S(2)}) async-start(bf16[4,2,20480]{2,1,0:T(2,128)(2,1)} %reshape.62), calls=%async_computation | async-start | bytes 655360 | tf_op jit(solution)/shard_map/all_to_all | solution.py:40
  43.0 13.3 %collective-permute-start = (bf16[1,74368]{1,0:T(2,128)(2,1)S(1)}, bf16[1,74368]{1,0:T(2,128)(2,1)S(1)}, u32[]{:S(2)}, u32[]{:S(2)}) collective-permute-start(bf16[1,74368]{1,0:T(2,128)(2,1)S(1)} %constant_dynamic-update-slice_fusion.3), channel_id=1, source_target_pairs={{0,8},{1,25},{2,10},{3,27},{4,12},{5,29},{6,14},{7,31},{8,16},{9,1... | collective-permute-start | bytes 446216 | tf_op jit(solution)/shard_map/ppermute | solution.py:68
  46.5 10.5 %collective-permute-start.1 = (bf16[1,74368]{1,0:T(2,128)(2,1)S(1)}, bf16[1,74368]{1,0:T(2,128)(2,1)S(1)}, u32[]{:S(2)}, u32[]{:S(2)}) collective-permute-start(bf16[1,74368]{1,0:T(2,128)(2,1)S(1)} %constant_dynamic-update-slice_fusion.3), channel_id=1, source_target_pairs={{0,24},{1,9},{2,26},{3,11},{4,28},{5,13},{6,30},{7,15},{8,0},{9,17... | collective-permute-start | bytes 446216 | tf_op jit(solution)/shard_map/ppermute | solution.py:68
  50.1 12.4 %collective-permute-start.2 = (bf16[1,74368]{1,0:T(2,128)(2,1)S(1)}, bf16[1,74368]{1,0:T(2,128)(2,1)S(1)}, u32[]{:S(2)}, u32[]{:S(2)}) collective-permute-start(bf16[1,74368]{1,0:T(2,128)(2,1)S(1)} %constant_dynamic-update-slice_fusion.3), channel_id=1, source_target_pairs={{0,16},{1,17},{2,18},{3,19},{4,20},{5,21},{6,22},{7,23},{8,24},{9,... | collective-permute-start | bytes 446216 | tf_op jit(solution)/shard_map/ppermute | solution.py:68
  62.9 13.4 %copy-start.1 = (f32[150,896]{1,0:T(8,128)S(1)}, f32[150,896]{1,0:T(8,128)}, u32[]{:S(2)}) copy-start(f32[150,896]{1,0:T(8,128)} %param.12) | copy-start | bytes 1612804
  62.9 13.4 %copy-start.2 = (f32[150,896]{1,0:T(8,128)S(1)}, f32[150,896]{1,0:T(8,128)}, u32[]{:S(2)}) copy-start(f32[150,896]{1,0:T(8,128)} %param.13) | copy-start | bytes 1612804
  63.0 16.0 %collective-permute-start.3 = (bf16[4,2,14,608]{3,1,2,0:T(2,128)(2,1)S(1)}, bf16[4,2,14,608]{3,1,2,0:T(2,128)(2,1)S(1)}, u32[]{:S(2)}, u32[]{:S(2)}) collective-permute-start(bf16[4,2,14,608]{3,1,2,0:T(2,128)(2,1)S(1)} %copy_dynamic-update-slice_fusion), channel_id=1, source_target_pairs={{0,32},{1,481},{2,34},{3,483},{4,36},{5,485},{6,38},{7,487},{8,40}... | collective-permute-start | bytes 408584 | tf_op jit(solution)/shard_map/ppermute | solution.py:94
  71.2 11.7 %collective-permute-start.4 = (bf16[4,2,14,608]{3,1,2,0:T(2,128)(2,1)S(1)}, bf16[4,2,14,608]{3,1,2,0:T(2,128)(2,1)S(1)}, u32[]{:S(2)}, u32[]{:S(2)}) collective-permute-start(bf16[4,2,14,608]{3,1,2,0:T(2,128)(2,1)S(1)} %copy_dynamic-update-slice_fusion), channel_id=1, source_target_pairs={{0,480},{1,33},{2,482},{3,35},{4,484},{5,37},{6,486},{7,39},{8,488... | collective-permute-start | bytes 408584 | tf_op jit(solution)/shard_map/ppermute | solution.py:97
  78.9 8.2 %collective-permute-start.5 = (bf16[4,2,14,608]{3,1,2,0:T(2,128)(2,1)S(1)}, bf16[4,2,14,608]{3,1,2,0:T(2,128)(2,1)S(1)}, u32[]{:S(2)}, u32[]{:S(2)}) collective-permute-start(bf16[4,2,14,608]{3,1,2,0:T(2,128)(2,1)S(1)} %collective-permute-done.3), channel_id=1, source_target_pairs={{0,32},{1,481},{2,34},{3,483},{4,36},{5,485},{6,38},{7,487},{8,40}... | collective-permute-start | bytes 408584 | tf_op jit(solution)/shard_map/ppermute | solution.py:94
  82.9 7.5 %collective-permute-start.6 = (bf16[4,2,14,608]{3,1,2,0:T(2,128)(2,1)S(1)}, bf16[4,2,14,608]{3,1,2,0:T(2,128)(2,1)S(1)}, u32[]{:S(2)}, u32[]{:S(2)}) collective-permute-start(bf16[4,2,14,608]{3,1,2,0:T(2,128)(2,1)S(1)} %collective-permute-done.4), channel_id=1, source_target_pairs={{0,480},{1,33},{2,482},{3,35},{4,484},{5,37},{6,486},{7,39},{8,488... | collective-permute-start | bytes 408584 | tf_op jit(solution)/shard_map/ppermute | solution.py:97
  87.1 8.2 %collective-permute-start.7 = (bf16[4,2,14,608]{3,1,2,0:T(2,128)(2,1)S(1)}, bf16[4,2,14,608]{3,1,2,0:T(2,128)(2,1)S(1)}, u32[]{:S(2)}, u32[]{:S(2)}) collective-permute-start(bf16[4,2,14,608]{3,1,2,0:T(2,128)(2,1)S(1)} %collective-permute-done.5), channel_id=1, source_target_pairs={{0,32},{1,481},{2,34},{3,483},{4,36},{5,485},{6,38},{7,487},{8,40}... | collective-permute-start | bytes 408584 | tf_op jit(solution)/shard_map/ppermute | solution.py:94
  90.4 8.0 %collective-permute-start.8 = (bf16[4,2,14,608]{3,1,2,0:T(2,128)(2,1)S(1)}, bf16[4,2,14,608]{3,1,2,0:T(2,128)(2,1)S(1)}, u32[]{:S(2)}, u32[]{:S(2)}) collective-permute-start(bf16[4,2,14,608]{3,1,2,0:T(2,128)(2,1)S(1)} %collective-permute-done.6), channel_id=1, source_target_pairs={{0,480},{1,33},{2,482},{3,35},{4,484},{5,37},{6,486},{7,39},{8,488... | collective-permute-start | bytes 408584 | tf_op jit(solution)/shard_map/ppermute | solution.py:97
  95.3 9.3 %collective-permute-start.9 = (bf16[4,2,14,608]{3,1,2,0:T(2,128)(2,1)S(1)}, bf16[4,2,14,608]{3,1,2,0:T(2,128)(2,1)S(1)}, u32[]{:S(2)}, u32[]{:S(2)}) collective-permute-start(bf16[4,2,14,608]{3,1,2,0:T(2,128)(2,1)S(1)} %collective-permute-done.7), channel_id=1, source_target_pairs={{0,32},{1,481},{2,34},{3,483},{4,36},{5,485},{6,38},{7,487},{8,40}... | collective-permute-start | bytes 408584 | tf_op jit(solution)/shard_map/ppermute | solution.py:94
  98.5 8.1 %collective-permute-start.10 = (bf16[4,2,14,608]{3,1,2,0:T(2,128)(2,1)S(1)}, bf16[4,2,14,608]{3,1,2,0:T(2,128)(2,1)S(1)}, u32[]{:S(2)}, u32[]{:S(2)}) collective-permute-start(bf16[4,2,14,608]{3,1,2,0:T(2,128)(2,1)S(1)} %collective-permute-done.8), channel_id=1, source_target_pairs={{0,480},{1,33},{2,482},{3,35},{4,484},{5,37},{6,486},{7,39},{8,488... | collective-permute-start | bytes 408584 | tf_op jit(solution)/shard_map/ppermute | solution.py:97
  104.7 9.0 %collective-permute-start.11 = (bf16[4,2,14,608]{3,1,2,0:T(2,128)(2,1)S(1)}, bf16[4,2,14,608]{3,1,2,0:T(2,128)(2,1)S(1)}, u32[]{:S(2)}, u32[]{:S(2)}) collective-permute-start(bf16[4,2,14,608]{3,1,2,0:T(2,128)(2,1)S(1)} %collective-permute-done.9), channel_id=1, source_target_pairs={{0,32},{1,481},{2,34},{3,483},{4,36},{5,485},{6,38},{7,487},{8,40}... | collective-permute-start | bytes 408584 | tf_op jit(solution)/shard_map/ppermute | solution.py:94
  106.6 9.0 %collective-permute-start.12 = (bf16[4,2,14,608]{3,1,2,0:T(2,128)(2,1)S(1)}, bf16[4,2,14,608]{3,1,2,0:T(2,128)(2,1)S(1)}, u32[]{:S(2)}, u32[]{:S(2)}) collective-permute-start(bf16[4,2,14,608]{3,1,2,0:T(2,128)(2,1)S(1)} %collective-permute-done.10), channel_id=1, source_target_pairs={{0,480},{1,33},{2,482},{3,35},{4,484},{5,37},{6,486},{7,39},{8,488... | collective-permute-start | bytes 408584 | tf_op jit(solution)/shard_map/ppermute | solution.py:97
  113.6 8.2 %collective-permute-start.13 = (bf16[4,2,14,608]{3,1,2,0:T(2,128)(2,1)S(1)}, bf16[4,2,14,608]{3,1,2,0:T(2,128)(2,1)S(1)}, u32[]{:S(2)}, u32[]{:S(2)}) collective-permute-start(bf16[4,2,14,608]{3,1,2,0:T(2,128)(2,1)S(1)} %collective-permute-done.11), channel_id=1, source_target_pairs={{0,32},{1,481},{2,34},{3,483},{4,36},{5,485},{6,38},{7,487},{8,40}... | collective-permute-start | bytes 408584 | tf_op jit(solution)/shard_map/ppermute | solution.py:94
  115.6 8.2 %collective-permute-start.14 = (bf16[4,2,14,608]{3,1,2,0:T(2,128)(2,1)S(1)}, bf16[4,2,14,608]{3,1,2,0:T(2,128)(2,1)S(1)}, u32[]{:S(2)}, u32[]{:S(2)}) collective-permute-start(bf16[4,2,14,608]{3,1,2,0:T(2,128)(2,1)S(1)} %collective-permute-done.12), channel_id=1, source_target_pairs={{0,480},{1,33},{2,482},{3,35},{4,484},{5,37},{6,486},{7,39},{8,488... | collective-permute-start | bytes 408584 | tf_op jit(solution)/shard_map/ppermute | solution.py:97
  121.8 8.2 %collective-permute-start.15 = (bf16[4,2,14,608]{3,1,2,0:T(2,128)(2,1)S(1)}, bf16[4,2,14,608]{3,1,2,0:T(2,128)(2,1)S(1)}, u32[]{:S(2)}, u32[]{:S(2)}) collective-permute-start(bf16[4,2,14,608]{3,1,2,0:T(2,128)(2,1)S(1)} %collective-permute-done.13), channel_id=1, source_target_pairs={{0,32},{1,481},{2,34},{3,483},{4,36},{5,485},{6,38},{7,487},{8,40}... | collective-permute-start | bytes 408584 | tf_op jit(solution)/shard_map/ppermute | solution.py:94
  123.8 8.3 %collective-permute-start.16 = (bf16[4,2,14,608]{3,1,2,0:T(2,128)(2,1)S(1)}, bf16[4,2,14,608]{3,1,2,0:T(2,128)(2,1)S(1)}, u32[]{:S(2)}, u32[]{:S(2)}) collective-permute-start(bf16[4,2,14,608]{3,1,2,0:T(2,128)(2,1)S(1)} %collective-permute-done.14), channel_id=1, source_target_pairs={{0,480},{1,33},{2,482},{3,35},{4,484},{5,37},{6,486},{7,39},{8,488... | collective-permute-start | bytes 408584 | tf_op jit(solution)/shard_map/ppermute | solution.py:97
  130.0 8.2 %collective-permute-start.17 = (bf16[4,2,14,608]{3,1,2,0:T(2,128)(2,1)S(1)}, bf16[4,2,14,608]{3,1,2,0:T(2,128)(2,1)S(1)}, u32[]{:S(2)}, u32[]{:S(2)}) collective-permute-start(bf16[4,2,14,608]{3,1,2,0:T(2,128)(2,1)S(1)} %collective-permute-done.15), channel_id=1, source_target_pairs={{0,32},{1,481},{2,34},{3,483},{4,36},{5,485},{6,38},{7,487},{8,40}... | collective-permute-start | bytes 408584 | tf_op jit(solution)/shard_map/ppermute | solution.py:94

commit v8 on v7

--- a/solution.py
+++ b/solution.py
@@ -87,15 +87,33 @@
 
     out = jnp.zeros((nz,) + yblk.shape, piece.dtype)
     out = lax.dynamic_update_index_in_dim(out, yblk, zi, axis=0)
+    half = nz // 2
+    reach = half // 2
+    rel = jnp.zeros((2 * reach + 1,) + yblk.shape, piece.dtype)
+    rel = lax.dynamic_update_index_in_dim(rel, yblk, reach, axis=0)
     fwd = yblk
     bwd = yblk
     axes = ("group", "shard", "tensor")
-    for step in range(1, nz // 2 + 1):
-        fwd = lax.ppermute(fwd, axes, zshift(1))
-        out = lax.dynamic_update_index_in_dim(out, fwd, (zi - step * sgn) % nz, axis=0)
-        if step < nz - nz // 2:
-            bwd = lax.ppermute(bwd, axes, zshift(-1))
-            out = lax.dynamic_update_index_in_dim(out, bwd, (zi + step * sgn) % nz, axis=0)
+    for step in range(1, reach + 1):
+        fwd = lax.ppermute(fwd, axes, zshift(2))
+        j = -step * sgn
+        out = lax.dynamic_update_index_in_dim(out, fwd, (zi + 2 * j) % nz, axis=0)
+        rel = lax.dynamic_update_index_in_dim(rel, fwd, j + reach, axis=0)
+        if step < half - reach:
+            bwd = lax.ppermute(bwd, axes, zshift(-2))
+            out = lax.dynamic_update_index_in_dim(out, bwd, (zi - 2 * j) % nz, axis=0)
+            rel = lax.dynamic_update_index_in_dim(rel, bwd, reach - j, axis=0)
+    nsend = reach
+    up_start = reach
+    down_start = reach - (nsend - 1)
+    for k, first in ((-1, (up_start + down_start + (up_start - down_start) * sgn) // 2),
+                     (1, (up_start + down_start - (up_start - down_start) * sgn) // 2)):
+        part = lax.dynamic_slice_in_dim(rel, first, nsend, axis=0)
+        got = lax.ppermute(part, axes, zshift(k))
+        src_z = zi - k * sgn
+        for m in range(nsend):
+            zabs = (src_z + 2 * (first - reach + m)) % nz
+            out = lax.dynamic_update_index_in_dim(out, got[m], zabs, axis=0)
     layer_blocks = jnp.moveaxis(out, 2, 0).reshape(piece.shape[0], -1, piece.shape[2])
 
     lefts = recv[:, nlayer:nlayer + nleft].reshape((groups,) + left.shape[1:])

time: 145 us -> 137 us (0.945)
  starting transfers between devices: 80.3 us -> 64.2 us
  waiting for transfers between devices: 37.8 us -> 44.1 us
  local copies, waits for them, and re-layouts: 21.3 us -> 23.3 us
    ppermute x15 -> x9, starting transfers between devices: 54.3 us -> 38.1 us  [the longest x4 20.2 us: on_device(): fwd = lax.ppermute(fwd, axes, zshift(2))]
    ppermute x15 -> x9, waiting for transfers between devices: 13.1 us -> 19.5 us  [the longest x2 10.3 us: on_device(): got = lax.ppermute(part, axes, zshift(k))]
    dynamic_update_slice x15 -> x16, local copies, waits for them, and re-layouts: 1.88 us -> 3.06 us  [the longest x8 1 us: on_device(): out = lax.dynamic_update_index_in_dim(out, got[m], zabs, axis=0)]
  transfers between devices with their start and end apart: 19 -> 13, of which waited for: 10 -> 9; matrix products, arithmetic and copies ran while one was open for 7% -> 8% of each run, Pallas kernels for 0% -> 0%
where the time goes in v8:
time: 137 us; the launch traced here: 136 us
  starting transfers between devices  64.2 us (47%)
  waiting for transfers between devices  44.1 us (32%)
  local copies, waits for them, and re-layouts  23.3 us (17%)
  matrix products  1.98 us (1%)
  other arithmetic  1.46 us (1%)
    ppermute x4, starting transfers between devices, on_device(): fwd = lax.ppermute(fwd, axes, zshift(2))  20.2 us
    all_to_all x1, waiting for transfers between devices, on_device(): recv = lax.all_to_all(send, 'group', 0, 0, tiled=True)  19.1 us
    all_to_all x1, starting transfers between devices, on_device(): recv = lax.all_to_all(send, 'group', 0, 0, tiled=True)  15.2 us
    unnamed x19, local copies, waits for them, and re-layouts  11.1 us
    ppermute x3, starting transfers between devices, on_device(): got = lax.ppermute(payload, ('shard', 'tensor'), yshift(k))  10.9 us
    ppermute x2, waiting for transfers between devices, on_device(): got = lax.ppermute(part, axes, zshift(k))  10.3 us
    ppermute x2, starting transfers between devices, on_device(): got = lax.ppermute(part, axes, zshift(k))  9.85 us
    ppermute x3, starting transfers between devices, on_device(): bwd = lax.ppermute(bwd, axes, zshift(-2))  8.03 us
  transfers between devices with their start and end apart: 13, of which 9 were waited for; matrix products, arithmetic and copies ran while one was open for 8% of the time, Pallas kernels for 0%

profile of v8, /device:TPU:6, one launch (start us, length us, event | category | flops | bytes accessed | tf_op | source)
XLA Modules:
  0.0 136.3 jit_solution(10983916298290057257)
XLA Ops:
  0.7 0.9 copy-done
  1.6 0.9 copy.44
  2.5 0.3 reshape.46
  2.8 1.1 copy.45
  3.9 0.1 reshape_squeeze.15
  4.1 0.2 maximum_bitcast_fusion
  4.2 0.5 broadcast.57
  4.7 1.1 reduce.20
  5.8 1.1 reshape.62
  6.9 15.2 %all-to-all-start = ((bf16[4,2,20480]{2,1,0:T(2,128)(2,1)}), bf16[4,2,20480]{2,1,0:T(2,128)(2,1)S(1)}, u32[]{:S(2)}, u32[]{:S(2)}) async-start(bf16[4,2,20480]{2,1,0:T(2,128)(2,1)} %reshape.62), calls=%async_computation | async-start | bytes 655360 | tf_op jit(solution)/shard_map/all_to_all | solution.py:40
  22.1 19.1 %all-to-all-done = bf16[4,2,20480]{2,1,0:T(2,128)(2,1)S(1)} async-done(((bf16[4,2,20480]{2,1,0:T(2,128)(2,1)}), bf16[4,2,20480]{2,1,0:T(2,128)(2,1)S(1)}, u32[]{:S(2)}, u32[]{:S(2)}) %all-to-all-start) | async-done | bytes 327712 | tf_op jit(solution)/shard_map/all_to_all | solution.py:40
  41.2 0.3 reshape.63
  41.5 0.4 copy.73
  42.0 0.2 convert_reduce_fusion
  42.4 0.2 reshape.47
  42.6 0.2 copy.57
  42.8 0.3 constant_dynamic-update-slice_fusion.4
  43.1 3.5 %collective-permute-start = (bf16[1,74368]{1,0:T(2,128)(2,1)S(1)}, bf16[1,74368]{1,0:T(2,128)(2,1)S(1)}, u32[]{:S(2)}, u32[]{:S(2)}) collective-permute-start(bf16[1,74368]{1,0:T(2,128)(2,1)S(1)} %constant_dynamic-update-slice_fusion.4), channel_id=1, source_target_pairs={{0,8},{1,25},{2,10},{3,27},{4,12},{5,29},{6,14},{7,31},{8,16},{9,1... | collective-permute-start | bytes 446216 | tf_op jit(solution)/shard_map/ppermute | solution.py:68
  46.6 3.6 %collective-permute-start.1 = (bf16[1,74368]{1,0:T(2,128)(2,1)S(1)}, bf16[1,74368]{1,0:T(2,128)(2,1)S(1)}, u32[]{:S(2)}, u32[]{:S(2)}) collective-permute-start(bf16[1,74368]{1,0:T(2,128)(2,1)S(1)} %constant_dynamic-update-slice_fusion.4), channel_id=1, source_target_pairs={{0,24},{1,9},{2,26},{3,11},{4,28},{5,13},{6,30},{7,15},{8,0},{9,17... | collective-permute-start | bytes 446216 | tf_op jit(solution)/shard_map/ppermute | solution.py:68
  50.2 3.9 %collective-permute-start.2 = (bf16[1,74368]{1,0:T(2,128)(2,1)S(1)}, bf16[1,74368]{1,0:T(2,128)(2,1)S(1)}, u32[]{:S(2)}, u32[]{:S(2)}) collective-permute-start(bf16[1,74368]{1,0:T(2,128)(2,1)S(1)} %constant_dynamic-update-slice_fusion.4), channel_id=1, source_target_pairs={{0,16},{1,17},{2,18},{3,19},{4,20},{5,21},{6,22},{7,23},{8,24},{9,... | collective-permute-start | bytes 446216 | tf_op jit(solution)/shard_map/ppermute | solution.py:68
  54.3 0.4 slice_reduce_fusion.9
  55.1 0.7 copy.53
  55.7 0.7 copy.54
  56.4 0.2 slice_reduce_fusion.5
  56.7 0.4 collective-permute-done.1
  57.1 0.2 slice_reduce_fusion.4
  57.4 5.2 %collective-permute-done.2 = bf16[1,74368]{1,0:T(2,128)(2,1)S(1)} collective-permute-done((bf16[1,74368]{1,0:T(2,128)(2,1)S(1)}, bf16[1,74368]{1,0:T(2,128)(2,1)S(1)}, u32[]{:S(2)}, u32[]{:S(2)}) %collective-permute-start.2) | collective-permute-done | bytes 148768 | tf_op jit(solution)/shard_map/ppermute | solution.py:68
  62.6 0.2 slice_reduce_fusion.3
  63.0 8.6 %collective-permute-start.3 = (bf16[4,2,14,608]{3,1,2,0:T(2,128)(2,1)S(1)}, bf16[4,2,14,608]{3,1,2,0:T(2,128)(2,1)S(1)}, u32[]{:S(2)}, u32[]{:S(2)}) collective-permute-start(bf16[4,2,14,608]{3,1,2,0:T(2,128)(2,1)S(1)} %copy_dynamic-update-slice_fusion), channel_id=1, source_target_pairs={{0,64},{1,449},{2,66},{3,451},{4,68},{5,453},{6,70},{7,455},{8,72}... | collective-permute-start | bytes 408584 | tf_op jit(solution)/shard_map/ppermute | solution.py:98
  71.7 1.9 %collective-permute-start.4 = (bf16[4,2,14,608]{3,1,2,0:T(2,128)(2,1)S(1)}, bf16[4,2,14,608]{3,1,2,0:T(2,128)(2,1)S(1)}, u32[]{:S(2)}, u32[]{:S(2)}) collective-permute-start(bf16[4,2,14,608]{3,1,2,0:T(2,128)(2,1)S(1)} %copy_dynamic-update-slice_fusion), channel_id=1, source_target_pairs={{0,448},{1,65},{2,450},{3,67},{4,452},{5,69},{6,454},{7,71},{8,456... | collective-permute-start | bytes 408584 | tf_op jit(solution)/shard_map/ppermute | solution.py:103
  73.6 0.7 slice_reduce_fusion.2
  74.2 0.1 reshape_squeeze.16
  74.4 0.7 slice_reduce_fusion.1
  75.0 0.1 reshape_squeeze.17
  75.2 0.7 slice_reduce_fusion
  75.8 0.1 reshape_squeeze.18
  76.1 0.2 fusion.5
  76.3 0.2 fusion.6
  76.5 0.7 dynamic_update_slice.112
  77.2 1.2 broadcast_in_dim.75
  78.6 4.8 %collective-permute-start.5 = (bf16[4,2,14,608]{3,1,2,0:T(2,128)(2,1)S(1)}, bf16[4,2,14,608]{3,1,2,0:T(2,128)(2,1)S(1)}, u32[]{:S(2)}, u32[]{:S(2)}) collective-permute-start(bf16[4,2,14,608]{3,1,2,0:T(2,128)(2,1)S(1)} %collective-permute-done.3), channel_id=1, source_target_pairs={{0,64},{1,449},{2,66},{3,451},{4,68},{5,453},{6,70},{7,455},{8,72}... | collective-permute-start | bytes 408584 | tf_op jit(solution)/shard_map/ppermute | solution.py:98
  83.4 3.1 %collective-permute-start.6 = (bf16[4,2,14,608]{3,1,2,0:T(2,128)(2,1)S(1)}, bf16[4,2,14,608]{3,1,2,0:T(2,128)(2,1)S(1)}, u32[]{:S(2)}, u32[]{:S(2)}) collective-permute-start(bf16[4,2,14,608]{3,1,2,0:T(2,128)(2,1)S(1)} %collective-permute-done.4), channel_id=1, source_target_pairs={{0,448},{1,65},{2,450},{3,67},{4,452},{5,69},{6,454},{7,71},{8,456... | collective-permute-start | bytes 408584 | tf_op jit(solution)/shard_map/ppermute | solution.py:103
  86.5 0.2 bitcast_dynamic-update-slice_fusion.12
  86.7 0.2 bitcast_dynamic-update-slice_fusion.10
  86.9 1.2 collective-permute-done.5
  88.2 3.2 %collective-permute-start.7 = (bf16[4,2,14,608]{3,1,2,0:T(2,128)(2,1)S(1)}, bf16[4,2,14,608]{3,1,2,0:T(2,128)(2,1)S(1)}, u32[]{:S(2)}, u32[]{:S(2)}) collective-permute-start(bf16[4,2,14,608]{3,1,2,0:T(2,128)(2,1)S(1)} %collective-permute-done.5), channel_id=1, source_target_pairs={{0,64},{1,449},{2,66},{3,451},{4,68},{5,453},{6,70},{7,455},{8,72}... | collective-permute-start | bytes 408584 | tf_op jit(solution)/shard_map/ppermute | solution.py:98
  91.4 2.0 %collective-permute-done.6 = bf16[4,2,14,608]{3,1,2,0:T(2,128)(2,1)S(1)} collective-permute-done((bf16[4,2,14,608]{3,1,2,0:T(2,128)(2,1)S(1)}, bf16[4,2,14,608]{3,1,2,0:T(2,128)(2,1)S(1)}, u32[]{:S(2)}, u32[]{:S(2)}) %collective-permute-start.6) | collective-permute-done | bytes 136224 | tf_op jit(solution)/shard_map/ppermute | solution.py:103
  93.3 3.0 %collective-permute-start.8 = (bf16[4,2,14,608]{3,1,2,0:T(2,128)(2,1)S(1)}, bf16[4,2,14,608]{3,1,2,0:T(2,128)(2,1)S(1)}, u32[]{:S(2)}, u32[]{:S(2)}) collective-permute-start(bf16[4,2,14,608]{3,1,2,0:T(2,128)(2,1)S(1)} %collective-permute-done.6), channel_id=1, source_target_pairs={{0,448},{1,65},{2,450},{3,67},{4,452},{5,69},{6,454},{7,71},{8,456... | collective-permute-start | bytes 408584 | tf_op jit(solution)/shard_map/ppermute | solution.py:103
  96.3 0.2 bitcast_dynamic-update-slice_fusion.8
  96.5 0.2 bitcast_dynamic-update-slice_fusion.6
  96.7 0.5 collective-permute-done.7
  97.3 3.6 %collective-permute-start.9 = (bf16[4,2,14,608]{3,1,2,0:T(2,128)(2,1)S(1)}, bf16[4,2,14,608]{3,1,2,0:T(2,128)(2,1)S(1)}, u32[]{:S(2)}, u32[]{:S(2)}) collective-permute-start(bf16[4,2,14,608]{3,1,2,0:T(2,128)(2,1)S(1)} %collective-permute-done.7), channel_id=1, source_target_pairs={{0,64},{1,449},{2,66},{3,451},{4,68},{5,453},{6,70},{7,455},{8,72}... | collective-permute-start | bytes 408584 | tf_op jit(solution)/shard_map/ppermute | solution.py:98
  100.8 0.2 bitcast_dynamic-update-slice_fusion.4
  101.0 0.2 collective-permute-done.8
  101.2 0.2 bitcast_dynamic-update-slice_fusion.2
  101.4 5.3 %collective-permute-done.9 = bf16[4,2,14,608]{3,1,2,0:T(2,128)(2,1)S(1)} collective-permute-done((bf16[4,2,14,608]{3,1,2,0:T(2,128)(2,1)S(1)}, bf16[4,2,14,608]{3,1,2,0:T(2,128)(2,1)S(1)}, u32[]{:S(2)}, u32[]{:S(2)}) %collective-permute-start.9) | collective-permute-done | bytes 136224 | tf_op jit(solution)/shard_map/ppermute | solution.py:98
  106.7 0.2 bitcast_dynamic-update-slice_fusion
  106.9 0.8 constant_dynamic-slice_fusion
  107.7 6.7 %collective-permute-start.10 = (bf16[4,4,2,14,608]{4,2,3,1,0:T(2,128)(2,1)S(1)}, bf16[4,4,2,14,608]{4,2,3,1,0:T(2,128)(2,1)S(1)}, u32[]{:S(2)}, u32[]{:S(2)}) collective-permute-start(bf16[4,4,2,14,608]{4,2,3,1,0:T(2,128)(2,1)S(1)} %get-tuple-element.29), channel_id=1, source_target_pairs={{0,480},{1,33},{2,482},{3,35},{4,484},{5,37},{6,486},{7,39},{8,488... | collective-permute-start | bytes 1634312 | tf_op jit(solution)/shard_map/ppermute | solution.py:112
  114.5 0.2 fusion.7
  114.7 1.4 multiply_subtract_fusion
  116.1 3.1 %collective-permute-start.11 = (bf16[4,4,2,14,608]{4,2,3,1,0:T(2,128)(2,1)S(1)}, bf16[4,4,2,14,608]{4,2,3,1,0:T(2,128)(2,1)S(1)}, u32[]{:S(2)}, u32[]{:S(2)}) collective-permute-start(bf16[4,4,2,14,608]{4,2,3,1,0:T(2,128)(2,1)S(1)} %get-tuple-element.28), channel_id=1, source_target_pairs={{0,32},{1,481},{2,34},{3,483},{4,36},{5,485},{6,38},{7,487},{8,40}... | collective-permute-start | bytes 1634312 | tf_op jit(solution)/shard_map/ppermute | solution.py:112
  119.2 10.3 %collective-permute-done.10 = bf16[4,4,2,14,608]{4,2,3,1,0:T(2,128)(2,1)S(1)} collective-permute-done((bf16[4,4,2,14,608]{4,2,3,1,0:T(2,128)(2,1)S(1)}, bf16[4,4,2,14,608]{4,2,3,1,0:T(2,128)(2,1)S(1)}, u32[]{:S(2)}, u32[]{:S(2)}) %collective-permute-start.10) | collective-permute-done | bytes 544800 | tf_op jit(solution)/shard_map/ppermute | solution.py:112
  130.5 5.7 %copy.55 = bf16[2,896,608]{1,2,0:T(8,128)(2,1)} copy(bf16[2,896,608]{2,0,1:T(2,128)(2,1)S(1)} %bitcast.60) | data formatting | bytes 4358144
  (47 shorter events, 2.6 us)
Async XLA Ops:
  0.6 0.9 copy-start
  6.9 35.5 %copy-start.3 = (f32[2,14,608]{2,0,1:T(2,128)S(1)}, f32[2,14,608]{2,0,1:T(2,128)}, u32[]{:S(2)}) copy-start(f32[2,14,608]{2,0,1:T(2,128)} %param.11) | copy-start | bytes 204292
  6.9 35.5 %copy-start.4 = (f32[2,14,608]{2,0,1:T(2,128)S(1)}, f32[2,14,608]{2,0,1:T(2,128)}, u32[]{:S(2)}) copy-start(f32[2,14,608]{2,0,1:T(2,128)} %param.10) | copy-start | bytes 204292
  6.9 34.3 %all-to-all-start = ((bf16[4,2,20480]{2,1,0:T(2,128)(2,1)}), bf16[4,2,20480]{2,1,0:T(2,128)(2,1)S(1)}, u32[]{:S(2)}, u32[]{:S(2)}) async-start(bf16[4,2,20480]{2,1,0:T(2,128)(2,1)} %reshape.62), calls=%async_computation | async-start | bytes 655360 | tf_op jit(solution)/shard_map/all_to_all | solution.py:40
  43.1 13.3 %collective-permute-start = (bf16[1,74368]{1,0:T(2,128)(2,1)S(1)}, bf16[1,74368]{1,0:T(2,128)(2,1)S(1)}, u32[]{:S(2)}, u32[]{:S(2)}) collective-permute-start(bf16[1,74368]{1,0:T(2,128)(2,1)S(1)} %constant_dynamic-update-slice_fusion.4), channel_id=1, source_target_pairs={{0,8},{1,25},{2,10},{3,27},{4,12},{5,29},{6,14},{7,31},{8,16},{9,1... | collective-permute-start | bytes 446216 | tf_op jit(solution)/shard_map/ppermute | solution.py:68
  46.6 10.5 %collective-permute-start.1 = (bf16[1,74368]{1,0:T(2,128)(2,1)S(1)}, bf16[1,74368]{1,0:T(2,128)(2,1)S(1)}, u32[]{:S(2)}, u32[]{:S(2)}) collective-permute-start(bf16[1,74368]{1,0:T(2,128)(2,1)S(1)} %constant_dynamic-update-slice_fusion.4), channel_id=1, source_target_pairs={{0,24},{1,9},{2,26},{3,11},{4,28},{5,13},{6,30},{7,15},{8,0},{9,17... | collective-permute-start | bytes 446216 | tf_op jit(solution)/shard_map/ppermute | solution.py:68
  50.2 12.4 %collective-permute-start.2 = (bf16[1,74368]{1,0:T(2,128)(2,1)S(1)}, bf16[1,74368]{1,0:T(2,128)(2,1)S(1)}, u32[]{:S(2)}, u32[]{:S(2)}) collective-permute-start(bf16[1,74368]{1,0:T(2,128)(2,1)S(1)} %constant_dynamic-update-slice_fusion.4), channel_id=1, source_target_pairs={{0,16},{1,17},{2,18},{3,19},{4,20},{5,21},{6,22},{7,23},{8,24},{9,... | collective-permute-start | bytes 446216 | tf_op jit(solution)/shard_map/ppermute | solution.py:68
  63.0 15.5 %collective-permute-start.3 = (bf16[4,2,14,608]{3,1,2,0:T(2,128)(2,1)S(1)}, bf16[4,2,14,608]{3,1,2,0:T(2,128)(2,1)S(1)}, u32[]{:S(2)}, u32[]{:S(2)}) collective-permute-start(bf16[4,2,14,608]{3,1,2,0:T(2,128)(2,1)S(1)} %copy_dynamic-update-slice_fusion), channel_id=1, source_target_pairs={{0,64},{1,449},{2,66},{3,451},{4,68},{5,453},{6,70},{7,455},{8,72}... | collective-permute-start | bytes 408584 | tf_op jit(solution)/shard_map/ppermute | solution.py:98
  71.7 11.7 %collective-permute-start.4 = (bf16[4,2,14,608]{3,1,2,0:T(2,128)(2,1)S(1)}, bf16[4,2,14,608]{3,1,2,0:T(2,128)(2,1)S(1)}, u32[]{:S(2)}, u32[]{:S(2)}) collective-permute-start(bf16[4,2,14,608]{3,1,2,0:T(2,128)(2,1)S(1)} %copy_dynamic-update-slice_fusion), channel_id=1, source_target_pairs={{0,448},{1,65},{2,450},{3,67},{4,452},{5,69},{6,454},{7,71},{8,456... | collective-permute-start | bytes 408584 | tf_op jit(solution)/shard_map/ppermute | solution.py:103
  78.6 9.6 %collective-permute-start.5 = (bf16[4,2,14,608]{3,1,2,0:T(2,128)(2,1)S(1)}, bf16[4,2,14,608]{3,1,2,0:T(2,128)(2,1)S(1)}, u32[]{:S(2)}, u32[]{:S(2)}) collective-permute-start(bf16[4,2,14,608]{3,1,2,0:T(2,128)(2,1)S(1)} %collective-permute-done.3), channel_id=1, source_target_pairs={{0,64},{1,449},{2,66},{3,451},{4,68},{5,453},{6,70},{7,455},{8,72}... | collective-permute-start | bytes 408584 | tf_op jit(solution)/shard_map/ppermute | solution.py:98
  83.4 9.9 %collective-permute-start.6 = (bf16[4,2,14,608]{3,1,2,0:T(2,128)(2,1)S(1)}, bf16[4,2,14,608]{3,1,2,0:T(2,128)(2,1)S(1)}, u32[]{:S(2)}, u32[]{:S(2)}) collective-permute-start(bf16[4,2,14,608]{3,1,2,0:T(2,128)(2,1)S(1)} %collective-permute-done.4), channel_id=1, source_target_pairs={{0,448},{1,65},{2,450},{3,67},{4,452},{5,69},{6,454},{7,71},{8,456... | collective-permute-start | bytes 408584 | tf_op jit(solution)/shard_map/ppermute | solution.py:103
  88.2 9.1 %collective-permute-start.7 = (bf16[4,2,14,608]{3,1,2,0:T(2,128)(2,1)S(1)}, bf16[4,2,14,608]{3,1,2,0:T(2,128)(2,1)S(1)}, u32[]{:S(2)}, u32[]{:S(2)}) collective-permute-start(bf16[4,2,14,608]{3,1,2,0:T(2,128)(2,1)S(1)} %collective-permute-done.5), channel_id=1, source_target_pairs={{0,64},{1,449},{2,66},{3,451},{4,68},{5,453},{6,70},{7,455},{8,72}... | collective-permute-start | bytes 408584 | tf_op jit(solution)/shard_map/ppermute | solution.py:98
  93.3 7.9 %collective-permute-start.8 = (bf16[4,2,14,608]{3,1,2,0:T(2,128)(2,1)S(1)}, bf16[4,2,14,608]{3,1,2,0:T(2,128)(2,1)S(1)}, u32[]{:S(2)}, u32[]{:S(2)}) collective-permute-start(bf16[4,2,14,608]{3,1,2,0:T(2,128)(2,1)S(1)} %collective-permute-done.6), channel_id=1, source_target_pairs={{0,448},{1,65},{2,450},{3,67},{4,452},{5,69},{6,454},{7,71},{8,456... | collective-permute-start | bytes 408584 | tf_op jit(solution)/shard_map/ppermute | solution.py:103
  96.5 18.2 %copy-start.1 = (f32[150,896]{1,0:T(8,128)S(1)}, f32[150,896]{1,0:T(8,128)}, u32[]{:S(2)}) copy-start(f32[150,896]{1,0:T(8,128)} %param.12) | copy-start | bytes 1612804
  96.5 18.2 %copy-start.2 = (f32[150,896]{1,0:T(8,128)S(1)}, f32[150,896]{1,0:T(8,128)}, u32[]{:S(2)}) copy-start(f32[150,896]{1,0:T(8,128)} %param.13) | copy-start | bytes 1612804
  97.3 9.5 %collective-permute-start.9 = (bf16[4,2,14,608]{3,1,2,0:T(2,128)(2,1)S(1)}, bf16[4,2,14,608]{3,1,2,0:T(2,128)(2,1)S(1)}, u32[]{:S(2)}, u32[]{:S(2)}) collective-permute-start(bf16[4,2,14,608]{3,1,2,0:T(2,128)(2,1)S(1)} %collective-permute-done.7), channel_id=1, source_target_pairs={{0,64},{1,449},{2,66},{3,451},{4,68},{5,453},{6,70},{7,455},{8,72}... | collective-permute-start | bytes 408584 | tf_op jit(solution)/shard_map/ppermute | solution.py:98
  107.7 21.7 %collective-permute-start.10 = (bf16[4,4,2,14,608]{4,2,3,1,0:T(2,128)(2,1)S(1)}, bf16[4,4,2,14,608]{4,2,3,1,0:T(2,128)(2,1)S(1)}, u32[]{:S(2)}, u32[]{:S(2)}) collective-permute-start(bf16[4,4,2,14,608]{4,2,3,1,0:T(2,128)(2,1)S(1)} %get-tuple-element.29), channel_id=1, source_target_pairs={{0,480},{1,33},{2,482},{3,35},{4,484},{5,37},{6,486},{7,39},{8,488... | collective-permute-start | bytes 1634312 | tf_op jit(solution)/shard_map/ppermute | solution.py:112
  116.1 13.9 %collective-permute-start.11 = (bf16[4,4,2,14,608]{4,2,3,1,0:T(2,128)(2,1)S(1)}, bf16[4,4,2,14,608]{4,2,3,1,0:T(2,128)(2,1)S(1)}, u32[]{:S(2)}, u32[]{:S(2)}) collective-permute-start(bf16[4,4,2,14,608]{4,2,3,1,0:T(2,128)(2,1)S(1)} %get-tuple-element.28), channel_id=1, source_target_pairs={{0,32},{1,481},{2,34},{3,483},{4,36},{5,485},{6,38},{7,487},{8,40}... | collective-permute-start | bytes 1634312 | tf_op jit(solution)/shard_map/ppermute | solution.py:112

commit v9 on v8

--- a/solution.py
+++ b/solution.py
@@ -33,9 +33,7 @@
     send_left = left.reshape(groups, nleft)
     right = emb_right[0]
     rank, width = right.shape
-    rrows = rank // Y_SIZE
-    ry = lax.dynamic_slice_in_dim(right, (si % Y_SIZE) * rrows, rrows, axis=0)
-    send_right = jnp.broadcast_to(ry.reshape(1, rrows * width), (groups, rrows * width))
+    send_right = jnp.broadcast_to(right.reshape(1, rank * width), (groups, rank * width))
     send = jnp.concatenate([send_layer, send_left, send_right], axis=1)
     recv = lax.all_to_all(send, "group", 0, 0, tiled=True)
 
@@ -56,21 +54,7 @@
             pairs.append((i, ((s - s % Y_SIZE) + (s % Y_SIZE + d) % Y_SIZE) * tensors + t))
         return pairs
 
-    yi = si % Y_SIZE
-    rgot = recv[:, nlayer + nleft:]
-    npiece = piece.size
-    payload = jnp.concatenate([piece.reshape(1, npiece), rgot.reshape(1, -1)], axis=1)
-    yblk = jnp.zeros((Y_SIZE,) + piece.shape, piece.dtype)
-    yblk = lax.dynamic_update_index_in_dim(yblk, piece, yi, axis=0)
-    rights = jnp.zeros((groups, rank, width), rgot.dtype)
-    rights = lax.dynamic_update_slice_in_dim(rights, rgot.reshape(groups, rrows, width), yi * rrows, axis=1)
-    for k in (1, -1, 2):
-        got = lax.ppermute(payload, ("shard", "tensor"), yshift(k))
-        src = (yi - k * sgn) % Y_SIZE
-        yblk = lax.dynamic_update_index_in_dim(yblk, got[0, :npiece].reshape(piece.shape), src, axis=0)
-        rpart = got[0, npiece:].reshape(groups, rrows, width)
-        rights = lax.dynamic_update_slice_in_dim(rights, rpart, src * rrows, axis=1)
-
+    axes = ("group", "shard", "tensor")
     zlo_size = shards // Y_SIZE
     nz = groups * zlo_size
     zi = gi * zlo_size + si // Y_SIZE
@@ -85,23 +69,22 @@
             pairs.append((i, (((z + d) % nz) * Y_SIZE + y) * tensors + t))
         return pairs
 
-    out = jnp.zeros((nz,) + yblk.shape, piece.dtype)
-    out = lax.dynamic_update_index_in_dim(out, yblk, zi, axis=0)
+    zblk = jnp.zeros((nz,) + piece.shape, piece.dtype)
+    zblk = lax.dynamic_update_index_in_dim(zblk, piece, zi, axis=0)
     half = nz // 2
     reach = half // 2
-    rel = jnp.zeros((2 * reach + 1,) + yblk.shape, piece.dtype)
-    rel = lax.dynamic_update_index_in_dim(rel, yblk, reach, axis=0)
-    fwd = yblk
-    bwd = yblk
-    axes = ("group", "shard", "tensor")
+    rel = jnp.zeros((2 * reach + 1,) + piece.shape, piece.dtype)
+    rel = lax.dynamic_update_index_in_dim(rel, piece, reach, axis=0)
+    fwd = piece
+    bwd = piece
     for step in range(1, reach + 1):
         fwd = lax.ppermute(fwd, axes, zshift(2))
         j = -step * sgn
-        out = lax.dynamic_update_index_in_dim(out, fwd, (zi + 2 * j) % nz, axis=0)
+        zblk = lax.dynamic_update_index_in_dim(zblk, fwd, (zi + 2 * j) % nz, axis=0)
         rel = lax.dynamic_update_index_in_dim(rel, fwd, j + reach, axis=0)
         if step < half - reach:
             bwd = lax.ppermute(bwd, axes, zshift(-2))
-            out = lax.dynamic_update_index_in_dim(out, bwd, (zi - 2 * j) % nz, axis=0)
+            zblk = lax.dynamic_update_index_in_dim(zblk, bwd, (zi - 2 * j) % nz, axis=0)
             rel = lax.dynamic_update_index_in_dim(rel, bwd, reach - j, axis=0)
     nsend = reach
     up_start = reach
@@ -113,10 +96,19 @@
         src_z = zi - k * sgn
         for m in range(nsend):
             zabs = (src_z + 2 * (first - reach + m)) % nz
-            out = lax.dynamic_update_index_in_dim(out, got[m], zabs, axis=0)
+            zblk = lax.dynamic_update_index_in_dim(zblk, got[m], zabs, axis=0)
+
+    yi = si % Y_SIZE
+    yout = jnp.zeros((Y_SIZE,) + zblk.shape, piece.dtype)
+    yout = lax.dynamic_update_index_in_dim(yout, zblk, yi, axis=0)
+    for k in (1, -1, 2):
+        got = lax.ppermute(zblk, ("shard", "tensor"), yshift(k))
+        yout = lax.dynamic_update_index_in_dim(yout, got, (yi - k * sgn) % Y_SIZE, axis=0)
+    out = jnp.swapaxes(yout, 0, 1)
     layer_blocks = jnp.moveaxis(out, 2, 0).reshape(piece.shape[0], -1, piece.shape[2])
 
     lefts = recv[:, nlayer:nlayer + nleft].reshape((groups,) + left.shape[1:])
+    rights = recv[:, nlayer + nleft:].reshape(groups, rank, width)
     total = jnp.zeros(emb_weight.shape, f32)
     for g in range(groups):
         product = jnp.dot(lefts[g], rights[g], preferred_element_type=f32).astype(bf16)

time: 137 us -> 211 us (1.54); the launches traced: 136 us -> 208 us
  local copies, waits for them, and re-layouts: 23.3 us -> 86.3 us
  waiting for transfers between devices: 44.1 us -> 57 us
  starting transfers between devices: 64.2 us -> 58 us
    dynamic_update_slice x18 -> x21, local copies, waits for them, and re-layouts: 2.1 us -> 49.4 us  [the longest x8 24.3 us: on_device(): zblk = lax.dynamic_update_index_in_dim(zblk, got[m], zabs, axis=0)]
    all_to_all x1, waiting for transfers between devices: 19.1 us -> 38.6 us  [on_device(): recv = lax.all_to_all(send, 'group', 0, 0, tiled=True)]
    ppermute x4, starting transfers between devices: 20.2 us -> 7.66 us  [on_device(): fwd = lax.ppermute(fwd, axes, zshift(2))]
    ppermute x2, waiting for transfers between devices: 10.3 us -> 0.01 us  [on_device(): got = lax.ppermute(part, axes, zshift(k))]
    ppermute x3, starting transfers between devices: 8.03 us -> 18.2 us  [on_device(): bwd = lax.ppermute(bwd, axes, zshift(-2))]
    broadcast_in_dim x7 -> x11, local copies, waits for them, and re-layouts: 1.73 us -> 11.8 us  [the longest x4 5.08 us: on_device(): zblk = lax.dynamic_update_index_in_dim(zblk, fwd, (zi + 2 * j) % nz, axis=0)]
    slice x7 -> x11, local copies, waits for them, and re-layouts: 2.58 us -> 9.69 us  [the longest x10 7.18 us: on_device(): zblk = lax.dynamic_update_index_in_dim(zblk, got[m], zabs, axis=0)]
    ppermute x3, waiting for transfers between devices: 5.55 us -> 12.1 us  [on_device(): got = lax.ppermute(zblk, ('shard', 'tensor'), yshift(k))]
  transfers between devices with their start and end apart: 13 -> 13, of which waited for: 9 -> 4; matrix products, arithmetic and copies ran while one was open for 8% -> 23% of each run, Pallas kernels for 0% -> 0%
where the time goes in v9:
time: 211 us; the launch traced here: 208 us
  local copies, waits for them, and re-layouts  86.3 us (41%)
  starting transfers between devices  58 us (27%)
  waiting for transfers between devices  57 us (27%)
  matrix products  2.77 us (1%)
  other arithmetic  2.64 us (1%)
    all_to_all x1, waiting for transfers between devices, on_device(): recv = lax.all_to_all(send, 'group', 0, 0, tiled=True)  38.6 us
    dynamic_update_slice x8, local copies, waits for them, and re-layouts, on_device(): zblk = lax.dynamic_update_index_in_dim(zblk, got[m], zabs, axis=0)  24.3 us
    ppermute x3, starting transfers between devices, on_device(): bwd = lax.ppermute(bwd, axes, zshift(-2))  18.2 us
    all_to_all x1, starting transfers between devices, on_device(): recv = lax.all_to_all(send, 'group', 0, 0, tiled=True)  15.1 us
    ppermute x3, waiting for transfers between devices, on_device(): got = lax.ppermute(zblk, ('shard', 'tensor'), yshift(k))  12.1 us
    dynamic_update_slice x4, local copies, waits for them, and re-layouts, on_device(): zblk = lax.dynamic_update_index_in_dim(zblk, fwd, (zi + 2 * j) % nz, axis=0)  12 us
    ppermute x3, starting transfers between devices, on_device(): got = lax.ppermute(zblk, ('shard', 'tensor'), yshift(k))  11.1 us
    unnamed x29, local copies, waits for them, and re-layouts  10.5 us
  transfers between devices with their start and end apart: 13, of which 4 were waited for; matrix products, arithmetic and copies ran while one was open for 23% of the time, Pallas kernels for 0%

profile of v9, /device:TPU:6, one launch (start us, length us, event | category | flops | bytes accessed | tf_op | source)
XLA Modules:
  0.0 207.9 jit_solution(8368663558062222112)
XLA Ops:
  0.6 1.1 copy.86
  1.8 0.9 copy.85
  3.1 1.0 reshape.50
  4.9 1.5 reduce.16
  6.4 1.3 reshape.51
  7.7 15.1 %all-to-all-start = ((bf16[4,2,41984]{2,1,0:T(2,128)(2,1)}), bf16[4,2,41984]{2,1,0:T(2,128)(2,1)S(1)}, u32[]{:S(2)}, u32[]{:S(2)}) async-start(bf16[4,2,41984]{2,1,0:T(2,128)(2,1)} %reshape.51), calls=%async_computation | async-start | bytes 1343488 | tf_op jit(solution)/shard_map/all_to_all | solution.py:38
  22.8 38.6 %all-to-all-done = bf16[4,2,41984]{2,1,0:T(2,128)(2,1)S(1)} async-done(((bf16[4,2,41984]{2,1,0:T(2,128)(2,1)}), bf16[4,2,41984]{2,1,0:T(2,128)(2,1)S(1)}, u32[]{:S(2)}, u32[]{:S(2)}) %all-to-all-start) | async-done | bytes 671776 | tf_op jit(solution)/shard_map/all_to_all | solution.py:38
  61.4 0.5 reshape.52
  62.8 0.7 fusion.9
  63.4 1.9 collective-permute-start
  65.3 6.0 %collective-permute-start.1 = (bf16[2,14,608]{2,1,0:T(8,128)(2,1)S(1)}, bf16[2,14,608]{2,1,0:T(8,128)(2,1)S(1)}, u32[]{:S(2)}, u32[]{:S(2)}) collective-permute-start(bf16[2,14,608]{2,1,0:T(8,128)(2,1)S(1)} %get-tuple-element.30), channel_id=1, source_target_pairs={{0,448},{1,65},{2,450},{3,67},{4,452},{5,69},{6,454},{7,71},{8,456... | collective-permute-start | bytes 102152 | tf_op jit(solution)/shard_map/ppermute | solution.py:86
  71.8 2.5 %slice_reduce_fusion.3 = (bf16[57344]{0:T(1024)(128)(2,1)S(1)}, bf16[57344]{0:T(1024)(128)(2,1)S(1)}, bf16[57344]{0:T(1024)(128)(2,1)S(1)}, bf16[57344]{0:T(1024)(128)(2,1)S(1)}) fusion(bf16[4,83968]{1,0:T(4,128)(2,1)S(1)} %bitcast.41), kind=kLoop, calls=%fused_computation.24 | loop fusion | bytes 917504 | tf_op jit(solution)/shard_map/slice | solution.py:114
  75.6 0.7 squeeze.36
  76.5 2.0 dynamic_update_slice.88
  78.4 1.9 collective-permute-start.2
  80.4 6.0 %collective-permute-start.3 = (bf16[2,14,608]{2,1,0:T(8,128)(2,1)S(1)}, bf16[2,14,608]{2,1,0:T(8,128)(2,1)S(1)}, u32[]{:S(2)}, u32[]{:S(2)}) collective-permute-start(bf16[2,14,608]{2,1,0:T(8,128)(2,1)S(1)} %collective-permute-done.1), channel_id=1, source_target_pairs={{0,448},{1,65},{2,450},{3,67},{4,452},{5,69},{6,454},{7,71},{8,456... | collective-permute-start | bytes 102152 | tf_op jit(solution)/shard_map/ppermute | solution.py:86
  86.7 1.9 collective-permute-start.4
  88.7 6.1 %collective-permute-start.5 = (bf16[2,14,608]{2,1,0:T(8,128)(2,1)S(1)}, bf16[2,14,608]{2,1,0:T(8,128)(2,1)S(1)}, u32[]{:S(2)}, u32[]{:S(2)}) collective-permute-start(bf16[2,14,608]{2,1,0:T(8,128)(2,1)S(1)} %collective-permute-done.3), channel_id=1, source_target_pairs={{0,448},{1,65},{2,450},{3,67},{4,452},{5,69},{6,454},{7,71},{8,456... | collective-permute-start | bytes 102152 | tf_op jit(solution)/shard_map/ppermute | solution.py:86
  94.9 1.9 collective-permute-start.6
  96.8 6.1 %collective-permute-done.6 = bf16[2,14,608]{2,1,0:T(8,128)(2,1)S(1)} collective-permute-done((bf16[2,14,608]{2,1,0:T(8,128)(2,1)S(1)}, bf16[2,14,608]{2,1,0:T(8,128)(2,1)S(1)}, u32[]{:S(2)}, u32[]{:S(2)}) %collective-permute-start.6) | collective-permute-done | bytes 34080 | tf_op jit(solution)/shard_map/ppermute | solution.py:81
  103.0 0.8 constant_dynamic-slice_fusion
  103.8 1.9 collective-permute-start.7
  106.0 0.7 copy.91
  106.7 1.5 copy.92
  108.1 3.0 %dynamic_update_slice.89 = bf16[16,2,14,608]{3,0,2,1:T(8,128)(2,1)S(1)} dynamic-update-slice(bf16[16,2,14,608]{3,0,2,1:T(8,128)(2,1)S(1)} %dynamic_update_slice.88, bf16[1,2,14,608]{3,0,2,1:T(2,128)(2,1)} %copy.91, s32[]{:T(128)S(6)} %select_n.189, s32[]{:T(128)} %constant.244.clone.1, s32[]{:T(128)} %constant.244.clone.1, s32[]{:T(128)} %constant.244.clone.1) | dynamic-update-slice | bytes 68100 | tf_op jit(solution)/shard_map/jit(dynamic_update_index_in_dim)/dynamic_update_slice | solution.py:83
  111.1 3.0 %dynamic_update_slice.90 = bf16[16,2,14,608]{3,0,2,1:T(8,128)(2,1)S(1)} dynamic-update-slice(bf16[16,2,14,608]{3,0,2,1:T(8,128)(2,1)S(1)} %dynamic_update_slice.89, bf16[1,2,14,608]{3,0,2,1:T(2,128)(2,1)} %copy.92, s32[]{:T(128)S(6)} %select_n.191, s32[]{:T(128)} %constant.244.clone.1, s32[]{:T(128)} %constant.244.clone.1, s32[]{:T(128)} %constant.244.clone.1) | dynamic-update-slice | bytes 68100 | tf_op jit(solution)/shard_map/jit(dynamic_update_index_in_dim)/dynamic_update_slice | solution.py:87
  114.2 1.5 copy.93
  115.6 1.5 copy.94
  117.1 3.0 %dynamic_update_slice.91 = bf16[16,2,14,608]{3,0,2,1:T(8,128)(2,1)S(1)} dynamic-update-slice(bf16[16,2,14,608]{3,0,2,1:T(8,128)(2,1)S(1)} %dynamic_update_slice.90, bf16[1,2,14,608]{3,0,2,1:T(2,128)(2,1)} %copy.93, s32[]{:T(128)S(6)} %select_n.193, s32[]{:T(128)} %constant.244.clone.1, s32[]{:T(128)} %constant.244.clone.1, s32[]{:T(128)} %constant.244.clone.1) | dynamic-update-slice | bytes 68100 | tf_op jit(solution)/shard_map/jit(dynamic_update_index_in_dim)/dynamic_update_slice | solution.py:83
  120.1 3.0 %dynamic_update_slice.92 = bf16[16,2,14,608]{3,0,2,1:T(8,128)(2,1)S(1)} dynamic-update-slice(bf16[16,2,14,608]{3,0,2,1:T(8,128)(2,1)S(1)} %dynamic_update_slice.91, bf16[1,2,14,608]{3,0,2,1:T(2,128)(2,1)} %copy.94, s32[]{:T(128)S(6)} %select_n.195, s32[]{:T(128)} %constant.244.clone.1, s32[]{:T(128)} %constant.244.clone.1, s32[]{:T(128)} %constant.244.clone.1) | dynamic-update-slice | bytes 68100 | tf_op jit(solution)/shard_map/jit(dynamic_update_index_in_dim)/dynamic_update_slice | solution.py:87
  123.1 1.5 copy.95
  124.6 1.5 copy.96
  126.1 3.0 %dynamic_update_slice.93 = bf16[16,2,14,608]{3,0,2,1:T(8,128)(2,1)S(1)} dynamic-update-slice(bf16[16,2,14,608]{3,0,2,1:T(8,128)(2,1)S(1)} %dynamic_update_slice.92, bf16[1,2,14,608]{3,0,2,1:T(2,128)(2,1)} %copy.95, s32[]{:T(128)S(6)} %select_n.197, s32[]{:T(128)} %constant.244.clone.1, s32[]{:T(128)} %constant.244.clone.1, s32[]{:T(128)} %constant.244.clone.1) | dynamic-update-slice | bytes 68100 | tf_op jit(solution)/shard_map/jit(dynamic_update_index_in_dim)/dynamic_update_slice | solution.py:83
  129.1 3.0 %dynamic_update_slice.94 = bf16[16,2,14,608]{3,0,2,1:T(8,128)(2,1)S(1)} dynamic-update-slice(bf16[16,2,14,608]{3,0,2,1:T(8,128)(2,1)S(1)} %dynamic_update_slice.93, bf16[1,2,14,608]{3,0,2,1:T(2,128)(2,1)} %copy.96, s32[]{:T(128)S(6)} %select_n.199, s32[]{:T(128)} %constant.244.clone.1, s32[]{:T(128)} %constant.244.clone.1, s32[]{:T(128)} %constant.244.clone.1) | dynamic-update-slice | bytes 68100 | tf_op jit(solution)/shard_map/jit(dynamic_update_index_in_dim)/dynamic_update_slice | solution.py:87
  132.1 1.5 copy.97
  133.6 4.1 %collective-permute-start.8 = (bf16[4,2,14,608]{3,2,1,0:T(8,128)(2,1)}, bf16[4,2,14,608]{3,2,1,0:T(8,128)(2,1)}, u32[]{:S(2)}, u32[]{:S(2)}) collective-permute-start(bf16[4,2,14,608]{3,2,1,0:T(8,128)(2,1)} %get-tuple-element.32), channel_id=1, source_target_pairs={{0,32},{1,481},{2,34},{3,483},{4,36},{5,485},{6,38},{7,487},{8,40}... | collective-permute-start | bytes 408584 | tf_op jit(solution)/shard_map/ppermute | solution.py:95
  137.7 3.0 %dynamic_update_slice.95 = bf16[16,2,14,608]{3,0,2,1:T(8,128)(2,1)S(1)} dynamic-update-slice(bf16[16,2,14,608]{3,0,2,1:T(8,128)(2,1)S(1)} %dynamic_update_slice.94, bf16[1,2,14,608]{3,0,2,1:T(2,128)(2,1)} %copy.97, s32[]{:T(128)S(6)} %select_n.201, s32[]{:T(128)} %constant.244.clone.1, s32[]{:T(128)} %constant.244.clone.1, s32[]{:T(128)} %constant.244.clone.1) | dynamic-update-slice | bytes 68100 | tf_op jit(solution)/shard_map/jit(dynamic_update_index_in_dim)/dynamic_update_slice | solution.py:83
  140.7 0.9 fusion.11
  141.6 0.7 copy.98
  142.3 0.7 copy.99
  143.0 0.7 copy.100
  143.6 0.7 copy.101
  144.3 0.9 fusion.10
  145.2 0.7 copy.102
  145.9 0.7 copy.103
  146.5 0.7 copy.104
  147.2 0.7 copy.105
  147.9 3.0 %dynamic_update_slice.104 = bf16[16,2,14,608]{3,0,2,1:T(8,128)(2,1)S(1)} dynamic-update-slice(bf16[16,2,14,608]{3,0,2,1:T(8,128)(2,1)S(1)} %dynamic_update_slice.95, bf16[1,2,14,608]{3,0,2,1:T(2,128)(2,1)} %copy.98, s32[]{:T(128)S(6)} %select_n.212, s32[]{:T(128)} %constant.244.clone.1, s32[]{:T(128)} %constant.244.clone.1, s32[]{:T(128)} %constant.244.clone.1) | dynamic-update-slice | bytes 68100 | tf_op jit(solution)/shard_map/jit(dynamic_update_index_in_dim)/dynamic_update_slice | solution.py:99
  150.9 3.0 %dynamic_update_slice.105 = bf16[16,2,14,608]{3,0,2,1:T(8,128)(2,1)S(1)} dynamic-update-slice(bf16[16,2,14,608]{3,0,2,1:T(8,128)(2,1)S(1)} %dynamic_update_slice.104, bf16[1,2,14,608]{3,0,2,1:T(2,128)(2,1)} %copy.99, s32[]{:T(128)S(6)} %select_n.214, s32[]{:T(128)} %constant.244.clone.1, s32[]{:T(128)} %constant.244.clone.1, s32[]{:T(128)} %constant.244.clone.1) | dynamic-update-slice | bytes 68100 | tf_op jit(solution)/shard_map/jit(dynamic_update_index_in_dim)/dynamic_update_slice | solution.py:99
  153.9 3.0 %dynamic_update_slice.106 = bf16[16,2,14,608]{3,0,2,1:T(8,128)(2,1)S(1)} dynamic-update-slice(bf16[16,2,14,608]{3,0,2,1:T(8,128)(2,1)S(1)} %dynamic_update_slice.105, bf16[1,2,14,608]{3,0,2,1:T(2,128)(2,1)} %copy.100, s32[]{:T(128)S(6)} %select_n.216, s32[]{:T(128)} %constant.244.clone.1, s32[]{:T(128)} %constant.244.clone.1, s32[]{:T(128)} %constant.244.clone.1) | dynamic-update-slice | bytes 68100 | tf_op jit(solution)/shard_map/jit(dynamic_update_index_in_dim)/dynamic_update_slice | solution.py:99
  157.0 3.0 %dynamic_update_slice.107 = bf16[16,2,14,608]{3,0,2,1:T(8,128)(2,1)S(1)} dynamic-update-slice(bf16[16,2,14,608]{3,0,2,1:T(8,128)(2,1)S(1)} %dynamic_update_slice.106, bf16[1,2,14,608]{3,0,2,1:T(2,128)(2,1)} %copy.101, s32[]{:T(128)S(6)} %select_n.218, s32[]{:T(128)} %constant.244.clone.1, s32[]{:T(128)} %constant.244.clone.1, s32[]{:T(128)} %constant.244.clone.1) | dynamic-update-slice | bytes 68100 | tf_op jit(solution)/shard_map/jit(dynamic_update_index_in_dim)/dynamic_update_slice | solution.py:99
  160.0 3.0 %dynamic_update_slice.108 = bf16[16,2,14,608]{3,0,2,1:T(8,128)(2,1)S(1)} dynamic-update-slice(bf16[16,2,14,608]{3,0,2,1:T(8,128)(2,1)S(1)} %dynamic_update_slice.107, bf16[1,2,14,608]{3,0,2,1:T(2,128)(2,1)} %copy.102, s32[]{:T(128)S(6)} %select_n.222, s32[]{:T(128)} %constant.244.clone.1, s32[]{:T(128)} %constant.244.clone.1, s32[]{:T(128)} %constant.244.clone.1) | dynamic-update-slice | bytes 68100 | tf_op jit(solution)/shard_map/jit(dynamic_update_index_in_dim)/dynamic_update_slice | solution.py:99
  163.1 3.0 %dynamic_update_slice.109 = bf16[16,2,14,608]{3,0,2,1:T(8,128)(2,1)S(1)} dynamic-update-slice(bf16[16,2,14,608]{3,0,2,1:T(8,128)(2,1)S(1)} %dynamic_update_slice.108, bf16[1,2,14,608]{3,0,2,1:T(2,128)(2,1)} %copy.103, s32[]{:T(128)S(6)} %select_n.224, s32[]{:T(128)} %constant.244.clone.1, s32[]{:T(128)} %constant.244.clone.1, s32[]{:T(128)} %constant.244.clone.1) | dynamic-update-slice | bytes 68100 | tf_op jit(solution)/shard_map/jit(dynamic_update_index_in_dim)/dynamic_update_slice | solution.py:99
  166.1 3.0 %dynamic_update_slice.110 = bf16[16,2,14,608]{3,0,2,1:T(8,128)(2,1)S(1)} dynamic-update-slice(bf16[16,2,14,608]{3,0,2,1:T(8,128)(2,1)S(1)} %dynamic_update_slice.109, bf16[1,2,14,608]{3,0,2,1:T(2,128)(2,1)} %copy.104, s32[]{:T(128)S(6)} %select_n.226, s32[]{:T(128)} %constant.244.clone.1, s32[]{:T(128)} %constant.244.clone.1, s32[]{:T(128)} %constant.244.clone.1) | dynamic-update-slice | bytes 68100 | tf_op jit(solution)/shard_map/jit(dynamic_update_index_in_dim)/dynamic_update_slice | solution.py:99
  169.2 3.0 %dynamic_update_slice.111 = bf16[16,2,14,608]{3,0,2,1:T(8,128)(2,1)S(1)} dynamic-update-slice(bf16[16,2,14,608]{3,0,2,1:T(8,128)(2,1)S(1)} %dynamic_update_slice.110, bf16[1,2,14,608]{3,0,2,1:T(2,128)(2,1)} %copy.105, s32[]{:T(128)S(6)} %select_n.228, s32[]{:T(128)} %constant.244.clone.1, s32[]{:T(128)} %constant.244.clone.1, s32[]{:T(128)} %constant.244.clone.1) | dynamic-update-slice | bytes 68100 | tf_op jit(solution)/shard_map/jit(dynamic_update_index_in_dim)/dynamic_update_slice | solution.py:99
  172.2 3.6 %collective-permute-start.9 = (bf16[16,2,14,608]{3,0,2,1:T(8,128)(2,1)S(1)}, bf16[16,2,14,608]{3,0,2,1:T(8,128)(2,1)S(1)}, u32[]{:S(2)}, u32[]{:S(2)}) collective-permute-start(bf16[16,2,14,608]{3,0,2,1:T(8,128)(2,1)S(1)} %dynamic_update_slice.111), channel_id=1, source_target_pairs={{0,8},{1,25},{2,10},{3,27},{4,12},{5,29},{6,14},{7,31},{8,16},{9,1... | collective-permute-start | bytes 1634312 | tf_op jit(solution)/shard_map/ppermute | solution.py:105
  175.9 3.6 %collective-permute-start.10 = (bf16[16,2,14,608]{3,0,2,1:T(8,128)(2,1)S(1)}, bf16[16,2,14,608]{3,0,2,1:T(8,128)(2,1)S(1)}, u32[]{:S(2)}, u32[]{:S(2)}) collective-permute-start(bf16[16,2,14,608]{3,0,2,1:T(8,128)(2,1)S(1)} %dynamic_update_slice.111), channel_id=1, source_target_pairs={{0,24},{1,9},{2,26},{3,11},{4,28},{5,13},{6,30},{7,15},{8,0},{9,17... | collective-permute-start | bytes 1634312 | tf_op jit(solution)/shard_map/ppermute | solution.py:105
  179.5 2.1 %multiply_subtract_fusion = (f32[150,896]{1,0:T(8,128)}, f32[150,896]{1,0:T(8,128)}) fusion(f32[150,896]{1,0:T(8,128)S(1)} %copy-done, f32[150,896]{1,0:T(8,128)S(1)} %copy-done.1, f32[150,896]{1,0:T(8,128)S(1)} %fusion.7, f32[150,896]{1,0:T(8,128)S(1)} %fusion.6, f32[150,896]{1,0:T(8,128)S(1)} %fusion.5, bf16[150,64]{1,0:T(8,128)(2,1)} %squeeze.36, ...), kind=kOutput, calls=%fused_computation.18 | convolution fusion | flops 18816000 | bytes 3897088 | tf_op jit(solution)/shard_map/dot_general | solution.py:114
  181.6 0.7 copy.110
  182.3 0.7 copy.111
  182.9 3.9 %collective-permute-start.11 = (bf16[16,2,14,608]{3,0,2,1:T(8,128)(2,1)S(1)}, bf16[16,2,14,608]{3,0,2,1:T(8,128)(2,1)S(1)}, u32[]{:S(2)}, u32[]{:S(2)}) collective-permute-start(bf16[16,2,14,608]{3,0,2,1:T(8,128)(2,1)S(1)} %dynamic_update_slice.111), channel_id=1, source_target_pairs={{0,16},{1,17},{2,18},{3,19},{4,20},{5,21},{6,22},{7,23},{8,24},{9,... | collective-permute-start | bytes 1634312 | tf_op jit(solution)/shard_map/ppermute | solution.py:105
  186.8 1.2 broadcast_in_dim.72
  188.5 12.1 %collective-permute-done.9 = bf16[16,2,14,608]{3,0,2,1:T(8,128)(2,1)S(1)} collective-permute-done((bf16[16,2,14,608]{3,0,2,1:T(8,128)(2,1)S(1)}, bf16[16,2,14,608]{3,0,2,1:T(8,128)(2,1)S(1)}, u32[]{:S(2)}, u32[]{:S(2)}) %collective-permute-start.9) | collective-permute-done | bytes 544800 | tf_op jit(solution)/shard_map/ppermute | solution.py:105
  202.2 5.7 %copy.112 = bf16[2,896,608]{1,2,0:T(8,128)(2,1)} copy(bf16[2,896,608]{2,0,1:T(2,128)(2,1)S(1)} %bitcast.38) | data formatting | bytes 4358144
  (66 shorter events, 6.5 us)
Async XLA Ops:
  7.7 53.7 %all-to-all-start = ((bf16[4,2,41984]{2,1,0:T(2,128)(2,1)}), bf16[4,2,41984]{2,1,0:T(2,128)(2,1)S(1)}, u32[]{:S(2)}, u32[]{:S(2)}) async-start(bf16[4,2,41984]{2,1,0:T(2,128)(2,1)} %reshape.51), calls=%async_computation | async-start | bytes 1343488 | tf_op jit(solution)/shard_map/all_to_all | solution.py:38
  22.8 40.0 %copy-start.9 = (f32[2,14,608]{2,0,1:T(2,128)S(1)}, f32[2,14,608]{2,0,1:T(2,128)}, u32[]{:S(2)}) copy-start(f32[2,14,608]{2,0,1:T(2,128)} %param.11) | copy-start | bytes 204292
  22.8 40.0 %copy-start.10 = (f32[2,14,608]{2,0,1:T(2,128)S(1)}, f32[2,14,608]{2,0,1:T(2,128)}, u32[]{:S(2)}) copy-start(f32[2,14,608]{2,0,1:T(2,128)} %param.10) | copy-start | bytes 204292
  63.4 15.0 %collective-permute-start = (bf16[2,14,608]{2,1,0:T(8,128)(2,1)S(1)}, bf16[2,14,608]{2,1,0:T(8,128)(2,1)S(1)}, u32[]{:S(2)}, u32[]{:S(2)}) collective-permute-start(bf16[2,14,608]{2,1,0:T(8,128)(2,1)S(1)} %get-tuple-element.30), channel_id=1, source_target_pairs={{0,64},{1,449},{2,66},{3,451},{4,68},{5,453},{6,70},{7,455},{8,72}... | collective-permute-start | bytes 102152 | tf_op jit(solution)/shard_map/ppermute | solution.py:81
  65.3 15.0 %collective-permute-start.1 = (bf16[2,14,608]{2,1,0:T(8,128)(2,1)S(1)}, bf16[2,14,608]{2,1,0:T(8,128)(2,1)S(1)}, u32[]{:S(2)}, u32[]{:S(2)}) collective-permute-start(bf16[2,14,608]{2,1,0:T(8,128)(2,1)S(1)} %get-tuple-element.30), channel_id=1, source_target_pairs={{0,448},{1,65},{2,450},{3,67},{4,452},{5,69},{6,454},{7,71},{8,456... | collective-permute-start | bytes 102152 | tf_op jit(solution)/shard_map/ppermute | solution.py:86
  78.4 8.3 %collective-permute-start.2 = (bf16[2,14,608]{2,1,0:T(8,128)(2,1)S(1)}, bf16[2,14,608]{2,1,0:T(8,128)(2,1)S(1)}, u32[]{:S(2)}, u32[]{:S(2)}) collective-permute-start(bf16[2,14,608]{2,1,0:T(8,128)(2,1)S(1)} %collective-permute-done), channel_id=1, source_target_pairs={{0,64},{1,449},{2,66},{3,451},{4,68},{5,453},{6,70},{7,455},{8,72}... | collective-permute-start | bytes 102152 | tf_op jit(solution)/shard_map/ppermute | solution.py:81
  80.4 25.3 %copy-start.3 = (bf16[2,14,608]{2,1,0:T(8,128)(2,1)}, bf16[2,14,608]{2,1,0:T(8,128)(2,1)S(1)}, u32[]{:S(2)}) copy-start(bf16[2,14,608]{2,1,0:T(8,128)(2,1)S(1)} %collective-permute-done.1) | copy-start | bytes 102148
  80.4 8.3 %collective-permute-start.3 = (bf16[2,14,608]{2,1,0:T(8,128)(2,1)S(1)}, bf16[2,14,608]{2,1,0:T(8,128)(2,1)S(1)}, u32[]{:S(2)}, u32[]{:S(2)}) collective-permute-start(bf16[2,14,608]{2,1,0:T(8,128)(2,1)S(1)} %collective-permute-done.1), channel_id=1, source_target_pairs={{0,448},{1,65},{2,450},{3,67},{4,452},{5,69},{6,454},{7,71},{8,456... | collective-permute-start | bytes 102152 | tf_op jit(solution)/shard_map/ppermute | solution.py:86
  86.7 19.0 %copy-start.4 = (bf16[2,14,608]{2,1,0:T(8,128)(2,1)}, bf16[2,14,608]{2,1,0:T(8,128)(2,1)S(1)}, u32[]{:S(2)}) copy-start(bf16[2,14,608]{2,1,0:T(8,128)(2,1)S(1)} %collective-permute-done.2) | copy-start | bytes 102148
  86.7 8.1 %collective-permute-start.4 = (bf16[2,14,608]{2,1,0:T(8,128)(2,1)S(1)}, bf16[2,14,608]{2,1,0:T(8,128)(2,1)S(1)}, u32[]{:S(2)}, u32[]{:S(2)}) collective-permute-start(bf16[2,14,608]{2,1,0:T(8,128)(2,1)S(1)} %collective-permute-done.2), channel_id=1, source_target_pairs={{0,64},{1,449},{2,66},{3,451},{4,68},{5,453},{6,70},{7,455},{8,72}... | collective-permute-start | bytes 102152 | tf_op jit(solution)/shard_map/ppermute | solution.py:81
  88.7 15.1 %copy-start.5 = (bf16[2,14,608]{2,1,0:T(8,128)(2,1)}, bf16[2,14,608]{2,1,0:T(8,128)(2,1)S(1)}, u32[]{:S(2)}) copy-start(bf16[2,14,608]{2,1,0:T(8,128)(2,1)S(1)} %collective-permute-done.3) | copy-start | bytes 102148
  88.7 8.1 %collective-permute-start.5 = (bf16[2,14,608]{2,1,0:T(8,128)(2,1)S(1)}, bf16[2,14,608]{2,1,0:T(8,128)(2,1)S(1)}, u32[]{:S(2)}, u32[]{:S(2)}) collective-permute-start(bf16[2,14,608]{2,1,0:T(8,128)(2,1)S(1)} %collective-permute-done.3), channel_id=1, source_target_pairs={{0,448},{1,65},{2,450},{3,67},{4,452},{5,69},{6,454},{7,71},{8,456... | collective-permute-start | bytes 102152 | tf_op jit(solution)/shard_map/ppermute | solution.py:86
  94.8 8.9 %copy-start.6 = (bf16[2,14,608]{2,1,0:T(8,128)(2,1)}, bf16[2,14,608]{2,1,0:T(8,128)(2,1)S(1)}, u32[]{:S(2)}) copy-start(bf16[2,14,608]{2,1,0:T(8,128)(2,1)S(1)} %collective-permute-done.4) | copy-start | bytes 102148
  94.9 8.1 %collective-permute-start.6 = (bf16[2,14,608]{2,1,0:T(8,128)(2,1)S(1)}, bf16[2,14,608]{2,1,0:T(8,128)(2,1)S(1)}, u32[]{:S(2)}, u32[]{:S(2)}) collective-permute-start(bf16[2,14,608]{2,1,0:T(8,128)(2,1)S(1)} %collective-permute-done.4), channel_id=1, source_target_pairs={{0,64},{1,449},{2,66},{3,451},{4,68},{5,453},{6,70},{7,455},{8,72}... | collective-permute-start | bytes 102152 | tf_op jit(solution)/shard_map/ppermute | solution.py:81
  96.8 7.0 %copy-start.7 = (bf16[2,14,608]{2,1,0:T(8,128)(2,1)}, bf16[2,14,608]{2,1,0:T(8,128)(2,1)S(1)}, u32[]{:S(2)}) copy-start(bf16[2,14,608]{2,1,0:T(8,128)(2,1)S(1)} %collective-permute-done.5) | copy-start | bytes 102148
  103.0 0.8 copy-start.8
  103.8 36.9 %collective-permute-start.7 = (bf16[4,2,14,608]{3,2,1,0:T(8,128)(2,1)}, bf16[4,2,14,608]{3,2,1,0:T(8,128)(2,1)}, u32[]{:S(2)}, u32[]{:S(2)}) collective-permute-start(bf16[4,2,14,608]{3,2,1,0:T(8,128)(2,1)} %get-tuple-element.33), channel_id=1, source_target_pairs={{0,480},{1,33},{2,482},{3,35},{4,484},{5,37},{6,486},{7,39},{8,488... | collective-permute-start | bytes 408584 | tf_op jit(solution)/shard_map/ppermute | solution.py:95
  106.0 73.5 %copy-start = (f32[150,896]{1,0:T(8,128)S(1)}, f32[150,896]{1,0:T(8,128)}, u32[]{:S(2)}) copy-start(f32[150,896]{1,0:T(8,128)} %param.12) | copy-start | bytes 1612804
  106.0 73.5 %copy-start.1 = (f32[150,896]{1,0:T(8,128)S(1)}, f32[150,896]{1,0:T(8,128)}, u32[]{:S(2)}) copy-start(f32[150,896]{1,0:T(8,128)} %param.13) | copy-start | bytes 1612804
  133.6 10.7 %collective-permute-start.8 = (bf16[4,2,14,608]{3,2,1,0:T(8,128)(2,1)}, bf16[4,2,14,608]{3,2,1,0:T(8,128)(2,1)}, u32[]{:S(2)}, u32[]{:S(2)}) collective-permute-start(bf16[4,2,14,608]{3,2,1,0:T(8,128)(2,1)} %get-tuple-element.32), channel_id=1, source_target_pairs={{0,32},{1,481},{2,34},{3,483},{4,36},{5,485},{6,38},{7,487},{8,40}... | collective-permute-start | bytes 408584 | tf_op jit(solution)/shard_map/ppermute | solution.py:95
  172.2 9.4 %copy-start.2 = (f32[2,14,608]{2,1,0:T(8,128)S(1)}, f32[2,14,608]{2,1,0:T(8,128)}, u32[]{:S(2)}) copy-start(f32[2,14,608]{2,1,0:T(8,128)} %get-tuple-element.31) | copy-start | bytes 204292
  172.2 28.3 %collective-permute-start.9 = (bf16[16,2,14,608]{3,0,2,1:T(8,128)(2,1)S(1)}, bf16[16,2,14,608]{3,0,2,1:T(8,128)(2,1)S(1)}, u32[]{:S(2)}, u32[]{:S(2)}) collective-permute-start(bf16[16,2,14,608]{3,0,2,1:T(8,128)(2,1)S(1)} %dynamic_update_slice.111), channel_id=1, source_target_pairs={{0,8},{1,25},{2,10},{3,27},{4,12},{5,29},{6,14},{7,31},{8,16},{9,1... | collective-permute-start | bytes 1634312 | tf_op jit(solution)/shard_map/ppermute | solution.py:105
  175.9 25.2 %collective-permute-start.10 = (bf16[16,2,14,608]{3,0,2,1:T(8,128)(2,1)S(1)}, bf16[16,2,14,608]{3,0,2,1:T(8,128)(2,1)S(1)}, u32[]{:S(2)}, u32[]{:S(2)}) collective-permute-start(bf16[16,2,14,608]{3,0,2,1:T(8,128)(2,1)S(1)} %dynamic_update_slice.111), channel_id=1, source_target_pairs={{0,24},{1,9},{2,26},{3,11},{4,28},{5,13},{6,30},{7,15},{8,0},{9,17... | collective-permute-start | bytes 1634312 | tf_op jit(solution)/shard_map/ppermute | solution.py:105
  182.9 18.7 %collective-permute-start.11 = (bf16[16,2,14,608]{3,0,2,1:T(8,128)(2,1)S(1)}, bf16[16,2,14,608]{3,0,2,1:T(8,128)(2,1)S(1)}, u32[]{:S(2)}, u32[]{:S(2)}) collective-permute-start(bf16[16,2,14,608]{3,0,2,1:T(8,128)(2,1)S(1)} %dynamic_update_slice.111), channel_id=1, source_target_pairs={{0,16},{1,17},{2,18},{3,19},{4,20},{5,21},{6,22},{7,23},{8,24},{9,... | collective-permute-start | bytes 1634312 | tf_op jit(solution)/shard_map/ppermute | solution.py:105

commit v10 on v8

--- a/solution.py
+++ b/solution.py
@@ -98,7 +98,8 @@
         fwd = lax.ppermute(fwd, axes, zshift(2))
         j = -step * sgn
         out = lax.dynamic_update_index_in_dim(out, fwd, (zi + 2 * j) % nz, axis=0)
-        rel = lax.dynamic_update_index_in_dim(rel, fwd, j + reach, axis=0)
+        if step < reach:
+            rel = lax.dynamic_update_index_in_dim(rel, fwd, j + reach, axis=0)
         if step < half - reach:
             bwd = lax.ppermute(bwd, axes, zshift(-2))
             out = lax.dynamic_update_index_in_dim(out, bwd, (zi - 2 * j) % nz, axis=0)

time: 137 us -> 135 us (0.985)
  waiting for transfers between devices: 44.1 us -> 42.4 us
    ppermute x2, waiting for transfers between devices: 10.3 us -> 5.98 us  [on_device(): got = lax.ppermute(part, axes, zshift(k))]
    ppermute x3, waiting for transfers between devices: 2.14 us -> 5.74 us  [on_device(): bwd = lax.ppermute(bwd, axes, zshift(-2))]
    ppermute x4, starting transfers between devices: 20.2 us -> 18.5 us  [on_device(): fwd = lax.ppermute(fwd, axes, zshift(2))]
    ppermute x2, starting transfers between devices: 9.85 us -> 11.3 us  [on_device(): got = lax.ppermute(part, axes, zshift(k))]
  transfers between devices with their start and end apart: 13 -> 13, of which waited for: 9 -> 10; matrix products, arithmetic and copies ran while one was open for 8% -> 8% of each run, Pallas kernels for 0% -> 0%
where the time goes in v10:
time: 135 us; the launch traced here: 134 us
  starting transfers between devices  63.8 us (47%)
  waiting for transfers between devices  42.4 us (31%)
  local copies, waits for them, and re-layouts  23.2 us (17%)
  matrix products  1.97 us (1%)
  other arithmetic  1.46 us (1%)
    all_to_all x1, waiting for transfers between devices, on_device(): recv = lax.all_to_all(send, 'group', 0, 0, tiled=True)  19.1 us
    ppermute x4, starting transfers between devices, on_device(): fwd = lax.ppermute(fwd, axes, zshift(2))  18.5 us
    all_to_all x1, starting transfers between devices, on_device(): recv = lax.all_to_all(send, 'group', 0, 0, tiled=True)  15.1 us
    ppermute x2, starting transfers between devices, on_device(): got = lax.ppermute(part, axes, zshift(k))  11.3 us
    unnamed x19, local copies, waits for them, and re-layouts  11.1 us
    ppermute x3, starting transfers between devices, on_device(): got = lax.ppermute(payload, ('shard', 'tensor'), yshift(k))  10.9 us
    ppermute x3, starting transfers between devices, on_device(): bwd = lax.ppermute(bwd, axes, zshift(-2))  8.02 us
    ppermute x4, waiting for transfers between devices, on_device(): fwd = lax.ppermute(fwd, axes, zshift(2))  6 us
  transfers between devices with their start and end apart: 13, of which 10 were waited for; matrix products, arithmetic and copies ran while one was open for 8% of the time, Pallas kernels for 0%

profile of v10, /device:TPU:6, one launch (start us, length us, event | category | flops | bytes accessed | tf_op | source)
XLA Modules:
  0.0 134.0 jit_solution(15608127580286402147)
XLA Ops:
  0.7 0.9 copy-done
  1.6 0.9 copy.44
  2.5 0.3 reshape.46
  2.8 1.1 copy.45
  3.9 0.1 reshape_squeeze.15
  4.1 0.2 maximum_bitcast_fusion
  4.2 0.5 broadcast.57
  4.7 1.1 reduce.20
  5.8 1.1 reshape.62
  6.9 15.1 %all-to-all-start = ((bf16[4,2,20480]{2,1,0:T(2,128)(2,1)}), bf16[4,2,20480]{2,1,0:T(2,128)(2,1)S(1)}, u32[]{:S(2)}, u32[]{:S(2)}) async-start(bf16[4,2,20480]{2,1,0:T(2,128)(2,1)} %reshape.62), calls=%async_computation | async-start | bytes 655360 | tf_op jit(solution)/shard_map/all_to_all | solution.py:40
  22.0 19.1 %all-to-all-done = bf16[4,2,20480]{2,1,0:T(2,128)(2,1)S(1)} async-done(((bf16[4,2,20480]{2,1,0:T(2,128)(2,1)}), bf16[4,2,20480]{2,1,0:T(2,128)(2,1)S(1)}, u32[]{:S(2)}, u32[]{:S(2)}) %all-to-all-start) | async-done | bytes 327712 | tf_op jit(solution)/shard_map/all_to_all | solution.py:40
  41.1 0.3 reshape.63
  41.4 0.4 copy.73
  41.8 0.2 convert_reduce_fusion
  42.3 0.2 reshape.47
  42.5 0.2 copy.57
  42.7 0.3 constant_dynamic-update-slice_fusion.4
  43.0 3.5 %collective-permute-start = (bf16[1,74368]{1,0:T(2,128)(2,1)S(1)}, bf16[1,74368]{1,0:T(2,128)(2,1)S(1)}, u32[]{:S(2)}, u32[]{:S(2)}) collective-permute-start(bf16[1,74368]{1,0:T(2,128)(2,1)S(1)} %constant_dynamic-update-slice_fusion.4), channel_id=1, source_target_pairs={{0,8},{1,25},{2,10},{3,27},{4,12},{5,29},{6,14},{7,31},{8,16},{9,1... | collective-permute-start | bytes 446216 | tf_op jit(solution)/shard_map/ppermute | solution.py:68
  46.5 3.6 %collective-permute-start.1 = (bf16[1,74368]{1,0:T(2,128)(2,1)S(1)}, bf16[1,74368]{1,0:T(2,128)(2,1)S(1)}, u32[]{:S(2)}, u32[]{:S(2)}) collective-permute-start(bf16[1,74368]{1,0:T(2,128)(2,1)S(1)} %constant_dynamic-update-slice_fusion.4), channel_id=1, source_target_pairs={{0,24},{1,9},{2,26},{3,11},{4,28},{5,13},{6,30},{7,15},{8,0},{9,17... | collective-permute-start | bytes 446216 | tf_op jit(solution)/shard_map/ppermute | solution.py:68
  50.1 3.9 %collective-permute-start.2 = (bf16[1,74368]{1,0:T(2,128)(2,1)S(1)}, bf16[1,74368]{1,0:T(2,128)(2,1)S(1)}, u32[]{:S(2)}, u32[]{:S(2)}) collective-permute-start(bf16[1,74368]{1,0:T(2,128)(2,1)S(1)} %constant_dynamic-update-slice_fusion.4), channel_id=1, source_target_pairs={{0,16},{1,17},{2,18},{3,19},{4,20},{5,21},{6,22},{7,23},{8,24},{9,... | collective-permute-start | bytes 446216 | tf_op jit(solution)/shard_map/ppermute | solution.py:68
  54.2 0.4 slice_reduce_fusion.9
  54.9 0.7 copy.53
  55.6 0.7 copy.54
  56.3 0.2 slice_reduce_fusion.5
  56.6 0.4 collective-permute-done.1
  57.0 0.2 slice_reduce_fusion.4
  57.3 5.2 %collective-permute-done.2 = bf16[1,74368]{1,0:T(2,128)(2,1)S(1)} collective-permute-done((bf16[1,74368]{1,0:T(2,128)(2,1)S(1)}, bf16[1,74368]{1,0:T(2,128)(2,1)S(1)}, u32[]{:S(2)}, u32[]{:S(2)}) %collective-permute-start.2) | collective-permute-done | bytes 148768 | tf_op jit(solution)/shard_map/ppermute | solution.py:68
  62.5 0.2 slice_reduce_fusion.3
  62.9 8.6 %collective-permute-start.3 = (bf16[4,2,14,608]{3,1,2,0:T(2,128)(2,1)S(1)}, bf16[4,2,14,608]{3,1,2,0:T(2,128)(2,1)S(1)}, u32[]{:S(2)}, u32[]{:S(2)}) collective-permute-start(bf16[4,2,14,608]{3,1,2,0:T(2,128)(2,1)S(1)} %copy_dynamic-update-slice_fusion), channel_id=1, source_target_pairs={{0,64},{1,449},{2,66},{3,451},{4,68},{5,453},{6,70},{7,455},{8,72}... | collective-permute-start | bytes 408584 | tf_op jit(solution)/shard_map/ppermute | solution.py:98
  71.5 1.9 %collective-permute-start.4 = (bf16[4,2,14,608]{3,1,2,0:T(2,128)(2,1)S(1)}, bf16[4,2,14,608]{3,1,2,0:T(2,128)(2,1)S(1)}, u32[]{:S(2)}, u32[]{:S(2)}) collective-permute-start(bf16[4,2,14,608]{3,1,2,0:T(2,128)(2,1)S(1)} %copy_dynamic-update-slice_fusion), channel_id=1, source_target_pairs={{0,448},{1,65},{2,450},{3,67},{4,452},{5,69},{6,454},{7,71},{8,456... | collective-permute-start | bytes 408584 | tf_op jit(solution)/shard_map/ppermute | solution.py:104
  73.5 0.7 slice_reduce_fusion.2
  74.1 0.1 reshape_squeeze.16
  74.3 0.7 slice_reduce_fusion.1
  74.9 0.1 reshape_squeeze.17
  75.1 0.7 slice_reduce_fusion
  75.7 0.1 reshape_squeeze.18
  76.0 0.2 fusion.5
  76.2 0.2 fusion.6
  76.4 0.2 fusion.7
  76.6 0.7 dynamic_update_slice.109
  77.3 1.2 broadcast_in_dim.74
  78.7 4.8 %collective-permute-start.5 = (bf16[4,2,14,608]{3,1,2,0:T(2,128)(2,1)S(1)}, bf16[4,2,14,608]{3,1,2,0:T(2,128)(2,1)S(1)}, u32[]{:S(2)}, u32[]{:S(2)}) collective-permute-start(bf16[4,2,14,608]{3,1,2,0:T(2,128)(2,1)S(1)} %collective-permute-done.3), channel_id=1, source_target_pairs={{0,64},{1,449},{2,66},{3,451},{4,68},{5,453},{6,70},{7,455},{8,72}... | collective-permute-start | bytes 408584 | tf_op jit(solution)/shard_map/ppermute | solution.py:98
  83.5 3.1 %collective-permute-start.6 = (bf16[4,2,14,608]{3,1,2,0:T(2,128)(2,1)S(1)}, bf16[4,2,14,608]{3,1,2,0:T(2,128)(2,1)S(1)}, u32[]{:S(2)}, u32[]{:S(2)}) collective-permute-start(bf16[4,2,14,608]{3,1,2,0:T(2,128)(2,1)S(1)} %collective-permute-done.4), channel_id=1, source_target_pairs={{0,448},{1,65},{2,450},{3,67},{4,452},{5,69},{6,454},{7,71},{8,456... | collective-permute-start | bytes 408584 | tf_op jit(solution)/shard_map/ppermute | solution.py:104
  86.6 0.2 bitcast_dynamic-update-slice_fusion.11
  86.9 0.2 bitcast_dynamic-update-slice_fusion.9
  87.1 1.2 collective-permute-done.5
  88.3 3.2 %collective-permute-start.7 = (bf16[4,2,14,608]{3,1,2,0:T(2,128)(2,1)S(1)}, bf16[4,2,14,608]{3,1,2,0:T(2,128)(2,1)S(1)}, u32[]{:S(2)}, u32[]{:S(2)}) collective-permute-start(bf16[4,2,14,608]{3,1,2,0:T(2,128)(2,1)S(1)} %collective-permute-done.5), channel_id=1, source_target_pairs={{0,64},{1,449},{2,66},{3,451},{4,68},{5,453},{6,70},{7,455},{8,72}... | collective-permute-start | bytes 408584 | tf_op jit(solution)/shard_map/ppermute | solution.py:98
  91.5 2.0 %collective-permute-done.6 = bf16[4,2,14,608]{3,1,2,0:T(2,128)(2,1)S(1)} collective-permute-done((bf16[4,2,14,608]{3,1,2,0:T(2,128)(2,1)S(1)}, bf16[4,2,14,608]{3,1,2,0:T(2,128)(2,1)S(1)}, u32[]{:S(2)}, u32[]{:S(2)}) %collective-permute-start.6) | collective-permute-done | bytes 136224 | tf_op jit(solution)/shard_map/ppermute | solution.py:104
  93.4 3.0 %collective-permute-start.8 = (bf16[4,2,14,608]{3,1,2,0:T(2,128)(2,1)S(1)}, bf16[4,2,14,608]{3,1,2,0:T(2,128)(2,1)S(1)}, u32[]{:S(2)}, u32[]{:S(2)}) collective-permute-start(bf16[4,2,14,608]{3,1,2,0:T(2,128)(2,1)S(1)} %collective-permute-done.6), channel_id=1, source_target_pairs={{0,448},{1,65},{2,450},{3,67},{4,452},{5,69},{6,454},{7,71},{8,456... | collective-permute-start | bytes 408584 | tf_op jit(solution)/shard_map/ppermute | solution.py:104
  96.4 0.2 bitcast_dynamic-update-slice_fusion.7
  96.6 0.2 bitcast_dynamic-update-slice_fusion.5
  96.8 0.5 collective-permute-done.7
  97.4 0.2 bitcast_dynamic-update-slice_fusion.3
  97.5 3.8 %collective-permute-done.8 = bf16[4,2,14,608]{3,1,2,0:T(2,128)(2,1)S(1)} collective-permute-done((bf16[4,2,14,608]{3,1,2,0:T(2,128)(2,1)S(1)}, bf16[4,2,14,608]{3,1,2,0:T(2,128)(2,1)S(1)}, u32[]{:S(2)}, u32[]{:S(2)}) %collective-permute-start.8) | collective-permute-done | bytes 136224 | tf_op jit(solution)/shard_map/ppermute | solution.py:104
  101.3 0.2 bitcast_dynamic-update-slice_fusion.1
  101.5 0.8 constant_dynamic-slice_fusion
  102.3 9.3 %collective-permute-start.10 = (bf16[4,4,2,14,608]{4,2,3,1,0:T(2,128)(2,1)S(1)}, bf16[4,4,2,14,608]{4,2,3,1,0:T(2,128)(2,1)S(1)}, u32[]{:S(2)}, u32[]{:S(2)}) collective-permute-start(bf16[4,4,2,14,608]{4,2,3,1,0:T(2,128)(2,1)S(1)} %get-tuple-element.29), channel_id=1, source_target_pairs={{0,480},{1,33},{2,482},{3,35},{4,484},{5,37},{6,486},{7,39},{8,488... | collective-permute-start | bytes 1634312 | tf_op jit(solution)/shard_map/ppermute | solution.py:113
  111.7 1.9 %collective-permute-start.9 = (bf16[4,2,14,608]{3,1,2,0:T(2,128)(2,1)S(1)}, bf16[4,2,14,608]{3,1,2,0:T(2,128)(2,1)S(1)}, u32[]{:S(2)}, u32[]{:S(2)}) collective-permute-start(bf16[4,2,14,608]{3,1,2,0:T(2,128)(2,1)S(1)} %collective-permute-done.7), channel_id=1, source_target_pairs={{0,64},{1,449},{2,66},{3,451},{4,68},{5,453},{6,70},{7,455},{8,72}... | collective-permute-start | bytes 408584 | tf_op jit(solution)/shard_map/ppermute | solution.py:98
  113.6 1.4 %multiply_subtract_fusion = (f32[150,896]{1,0:T(8,128)}, f32[150,896]{1,0:T(8,128)}) fusion(f32[150,896]{1,0:T(8,128)S(1)} %copy-done.1, f32[150,896]{1,0:T(8,128)S(1)} %copy-done.2, f32[150,896]{1,0:T(8,128)S(1)} %fusion.7, f32[150,896]{1,0:T(8,128)S(1)} %fusion.6, f32[150,896]{1,0:T(8,128)S(1)} %fusion.5, bf16[150,64]{1,0:T(8,128)(2,1)S(1)} %squeeze.37, ...), kind=kOutput, calls=%fused_computation.12 | convolution fusion | flops 18816000 | bytes 3952640 | tf_op jit(solution)/shard_map/dot_general | solution.py:123
  115.0 1.9 %collective-permute-start.11 = (bf16[4,4,2,14,608]{4,2,3,1,0:T(2,128)(2,1)S(1)}, bf16[4,4,2,14,608]{4,2,3,1,0:T(2,128)(2,1)S(1)}, u32[]{:S(2)}, u32[]{:S(2)}) collective-permute-start(bf16[4,4,2,14,608]{4,2,3,1,0:T(2,128)(2,1)S(1)} %get-tuple-element.28), channel_id=1, source_target_pairs={{0,32},{1,481},{2,34},{3,483},{4,36},{5,485},{6,38},{7,487},{8,40}... | collective-permute-start | bytes 1634312 | tf_op jit(solution)/shard_map/ppermute | solution.py:113
  116.9 4.3 %collective-permute-done.9 = bf16[4,2,14,608]{3,1,2,0:T(2,128)(2,1)S(1)} collective-permute-done((bf16[4,2,14,608]{3,1,2,0:T(2,128)(2,1)S(1)}, bf16[4,2,14,608]{3,1,2,0:T(2,128)(2,1)S(1)}, u32[]{:S(2)}, u32[]{:S(2)}) %collective-permute-start.9) | collective-permute-done | bytes 136224 | tf_op jit(solution)/shard_map/ppermute | solution.py:98
  121.3 4.0 %collective-permute-done.10 = bf16[4,4,2,14,608]{4,2,3,1,0:T(2,128)(2,1)S(1)} collective-permute-done((bf16[4,4,2,14,608]{4,2,3,1,0:T(2,128)(2,1)S(1)}, bf16[4,4,2,14,608]{4,2,3,1,0:T(2,128)(2,1)S(1)}, u32[]{:S(2)}, u32[]{:S(2)}) %collective-permute-start.10) | collective-permute-done | bytes 544800 | tf_op jit(solution)/shard_map/ppermute | solution.py:113
  125.8 1.9 %collective-permute-done.11 = bf16[4,4,2,14,608]{4,2,3,1,0:T(2,128)(2,1)S(1)} collective-permute-done((bf16[4,4,2,14,608]{4,2,3,1,0:T(2,128)(2,1)S(1)}, bf16[4,4,2,14,608]{4,2,3,1,0:T(2,128)(2,1)S(1)}, u32[]{:S(2)}, u32[]{:S(2)}) %collective-permute-start.11) | collective-permute-done | bytes 544800 | tf_op jit(solution)/shard_map/ppermute | solution.py:113
  128.3 5.7 %copy.55 = bf16[2,896,608]{1,2,0:T(8,128)(2,1)} copy(bf16[2,896,608]{2,0,1:T(2,128)(2,1)S(1)} %bitcast.59) | data formatting | bytes 4358144
  (47 shorter events, 2.7 us)
Async XLA Ops:
  0.6 0.9 copy-start
  5.8 36.4 %copy-start.3 = (f32[2,14,608]{2,0,1:T(2,128)S(1)}, f32[2,14,608]{2,0,1:T(2,128)}, u32[]{:S(2)}) copy-start(f32[2,14,608]{2,0,1:T(2,128)} %param.11) | copy-start | bytes 204292
  5.8 36.4 %copy-start.4 = (f32[2,14,608]{2,0,1:T(2,128)S(1)}, f32[2,14,608]{2,0,1:T(2,128)}, u32[]{:S(2)}) copy-start(f32[2,14,608]{2,0,1:T(2,128)} %param.10) | copy-start | bytes 204292
  6.9 34.2 %all-to-all-start = ((bf16[4,2,20480]{2,1,0:T(2,128)(2,1)}), bf16[4,2,20480]{2,1,0:T(2,128)(2,1)S(1)}, u32[]{:S(2)}, u32[]{:S(2)}) async-start(bf16[4,2,20480]{2,1,0:T(2,128)(2,1)} %reshape.62), calls=%async_computation | async-start | bytes 655360 | tf_op jit(solution)/shard_map/all_to_all | solution.py:40
  43.0 13.3 %collective-permute-start = (bf16[1,74368]{1,0:T(2,128)(2,1)S(1)}, bf16[1,74368]{1,0:T(2,128)(2,1)S(1)}, u32[]{:S(2)}, u32[]{:S(2)}) collective-permute-start(bf16[1,74368]{1,0:T(2,128)(2,1)S(1)} %constant_dynamic-update-slice_fusion.4), channel_id=1, source_target_pairs={{0,8},{1,25},{2,10},{3,27},{4,12},{5,29},{6,14},{7,31},{8,16},{9,1... | collective-permute-start | bytes 446216 | tf_op jit(solution)/shard_map/ppermute | solution.py:68
  46.5 10.5 %collective-permute-start.1 = (bf16[1,74368]{1,0:T(2,128)(2,1)S(1)}, bf16[1,74368]{1,0:T(2,128)(2,1)S(1)}, u32[]{:S(2)}, u32[]{:S(2)}) collective-permute-start(bf16[1,74368]{1,0:T(2,128)(2,1)S(1)} %constant_dynamic-update-slice_fusion.4), channel_id=1, source_target_pairs={{0,24},{1,9},{2,26},{3,11},{4,28},{5,13},{6,30},{7,15},{8,0},{9,17... | collective-permute-start | bytes 446216 | tf_op jit(solution)/shard_map/ppermute | solution.py:68
  50.1 12.4 %collective-permute-start.2 = (bf16[1,74368]{1,0:T(2,128)(2,1)S(1)}, bf16[1,74368]{1,0:T(2,128)(2,1)S(1)}, u32[]{:S(2)}, u32[]{:S(2)}) collective-permute-start(bf16[1,74368]{1,0:T(2,128)(2,1)S(1)} %constant_dynamic-update-slice_fusion.4), channel_id=1, source_target_pairs={{0,16},{1,17},{2,18},{3,19},{4,20},{5,21},{6,22},{7,23},{8,24},{9,... | collective-permute-start | bytes 446216 | tf_op jit(solution)/shard_map/ppermute | solution.py:68
  62.9 15.7 %collective-permute-start.3 = (bf16[4,2,14,608]{3,1,2,0:T(2,128)(2,1)S(1)}, bf16[4,2,14,608]{3,1,2,0:T(2,128)(2,1)S(1)}, u32[]{:S(2)}, u32[]{:S(2)}) collective-permute-start(bf16[4,2,14,608]{3,1,2,0:T(2,128)(2,1)S(1)} %copy_dynamic-update-slice_fusion), channel_id=1, source_target_pairs={{0,64},{1,449},{2,66},{3,451},{4,68},{5,453},{6,70},{7,455},{8,72}... | collective-permute-start | bytes 408584 | tf_op jit(solution)/shard_map/ppermute | solution.py:98
  71.5 11.9 %collective-permute-start.4 = (bf16[4,2,14,608]{3,1,2,0:T(2,128)(2,1)S(1)}, bf16[4,2,14,608]{3,1,2,0:T(2,128)(2,1)S(1)}, u32[]{:S(2)}, u32[]{:S(2)}) collective-permute-start(bf16[4,2,14,608]{3,1,2,0:T(2,128)(2,1)S(1)} %copy_dynamic-update-slice_fusion), channel_id=1, source_target_pairs={{0,448},{1,65},{2,450},{3,67},{4,452},{5,69},{6,454},{7,71},{8,456... | collective-permute-start | bytes 408584 | tf_op jit(solution)/shard_map/ppermute | solution.py:104
  78.7 9.6 %collective-permute-start.5 = (bf16[4,2,14,608]{3,1,2,0:T(2,128)(2,1)S(1)}, bf16[4,2,14,608]{3,1,2,0:T(2,128)(2,1)S(1)}, u32[]{:S(2)}, u32[]{:S(2)}) collective-permute-start(bf16[4,2,14,608]{3,1,2,0:T(2,128)(2,1)S(1)} %collective-permute-done.3), channel_id=1, source_target_pairs={{0,64},{1,449},{2,66},{3,451},{4,68},{5,453},{6,70},{7,455},{8,72}... | collective-permute-start | bytes 408584 | tf_op jit(solution)/shard_map/ppermute | solution.py:98
  83.5 9.9 %collective-permute-start.6 = (bf16[4,2,14,608]{3,1,2,0:T(2,128)(2,1)S(1)}, bf16[4,2,14,608]{3,1,2,0:T(2,128)(2,1)S(1)}, u32[]{:S(2)}, u32[]{:S(2)}) collective-permute-start(bf16[4,2,14,608]{3,1,2,0:T(2,128)(2,1)S(1)} %collective-permute-done.4), channel_id=1, source_target_pairs={{0,448},{1,65},{2,450},{3,67},{4,452},{5,69},{6,454},{7,71},{8,456... | collective-permute-start | bytes 408584 | tf_op jit(solution)/shard_map/ppermute | solution.py:104
  86.8 26.8 %copy-start.1 = (f32[150,896]{1,0:T(8,128)S(1)}, f32[150,896]{1,0:T(8,128)}, u32[]{:S(2)}) copy-start(f32[150,896]{1,0:T(8,128)} %param.12) | copy-start | bytes 1612804
  86.8 26.8 %copy-start.2 = (f32[150,896]{1,0:T(8,128)S(1)}, f32[150,896]{1,0:T(8,128)}, u32[]{:S(2)}) copy-start(f32[150,896]{1,0:T(8,128)} %param.13) | copy-start | bytes 1612804
  88.3 9.1 %collective-permute-start.7 = (bf16[4,2,14,608]{3,1,2,0:T(2,128)(2,1)S(1)}, bf16[4,2,14,608]{3,1,2,0:T(2,128)(2,1)S(1)}, u32[]{:S(2)}, u32[]{:S(2)}) collective-permute-start(bf16[4,2,14,608]{3,1,2,0:T(2,128)(2,1)S(1)} %collective-permute-done.5), channel_id=1, source_target_pairs={{0,64},{1,449},{2,66},{3,451},{4,68},{5,453},{6,70},{7,455},{8,72}... | collective-permute-start | bytes 408584 | tf_op jit(solution)/shard_map/ppermute | solution.py:98
  93.4 7.9 %collective-permute-start.8 = (bf16[4,2,14,608]{3,1,2,0:T(2,128)(2,1)S(1)}, bf16[4,2,14,608]{3,1,2,0:T(2,128)(2,1)S(1)}, u32[]{:S(2)}, u32[]{:S(2)}) collective-permute-start(bf16[4,2,14,608]{3,1,2,0:T(2,128)(2,1)S(1)} %collective-permute-done.6), channel_id=1, source_target_pairs={{0,448},{1,65},{2,450},{3,67},{4,452},{5,69},{6,454},{7,71},{8,456... | collective-permute-start | bytes 408584 | tf_op jit(solution)/shard_map/ppermute | solution.py:104
  102.3 23.0 %collective-permute-start.10 = (bf16[4,4,2,14,608]{4,2,3,1,0:T(2,128)(2,1)S(1)}, bf16[4,4,2,14,608]{4,2,3,1,0:T(2,128)(2,1)S(1)}, u32[]{:S(2)}, u32[]{:S(2)}) collective-permute-start(bf16[4,4,2,14,608]{4,2,3,1,0:T(2,128)(2,1)S(1)} %get-tuple-element.29), channel_id=1, source_target_pairs={{0,480},{1,33},{2,482},{3,35},{4,484},{5,37},{6,486},{7,39},{8,488... | collective-permute-start | bytes 1634312 | tf_op jit(solution)/shard_map/ppermute | solution.py:113
  111.7 9.5 %collective-permute-start.9 = (bf16[4,2,14,608]{3,1,2,0:T(2,128)(2,1)S(1)}, bf16[4,2,14,608]{3,1,2,0:T(2,128)(2,1)S(1)}, u32[]{:S(2)}, u32[]{:S(2)}) collective-permute-start(bf16[4,2,14,608]{3,1,2,0:T(2,128)(2,1)S(1)} %collective-permute-done.7), channel_id=1, source_target_pairs={{0,64},{1,449},{2,66},{3,451},{4,68},{5,453},{6,70},{7,455},{8,72}... | collective-permute-start | bytes 408584 | tf_op jit(solution)/shard_map/ppermute | solution.py:98
  115.0 12.8 %collective-permute-start.11 = (bf16[4,4,2,14,608]{4,2,3,1,0:T(2,128)(2,1)S(1)}, bf16[4,4,2,14,608]{4,2,3,1,0:T(2,128)(2,1)S(1)}, u32[]{:S(2)}, u32[]{:S(2)}) collective-permute-start(bf16[4,4,2,14,608]{4,2,3,1,0:T(2,128)(2,1)S(1)} %get-tuple-element.28), channel_id=1, source_target_pairs={{0,32},{1,481},{2,34},{3,483},{4,36},{5,485},{6,38},{7,487},{8,40}... | collective-permute-start | bytes 1634312 | tf_op jit(solution)/shard_map/ppermute | solution.py:113

commit v11 on v10

--- a/solution.py
+++ b/solution.py
@@ -45,14 +45,14 @@
     new_layer_weight = layer_weight - rate_outer * (layer_mean + beta_outer * new_layer_momentum)
     piece = new_layer_weight.astype(bf16)
 
-    sgn = 1 - 2 * (ti % 2)
+    sgn = 1
     n_st = shards * tensors
 
     def yshift(k):
         pairs = []
         for i in range(n_st):
             s, t = i // tensors, i % tensors
-            d = k if t % 2 == 0 else -k
+            d = k
             pairs.append((i, ((s - s % Y_SIZE) + (s % Y_SIZE + d) % Y_SIZE) * tensors + t))
         return pairs
 
@@ -81,7 +81,7 @@
         for i in range(n_all):
             gs, t = i // tensors, i % tensors
             z, y = gs // Y_SIZE, gs % Y_SIZE
-            d = k if t % 2 == 0 else -k
+            d = k
             pairs.append((i, (((z + d) % nz) * Y_SIZE + y) * tensors + t))
         return pairs
 

time: 135 us -> 136 us (level)
  waiting for transfers between devices: 42.4 us -> 45.3 us
    ppermute x2, waiting for transfers between devices: 5.98 us -> 9.31 us  [on_device(): got = lax.ppermute(part, axes, zshift(k))]
    ppermute x4, waiting for transfers between devices: 6 us -> 8.53 us  [on_device(): fwd = lax.ppermute(fwd, axes, zshift(2))]
    ppermute x3, waiting for transfers between devices: 5.55 us -> 3.53 us  [on_device(): got = lax.ppermute(payload, ('shard', 'tensor'), yshift(k))]
    ppermute x2, starting transfers between devices: 11.3 us -> 9.33 us  [on_device(): got = lax.ppermute(part, axes, zshift(k))]
    ppermute x3, starting transfers between devices: 8.02 us -> 9.64 us  [on_device(): bwd = lax.ppermute(bwd, axes, zshift(-2))]
  transfers between devices with their start and end apart: 13 -> 13, of which waited for: 10 -> 9; matrix products, arithmetic and copies ran while one was open for 8% -> 8% of each run, Pallas kernels for 0% -> 0%
where the time goes in v11:
time: 136 us
  starting transfers between devices  62.5 us (46%)
  waiting for transfers between devices  45.3 us (33%)
  local copies, waits for them, and re-layouts  23.1 us (17%)
  matrix products  1.99 us (1%)
  other arithmetic  1.46 us (1%)
    all_to_all x1, waiting for transfers between devices, on_device(): recv = lax.all_to_all(send, 'group', 0, 0, tiled=True)  19.1 us
    ppermute x4, starting transfers between devices, on_device(): fwd = lax.ppermute(fwd, axes, zshift(2))  17.5 us
    all_to_all x1, starting transfers between devices, on_device(): recv = lax.all_to_all(send, 'group', 0, 0, tiled=True)  15.1 us
    unnamed x19, local copies, waits for them, and re-layouts  11.1 us
    ppermute x3, starting transfers between devices, on_device(): got = lax.ppermute(payload, ('shard', 'tensor'), yshift(k))  10.9 us
    ppermute x3, starting transfers between devices, on_device(): bwd = lax.ppermute(bwd, axes, zshift(-2))  9.64 us
    ppermute x2, starting transfers between devices, on_device(): got = lax.ppermute(part, axes, zshift(k))  9.33 us
    ppermute x2, waiting for transfers between devices, on_device(): got = lax.ppermute(part, axes, zshift(k))  9.31 us
  transfers between devices with their start and end apart: 13, of which 9 were waited for; matrix products, arithmetic and copies ran while one was open for 8% of the time, Pallas kernels for 0%

profile of v11, /device:TPU:6, one launch (start us, length us, event | category | flops | bytes accessed | tf_op | source)
XLA Modules:
  0.0 135.7 jit_solution(9871250411184452606)
XLA Ops:
  0.7 0.9 copy-done
  1.6 0.9 copy.44
  2.5 0.3 reshape.46
  2.8 1.1 copy.45
  3.9 0.1 reshape_squeeze.15
  4.1 0.2 maximum_bitcast_fusion
  4.2 0.5 broadcast.54
  4.7 1.1 reduce.20
  5.8 1.1 reshape.62
  6.9 15.1 %all-to-all-start = ((bf16[4,2,20480]{2,1,0:T(2,128)(2,1)}), bf16[4,2,20480]{2,1,0:T(2,128)(2,1)S(1)}, u32[]{:S(2)}, u32[]{:S(2)}) async-start(bf16[4,2,20480]{2,1,0:T(2,128)(2,1)} %reshape.62), calls=%async_computation | async-start | bytes 655360 | tf_op jit(solution)/shard_map/all_to_all | solution.py:40
  22.0 19.1 %all-to-all-done = bf16[4,2,20480]{2,1,0:T(2,128)(2,1)S(1)} async-done(((bf16[4,2,20480]{2,1,0:T(2,128)(2,1)}), bf16[4,2,20480]{2,1,0:T(2,128)(2,1)S(1)}, u32[]{:S(2)}, u32[]{:S(2)}) %all-to-all-start) | async-done | bytes 327712 | tf_op jit(solution)/shard_map/all_to_all | solution.py:40
  41.1 0.3 reshape.63
  41.4 0.4 copy.73
  41.8 0.2 convert_reduce_fusion
  42.3 0.2 reshape.47
  42.5 0.2 copy.57
  42.7 0.3 constant_dynamic-update-slice_fusion.4
  43.0 3.5 %collective-permute-start = (bf16[1,74368]{1,0:T(2,128)(2,1)S(1)}, bf16[1,74368]{1,0:T(2,128)(2,1)S(1)}, u32[]{:S(2)}, u32[]{:S(2)}) collective-permute-start(bf16[1,74368]{1,0:T(2,128)(2,1)S(1)} %constant_dynamic-update-slice_fusion.4), channel_id=1, source_target_pairs={{0,8},{1,9},{2,10},{3,11},{4,12},{5,13},{6,14},{7,15},{8,16},{9,17... | collective-permute-start | bytes 446216 | tf_op jit(solution)/shard_map/ppermute | solution.py:68
  46.5 3.6 %collective-permute-start.1 = (bf16[1,74368]{1,0:T(2,128)(2,1)S(1)}, bf16[1,74368]{1,0:T(2,128)(2,1)S(1)}, u32[]{:S(2)}, u32[]{:S(2)}) collective-permute-start(bf16[1,74368]{1,0:T(2,128)(2,1)S(1)} %constant_dynamic-update-slice_fusion.4), channel_id=1, source_target_pairs={{0,24},{1,25},{2,26},{3,27},{4,28},{5,29},{6,30},{7,31},{8,0},{9,1... | collective-permute-start | bytes 446216 | tf_op jit(solution)/shard_map/ppermute | solution.py:68
  50.1 3.9 %collective-permute-start.2 = (bf16[1,74368]{1,0:T(2,128)(2,1)S(1)}, bf16[1,74368]{1,0:T(2,128)(2,1)S(1)}, u32[]{:S(2)}, u32[]{:S(2)}) collective-permute-start(bf16[1,74368]{1,0:T(2,128)(2,1)S(1)} %constant_dynamic-update-slice_fusion.4), channel_id=1, source_target_pairs={{0,16},{1,17},{2,18},{3,19},{4,20},{5,21},{6,22},{7,23},{8,24},{9,... | collective-permute-start | bytes 446216 | tf_op jit(solution)/shard_map/ppermute | solution.py:68
  54.2 0.4 slice_reduce_fusion.9
  54.9 0.7 copy.53
  55.6 0.7 copy.54
  56.3 0.2 slice_reduce_fusion.5
  56.6 1.6 %collective-permute-done.1 = bf16[1,74368]{1,0:T(2,128)(2,1)S(1)} collective-permute-done((bf16[1,74368]{1,0:T(2,128)(2,1)S(1)}, bf16[1,74368]{1,0:T(2,128)(2,1)S(1)}, u32[]{:S(2)}, u32[]{:S(2)}) %collective-permute-start.1) | collective-permute-done | bytes 148768 | tf_op jit(solution)/shard_map/ppermute | solution.py:68
  58.2 0.2 slice_reduce_fusion.4
  58.5 1.9 %collective-permute-done.2 = bf16[1,74368]{1,0:T(2,128)(2,1)S(1)} collective-permute-done((bf16[1,74368]{1,0:T(2,128)(2,1)S(1)}, bf16[1,74368]{1,0:T(2,128)(2,1)S(1)}, u32[]{:S(2)}, u32[]{:S(2)}) %collective-permute-start.2) | collective-permute-done | bytes 148768 | tf_op jit(solution)/shard_map/ppermute | solution.py:68
  60.5 0.2 slice_reduce_fusion.3
  60.9 8.9 %collective-permute-start.3 = (bf16[4,2,14,608]{3,1,2,0:T(2,128)(2,1)S(1)}, bf16[4,2,14,608]{3,1,2,0:T(2,128)(2,1)S(1)}, u32[]{:S(2)}, u32[]{:S(2)}) collective-permute-start(bf16[4,2,14,608]{3,1,2,0:T(2,128)(2,1)S(1)} %copy_dynamic-update-slice_fusion), channel_id=1, source_target_pairs={{0,64},{1,65},{2,66},{3,67},{4,68},{5,69},{6,70},{7,71},{8,72},{9,... | collective-permute-start | bytes 408584 | tf_op jit(solution)/shard_map/ppermute | solution.py:98
  69.8 2.0 %collective-permute-start.4 = (bf16[4,2,14,608]{3,1,2,0:T(2,128)(2,1)S(1)}, bf16[4,2,14,608]{3,1,2,0:T(2,128)(2,1)S(1)}, u32[]{:S(2)}, u32[]{:S(2)}) collective-permute-start(bf16[4,2,14,608]{3,1,2,0:T(2,128)(2,1)S(1)} %copy_dynamic-update-slice_fusion), channel_id=1, source_target_pairs={{0,448},{1,449},{2,450},{3,451},{4,452},{5,453},{6,454},{7,455},{8... | collective-permute-start | bytes 408584 | tf_op jit(solution)/shard_map/ppermute | solution.py:104
  71.8 0.7 slice_reduce_fusion.2
  72.4 0.1 reshape_squeeze.16
  72.6 0.7 slice_reduce_fusion.1
  73.2 0.1 reshape_squeeze.17
  73.4 0.7 slice_reduce_fusion
  74.0 0.1 reshape_squeeze.18
  74.2 0.2 fusion.5
  74.5 0.2 fusion.6
  74.7 0.2 fusion.7
  74.9 0.7 dynamic_update_slice.108
  75.6 1.2 broadcast_in_dim.73
  76.9 4.8 %collective-permute-start.5 = (bf16[4,2,14,608]{3,1,2,0:T(2,128)(2,1)S(1)}, bf16[4,2,14,608]{3,1,2,0:T(2,128)(2,1)S(1)}, u32[]{:S(2)}, u32[]{:S(2)}) collective-permute-start(bf16[4,2,14,608]{3,1,2,0:T(2,128)(2,1)S(1)} %collective-permute-done.3), channel_id=1, source_target_pairs={{0,64},{1,65},{2,66},{3,67},{4,68},{5,69},{6,70},{7,71},{8,72},{9,... | collective-permute-start | bytes 408584 | tf_op jit(solution)/shard_map/ppermute | solution.py:98
  81.7 3.2 %collective-permute-start.6 = (bf16[4,2,14,608]{3,1,2,0:T(2,128)(2,1)S(1)}, bf16[4,2,14,608]{3,1,2,0:T(2,128)(2,1)S(1)}, u32[]{:S(2)}, u32[]{:S(2)}) collective-permute-start(bf16[4,2,14,608]{3,1,2,0:T(2,128)(2,1)S(1)} %collective-permute-done.4), channel_id=1, source_target_pairs={{0,448},{1,449},{2,450},{3,451},{4,452},{5,453},{6,454},{7,455},{8... | collective-permute-start | bytes 408584 | tf_op jit(solution)/shard_map/ppermute | solution.py:104
  84.9 0.2 bitcast_dynamic-update-slice_fusion.11
  85.1 0.2 bitcast_dynamic-update-slice_fusion.9
  85.3 2.6 %collective-permute-done.5 = bf16[4,2,14,608]{3,1,2,0:T(2,128)(2,1)S(1)} collective-permute-done((bf16[4,2,14,608]{3,1,2,0:T(2,128)(2,1)S(1)}, bf16[4,2,14,608]{3,1,2,0:T(2,128)(2,1)S(1)}, u32[]{:S(2)}, u32[]{:S(2)}) %collective-permute-start.5) | collective-permute-done | bytes 136224 | tf_op jit(solution)/shard_map/ppermute | solution.py:98
  88.0 2.0 %collective-permute-start.7 = (bf16[4,2,14,608]{3,1,2,0:T(2,128)(2,1)S(1)}, bf16[4,2,14,608]{3,1,2,0:T(2,128)(2,1)S(1)}, u32[]{:S(2)}, u32[]{:S(2)}) collective-permute-start(bf16[4,2,14,608]{3,1,2,0:T(2,128)(2,1)S(1)} %collective-permute-done.5), channel_id=1, source_target_pairs={{0,64},{1,65},{2,66},{3,67},{4,68},{5,69},{6,70},{7,71},{8,72},{9,... | collective-permute-start | bytes 408584 | tf_op jit(solution)/shard_map/ppermute | solution.py:98
  89.9 1.7 %collective-permute-done.6 = bf16[4,2,14,608]{3,1,2,0:T(2,128)(2,1)S(1)} collective-permute-done((bf16[4,2,14,608]{3,1,2,0:T(2,128)(2,1)S(1)}, bf16[4,2,14,608]{3,1,2,0:T(2,128)(2,1)S(1)}, u32[]{:S(2)}, u32[]{:S(2)}) %collective-permute-start.6) | collective-permute-done | bytes 136224 | tf_op jit(solution)/shard_map/ppermute | solution.py:104
  91.6 4.5 %collective-permute-start.8 = (bf16[4,2,14,608]{3,1,2,0:T(2,128)(2,1)S(1)}, bf16[4,2,14,608]{3,1,2,0:T(2,128)(2,1)S(1)}, u32[]{:S(2)}, u32[]{:S(2)}) collective-permute-start(bf16[4,2,14,608]{3,1,2,0:T(2,128)(2,1)S(1)} %collective-permute-done.6), channel_id=1, source_target_pairs={{0,448},{1,449},{2,450},{3,451},{4,452},{5,453},{6,454},{7,455},{8... | collective-permute-start | bytes 408584 | tf_op jit(solution)/shard_map/ppermute | solution.py:104
  96.1 0.2 bitcast_dynamic-update-slice_fusion.7
  96.3 0.2 bitcast_dynamic-update-slice_fusion.5
  96.5 2.0 %collective-permute-done.7 = bf16[4,2,14,608]{3,1,2,0:T(2,128)(2,1)S(1)} collective-permute-done((bf16[4,2,14,608]{3,1,2,0:T(2,128)(2,1)S(1)}, bf16[4,2,14,608]{3,1,2,0:T(2,128)(2,1)S(1)}, u32[]{:S(2)}, u32[]{:S(2)}) %collective-permute-start.7) | collective-permute-done | bytes 136224 | tf_op jit(solution)/shard_map/ppermute | solution.py:98
  98.5 0.2 bitcast_dynamic-update-slice_fusion.3
  98.6 3.2 %collective-permute-done.8 = bf16[4,2,14,608]{3,1,2,0:T(2,128)(2,1)S(1)} collective-permute-done((bf16[4,2,14,608]{3,1,2,0:T(2,128)(2,1)S(1)}, bf16[4,2,14,608]{3,1,2,0:T(2,128)(2,1)S(1)}, u32[]{:S(2)}, u32[]{:S(2)}) %collective-permute-start.8) | collective-permute-done | bytes 136224 | tf_op jit(solution)/shard_map/ppermute | solution.py:104
  101.8 0.2 bitcast_dynamic-update-slice_fusion.1
  102.0 0.7 fusion.10
  102.8 5.9 %collective-permute-start.10 = (bf16[4,4,2,14,608]{4,2,3,1,0:T(2,128)(2,1)S(1)}, bf16[4,4,2,14,608]{4,2,3,1,0:T(2,128)(2,1)S(1)}, u32[]{:S(2)}, u32[]{:S(2)}) collective-permute-start(bf16[4,4,2,14,608]{4,2,3,1,0:T(2,128)(2,1)S(1)} %get-tuple-element.29), channel_id=1, source_target_pairs={{0,480},{1,481},{2,482},{3,483},{4,484},{5,485},{6,486},{7,487},{8... | collective-permute-start | bytes 1634312 | tf_op jit(solution)/shard_map/ppermute | solution.py:113
  108.7 1.9 %collective-permute-start.9 = (bf16[4,2,14,608]{3,1,2,0:T(2,128)(2,1)S(1)}, bf16[4,2,14,608]{3,1,2,0:T(2,128)(2,1)S(1)}, u32[]{:S(2)}, u32[]{:S(2)}) collective-permute-start(bf16[4,2,14,608]{3,1,2,0:T(2,128)(2,1)S(1)} %collective-permute-done.7), channel_id=1, source_target_pairs={{0,64},{1,65},{2,66},{3,67},{4,68},{5,69},{6,70},{7,71},{8,72},{9,... | collective-permute-start | bytes 408584 | tf_op jit(solution)/shard_map/ppermute | solution.py:98
  110.7 1.4 multiply_subtract_fusion
  112.0 3.4 %collective-permute-start.11 = (bf16[4,4,2,14,608]{4,2,3,1,0:T(2,128)(2,1)S(1)}, bf16[4,4,2,14,608]{4,2,3,1,0:T(2,128)(2,1)S(1)}, u32[]{:S(2)}, u32[]{:S(2)}) collective-permute-start(bf16[4,4,2,14,608]{4,2,3,1,0:T(2,128)(2,1)S(1)} %get-tuple-element.28), channel_id=1, source_target_pairs={{0,32},{1,33},{2,34},{3,35},{4,36},{5,37},{6,38},{7,39},{8,40},{9,... | collective-permute-start | bytes 1634312 | tf_op jit(solution)/shard_map/ppermute | solution.py:113
  115.4 4.0 %collective-permute-done.9 = bf16[4,2,14,608]{3,1,2,0:T(2,128)(2,1)S(1)} collective-permute-done((bf16[4,2,14,608]{3,1,2,0:T(2,128)(2,1)S(1)}, bf16[4,2,14,608]{3,1,2,0:T(2,128)(2,1)S(1)}, u32[]{:S(2)}, u32[]{:S(2)}) %collective-permute-start.9) | collective-permute-done | bytes 136224 | tf_op jit(solution)/shard_map/ppermute | solution.py:98
  120.1 9.3 %collective-permute-done.11 = bf16[4,4,2,14,608]{4,2,3,1,0:T(2,128)(2,1)S(1)} collective-permute-done((bf16[4,4,2,14,608]{4,2,3,1,0:T(2,128)(2,1)S(1)}, bf16[4,4,2,14,608]{4,2,3,1,0:T(2,128)(2,1)S(1)}, u32[]{:S(2)}, u32[]{:S(2)}) %collective-permute-start.11) | collective-permute-done | bytes 544800 | tf_op jit(solution)/shard_map/ppermute | solution.py:113
  129.6 0.1 slice_dynamic-update-slice_fusion.1
  129.9 5.7 %copy.55 = bf16[2,896,608]{1,2,0:T(8,128)(2,1)} copy(bf16[2,896,608]{2,0,1:T(2,128)(2,1)S(1)} %bitcast.59) | data formatting | bytes 4358144
  (47 shorter events, 2.6 us)
Async XLA Ops:
  0.6 0.9 copy-start
  5.8 36.4 %copy-start.3 = (f32[2,14,608]{2,0,1:T(2,128)S(1)}, f32[2,14,608]{2,0,1:T(2,128)}, u32[]{:S(2)}) copy-start(f32[2,14,608]{2,0,1:T(2,128)} %param.11) | copy-start | bytes 204292
  5.8 36.4 %copy-start.4 = (f32[2,14,608]{2,0,1:T(2,128)S(1)}, f32[2,14,608]{2,0,1:T(2,128)}, u32[]{:S(2)}) copy-start(f32[2,14,608]{2,0,1:T(2,128)} %param.10) | copy-start | bytes 204292
  6.9 34.2 %all-to-all-start = ((bf16[4,2,20480]{2,1,0:T(2,128)(2,1)}), bf16[4,2,20480]{2,1,0:T(2,128)(2,1)S(1)}, u32[]{:S(2)}, u32[]{:S(2)}) async-start(bf16[4,2,20480]{2,1,0:T(2,128)(2,1)} %reshape.62), calls=%async_computation | async-start | bytes 655360 | tf_op jit(solution)/shard_map/all_to_all | solution.py:40
  43.0 13.3 %collective-permute-start = (bf16[1,74368]{1,0:T(2,128)(2,1)S(1)}, bf16[1,74368]{1,0:T(2,128)(2,1)S(1)}, u32[]{:S(2)}, u32[]{:S(2)}) collective-permute-start(bf16[1,74368]{1,0:T(2,128)(2,1)S(1)} %constant_dynamic-update-slice_fusion.4), channel_id=1, source_target_pairs={{0,8},{1,9},{2,10},{3,11},{4,12},{5,13},{6,14},{7,15},{8,16},{9,17... | collective-permute-start | bytes 446216 | tf_op jit(solution)/shard_map/ppermute | solution.py:68
  46.5 11.7 %collective-permute-start.1 = (bf16[1,74368]{1,0:T(2,128)(2,1)S(1)}, bf16[1,74368]{1,0:T(2,128)(2,1)S(1)}, u32[]{:S(2)}, u32[]{:S(2)}) collective-permute-start(bf16[1,74368]{1,0:T(2,128)(2,1)S(1)} %constant_dynamic-update-slice_fusion.4), channel_id=1, source_target_pairs={{0,24},{1,25},{2,26},{3,27},{4,28},{5,29},{6,30},{7,31},{8,0},{9,1... | collective-permute-start | bytes 446216 | tf_op jit(solution)/shard_map/ppermute | solution.py:68
  50.1 10.4 %collective-permute-start.2 = (bf16[1,74368]{1,0:T(2,128)(2,1)S(1)}, bf16[1,74368]{1,0:T(2,128)(2,1)S(1)}, u32[]{:S(2)}, u32[]{:S(2)}) collective-permute-start(bf16[1,74368]{1,0:T(2,128)(2,1)S(1)} %constant_dynamic-update-slice_fusion.4), channel_id=1, source_target_pairs={{0,16},{1,17},{2,18},{3,19},{4,20},{5,21},{6,22},{7,23},{8,24},{9,... | collective-permute-start | bytes 446216 | tf_op jit(solution)/shard_map/ppermute | solution.py:68
  60.9 16.0 %collective-permute-start.3 = (bf16[4,2,14,608]{3,1,2,0:T(2,128)(2,1)S(1)}, bf16[4,2,14,608]{3,1,2,0:T(2,128)(2,1)S(1)}, u32[]{:S(2)}, u32[]{:S(2)}) collective-permute-start(bf16[4,2,14,608]{3,1,2,0:T(2,128)(2,1)S(1)} %copy_dynamic-update-slice_fusion), channel_id=1, source_target_pairs={{0,64},{1,65},{2,66},{3,67},{4,68},{5,69},{6,70},{7,71},{8,72},{9,... | collective-permute-start | bytes 408584 | tf_op jit(solution)/shard_map/ppermute | solution.py:98
  69.8 11.9 %collective-permute-start.4 = (bf16[4,2,14,608]{3,1,2,0:T(2,128)(2,1)S(1)}, bf16[4,2,14,608]{3,1,2,0:T(2,128)(2,1)S(1)}, u32[]{:S(2)}, u32[]{:S(2)}) collective-permute-start(bf16[4,2,14,608]{3,1,2,0:T(2,128)(2,1)S(1)} %copy_dynamic-update-slice_fusion), channel_id=1, source_target_pairs={{0,448},{1,449},{2,450},{3,451},{4,452},{5,453},{6,454},{7,455},{8... | collective-permute-start | bytes 408584 | tf_op jit(solution)/shard_map/ppermute | solution.py:104
  76.9 11.0 %collective-permute-start.5 = (bf16[4,2,14,608]{3,1,2,0:T(2,128)(2,1)S(1)}, bf16[4,2,14,608]{3,1,2,0:T(2,128)(2,1)S(1)}, u32[]{:S(2)}, u32[]{:S(2)}) collective-permute-start(bf16[4,2,14,608]{3,1,2,0:T(2,128)(2,1)S(1)} %collective-permute-done.3), channel_id=1, source_target_pairs={{0,64},{1,65},{2,66},{3,67},{4,68},{5,69},{6,70},{7,71},{8,72},{9,... | collective-permute-start | bytes 408584 | tf_op jit(solution)/shard_map/ppermute | solution.py:98
  81.7 9.9 %collective-permute-start.6 = (bf16[4,2,14,608]{3,1,2,0:T(2,128)(2,1)S(1)}, bf16[4,2,14,608]{3,1,2,0:T(2,128)(2,1)S(1)}, u32[]{:S(2)}, u32[]{:S(2)}) collective-permute-start(bf16[4,2,14,608]{3,1,2,0:T(2,128)(2,1)S(1)} %collective-permute-done.4), channel_id=1, source_target_pairs={{0,448},{1,449},{2,450},{3,451},{4,452},{5,453},{6,454},{7,455},{8... | collective-permute-start | bytes 408584 | tf_op jit(solution)/shard_map/ppermute | solution.py:104
  85.1 25.5 %copy-start.1 = (f32[150,896]{1,0:T(8,128)S(1)}, f32[150,896]{1,0:T(8,128)}, u32[]{:S(2)}) copy-start(f32[150,896]{1,0:T(8,128)} %param.12) | copy-start | bytes 1612804
  85.1 25.5 %copy-start.2 = (f32[150,896]{1,0:T(8,128)S(1)}, f32[150,896]{1,0:T(8,128)}, u32[]{:S(2)}) copy-start(f32[150,896]{1,0:T(8,128)} %param.13) | copy-start | bytes 1612804
  88.0 10.5 %collective-permute-start.7 = (bf16[4,2,14,608]{3,1,2,0:T(2,128)(2,1)S(1)}, bf16[4,2,14,608]{3,1,2,0:T(2,128)(2,1)S(1)}, u32[]{:S(2)}, u32[]{:S(2)}) collective-permute-start(bf16[4,2,14,608]{3,1,2,0:T(2,128)(2,1)S(1)} %collective-permute-done.5), channel_id=1, source_target_pairs={{0,64},{1,65},{2,66},{3,67},{4,68},{5,69},{6,70},{7,71},{8,72},{9,... | collective-permute-start | bytes 408584 | tf_op jit(solution)/shard_map/ppermute | solution.py:98
  91.6 10.2 %collective-permute-start.8 = (bf16[4,2,14,608]{3,1,2,0:T(2,128)(2,1)S(1)}, bf16[4,2,14,608]{3,1,2,0:T(2,128)(2,1)S(1)}, u32[]{:S(2)}, u32[]{:S(2)}) collective-permute-start(bf16[4,2,14,608]{3,1,2,0:T(2,128)(2,1)S(1)} %collective-permute-done.6), channel_id=1, source_target_pairs={{0,448},{1,449},{2,450},{3,451},{4,452},{5,453},{6,454},{7,455},{8... | collective-permute-start | bytes 408584 | tf_op jit(solution)/shard_map/ppermute | solution.py:104
  102.8 16.8 %collective-permute-start.10 = (bf16[4,4,2,14,608]{4,2,3,1,0:T(2,128)(2,1)S(1)}, bf16[4,4,2,14,608]{4,2,3,1,0:T(2,128)(2,1)S(1)}, u32[]{:S(2)}, u32[]{:S(2)}) collective-permute-start(bf16[4,4,2,14,608]{4,2,3,1,0:T(2,128)(2,1)S(1)} %get-tuple-element.29), channel_id=1, source_target_pairs={{0,480},{1,481},{2,482},{3,483},{4,484},{5,485},{6,486},{7,487},{8... | collective-permute-start | bytes 1634312 | tf_op jit(solution)/shard_map/ppermute | solution.py:113
  108.7 10.7 %collective-permute-start.9 = (bf16[4,2,14,608]{3,1,2,0:T(2,128)(2,1)S(1)}, bf16[4,2,14,608]{3,1,2,0:T(2,128)(2,1)S(1)}, u32[]{:S(2)}, u32[]{:S(2)}) collective-permute-start(bf16[4,2,14,608]{3,1,2,0:T(2,128)(2,1)S(1)} %collective-permute-done.7), channel_id=1, source_target_pairs={{0,64},{1,65},{2,66},{3,67},{4,68},{5,69},{6,70},{7,71},{8,72},{9,... | collective-permute-start | bytes 408584 | tf_op jit(solution)/shard_map/ppermute | solution.py:98
  112.0 17.4 %collective-permute-start.11 = (bf16[4,4,2,14,608]{4,2,3,1,0:T(2,128)(2,1)S(1)}, bf16[4,4,2,14,608]{4,2,3,1,0:T(2,128)(2,1)S(1)}, u32[]{:S(2)}, u32[]{:S(2)}) collective-permute-start(bf16[4,4,2,14,608]{4,2,3,1,0:T(2,128)(2,1)S(1)} %get-tuple-element.28), channel_id=1, source_target_pairs={{0,32},{1,33},{2,34},{3,35},{4,36},{5,37},{6,38},{7,39},{8,40},{9,... | collective-permute-start | bytes 1634312 | tf_op jit(solution)/shard_map/ppermute | solution.py:113

commit v12 on v10

--- a/solution.py
+++ b/solution.py
@@ -36,10 +36,14 @@
     rrows = rank // Y_SIZE
     ry = lax.dynamic_slice_in_dim(right, (si % Y_SIZE) * rrows, rrows, axis=0)
     send_right = jnp.broadcast_to(ry.reshape(1, rrows * width), (groups, rrows * width))
-    send = jnp.concatenate([send_layer, send_left, send_right], axis=1)
-    recv = lax.all_to_all(send, "group", 0, 0, tiled=True)
+    parts = [send_layer, send_left, send_right]
+    send = jnp.concatenate([p.reshape(groups, 2, p.shape[1] // 2) for p in parts], axis=2)
+    recv_halves = lax.all_to_all(send, "group", 0, 0, tiled=True)
 
-    acc = recv[:, :nlayer].astype(f32).sum(axis=0)
+    def received(offset, n):
+        return recv_halves[:, :, offset // 2:(offset + n) // 2].reshape(groups, n)
+
+    acc = received(0, nlayer).astype(f32).sum(axis=0)
     layer_mean = acc.reshape(layer_weight.shape) / groups
     new_layer_momentum = beta_outer * layer_momentum + layer_mean
     new_layer_weight = layer_weight - rate_outer * (layer_mean + beta_outer * new_layer_momentum)
@@ -57,7 +61,7 @@
         return pairs
 
     yi = si % Y_SIZE
-    rgot = recv[:, nlayer + nleft:]
+    rgot = received(nlayer + nleft, rrows * width)
     npiece = piece.size
     payload = jnp.concatenate([piece.reshape(1, npiece), rgot.reshape(1, -1)], axis=1)
     yblk = jnp.zeros((Y_SIZE,) + piece.shape, piece.dtype)
@@ -117,7 +121,7 @@
             out = lax.dynamic_update_index_in_dim(out, got[m], zabs, axis=0)
     layer_blocks = jnp.moveaxis(out, 2, 0).reshape(piece.shape[0], -1, piece.shape[2])
 
-    lefts = recv[:, nlayer:nlayer + nleft].reshape((groups,) + left.shape[1:])
+    lefts = received(nlayer, nleft).reshape((groups,) + left.shape[1:])
     total = jnp.zeros(emb_weight.shape, f32)
     for g in range(groups):
         product = jnp.dot(lefts[g], rights[g], preferred_element_type=f32).astype(bf16)

time: 135 us -> 133 us (0.985)
    unnamed x19 -> x15, local copies, waits for them, and re-layouts: 11.1 us -> 9.09 us
    concatenate x1, local copies, waits for them, and re-layouts: 0.01 us -> 1.88 us  [on_device(): jnp.concatenate([p.reshape(groups, 2, p.shape[1] // 2) for p in parts], a...]
where the time goes in v12:
time: 133 us; the launch traced here: 132 us
  starting transfers between devices  63.8 us (48%)
  waiting for transfers between devices  42.4 us (32%)
  local copies, waits for them, and re-layouts  22.6 us (17%)
  matrix products  1.99 us (1%)
    all_to_all x1, waiting for transfers between devices, on_device(): recv_halves = lax.all_to_all(send, 'group', 0, 0, tiled=True)  19.1 us
    ppermute x4, starting transfers between devices, on_device(): fwd = lax.ppermute(fwd, axes, zshift(2))  18.5 us
    all_to_all x1, starting transfers between devices, on_device(): recv_halves = lax.all_to_all(send, 'group', 0, 0, tiled=True)  15.1 us
    ppermute x2, starting transfers between devices, on_device(): got = lax.ppermute(part, axes, zshift(k))  11.2 us
    ppermute x3, starting transfers between devices, on_device(): got = lax.ppermute(payload, ('shard', 'tensor'), yshift(k))  10.9 us
    unnamed x15, local copies, waits for them, and re-layouts  9.09 us
    ppermute x3, starting transfers between devices, on_device(): bwd = lax.ppermute(bwd, axes, zshift(-2))  8.05 us
    ppermute x4, waiting for transfers between devices, on_device(): fwd = lax.ppermute(fwd, axes, zshift(2))  6 us
  transfers between devices with their start and end apart: 13, of which 10 were waited for; matrix products, arithmetic and copies ran while one was open for 8% of the time, Pallas kernels for 0%

profile of v12, /device:TPU:6, one launch (start us, length us, event | category | flops | bytes accessed | tf_op | source)
XLA Modules:
  0.0 132.1 jit_solution(9314947571761008691)
XLA Ops:
  0.7 0.8 copy-done
  1.6 0.9 copy.21
  2.5 0.3 reshape_reshape.10
  2.7 1.1 copy.22
  3.8 0.2 reshape_reshape_squeeze.3
  4.0 1.9 %concatenate.6 = bf16[4,2,20480]{2,1,0:T(2,128)(2,1)} concatenate(bf16[4,2,8512]{2,1,0:T(2,128)(2,1)S(1)} %reshape_reshape.10, bf16[4,2,4800]{2,1,0:T(2,128)(2,1)S(1)} %reshape_reshape_squeeze.3, bf16[4,2,7168]{2,1,0:T(2,128)(2,1)S(1)} %broadcast_in_dim.73), dimensions={2} | concatenate | bytes 655360 | tf_op jit(solution)/shard_map/concatenate | solution.py:40
  5.9 15.1 %all-to-all-start = ((bf16[4,2,20480]{2,1,0:T(2,128)(2,1)}), bf16[4,2,20480]{2,1,0:T(2,128)(2,1)S(1)}, u32[]{:S(2)}, u32[]{:S(2)}) async-start(bf16[4,2,20480]{2,1,0:T(2,128)(2,1)} %concatenate.6), calls=%async_computation | async-start | bytes 655360 | tf_op jit(solution)/shard_map/all_to_all | solution.py:41
  21.0 19.1 %all-to-all-done = bf16[4,2,20480]{2,1,0:T(2,128)(2,1)S(1)} async-done(((bf16[4,2,20480]{2,1,0:T(2,128)(2,1)}), bf16[4,2,20480]{2,1,0:T(2,128)(2,1)S(1)}, u32[]{:S(2)}, u32[]{:S(2)}) %all-to-all-start) | async-done | bytes 327712 | tf_op jit(solution)/shard_map/all_to_all | solution.py:41
  40.3 0.1 div.38
  40.4 0.2 reshape.43
  40.9 0.3 constant_dynamic-update-slice_fusion.5
  41.1 3.5 %collective-permute-start = (bf16[1,74368]{1,0:T(2,128)(2,1)S(1)}, bf16[1,74368]{1,0:T(2,128)(2,1)S(1)}, u32[]{:S(2)}, u32[]{:S(2)}) collective-permute-start(bf16[1,74368]{1,0:T(2,128)(2,1)S(1)} %constant_dynamic-update-slice_fusion.5), channel_id=1, source_target_pairs={{0,8},{1,25},{2,10},{3,27},{4,12},{5,29},{6,14},{7,31},{8,16},{9,1... | collective-permute-start | bytes 446216 | tf_op jit(solution)/shard_map/ppermute | solution.py:72
  44.6 3.6 %collective-permute-start.1 = (bf16[1,74368]{1,0:T(2,128)(2,1)S(1)}, bf16[1,74368]{1,0:T(2,128)(2,1)S(1)}, u32[]{:S(2)}, u32[]{:S(2)}) collective-permute-start(bf16[1,74368]{1,0:T(2,128)(2,1)S(1)} %constant_dynamic-update-slice_fusion.5), channel_id=1, source_target_pairs={{0,24},{1,9},{2,26},{3,11},{4,28},{5,13},{6,30},{7,15},{8,0},{9,17... | collective-permute-start | bytes 446216 | tf_op jit(solution)/shard_map/ppermute | solution.py:72
  48.2 3.9 %collective-permute-start.2 = (bf16[1,74368]{1,0:T(2,128)(2,1)S(1)}, bf16[1,74368]{1,0:T(2,128)(2,1)S(1)}, u32[]{:S(2)}, u32[]{:S(2)}) collective-permute-start(bf16[1,74368]{1,0:T(2,128)(2,1)S(1)} %constant_dynamic-update-slice_fusion.5), channel_id=1, source_target_pairs={{0,16},{1,17},{2,18},{3,19},{4,20},{5,21},{6,22},{7,23},{8,24},{9,... | collective-permute-start | bytes 446216 | tf_op jit(solution)/shard_map/ppermute | solution.py:72
  52.1 0.2 fusion.10
  53.0 0.7 copy.29
  53.7 0.7 copy.30
  54.4 0.2 slice_reduce_fusion.5
  54.6 0.1 broadcast_in_dim.77
  54.7 0.4 collective-permute-done.1
  55.1 0.2 slice_reduce_fusion.4
  55.3 0.1 broadcast_in_dim.78
  55.4 5.2 %collective-permute-done.2 = bf16[1,74368]{1,0:T(2,128)(2,1)S(1)} collective-permute-done((bf16[1,74368]{1,0:T(2,128)(2,1)S(1)}, bf16[1,74368]{1,0:T(2,128)(2,1)S(1)}, u32[]{:S(2)}, u32[]{:S(2)}) %collective-permute-start.2) | collective-permute-done | bytes 148768 | tf_op jit(solution)/shard_map/ppermute | solution.py:72
  60.6 0.2 slice_reduce_fusion.3
  60.8 0.1 broadcast_in_dim.79
  61.1 8.6 %collective-permute-start.3 = (bf16[4,2,14,608]{3,1,2,0:T(2,128)(2,1)S(1)}, bf16[4,2,14,608]{3,1,2,0:T(2,128)(2,1)S(1)}, u32[]{:S(2)}, u32[]{:S(2)}) collective-permute-start(bf16[4,2,14,608]{3,1,2,0:T(2,128)(2,1)S(1)} %copy_dynamic-update-slice_fusion), channel_id=1, source_target_pairs={{0,64},{1,449},{2,66},{3,451},{4,68},{5,453},{6,70},{7,455},{8,72}... | collective-permute-start | bytes 408584 | tf_op jit(solution)/shard_map/ppermute | solution.py:102
  69.7 1.9 %collective-permute-start.4 = (bf16[4,2,14,608]{3,1,2,0:T(2,128)(2,1)S(1)}, bf16[4,2,14,608]{3,1,2,0:T(2,128)(2,1)S(1)}, u32[]{:S(2)}, u32[]{:S(2)}) collective-permute-start(bf16[4,2,14,608]{3,1,2,0:T(2,128)(2,1)S(1)} %copy_dynamic-update-slice_fusion), channel_id=1, source_target_pairs={{0,448},{1,65},{2,450},{3,67},{4,452},{5,69},{6,454},{7,71},{8,456... | collective-permute-start | bytes 408584 | tf_op jit(solution)/shard_map/ppermute | solution.py:108
  71.6 0.7 slice_reduce_fusion.2
  72.3 0.1 reshape_squeeze.12
  72.4 0.7 slice_reduce_fusion.1
  73.1 0.1 reshape_squeeze.13
  73.2 0.7 slice_reduce_fusion
  73.9 0.1 reshape_squeeze.14
  74.1 0.2 fusion.5
  74.3 0.2 fusion.6
  74.5 0.2 fusion.7
  74.8 0.7 dynamic_update_slice.109
  75.5 1.2 broadcast_in_dim.74
  76.7 0.1 constant_dynamic-update-slice_fusion.4
  76.8 4.8 %collective-permute-start.5 = (bf16[4,2,14,608]{3,1,2,0:T(2,128)(2,1)S(1)}, bf16[4,2,14,608]{3,1,2,0:T(2,128)(2,1)S(1)}, u32[]{:S(2)}, u32[]{:S(2)}) collective-permute-start(bf16[4,2,14,608]{3,1,2,0:T(2,128)(2,1)S(1)} %collective-permute-done.3), channel_id=1, source_target_pairs={{0,64},{1,449},{2,66},{3,451},{4,68},{5,453},{6,70},{7,455},{8,72}... | collective-permute-start | bytes 408584 | tf_op jit(solution)/shard_map/ppermute | solution.py:102
  81.6 3.1 %collective-permute-start.6 = (bf16[4,2,14,608]{3,1,2,0:T(2,128)(2,1)S(1)}, bf16[4,2,14,608]{3,1,2,0:T(2,128)(2,1)S(1)}, u32[]{:S(2)}, u32[]{:S(2)}) collective-permute-start(bf16[4,2,14,608]{3,1,2,0:T(2,128)(2,1)S(1)} %collective-permute-done.4), channel_id=1, source_target_pairs={{0,448},{1,65},{2,450},{3,67},{4,452},{5,69},{6,454},{7,71},{8,456... | collective-permute-start | bytes 408584 | tf_op jit(solution)/shard_map/ppermute | solution.py:108
  84.8 0.2 bitcast_dynamic-update-slice_fusion.11
  85.0 0.2 bitcast_dynamic-update-slice_fusion.9
  85.2 1.2 collective-permute-done.5
  86.4 3.2 %collective-permute-start.7 = (bf16[4,2,14,608]{3,1,2,0:T(2,128)(2,1)S(1)}, bf16[4,2,14,608]{3,1,2,0:T(2,128)(2,1)S(1)}, u32[]{:S(2)}, u32[]{:S(2)}) collective-permute-start(bf16[4,2,14,608]{3,1,2,0:T(2,128)(2,1)S(1)} %collective-permute-done.5), channel_id=1, source_target_pairs={{0,64},{1,449},{2,66},{3,451},{4,68},{5,453},{6,70},{7,455},{8,72}... | collective-permute-start | bytes 408584 | tf_op jit(solution)/shard_map/ppermute | solution.py:102
  89.6 2.0 %collective-permute-done.6 = bf16[4,2,14,608]{3,1,2,0:T(2,128)(2,1)S(1)} collective-permute-done((bf16[4,2,14,608]{3,1,2,0:T(2,128)(2,1)S(1)}, bf16[4,2,14,608]{3,1,2,0:T(2,128)(2,1)S(1)}, u32[]{:S(2)}, u32[]{:S(2)}) %collective-permute-start.6) | collective-permute-done | bytes 136224 | tf_op jit(solution)/shard_map/ppermute | solution.py:108
  91.6 3.0 %collective-permute-start.8 = (bf16[4,2,14,608]{3,1,2,0:T(2,128)(2,1)S(1)}, bf16[4,2,14,608]{3,1,2,0:T(2,128)(2,1)S(1)}, u32[]{:S(2)}, u32[]{:S(2)}) collective-permute-start(bf16[4,2,14,608]{3,1,2,0:T(2,128)(2,1)S(1)} %collective-permute-done.6), channel_id=1, source_target_pairs={{0,448},{1,65},{2,450},{3,67},{4,452},{5,69},{6,454},{7,71},{8,456... | collective-permute-start | bytes 408584 | tf_op jit(solution)/shard_map/ppermute | solution.py:108
  94.6 0.2 bitcast_dynamic-update-slice_fusion.7
  94.8 0.2 bitcast_dynamic-update-slice_fusion.5
  95.0 0.5 collective-permute-done.7
  95.5 0.2 bitcast_dynamic-update-slice_fusion.3
  95.7 3.7 %collective-permute-done.8 = bf16[4,2,14,608]{3,1,2,0:T(2,128)(2,1)S(1)} collective-permute-done((bf16[4,2,14,608]{3,1,2,0:T(2,128)(2,1)S(1)}, bf16[4,2,14,608]{3,1,2,0:T(2,128)(2,1)S(1)}, u32[]{:S(2)}, u32[]{:S(2)}) %collective-permute-start.8) | collective-permute-done | bytes 136224 | tf_op jit(solution)/shard_map/ppermute | solution.py:108
  99.4 0.2 bitcast_dynamic-update-slice_fusion.1
  99.6 0.8 constant_dynamic-slice_fusion
  100.4 9.3 %collective-permute-start.10 = (bf16[4,4,2,14,608]{4,2,3,1,0:T(2,128)(2,1)S(1)}, bf16[4,4,2,14,608]{4,2,3,1,0:T(2,128)(2,1)S(1)}, u32[]{:S(2)}, u32[]{:S(2)}) collective-permute-start(bf16[4,4,2,14,608]{4,2,3,1,0:T(2,128)(2,1)S(1)} %get-tuple-element.15), channel_id=1, source_target_pairs={{0,480},{1,33},{2,482},{3,35},{4,484},{5,37},{6,486},{7,39},{8,488... | collective-permute-start | bytes 1634312 | tf_op jit(solution)/shard_map/ppermute | solution.py:117
  109.8 1.9 %collective-permute-start.9 = (bf16[4,2,14,608]{3,1,2,0:T(2,128)(2,1)S(1)}, bf16[4,2,14,608]{3,1,2,0:T(2,128)(2,1)S(1)}, u32[]{:S(2)}, u32[]{:S(2)}) collective-permute-start(bf16[4,2,14,608]{3,1,2,0:T(2,128)(2,1)S(1)} %collective-permute-done.7), channel_id=1, source_target_pairs={{0,64},{1,449},{2,66},{3,451},{4,68},{5,453},{6,70},{7,455},{8,72}... | collective-permute-start | bytes 408584 | tf_op jit(solution)/shard_map/ppermute | solution.py:102
  111.7 1.4 %multiply_subtract_fusion = (f32[150,896]{1,0:T(8,128)}, f32[150,896]{1,0:T(8,128)}) fusion(f32[150,896]{1,0:T(8,128)S(1)} %copy-done.1, f32[150,896]{1,0:T(8,128)S(1)} %copy-done.2, f32[150,896]{1,0:T(8,128)S(1)} %fusion.7, f32[150,896]{1,0:T(8,128)S(1)} %fusion.6, f32[150,896]{1,0:T(8,128)S(1)} %fusion.5, bf16[150,64]{1,0:T(8,128)(2,1)S(1)} %squeeze.37, ...), kind=kOutput, calls=%fused_computation.12 | convolution fusion | flops 18816000 | bytes 3952640 | tf_op jit(solution)/shard_map/dot_general | solution.py:127
  113.1 1.9 %collective-permute-start.11 = (bf16[4,4,2,14,608]{4,2,3,1,0:T(2,128)(2,1)S(1)}, bf16[4,4,2,14,608]{4,2,3,1,0:T(2,128)(2,1)S(1)}, u32[]{:S(2)}, u32[]{:S(2)}) collective-permute-start(bf16[4,4,2,14,608]{4,2,3,1,0:T(2,128)(2,1)S(1)} %get-tuple-element.14), channel_id=1, source_target_pairs={{0,32},{1,481},{2,34},{3,483},{4,36},{5,485},{6,38},{7,487},{8,40}... | collective-permute-start | bytes 1634312 | tf_op jit(solution)/shard_map/ppermute | solution.py:117
  115.0 4.3 %collective-permute-done.9 = bf16[4,2,14,608]{3,1,2,0:T(2,128)(2,1)S(1)} collective-permute-done((bf16[4,2,14,608]{3,1,2,0:T(2,128)(2,1)S(1)}, bf16[4,2,14,608]{3,1,2,0:T(2,128)(2,1)S(1)}, u32[]{:S(2)}, u32[]{:S(2)}) %collective-permute-start.9) | collective-permute-done | bytes 136224 | tf_op jit(solution)/shard_map/ppermute | solution.py:102
  119.4 4.0 %collective-permute-done.10 = bf16[4,4,2,14,608]{4,2,3,1,0:T(2,128)(2,1)S(1)} collective-permute-done((bf16[4,4,2,14,608]{4,2,3,1,0:T(2,128)(2,1)S(1)}, bf16[4,4,2,14,608]{4,2,3,1,0:T(2,128)(2,1)S(1)}, u32[]{:S(2)}, u32[]{:S(2)}) %collective-permute-start.10) | collective-permute-done | bytes 544800 | tf_op jit(solution)/shard_map/ppermute | solution.py:117
  123.9 2.0 %collective-permute-done.11 = bf16[4,4,2,14,608]{4,2,3,1,0:T(2,128)(2,1)S(1)} collective-permute-done((bf16[4,4,2,14,608]{4,2,3,1,0:T(2,128)(2,1)S(1)}, bf16[4,4,2,14,608]{4,2,3,1,0:T(2,128)(2,1)S(1)}, u32[]{:S(2)}, u32[]{:S(2)}) %collective-permute-start.11) | collective-permute-done | bytes 544800 | tf_op jit(solution)/shard_map/ppermute | solution.py:117
  126.1 0.1 slice_dynamic-update-slice_fusion.1
  126.3 0.1 slice_dynamic-update-slice_fusion
  126.4 5.7 %copy.31 = bf16[2,896,608]{1,2,0:T(8,128)(2,1)} copy(bf16[2,896,608]{2,0,1:T(2,128)(2,1)S(1)} %bitcast.47) | data formatting | bytes 4358144
  (43 shorter events, 2.3 us)
Async XLA Ops:
  0.6 0.9 copy-start
  0.6 39.7 %copy-start.4 = (f32[2,14,608]{2,0,1:T(2,128)S(1)}, f32[2,14,608]{2,0,1:T(2,128)}, u32[]{:S(2)}) copy-start(f32[2,14,608]{2,0,1:T(2,128)} %param.10) | copy-start | bytes 204292
  0.7 39.7 %copy-start.3 = (f32[2,14,608]{2,0,1:T(2,128)S(1)}, f32[2,14,608]{2,0,1:T(2,128)}, u32[]{:S(2)}) copy-start(f32[2,14,608]{2,0,1:T(2,128)} %param.11) | copy-start | bytes 204292
  5.9 34.2 %all-to-all-start = ((bf16[4,2,20480]{2,1,0:T(2,128)(2,1)}), bf16[4,2,20480]{2,1,0:T(2,128)(2,1)S(1)}, u32[]{:S(2)}, u32[]{:S(2)}) async-start(bf16[4,2,20480]{2,1,0:T(2,128)(2,1)} %concatenate.6), calls=%async_computation | async-start | bytes 655360 | tf_op jit(solution)/shard_map/all_to_all | solution.py:41
  41.1 13.3 %collective-permute-start = (bf16[1,74368]{1,0:T(2,128)(2,1)S(1)}, bf16[1,74368]{1,0:T(2,128)(2,1)S(1)}, u32[]{:S(2)}, u32[]{:S(2)}) collective-permute-start(bf16[1,74368]{1,0:T(2,128)(2,1)S(1)} %constant_dynamic-update-slice_fusion.5), channel_id=1, source_target_pairs={{0,8},{1,25},{2,10},{3,27},{4,12},{5,29},{6,14},{7,31},{8,16},{9,1... | collective-permute-start | bytes 446216 | tf_op jit(solution)/shard_map/ppermute | solution.py:72
  44.6 10.5 %collective-permute-start.1 = (bf16[1,74368]{1,0:T(2,128)(2,1)S(1)}, bf16[1,74368]{1,0:T(2,128)(2,1)S(1)}, u32[]{:S(2)}, u32[]{:S(2)}) collective-permute-start(bf16[1,74368]{1,0:T(2,128)(2,1)S(1)} %constant_dynamic-update-slice_fusion.5), channel_id=1, source_target_pairs={{0,24},{1,9},{2,26},{3,11},{4,28},{5,13},{6,30},{7,15},{8,0},{9,17... | collective-permute-start | bytes 446216 | tf_op jit(solution)/shard_map/ppermute | solution.py:72
  48.2 12.4 %collective-permute-start.2 = (bf16[1,74368]{1,0:T(2,128)(2,1)S(1)}, bf16[1,74368]{1,0:T(2,128)(2,1)S(1)}, u32[]{:S(2)}, u32[]{:S(2)}) collective-permute-start(bf16[1,74368]{1,0:T(2,128)(2,1)S(1)} %constant_dynamic-update-slice_fusion.5), channel_id=1, source_target_pairs={{0,16},{1,17},{2,18},{3,19},{4,20},{5,21},{6,22},{7,23},{8,24},{9,... | collective-permute-start | bytes 446216 | tf_op jit(solution)/shard_map/ppermute | solution.py:72
  61.1 15.7 %collective-permute-start.3 = (bf16[4,2,14,608]{3,1,2,0:T(2,128)(2,1)S(1)}, bf16[4,2,14,608]{3,1,2,0:T(2,128)(2,1)S(1)}, u32[]{:S(2)}, u32[]{:S(2)}) collective-permute-start(bf16[4,2,14,608]{3,1,2,0:T(2,128)(2,1)S(1)} %copy_dynamic-update-slice_fusion), channel_id=1, source_target_pairs={{0,64},{1,449},{2,66},{3,451},{4,68},{5,453},{6,70},{7,455},{8,72}... | collective-permute-start | bytes 408584 | tf_op jit(solution)/shard_map/ppermute | solution.py:102
  69.7 11.9 %collective-permute-start.4 = (bf16[4,2,14,608]{3,1,2,0:T(2,128)(2,1)S(1)}, bf16[4,2,14,608]{3,1,2,0:T(2,128)(2,1)S(1)}, u32[]{:S(2)}, u32[]{:S(2)}) collective-permute-start(bf16[4,2,14,608]{3,1,2,0:T(2,128)(2,1)S(1)} %copy_dynamic-update-slice_fusion), channel_id=1, source_target_pairs={{0,448},{1,65},{2,450},{3,67},{4,452},{5,69},{6,454},{7,71},{8,456... | collective-permute-start | bytes 408584 | tf_op jit(solution)/shard_map/ppermute | solution.py:108
  76.8 9.6 %collective-permute-start.5 = (bf16[4,2,14,608]{3,1,2,0:T(2,128)(2,1)S(1)}, bf16[4,2,14,608]{3,1,2,0:T(2,128)(2,1)S(1)}, u32[]{:S(2)}, u32[]{:S(2)}) collective-permute-start(bf16[4,2,14,608]{3,1,2,0:T(2,128)(2,1)S(1)} %collective-permute-done.3), channel_id=1, source_target_pairs={{0,64},{1,449},{2,66},{3,451},{4,68},{5,453},{6,70},{7,455},{8,72}... | collective-permute-start | bytes 408584 | tf_op jit(solution)/shard_map/ppermute | solution.py:102
  81.6 9.9 %collective-permute-start.6 = (bf16[4,2,14,608]{3,1,2,0:T(2,128)(2,1)S(1)}, bf16[4,2,14,608]{3,1,2,0:T(2,128)(2,1)S(1)}, u32[]{:S(2)}, u32[]{:S(2)}) collective-permute-start(bf16[4,2,14,608]{3,1,2,0:T(2,128)(2,1)S(1)} %collective-permute-done.4), channel_id=1, source_target_pairs={{0,448},{1,65},{2,450},{3,67},{4,452},{5,69},{6,454},{7,71},{8,456... | collective-permute-start | bytes 408584 | tf_op jit(solution)/shard_map/ppermute | solution.py:108
  85.0 26.7 %copy-start.1 = (f32[150,896]{1,0:T(8,128)S(1)}, f32[150,896]{1,0:T(8,128)}, u32[]{:S(2)}) copy-start(f32[150,896]{1,0:T(8,128)} %param.12) | copy-start | bytes 1612804
  85.0 26.7 %copy-start.2 = (f32[150,896]{1,0:T(8,128)S(1)}, f32[150,896]{1,0:T(8,128)}, u32[]{:S(2)}) copy-start(f32[150,896]{1,0:T(8,128)} %param.13) | copy-start | bytes 1612804
  86.4 9.1 %collective-permute-start.7 = (bf16[4,2,14,608]{3,1,2,0:T(2,128)(2,1)S(1)}, bf16[4,2,14,608]{3,1,2,0:T(2,128)(2,1)S(1)}, u32[]{:S(2)}, u32[]{:S(2)}) collective-permute-start(bf16[4,2,14,608]{3,1,2,0:T(2,128)(2,1)S(1)} %collective-permute-done.5), channel_id=1, source_target_pairs={{0,64},{1,449},{2,66},{3,451},{4,68},{5,453},{6,70},{7,455},{8,72}... | collective-permute-start | bytes 408584 | tf_op jit(solution)/shard_map/ppermute | solution.py:102
  91.6 7.9 %collective-permute-start.8 = (bf16[4,2,14,608]{3,1,2,0:T(2,128)(2,1)S(1)}, bf16[4,2,14,608]{3,1,2,0:T(2,128)(2,1)S(1)}, u32[]{:S(2)}, u32[]{:S(2)}) collective-permute-start(bf16[4,2,14,608]{3,1,2,0:T(2,128)(2,1)S(1)} %collective-permute-done.6), channel_id=1, source_target_pairs={{0,448},{1,65},{2,450},{3,67},{4,452},{5,69},{6,454},{7,71},{8,456... | collective-permute-start | bytes 408584 | tf_op jit(solution)/shard_map/ppermute | solution.py:108
  100.4 22.9 %collective-permute-start.10 = (bf16[4,4,2,14,608]{4,2,3,1,0:T(2,128)(2,1)S(1)}, bf16[4,4,2,14,608]{4,2,3,1,0:T(2,128)(2,1)S(1)}, u32[]{:S(2)}, u32[]{:S(2)}) collective-permute-start(bf16[4,4,2,14,608]{4,2,3,1,0:T(2,128)(2,1)S(1)} %get-tuple-element.15), channel_id=1, source_target_pairs={{0,480},{1,33},{2,482},{3,35},{4,484},{5,37},{6,486},{7,39},{8,488... | collective-permute-start | bytes 1634312 | tf_op jit(solution)/shard_map/ppermute | solution.py:117
  109.8 9.5 %collective-permute-start.9 = (bf16[4,2,14,608]{3,1,2,0:T(2,128)(2,1)S(1)}, bf16[4,2,14,608]{3,1,2,0:T(2,128)(2,1)S(1)}, u32[]{:S(2)}, u32[]{:S(2)}) collective-permute-start(bf16[4,2,14,608]{3,1,2,0:T(2,128)(2,1)S(1)} %collective-permute-done.7), channel_id=1, source_target_pairs={{0,64},{1,449},{2,66},{3,451},{4,68},{5,453},{6,70},{7,455},{8,72}... | collective-permute-start | bytes 408584 | tf_op jit(solution)/shard_map/ppermute | solution.py:102
  113.1 12.8 %collective-permute-start.11 = (bf16[4,4,2,14,608]{4,2,3,1,0:T(2,128)(2,1)S(1)}, bf16[4,4,2,14,608]{4,2,3,1,0:T(2,128)(2,1)S(1)}, u32[]{:S(2)}, u32[]{:S(2)}) collective-permute-start(bf16[4,4,2,14,608]{4,2,3,1,0:T(2,128)(2,1)S(1)} %get-tuple-element.14), channel_id=1, source_target_pairs={{0,32},{1,481},{2,34},{3,483},{4,36},{5,485},{6,38},{7,487},{8,40}... | collective-permute-start | bytes 1634312 | tf_op jit(solution)/shard_map/ppermute | solution.py:117

commit v13 on v12

--- a/solution.py
+++ b/solution.py
@@ -63,7 +63,7 @@
     yi = si % Y_SIZE
     rgot = received(nlayer + nleft, rrows * width)
     npiece = piece.size
-    payload = jnp.concatenate([piece.reshape(1, npiece), rgot.reshape(1, -1)], axis=1)
+    payload = jnp.concatenate([piece.reshape(2, npiece // 2), rgot.reshape(2, -1)], axis=1)
     yblk = jnp.zeros((Y_SIZE,) + piece.shape, piece.dtype)
     yblk = lax.dynamic_update_index_in_dim(yblk, piece, yi, axis=0)
     rights = jnp.zeros((groups, rank, width), rgot.dtype)
@@ -71,8 +71,8 @@
     for k in (1, -1, 2):
         got = lax.ppermute(payload, ("shard", "tensor"), yshift(k))
         src = (yi - k * sgn) % Y_SIZE
-        yblk = lax.dynamic_update_index_in_dim(yblk, got[0, :npiece].reshape(piece.shape), src, axis=0)
-        rpart = got[0, npiece:].reshape(groups, rrows, width)
+        yblk = lax.dynamic_update_index_in_dim(yblk, got[:, :npiece // 2].reshape(piece.shape), src, axis=0)
+        rpart = got[:, npiece // 2:].reshape(groups, rrows, width)
         rights = lax.dynamic_update_slice_in_dim(rights, rpart, src * rrows, axis=1)
 
     zlo_size = shards // Y_SIZE

time: 133 us -> 127 us (0.955)
  starting transfers between devices: 63.8 us -> 61.6 us
  local copies, waits for them, and re-layouts: 22.6 us -> 20.5 us
  waiting for transfers between devices: 42.4 us -> 40.9 us
    ppermute x3, waiting for transfers between devices: 5.6 us -> 2.02 us  [on_device(): got = lax.ppermute(payload, ('shard', 'tensor'), yshift(k))]
    ppermute x2, starting transfers between devices: 11.2 us -> 9.3 us  [on_device(): got = lax.ppermute(part, axes, zshift(k))]
    slice x6, local copies, waits for them, and re-layouts: 2.52 us -> 0.65 us  [the longest x3 0.57 us: on_device(): rpart = got[:, npiece // 2:].reshape(groups, rrows, width)]
    unnamed x15 -> x16, local copies, waits for them, and re-layouts: 9.09 us -> 8.18 us
  transfers between devices with their start and end apart: 13 -> 13, of which waited for: 10 -> 9; matrix products, arithmetic and copies ran while one was open for 8% -> 8% of each run, Pallas kernels for 0% -> 0%
where the time goes in v13:
time: 127 us
  starting transfers between devices  61.6 us (49%)
  waiting for transfers between devices  40.9 us (32%)
  local copies, waits for them, and re-layouts  20.5 us (16%)
  matrix products  1.98 us (2%)
    ppermute x4, starting transfers between devices, on_device(): fwd = lax.ppermute(fwd, axes, zshift(2))  19.2 us
    all_to_all x1, waiting for transfers between devices, on_device(): recv_halves = lax.all_to_all(send, 'group', 0, 0, tiled=True)  19.1 us
    all_to_all x1, starting transfers between devices, on_device(): recv_halves = lax.all_to_all(send, 'group', 0, 0, tiled=True)  15.1 us
    ppermute x3, starting transfers between devices, on_device(): got = lax.ppermute(payload, ('shard', 'tensor'), yshift(k))  10.9 us
    ppermute x2, starting transfers between devices, on_device(): got = lax.ppermute(part, axes, zshift(k))  9.3 us
    unnamed x16, local copies, waits for them, and re-layouts  8.18 us
    ppermute x4, waiting for transfers between devices, on_device(): fwd = lax.ppermute(fwd, axes, zshift(2))  7.19 us
    ppermute x3, starting transfers between devices, on_device(): bwd = lax.ppermute(bwd, axes, zshift(-2))  7.11 us
  transfers between devices with their start and end apart: 13, of which 9 were waited for; matrix products, arithmetic and copies ran while one was open for 8% of the time, Pallas kernels for 0%

profile of v13, /device:TPU:6, one launch (start us, length us, event | category | flops | bytes accessed | tf_op | source)
XLA Modules:
  0.0 126.6 jit_solution(16787350265385346023)
XLA Ops:
  0.7 1.0 copy.21
  1.7 0.3 reshape_reshape.10
  1.9 1.1 copy.22
  3.0 0.2 reshape_reshape_squeeze.3
  3.3 1.9 %concatenate.6 = bf16[4,2,20480]{2,1,0:T(2,128)(2,1)} concatenate(bf16[4,2,8512]{2,1,0:T(2,128)(2,1)S(1)} %reshape_reshape.10, bf16[4,2,4800]{2,1,0:T(2,128)(2,1)S(1)} %reshape_reshape_squeeze.3, bf16[4,2,7168]{2,1,0:T(2,128)(2,1)S(1)} %broadcast_in_dim.73), dimensions={2} | concatenate | bytes 655360 | tf_op jit(solution)/shard_map/concatenate | solution.py:40
  5.2 15.1 %all-to-all-start = ((bf16[4,2,20480]{2,1,0:T(2,128)(2,1)}), bf16[4,2,20480]{2,1,0:T(2,128)(2,1)S(1)}, u32[]{:S(2)}, u32[]{:S(2)}) async-start(bf16[4,2,20480]{2,1,0:T(2,128)(2,1)} %concatenate.6), calls=%async_computation | async-start | bytes 655360 | tf_op jit(solution)/shard_map/all_to_all | solution.py:41
  20.3 19.1 %all-to-all-done = bf16[4,2,20480]{2,1,0:T(2,128)(2,1)S(1)} async-done(((bf16[4,2,20480]{2,1,0:T(2,128)(2,1)}), bf16[4,2,20480]{2,1,0:T(2,128)(2,1)S(1)}, u32[]{:S(2)}, u32[]{:S(2)}) %all-to-all-start) | async-done | bytes 327712 | tf_op jit(solution)/shard_map/all_to_all | solution.py:41
  39.5 0.1 div.38
  39.9 0.1 reshape.55
  40.0 0.2 pad_maximum_fusion
  40.2 3.5 %collective-permute-start = (bf16[2,37184]{1,0:T(2,128)(2,1)S(1)}, bf16[2,37184]{1,0:T(2,128)(2,1)S(1)}, u32[]{:S(2)}, u32[]{:S(2)}) collective-permute-start(bf16[2,37184]{1,0:T(2,128)(2,1)S(1)} %pad_maximum_fusion), channel_id=1, source_target_pairs={{0,8},{1,25},{2,10},{3,27},{4,12},{5,29},{6,14},{7,31},{8,16},{9,1... | collective-permute-start | bytes 446216 | tf_op jit(solution)/shard_map/ppermute | solution.py:72
  43.7 3.6 %collective-permute-start.1 = (bf16[2,37184]{1,0:T(2,128)(2,1)S(1)}, bf16[2,37184]{1,0:T(2,128)(2,1)S(1)}, u32[]{:S(2)}, u32[]{:S(2)}) collective-permute-start(bf16[2,37184]{1,0:T(2,128)(2,1)S(1)} %pad_maximum_fusion), channel_id=1, source_target_pairs={{0,24},{1,9},{2,26},{3,11},{4,28},{5,13},{6,30},{7,15},{8,0},{9,17... | collective-permute-start | bytes 446216 | tf_op jit(solution)/shard_map/ppermute | solution.py:72
  47.3 3.9 %collective-permute-start.2 = (bf16[2,37184]{1,0:T(2,128)(2,1)S(1)}, bf16[2,37184]{1,0:T(2,128)(2,1)S(1)}, u32[]{:S(2)}, u32[]{:S(2)}) collective-permute-start(bf16[2,37184]{1,0:T(2,128)(2,1)S(1)} %pad_maximum_fusion), channel_id=1, source_target_pairs={{0,16},{1,17},{2,18},{3,19},{4,20},{5,21},{6,22},{7,23},{8,24},{9,... | collective-permute-start | bytes 446216 | tf_op jit(solution)/shard_map/ppermute | solution.py:72
  51.2 0.2 fusion.10
  51.5 0.7 copy.29
  52.2 0.7 copy.30
  52.9 0.1 squeeze.43
  53.0 0.1 squeeze.41
  53.1 0.1 squeeze.39
  53.3 0.1 squeeze.37
  53.5 0.1 broadcast_in_dim.77
  53.7 0.1 broadcast_in_dim.78
  53.8 2.0 %collective-permute-done.2 = bf16[2,37184]{1,0:T(2,128)(2,1)S(1)} collective-permute-done((bf16[2,37184]{1,0:T(2,128)(2,1)S(1)}, bf16[2,37184]{1,0:T(2,128)(2,1)S(1)}, u32[]{:S(2)}, u32[]{:S(2)}) %collective-permute-start.2) | collective-permute-done | bytes 148768 | tf_op jit(solution)/shard_map/ppermute | solution.py:72
  55.9 0.1 broadcast_in_dim.79
  56.1 7.7 %collective-permute-start.3 = (bf16[4,2,14,608]{3,1,2,0:T(2,128)(2,1)S(1)}, bf16[4,2,14,608]{3,1,2,0:T(2,128)(2,1)S(1)}, u32[]{:S(2)}, u32[]{:S(2)}) collective-permute-start(bf16[4,2,14,608]{3,1,2,0:T(2,128)(2,1)S(1)} %copy_dynamic-update-slice_fusion), channel_id=1, source_target_pairs={{0,64},{1,449},{2,66},{3,451},{4,68},{5,453},{6,70},{7,455},{8,72}... | collective-permute-start | bytes 408584 | tf_op jit(solution)/shard_map/ppermute | solution.py:102
  63.8 1.9 %collective-permute-start.4 = (bf16[4,2,14,608]{3,1,2,0:T(2,128)(2,1)S(1)}, bf16[4,2,14,608]{3,1,2,0:T(2,128)(2,1)S(1)}, u32[]{:S(2)}, u32[]{:S(2)}) collective-permute-start(bf16[4,2,14,608]{3,1,2,0:T(2,128)(2,1)S(1)} %copy_dynamic-update-slice_fusion), channel_id=1, source_target_pairs={{0,448},{1,65},{2,450},{3,67},{4,452},{5,69},{6,454},{7,71},{8,456... | collective-permute-start | bytes 408584 | tf_op jit(solution)/shard_map/ppermute | solution.py:108
  65.8 1.8 %dynamic_update_slice.109 = bf16[9,4,2,14,608]{4,2,3,1,0:T(2,128)(2,1)} pad(bf16[1,4,2,14,608]{4,2,3,1,0:T(2,128)(2,1)S(1)} %bitcast.48, bf16[]{:T(256)} %constant.247.clone.1), padding=4_4x0_0x0_0x0_0x0_0 | pad | bytes 1361922 | tf_op jit(solution)/shard_map/jit(dynamic_update_index_in_dim)/dynamic_update_slice | solution.py:97
  67.5 0.2 slice.119
  67.8 0.2 slice.120
  68.1 0.2 slice.121
  68.5 0.2 fusion.7
  68.7 0.2 fusion.6
  68.9 0.2 fusion.5
  69.1 1.2 broadcast_in_dim.74
  70.3 0.1 constant_dynamic-update-slice_fusion.4
  70.4 4.8 %collective-permute-start.5 = (bf16[4,2,14,608]{3,1,2,0:T(2,128)(2,1)S(1)}, bf16[4,2,14,608]{3,1,2,0:T(2,128)(2,1)S(1)}, u32[]{:S(2)}, u32[]{:S(2)}) collective-permute-start(bf16[4,2,14,608]{3,1,2,0:T(2,128)(2,1)S(1)} %collective-permute-done.3), channel_id=1, source_target_pairs={{0,64},{1,449},{2,66},{3,451},{4,68},{5,453},{6,70},{7,455},{8,72}... | collective-permute-start | bytes 408584 | tf_op jit(solution)/shard_map/ppermute | solution.py:102
  75.3 3.1 %collective-permute-start.6 = (bf16[4,2,14,608]{3,1,2,0:T(2,128)(2,1)S(1)}, bf16[4,2,14,608]{3,1,2,0:T(2,128)(2,1)S(1)}, u32[]{:S(2)}, u32[]{:S(2)}) collective-permute-start(bf16[4,2,14,608]{3,1,2,0:T(2,128)(2,1)S(1)} %collective-permute-done.4), channel_id=1, source_target_pairs={{0,448},{1,65},{2,450},{3,67},{4,452},{5,69},{6,454},{7,71},{8,456... | collective-permute-start | bytes 408584 | tf_op jit(solution)/shard_map/ppermute | solution.py:108
  78.4 0.2 bitcast_dynamic-update-slice_fusion.11
  78.7 0.2 bitcast_dynamic-update-slice_fusion.9
  78.9 3.0 %collective-permute-done.5 = bf16[4,2,14,608]{3,1,2,0:T(2,128)(2,1)S(1)} collective-permute-done((bf16[4,2,14,608]{3,1,2,0:T(2,128)(2,1)S(1)}, bf16[4,2,14,608]{3,1,2,0:T(2,128)(2,1)S(1)}, u32[]{:S(2)}, u32[]{:S(2)}) %collective-permute-start.5) | collective-permute-done | bytes 136224 | tf_op jit(solution)/shard_map/ppermute | solution.py:102
  81.9 4.2 %collective-permute-start.7 = (bf16[4,2,14,608]{3,1,2,0:T(2,128)(2,1)S(1)}, bf16[4,2,14,608]{3,1,2,0:T(2,128)(2,1)S(1)}, u32[]{:S(2)}, u32[]{:S(2)}) collective-permute-start(bf16[4,2,14,608]{3,1,2,0:T(2,128)(2,1)S(1)} %collective-permute-done.5), channel_id=1, source_target_pairs={{0,64},{1,449},{2,66},{3,451},{4,68},{5,453},{6,70},{7,455},{8,72}... | collective-permute-start | bytes 408584 | tf_op jit(solution)/shard_map/ppermute | solution.py:102
  86.1 1.7 %collective-permute-done.6 = bf16[4,2,14,608]{3,1,2,0:T(2,128)(2,1)S(1)} collective-permute-done((bf16[4,2,14,608]{3,1,2,0:T(2,128)(2,1)S(1)}, bf16[4,2,14,608]{3,1,2,0:T(2,128)(2,1)S(1)}, u32[]{:S(2)}, u32[]{:S(2)}) %collective-permute-start.6) | collective-permute-done | bytes 136224 | tf_op jit(solution)/shard_map/ppermute | solution.py:108
  87.8 2.1 %collective-permute-start.8 = (bf16[4,2,14,608]{3,1,2,0:T(2,128)(2,1)S(1)}, bf16[4,2,14,608]{3,1,2,0:T(2,128)(2,1)S(1)}, u32[]{:S(2)}, u32[]{:S(2)}) collective-permute-start(bf16[4,2,14,608]{3,1,2,0:T(2,128)(2,1)S(1)} %collective-permute-done.6), channel_id=1, source_target_pairs={{0,448},{1,65},{2,450},{3,67},{4,452},{5,69},{6,454},{7,71},{8,456... | collective-permute-start | bytes 408584 | tf_op jit(solution)/shard_map/ppermute | solution.py:108
  89.9 0.2 bitcast_dynamic-update-slice_fusion.7
  90.1 0.2 bitcast_dynamic-update-slice_fusion.5
  90.3 2.8 %collective-permute-done.7 = bf16[4,2,14,608]{3,1,2,0:T(2,128)(2,1)S(1)} collective-permute-done((bf16[4,2,14,608]{3,1,2,0:T(2,128)(2,1)S(1)}, bf16[4,2,14,608]{3,1,2,0:T(2,128)(2,1)S(1)}, u32[]{:S(2)}, u32[]{:S(2)}) %collective-permute-start.7) | collective-permute-done | bytes 136224 | tf_op jit(solution)/shard_map/ppermute | solution.py:102
  93.1 0.2 bitcast_dynamic-update-slice_fusion.3
  93.3 4.1 %collective-permute-done.8 = bf16[4,2,14,608]{3,1,2,0:T(2,128)(2,1)S(1)} collective-permute-done((bf16[4,2,14,608]{3,1,2,0:T(2,128)(2,1)S(1)}, bf16[4,2,14,608]{3,1,2,0:T(2,128)(2,1)S(1)}, u32[]{:S(2)}, u32[]{:S(2)}) %collective-permute-start.8) | collective-permute-done | bytes 136224 | tf_op jit(solution)/shard_map/ppermute | solution.py:108
  97.3 0.2 bitcast_dynamic-update-slice_fusion.1
  97.5 0.8 constant_dynamic-slice_fusion
  98.3 5.4 %collective-permute-start.10 = (bf16[4,4,2,14,608]{4,2,3,1,0:T(2,128)(2,1)S(1)}, bf16[4,4,2,14,608]{4,2,3,1,0:T(2,128)(2,1)S(1)}, u32[]{:S(2)}, u32[]{:S(2)}) collective-permute-start(bf16[4,4,2,14,608]{4,2,3,1,0:T(2,128)(2,1)S(1)} %get-tuple-element.15), channel_id=1, source_target_pairs={{0,480},{1,33},{2,482},{3,35},{4,484},{5,37},{6,486},{7,39},{8,488... | collective-permute-start | bytes 1634312 | tf_op jit(solution)/shard_map/ppermute | solution.py:117
  103.7 2.5 %collective-permute-start.9 = (bf16[4,2,14,608]{3,1,2,0:T(2,128)(2,1)S(1)}, bf16[4,2,14,608]{3,1,2,0:T(2,128)(2,1)S(1)}, u32[]{:S(2)}, u32[]{:S(2)}) collective-permute-start(bf16[4,2,14,608]{3,1,2,0:T(2,128)(2,1)S(1)} %collective-permute-done.7), channel_id=1, source_target_pairs={{0,64},{1,449},{2,66},{3,451},{4,68},{5,453},{6,70},{7,455},{8,72}... | collective-permute-start | bytes 408584 | tf_op jit(solution)/shard_map/ppermute | solution.py:102
  106.2 1.4 %multiply_subtract_fusion = (f32[150,896]{1,0:T(8,128)}, f32[150,896]{1,0:T(8,128)}) fusion(f32[150,896]{1,0:T(8,128)S(1)} %copy-done.2, f32[150,896]{1,0:T(8,128)S(1)} %copy-done.3, f32[150,896]{1,0:T(8,128)S(1)} %fusion.7, f32[150,896]{1,0:T(8,128)S(1)} %fusion.6, f32[150,896]{1,0:T(8,128)S(1)} %fusion.5, bf16[150,64]{1,0:T(8,128)(2,1)S(1)} %squeeze.37, ...), kind=kOutput, calls=%fused_computation.12 | convolution fusion | flops 18816000 | bytes 3952640 | tf_op jit(solution)/shard_map/dot_general | solution.py:127
  107.6 3.9 %collective-permute-start.11 = (bf16[4,4,2,14,608]{4,2,3,1,0:T(2,128)(2,1)S(1)}, bf16[4,4,2,14,608]{4,2,3,1,0:T(2,128)(2,1)S(1)}, u32[]{:S(2)}, u32[]{:S(2)}) collective-permute-start(bf16[4,4,2,14,608]{4,2,3,1,0:T(2,128)(2,1)S(1)} %get-tuple-element.14), channel_id=1, source_target_pairs={{0,32},{1,481},{2,34},{3,483},{4,36},{5,485},{6,38},{7,487},{8,40}... | collective-permute-start | bytes 1634312 | tf_op jit(solution)/shard_map/ppermute | solution.py:117
  111.5 1.3 %collective-permute-done.9 = bf16[4,2,14,608]{3,1,2,0:T(2,128)(2,1)S(1)} collective-permute-done((bf16[4,2,14,608]{3,1,2,0:T(2,128)(2,1)S(1)}, bf16[4,2,14,608]{3,1,2,0:T(2,128)(2,1)S(1)}, u32[]{:S(2)}, u32[]{:S(2)}) %collective-permute-start.9) | collective-permute-done | bytes 136224 | tf_op jit(solution)/shard_map/ppermute | solution.py:102
  113.0 4.3 %collective-permute-done.10 = bf16[4,4,2,14,608]{4,2,3,1,0:T(2,128)(2,1)S(1)} collective-permute-done((bf16[4,4,2,14,608]{4,2,3,1,0:T(2,128)(2,1)S(1)}, bf16[4,4,2,14,608]{4,2,3,1,0:T(2,128)(2,1)S(1)}, u32[]{:S(2)}, u32[]{:S(2)}) %collective-permute-start.10) | collective-permute-done | bytes 544800 | tf_op jit(solution)/shard_map/ppermute | solution.py:117
  117.4 0.1 slice_dynamic-update-slice_fusion.6
  117.5 0.1 slice_dynamic-update-slice_fusion.5
  117.6 0.1 slice_dynamic-update-slice_fusion.4
  117.8 2.6 %collective-permute-done.11 = bf16[4,4,2,14,608]{4,2,3,1,0:T(2,128)(2,1)S(1)} collective-permute-done((bf16[4,4,2,14,608]{4,2,3,1,0:T(2,128)(2,1)S(1)}, bf16[4,4,2,14,608]{4,2,3,1,0:T(2,128)(2,1)S(1)}, u32[]{:S(2)}, u32[]{:S(2)}) %collective-permute-start.11) | collective-permute-done | bytes 544800 | tf_op jit(solution)/shard_map/ppermute | solution.py:117
  120.5 0.1 slice_dynamic-update-slice_fusion.2
  120.6 0.1 slice_dynamic-update-slice_fusion.1
  120.8 0.1 slice_dynamic-update-slice_fusion
  120.9 5.7 %copy.31 = bf16[2,896,608]{1,2,0:T(8,128)(2,1)} copy(bf16[2,896,608]{2,0,1:T(2,128)(2,1)S(1)} %bitcast.47) | data formatting | bytes 4358144
  (44 shorter events, 1.6 us)
Async XLA Ops:
  0.6 2.6 %copy-start = (bf16[1,64,896]{2,1,0:T(8,128)(2,1)S(1)}, bf16[1,64,896]{2,1,0:T(8,128)(2,1)}, u32[]{:S(2)}) copy-start(bf16[1,64,896]{2,1,0:T(8,128)(2,1)} %param.9) | copy-start | bytes 344068
  0.6 39.2 %copy-start.4 = (f32[2,14,608]{2,0,1:T(2,128)S(1)}, f32[2,14,608]{2,0,1:T(2,128)}, u32[]{:S(2)}) copy-start(f32[2,14,608]{2,0,1:T(2,128)} %param.11) | copy-start | bytes 204292
  0.7 39.2 %copy-start.5 = (f32[2,14,608]{2,0,1:T(2,128)S(1)}, f32[2,14,608]{2,0,1:T(2,128)}, u32[]{:S(2)}) copy-start(f32[2,14,608]{2,0,1:T(2,128)} %param.10) | copy-start | bytes 204292
  5.2 34.2 %all-to-all-start = ((bf16[4,2,20480]{2,1,0:T(2,128)(2,1)}), bf16[4,2,20480]{2,1,0:T(2,128)(2,1)S(1)}, u32[]{:S(2)}, u32[]{:S(2)}) async-start(bf16[4,2,20480]{2,1,0:T(2,128)(2,1)} %concatenate.6), calls=%async_computation | async-start | bytes 655360 | tf_op jit(solution)/shard_map/all_to_all | solution.py:41
  40.2 13.3 %collective-permute-start = (bf16[2,37184]{1,0:T(2,128)(2,1)S(1)}, bf16[2,37184]{1,0:T(2,128)(2,1)S(1)}, u32[]{:S(2)}, u32[]{:S(2)}) collective-permute-start(bf16[2,37184]{1,0:T(2,128)(2,1)S(1)} %pad_maximum_fusion), channel_id=1, source_target_pairs={{0,8},{1,25},{2,10},{3,27},{4,12},{5,29},{6,14},{7,31},{8,16},{9,1... | collective-permute-start | bytes 446216 | tf_op jit(solution)/shard_map/ppermute | solution.py:72
  43.7 9.9 %collective-permute-start.1 = (bf16[2,37184]{1,0:T(2,128)(2,1)S(1)}, bf16[2,37184]{1,0:T(2,128)(2,1)S(1)}, u32[]{:S(2)}, u32[]{:S(2)}) collective-permute-start(bf16[2,37184]{1,0:T(2,128)(2,1)S(1)} %pad_maximum_fusion), channel_id=1, source_target_pairs={{0,24},{1,9},{2,26},{3,11},{4,28},{5,13},{6,30},{7,15},{8,0},{9,17... | collective-permute-start | bytes 446216 | tf_op jit(solution)/shard_map/ppermute | solution.py:72
  47.3 8.6 %collective-permute-start.2 = (bf16[2,37184]{1,0:T(2,128)(2,1)S(1)}, bf16[2,37184]{1,0:T(2,128)(2,1)S(1)}, u32[]{:S(2)}, u32[]{:S(2)}) collective-permute-start(bf16[2,37184]{1,0:T(2,128)(2,1)S(1)} %pad_maximum_fusion), channel_id=1, source_target_pairs={{0,16},{1,17},{2,18},{3,19},{4,20},{5,21},{6,22},{7,23},{8,24},{9,... | collective-permute-start | bytes 446216 | tf_op jit(solution)/shard_map/ppermute | solution.py:72
  56.1 14.3 %collective-permute-start.3 = (bf16[4,2,14,608]{3,1,2,0:T(2,128)(2,1)S(1)}, bf16[4,2,14,608]{3,1,2,0:T(2,128)(2,1)S(1)}, u32[]{:S(2)}, u32[]{:S(2)}) collective-permute-start(bf16[4,2,14,608]{3,1,2,0:T(2,128)(2,1)S(1)} %copy_dynamic-update-slice_fusion), channel_id=1, source_target_pairs={{0,64},{1,449},{2,66},{3,451},{4,68},{5,453},{6,70},{7,455},{8,72}... | collective-permute-start | bytes 408584 | tf_op jit(solution)/shard_map/ppermute | solution.py:102
  63.8 11.4 %collective-permute-start.4 = (bf16[4,2,14,608]{3,1,2,0:T(2,128)(2,1)S(1)}, bf16[4,2,14,608]{3,1,2,0:T(2,128)(2,1)S(1)}, u32[]{:S(2)}, u32[]{:S(2)}) collective-permute-start(bf16[4,2,14,608]{3,1,2,0:T(2,128)(2,1)S(1)} %copy_dynamic-update-slice_fusion), channel_id=1, source_target_pairs={{0,448},{1,65},{2,450},{3,67},{4,452},{5,69},{6,454},{7,71},{8,456... | collective-permute-start | bytes 408584 | tf_op jit(solution)/shard_map/ppermute | solution.py:108
  68.5 10.0 %copy-start.1 = (bf16[9,4,2,14,608]{4,2,3,1,0:T(2,128)(2,1)S(1)}, bf16[9,4,2,14,608]{4,2,3,1,0:T(2,128)(2,1)}, u32[]{:S(2)}) copy-start(bf16[9,4,2,14,608]{4,2,3,1,0:T(2,128)(2,1)} %dynamic_update_slice.109) | copy-start | bytes 3677188
  70.4 11.5 %collective-permute-start.5 = (bf16[4,2,14,608]{3,1,2,0:T(2,128)(2,1)S(1)}, bf16[4,2,14,608]{3,1,2,0:T(2,128)(2,1)S(1)}, u32[]{:S(2)}, u32[]{:S(2)}) collective-permute-start(bf16[4,2,14,608]{3,1,2,0:T(2,128)(2,1)S(1)} %collective-permute-done.3), channel_id=1, source_target_pairs={{0,64},{1,449},{2,66},{3,451},{4,68},{5,453},{6,70},{7,455},{8,72}... | collective-permute-start | bytes 408584 | tf_op jit(solution)/shard_map/ppermute | solution.py:102
  75.3 12.5 %collective-permute-start.6 = (bf16[4,2,14,608]{3,1,2,0:T(2,128)(2,1)S(1)}, bf16[4,2,14,608]{3,1,2,0:T(2,128)(2,1)S(1)}, u32[]{:S(2)}, u32[]{:S(2)}) collective-permute-start(bf16[4,2,14,608]{3,1,2,0:T(2,128)(2,1)S(1)} %collective-permute-done.4), channel_id=1, source_target_pairs={{0,448},{1,65},{2,450},{3,67},{4,452},{5,69},{6,454},{7,71},{8,456... | collective-permute-start | bytes 408584 | tf_op jit(solution)/shard_map/ppermute | solution.py:108
  78.6 27.6 %copy-start.2 = (f32[150,896]{1,0:T(8,128)S(1)}, f32[150,896]{1,0:T(8,128)}, u32[]{:S(2)}) copy-start(f32[150,896]{1,0:T(8,128)} %param.12) | copy-start | bytes 1612804
  78.6 27.6 %copy-start.3 = (f32[150,896]{1,0:T(8,128)S(1)}, f32[150,896]{1,0:T(8,128)}, u32[]{:S(2)}) copy-start(f32[150,896]{1,0:T(8,128)} %param.13) | copy-start | bytes 1612804
  81.9 11.2 %collective-permute-start.7 = (bf16[4,2,14,608]{3,1,2,0:T(2,128)(2,1)S(1)}, bf16[4,2,14,608]{3,1,2,0:T(2,128)(2,1)S(1)}, u32[]{:S(2)}, u32[]{:S(2)}) collective-permute-start(bf16[4,2,14,608]{3,1,2,0:T(2,128)(2,1)S(1)} %collective-permute-done.5), channel_id=1, source_target_pairs={{0,64},{1,449},{2,66},{3,451},{4,68},{5,453},{6,70},{7,455},{8,72}... | collective-permute-start | bytes 408584 | tf_op jit(solution)/shard_map/ppermute | solution.py:102
  87.8 9.5 %collective-permute-start.8 = (bf16[4,2,14,608]{3,1,2,0:T(2,128)(2,1)S(1)}, bf16[4,2,14,608]{3,1,2,0:T(2,128)(2,1)S(1)}, u32[]{:S(2)}, u32[]{:S(2)}) collective-permute-start(bf16[4,2,14,608]{3,1,2,0:T(2,128)(2,1)S(1)} %collective-permute-done.6), channel_id=1, source_target_pairs={{0,448},{1,65},{2,450},{3,67},{4,452},{5,69},{6,454},{7,71},{8,456... | collective-permute-start | bytes 408584 | tf_op jit(solution)/shard_map/ppermute | solution.py:108
  98.3 18.9 %collective-permute-start.10 = (bf16[4,4,2,14,608]{4,2,3,1,0:T(2,128)(2,1)S(1)}, bf16[4,4,2,14,608]{4,2,3,1,0:T(2,128)(2,1)S(1)}, u32[]{:S(2)}, u32[]{:S(2)}) collective-permute-start(bf16[4,4,2,14,608]{4,2,3,1,0:T(2,128)(2,1)S(1)} %get-tuple-element.15), channel_id=1, source_target_pairs={{0,480},{1,33},{2,482},{3,35},{4,484},{5,37},{6,486},{7,39},{8,488... | collective-permute-start | bytes 1634312 | tf_op jit(solution)/shard_map/ppermute | solution.py:117
  103.7 9.1 %collective-permute-start.9 = (bf16[4,2,14,608]{3,1,2,0:T(2,128)(2,1)S(1)}, bf16[4,2,14,608]{3,1,2,0:T(2,128)(2,1)S(1)}, u32[]{:S(2)}, u32[]{:S(2)}) collective-permute-start(bf16[4,2,14,608]{3,1,2,0:T(2,128)(2,1)S(1)} %collective-permute-done.7), channel_id=1, source_target_pairs={{0,64},{1,449},{2,66},{3,451},{4,68},{5,453},{6,70},{7,455},{8,72}... | collective-permute-start | bytes 408584 | tf_op jit(solution)/shard_map/ppermute | solution.py:102
  107.6 12.8 %collective-permute-start.11 = (bf16[4,4,2,14,608]{4,2,3,1,0:T(2,128)(2,1)S(1)}, bf16[4,4,2,14,608]{4,2,3,1,0:T(2,128)(2,1)S(1)}, u32[]{:S(2)}, u32[]{:S(2)}) collective-permute-start(bf16[4,4,2,14,608]{4,2,3,1,0:T(2,128)(2,1)S(1)} %get-tuple-element.14), channel_id=1, source_target_pairs={{0,32},{1,481},{2,34},{3,483},{4,36},{5,485},{6,38},{7,487},{8,40}... | collective-permute-start | bytes 1634312 | tf_op jit(solution)/shard_map/ppermute | solution.py:117

commit v14 on v13

--- a/solution.py
+++ b/solution.py
@@ -122,10 +122,10 @@
     layer_blocks = jnp.moveaxis(out, 2, 0).reshape(piece.shape[0], -1, piece.shape[2])
 
     lefts = received(nlayer, nleft).reshape((groups,) + left.shape[1:])
-    total = jnp.zeros(emb_weight.shape, f32)
-    for g in range(groups):
-        product = jnp.dot(lefts[g], rights[g], preferred_element_type=f32).astype(bf16)
-        total = total + product.astype(f32)
+    products = jnp.einsum("gvr,grd->gvd", lefts, rights, preferred_element_type=f32).astype(bf16)
+    total = products[0].astype(f32)
+    for g in range(1, groups):
+        total = total + products[g].astype(f32)
     emb_mean = total / groups
     new_emb_momentum = beta_outer * emb_momentum + emb_mean
     new_emb_weight = emb_weight - rate_outer * (emb_mean + beta_outer * new_emb_momentum)

time: 127 us -> 130 us (1.024)
  local copies, waits for them, and re-layouts: 20.5 us -> 27 us
  waiting for transfers between devices: 40.9 us -> 35.3 us
  starting transfers between devices: 61.6 us -> 63.4 us
  matrix products: 1.98 us -> 0.47 us
    dynamic_update_slice x3, local copies, waits for them, and re-layouts: 0.58 us -> 3.39 us  [on_device(): rel = lax.dynamic_update_index_in_dim(rel, fwd, j + reach, axis=0)]
    dynamic_update_slice x3, local copies, waits for them, and re-layouts: 0.58 us -> 3.38 us  [on_device(): rel = lax.dynamic_update_index_in_dim(rel, bwd, reach - j, axis=0)]
    ppermute x3, waiting for transfers between devices: 5.74 us -> 2.95 us  [on_device(): bwd = lax.ppermute(bwd, axes, zshift(-2))]
    ppermute x4, waiting for transfers between devices: 7.19 us -> 5.11 us  [on_device(): fwd = lax.ppermute(fwd, axes, zshift(2))]
    dot_general x4 -> x1, matrix products: 1.98 us -> 0.47 us  [on_device(): jnp.einsum('gvr,grd->gvd', lefts, rights, preferred_element_type=f32)]
    unnamed x16 -> x14, local copies, waits for them, and re-layouts: 8.18 us -> 8.17 us
  transfers between devices with their start and end apart: 13 -> 13, of which waited for: 9 -> 8; matrix products, arithmetic and copies ran while one was open for 8% -> 11% of each run, Pallas kernels for 0% -> 0%
where the time goes in v14:
time: 130 us; the launch traced here: 129 us
  starting transfers between devices  63.4 us (49%)
  waiting for transfers between devices  35.3 us (27%)
  local copies, waits for them, and re-layouts  27 us (21%)
  other arithmetic  1.65 us (1%)
    ppermute x4, starting transfers between devices, on_device(): fwd = lax.ppermute(fwd, axes, zshift(2))  19.3 us
    all_to_all x1, waiting for transfers between devices, on_device(): recv_halves = lax.all_to_all(send, 'group', 0, 0, tiled=True)  19.1 us
    all_to_all x1, starting transfers between devices, on_device(): recv_halves = lax.all_to_all(send, 'group', 0, 0, tiled=True)  15.1 us
    ppermute x3, starting transfers between devices, on_device(): got = lax.ppermute(payload, ('shard', 'tensor'), yshift(k))  10.9 us
    ppermute x2, starting transfers between devices, on_device(): got = lax.ppermute(part, axes, zshift(k))  9.92 us
    unnamed x14, local copies, waits for them, and re-layouts  8.17 us
    ppermute x3, starting transfers between devices, on_device(): bwd = lax.ppermute(bwd, axes, zshift(-2))  8.17 us
    ppermute x2, waiting for transfers between devices, on_device(): got = lax.ppermute(part, axes, zshift(k))  5.77 us
  transfers between devices with their start and end apart: 13, of which 8 were waited for; matrix products, arithmetic and copies ran while one was open for 11% of the time, Pallas kernels for 0%

profile of v14, /device:TPU:6, one launch (start us, length us, event | category | flops | bytes accessed | tf_op | source)
XLA Modules:
  0.0 128.9 jit_solution(17442936515943431401)
XLA Ops:
  0.7 1.0 copy.21
  1.7 0.3 reshape_reshape.12
  1.9 1.1 copy.22
  3.0 0.2 reshape_reshape_squeeze.3
  3.3 1.9 %concatenate.6 = bf16[4,2,20480]{2,1,0:T(2,128)(2,1)} concatenate(bf16[4,2,8512]{2,1,0:T(2,128)(2,1)S(1)} %reshape_reshape.12, bf16[4,2,4800]{2,1,0:T(2,128)(2,1)S(1)} %reshape_reshape_squeeze.3, bf16[4,2,7168]{2,1,0:T(2,128)(2,1)S(1)} %broadcast_in_dim.73), dimensions={2} | concatenate | bytes 655360 | tf_op jit(solution)/shard_map/concatenate | solution.py:40
  5.2 15.1 %all-to-all-start = ((bf16[4,2,20480]{2,1,0:T(2,128)(2,1)}), bf16[4,2,20480]{2,1,0:T(2,128)(2,1)S(1)}, u32[]{:S(2)}, u32[]{:S(2)}) async-start(bf16[4,2,20480]{2,1,0:T(2,128)(2,1)} %concatenate.6), calls=%async_computation | async-start | bytes 655360 | tf_op jit(solution)/shard_map/all_to_all | solution.py:41
  20.3 19.1 %all-to-all-done = bf16[4,2,20480]{2,1,0:T(2,128)(2,1)S(1)} async-done(((bf16[4,2,20480]{2,1,0:T(2,128)(2,1)}), bf16[4,2,20480]{2,1,0:T(2,128)(2,1)S(1)}, u32[]{:S(2)}, u32[]{:S(2)}) %all-to-all-start) | async-done | bytes 327712 | tf_op jit(solution)/shard_map/all_to_all | solution.py:41
  39.3 0.1 convert_reduce_fusion
  39.5 0.1 div.38
  39.6 0.1 slice.85
  39.9 0.1 reshape.54
  40.0 0.2 pad_maximum_fusion
  40.2 3.5 %collective-permute-start = (bf16[2,37184]{1,0:T(2,128)(2,1)S(1)}, bf16[2,37184]{1,0:T(2,128)(2,1)S(1)}, u32[]{:S(2)}, u32[]{:S(2)}) collective-permute-start(bf16[2,37184]{1,0:T(2,128)(2,1)S(1)} %pad_maximum_fusion), channel_id=1, source_target_pairs={{0,8},{1,25},{2,10},{3,27},{4,12},{5,29},{6,14},{7,31},{8,16},{9,1... | collective-permute-start | bytes 446216 | tf_op jit(solution)/shard_map/ppermute | solution.py:72
  43.7 3.6 %collective-permute-start.1 = (bf16[2,37184]{1,0:T(2,128)(2,1)S(1)}, bf16[2,37184]{1,0:T(2,128)(2,1)S(1)}, u32[]{:S(2)}, u32[]{:S(2)}) collective-permute-start(bf16[2,37184]{1,0:T(2,128)(2,1)S(1)} %pad_maximum_fusion), channel_id=1, source_target_pairs={{0,24},{1,9},{2,26},{3,11},{4,28},{5,13},{6,30},{7,15},{8,0},{9,17... | collective-permute-start | bytes 446216 | tf_op jit(solution)/shard_map/ppermute | solution.py:72
  47.3 3.9 %collective-permute-start.2 = (bf16[2,37184]{1,0:T(2,128)(2,1)S(1)}, bf16[2,37184]{1,0:T(2,128)(2,1)S(1)}, u32[]{:S(2)}, u32[]{:S(2)}) collective-permute-start(bf16[2,37184]{1,0:T(2,128)(2,1)S(1)} %pad_maximum_fusion), channel_id=1, source_target_pairs={{0,16},{1,17},{2,18},{3,19},{4,20},{5,21},{6,22},{7,23},{8,24},{9,... | collective-permute-start | bytes 446216 | tf_op jit(solution)/shard_map/ppermute | solution.py:72
  51.4 0.7 copy.30
  52.1 0.7 copy.31
  52.7 0.2 slice.97
  52.9 0.2 reshape_reshape.14
  53.2 0.1 broadcast_in_dim.77
  53.3 0.1 broadcast_in_dim.78
  53.5 2.4 %collective-permute-done.2 = bf16[2,37184]{1,0:T(2,128)(2,1)S(1)} collective-permute-done((bf16[2,37184]{1,0:T(2,128)(2,1)S(1)}, bf16[2,37184]{1,0:T(2,128)(2,1)S(1)}, u32[]{:S(2)}, u32[]{:S(2)}) %collective-permute-start.2) | collective-permute-done | bytes 148768 | tf_op jit(solution)/shard_map/ppermute | solution.py:72
  55.9 0.1 broadcast_in_dim.79
  56.1 7.7 %collective-permute-start.3 = (bf16[4,2,14,608]{3,1,2,0:T(2,128)(2,1)S(1)}, bf16[4,2,14,608]{3,1,2,0:T(2,128)(2,1)}, u32[]{:S(2)}, u32[]{:S(2)}) collective-permute-start(bf16[4,2,14,608]{3,1,2,0:T(2,128)(2,1)S(1)} %copy_dynamic-update-slice_fusion), channel_id=1, source_target_pairs={{0,64},{1,449},{2,66},{3,451},{4,68},{5,453},{6,70},{7,455},{8,72}... | collective-permute-start | bytes 408584 | tf_op jit(solution)/shard_map/ppermute | solution.py:102
  63.8 1.9 %collective-permute-start.4 = (bf16[4,2,14,608]{3,1,2,0:T(2,128)(2,1)S(1)}, bf16[4,2,14,608]{3,1,2,0:T(2,128)(2,1)}, u32[]{:S(2)}, u32[]{:S(2)}) collective-permute-start(bf16[4,2,14,608]{3,1,2,0:T(2,128)(2,1)S(1)} %copy_dynamic-update-slice_fusion), channel_id=1, source_target_pairs={{0,448},{1,65},{2,450},{3,67},{4,452},{5,69},{6,454},{7,71},{8,456... | collective-permute-start | bytes 408584 | tf_op jit(solution)/shard_map/ppermute | solution.py:108
  65.8 0.2 slice.98
  66.0 0.1 reshape.56
  66.1 0.2 slice.99
  66.3 1.2 broadcast_in_dim.74
  67.5 0.1 constant_dynamic-update-slice_fusion.4
  67.7 1.8 %dynamic_update_slice.109 = bf16[9,4,2,14,608]{4,2,3,1,0:T(2,128)(2,1)} pad(bf16[1,4,2,14,608]{4,2,3,1,0:T(2,128)(2,1)S(1)} %bitcast.40, bf16[]{:T(256)} %constant.247.clone.1), padding=4_4x0_0x0_0x0_0x0_0 | pad | bytes 1361922 | tf_op jit(solution)/shard_map/jit(dynamic_update_index_in_dim)/dynamic_update_slice | solution.py:97
  69.5 0.2 slice.100
  69.8 4.8 %collective-permute-start.5 = (bf16[4,2,14,608]{3,1,2,0:T(2,128)(2,1)}, bf16[4,2,14,608]{3,1,2,0:T(2,128)(2,1)S(1)}, u32[]{:S(2)}, u32[]{:S(2)}) collective-permute-start(bf16[4,2,14,608]{3,1,2,0:T(2,128)(2,1)} %collective-permute-done.3), channel_id=1, source_target_pairs={{0,64},{1,449},{2,66},{3,451},{4,68},{5,453},{6,70},{7,455},{8,72}... | collective-permute-start | bytes 408584 | tf_op jit(solution)/shard_map/ppermute | solution.py:102
  74.6 3.1 %collective-permute-start.6 = (bf16[4,2,14,608]{3,1,2,0:T(2,128)(2,1)}, bf16[4,2,14,608]{3,1,2,0:T(2,128)(2,1)S(1)}, u32[]{:S(2)}, u32[]{:S(2)}) collective-permute-start(bf16[4,2,14,608]{3,1,2,0:T(2,128)(2,1)} %collective-permute-done.4), channel_id=1, source_target_pairs={{0,448},{1,65},{2,450},{3,67},{4,452},{5,69},{6,454},{7,71},{8,456... | collective-permute-start | bytes 408584 | tf_op jit(solution)/shard_map/ppermute | solution.py:108
  77.8 1.7 %bitcast_dynamic-update-slice_fusion.11 = (bf16[9,4,2,14,608]{4,2,3,1,0:T(2,128)(2,1)}, bf16[16,4,2,14,608]{4,2,3,1,0:T(2,128)(2,1)S(1)}) fusion(bf16[9,4,2,14,608]{4,2,3,1,0:T(2,128)(2,1)} %dynamic_update_slice.109, s32[]{:T(128)S(6)} %select_n.223, bf16[4,2,14,608]{3,1,2,0:T(2,128)(2,1)} %collective-permute-done.3, ...), kind=kLoop, calls=%fused_computation.27 | loop fusion | bytes 430088 | tf_op jit(solution)/shard_map/jit(dynamic_update_index_in_dim)/dynamic_update_slice | solution.py:106
  79.5 1.7 %bitcast_dynamic-update-slice_fusion.9 = (bf16[9,4,2,14,608]{4,2,3,1,0:T(2,128)(2,1)}, bf16[16,4,2,14,608]{4,2,3,1,0:T(2,128)(2,1)S(1)}) fusion(bf16[9,4,2,14,608]{4,2,3,1,0:T(2,128)(2,1)} %get-tuple-element.27, s32[]{:T(128)S(6)} %select_n.224, bf16[4,2,14,608]{3,1,2,0:T(2,128)(2,1)} %collective-permute-done.4, ...), kind=kLoop, calls=%fused_computation.25 | loop fusion | bytes 430088 | tf_op jit(solution)/shard_map/jit(dynamic_update_index_in_dim)/dynamic_update_slice | solution.py:110
  81.2 0.2 collective-permute-done.5
  81.5 4.8 %collective-permute-start.7 = (bf16[4,2,14,608]{3,1,2,0:T(2,128)(2,1)S(1)}, bf16[4,2,14,608]{3,1,2,0:T(2,128)(2,1)S(1)}, u32[]{:S(2)}, u32[]{:S(2)}) collective-permute-start(bf16[4,2,14,608]{3,1,2,0:T(2,128)(2,1)S(1)} %collective-permute-done.5), channel_id=1, source_target_pairs={{0,64},{1,449},{2,66},{3,451},{4,68},{5,453},{6,70},{7,455},{8,72}... | collective-permute-start | bytes 408584 | tf_op jit(solution)/shard_map/ppermute | solution.py:102
  86.3 3.1 %collective-permute-start.8 = (bf16[4,2,14,608]{3,1,2,0:T(2,128)(2,1)S(1)}, bf16[4,2,14,608]{3,1,2,0:T(2,128)(2,1)S(1)}, u32[]{:S(2)}, u32[]{:S(2)}) collective-permute-start(bf16[4,2,14,608]{3,1,2,0:T(2,128)(2,1)S(1)} %collective-permute-done.6), channel_id=1, source_target_pairs={{0,448},{1,65},{2,450},{3,67},{4,452},{5,69},{6,454},{7,71},{8,456... | collective-permute-start | bytes 408584 | tf_op jit(solution)/shard_map/ppermute | solution.py:108
  89.4 0.8 bitcast_dynamic-update-slice_fusion.7
  90.3 0.8 bitcast_dynamic-update-slice_fusion.5
  91.1 2.4 %collective-permute-done.7 = bf16[4,2,14,608]{3,1,2,0:T(2,128)(2,1)S(1)} collective-permute-done((bf16[4,2,14,608]{3,1,2,0:T(2,128)(2,1)S(1)}, bf16[4,2,14,608]{3,1,2,0:T(2,128)(2,1)S(1)}, u32[]{:S(2)}, u32[]{:S(2)}) %collective-permute-start.7) | collective-permute-done | bytes 136224 | tf_op jit(solution)/shard_map/ppermute | solution.py:102
  93.5 0.8 bitcast_dynamic-update-slice_fusion.3
  94.3 2.9 %collective-permute-done.8 = bf16[4,2,14,608]{3,1,2,0:T(2,128)(2,1)S(1)} collective-permute-done((bf16[4,2,14,608]{3,1,2,0:T(2,128)(2,1)S(1)}, bf16[4,2,14,608]{3,1,2,0:T(2,128)(2,1)S(1)}, u32[]{:S(2)}, u32[]{:S(2)}) %collective-permute-start.8) | collective-permute-done | bytes 136224 | tf_op jit(solution)/shard_map/ppermute | solution.py:108
  97.3 0.8 bitcast_dynamic-update-slice_fusion.1
  98.1 2.0 %constant_dynamic-slice_fusion = (bf16[4,4,2,14,608]{4,2,3,1,0:T(2,128)(2,1)S(1)}, bf16[4,4,2,14,608]{4,2,3,1,0:T(2,128)(2,1)S(1)}) fusion(bf16[9,4,2,14,608]{4,2,3,1,0:T(2,128)(2,1)} %get-tuple-element.17, s32[]{:T(128)S(6)} %select_n.240, s32[]{:T(128)S(6)} %select_n.230), kind=kLoop, calls=%fused_computation.41 | loop fusion | bytes 2179080 | tf_op jit(solution)/shard_map/dynamic_slice | solution.py:116
  100.1 6.0 %collective-permute-start.10 = (bf16[4,4,2,14,608]{4,2,3,1,0:T(2,128)(2,1)S(1)}, bf16[4,4,2,14,608]{4,2,3,1,0:T(2,128)(2,1)S(1)}, u32[]{:S(2)}, u32[]{:S(2)}) collective-permute-start(bf16[4,4,2,14,608]{4,2,3,1,0:T(2,128)(2,1)S(1)} %get-tuple-element.15), channel_id=1, source_target_pairs={{0,480},{1,33},{2,482},{3,35},{4,484},{5,37},{6,486},{7,39},{8,488... | collective-permute-start | bytes 1634312 | tf_op jit(solution)/shard_map/ppermute | solution.py:117
  106.1 0.5 convolution_convert_fusion
  106.6 2.0 %collective-permute-start.9 = (bf16[4,2,14,608]{3,1,2,0:T(2,128)(2,1)S(1)}, bf16[4,2,14,608]{3,1,2,0:T(2,128)(2,1)S(1)}, u32[]{:S(2)}, u32[]{:S(2)}) collective-permute-start(bf16[4,2,14,608]{3,1,2,0:T(2,128)(2,1)S(1)} %collective-permute-done.7), channel_id=1, source_target_pairs={{0,64},{1,449},{2,66},{3,451},{4,68},{5,453},{6,70},{7,455},{8,72}... | collective-permute-start | bytes 408584 | tf_op jit(solution)/shard_map/ppermute | solution.py:102
  108.6 1.3 fusion.1
  109.9 3.9 %collective-permute-start.11 = (bf16[4,4,2,14,608]{4,2,3,1,0:T(2,128)(2,1)S(1)}, bf16[4,4,2,14,608]{4,2,3,1,0:T(2,128)(2,1)S(1)}, u32[]{:S(2)}, u32[]{:S(2)}) collective-permute-start(bf16[4,4,2,14,608]{4,2,3,1,0:T(2,128)(2,1)S(1)} %get-tuple-element.14), channel_id=1, source_target_pairs={{0,32},{1,481},{2,34},{3,483},{4,36},{5,485},{6,38},{7,487},{8,40}... | collective-permute-start | bytes 1634312 | tf_op jit(solution)/shard_map/ppermute | solution.py:117
  113.8 2.5 %collective-permute-done.9 = bf16[4,2,14,608]{3,1,2,0:T(2,128)(2,1)S(1)} collective-permute-done((bf16[4,2,14,608]{3,1,2,0:T(2,128)(2,1)S(1)}, bf16[4,2,14,608]{3,1,2,0:T(2,128)(2,1)S(1)}, u32[]{:S(2)}, u32[]{:S(2)}) %collective-permute-start.9) | collective-permute-done | bytes 136224 | tf_op jit(solution)/shard_map/ppermute | solution.py:102
  116.3 0.1 bitcast_dynamic-update-slice_fusion
  116.4 3.9 %collective-permute-done.10 = bf16[4,4,2,14,608]{4,2,3,1,0:T(2,128)(2,1)S(1)} collective-permute-done((bf16[4,4,2,14,608]{4,2,3,1,0:T(2,128)(2,1)S(1)}, bf16[4,4,2,14,608]{4,2,3,1,0:T(2,128)(2,1)S(1)}, u32[]{:S(2)}, u32[]{:S(2)}) %collective-permute-start.10) | collective-permute-done | bytes 544800 | tf_op jit(solution)/shard_map/ppermute | solution.py:117
  120.3 0.1 slice_dynamic-update-slice_fusion.7
  120.4 0.1 slice_dynamic-update-slice_fusion.6
  120.6 0.1 slice_dynamic-update-slice_fusion.5
  120.7 0.1 slice_dynamic-update-slice_fusion.4
  120.8 1.8 %collective-permute-done.11 = bf16[4,4,2,14,608]{4,2,3,1,0:T(2,128)(2,1)S(1)} collective-permute-done((bf16[4,4,2,14,608]{4,2,3,1,0:T(2,128)(2,1)S(1)}, bf16[4,4,2,14,608]{4,2,3,1,0:T(2,128)(2,1)S(1)}, u32[]{:S(2)}, u32[]{:S(2)}) %collective-permute-start.11) | collective-permute-done | bytes 544800 | tf_op jit(solution)/shard_map/ppermute | solution.py:117
  122.7 0.1 slice_dynamic-update-slice_fusion.3
  122.8 0.1 slice_dynamic-update-slice_fusion.2
  122.9 0.1 slice_dynamic-update-slice_fusion.1
  123.1 0.1 slice_dynamic-update-slice_fusion
  123.2 5.7 %copy.32 = bf16[2,896,608]{1,2,0:T(8,128)(2,1)} copy(bf16[2,896,608]{2,0,1:T(2,128)(2,1)S(1)} %bitcast.39) | data formatting | bytes 4358144
  (37 shorter events, 1.0 us)
Async XLA Ops:
  0.6 2.6 %copy-start = (bf16[1,64,896]{2,1,0:T(8,128)(2,1)S(1)}, bf16[1,64,896]{2,1,0:T(8,128)(2,1)}, u32[]{:S(2)}) copy-start(bf16[1,64,896]{2,1,0:T(8,128)(2,1)} %param.9) | copy-start | bytes 344068
  0.6 39.2 %copy-start.3 = (f32[2,14,608]{2,0,1:T(2,128)S(1)}, f32[2,14,608]{2,0,1:T(2,128)}, u32[]{:S(2)}) copy-start(f32[2,14,608]{2,0,1:T(2,128)} %param.11) | copy-start | bytes 204292
  0.7 39.2 %copy-start.4 = (f32[2,14,608]{2,0,1:T(2,128)S(1)}, f32[2,14,608]{2,0,1:T(2,128)}, u32[]{:S(2)}) copy-start(f32[2,14,608]{2,0,1:T(2,128)} %param.10) | copy-start | bytes 204292
  5.2 34.2 %all-to-all-start = ((bf16[4,2,20480]{2,1,0:T(2,128)(2,1)}), bf16[4,2,20480]{2,1,0:T(2,128)(2,1)S(1)}, u32[]{:S(2)}, u32[]{:S(2)}) async-start(bf16[4,2,20480]{2,1,0:T(2,128)(2,1)} %concatenate.6), calls=%async_computation | async-start | bytes 655360 | tf_op jit(solution)/shard_map/all_to_all | solution.py:41
  40.2 12.9 %collective-permute-start = (bf16[2,37184]{1,0:T(2,128)(2,1)S(1)}, bf16[2,37184]{1,0:T(2,128)(2,1)S(1)}, u32[]{:S(2)}, u32[]{:S(2)}) collective-permute-start(bf16[2,37184]{1,0:T(2,128)(2,1)S(1)} %pad_maximum_fusion), channel_id=1, source_target_pairs={{0,8},{1,25},{2,10},{3,27},{4,12},{5,29},{6,14},{7,31},{8,16},{9,1... | collective-permute-start | bytes 446216 | tf_op jit(solution)/shard_map/ppermute | solution.py:72
  43.7 9.6 %collective-permute-start.1 = (bf16[2,37184]{1,0:T(2,128)(2,1)S(1)}, bf16[2,37184]{1,0:T(2,128)(2,1)S(1)}, u32[]{:S(2)}, u32[]{:S(2)}) collective-permute-start(bf16[2,37184]{1,0:T(2,128)(2,1)S(1)} %pad_maximum_fusion), channel_id=1, source_target_pairs={{0,24},{1,9},{2,26},{3,11},{4,28},{5,13},{6,30},{7,15},{8,0},{9,17... | collective-permute-start | bytes 446216 | tf_op jit(solution)/shard_map/ppermute | solution.py:72
  47.3 8.6 %collective-permute-start.2 = (bf16[2,37184]{1,0:T(2,128)(2,1)S(1)}, bf16[2,37184]{1,0:T(2,128)(2,1)S(1)}, u32[]{:S(2)}, u32[]{:S(2)}) collective-permute-start(bf16[2,37184]{1,0:T(2,128)(2,1)S(1)} %pad_maximum_fusion), channel_id=1, source_target_pairs={{0,16},{1,17},{2,18},{3,19},{4,20},{5,21},{6,22},{7,23},{8,24},{9,... | collective-permute-start | bytes 446216 | tf_op jit(solution)/shard_map/ppermute | solution.py:72
  56.1 13.6 %collective-permute-start.3 = (bf16[4,2,14,608]{3,1,2,0:T(2,128)(2,1)S(1)}, bf16[4,2,14,608]{3,1,2,0:T(2,128)(2,1)}, u32[]{:S(2)}, u32[]{:S(2)}) collective-permute-start(bf16[4,2,14,608]{3,1,2,0:T(2,128)(2,1)S(1)} %copy_dynamic-update-slice_fusion), channel_id=1, source_target_pairs={{0,64},{1,449},{2,66},{3,451},{4,68},{5,453},{6,70},{7,455},{8,72}... | collective-permute-start | bytes 408584 | tf_op jit(solution)/shard_map/ppermute | solution.py:102
  63.8 10.8 %collective-permute-start.4 = (bf16[4,2,14,608]{3,1,2,0:T(2,128)(2,1)S(1)}, bf16[4,2,14,608]{3,1,2,0:T(2,128)(2,1)}, u32[]{:S(2)}, u32[]{:S(2)}) collective-permute-start(bf16[4,2,14,608]{3,1,2,0:T(2,128)(2,1)S(1)} %copy_dynamic-update-slice_fusion), channel_id=1, source_target_pairs={{0,448},{1,65},{2,450},{3,67},{4,452},{5,69},{6,454},{7,71},{8,456... | collective-permute-start | bytes 408584 | tf_op jit(solution)/shard_map/ppermute | solution.py:108
  69.8 11.7 %collective-permute-start.5 = (bf16[4,2,14,608]{3,1,2,0:T(2,128)(2,1)}, bf16[4,2,14,608]{3,1,2,0:T(2,128)(2,1)S(1)}, u32[]{:S(2)}, u32[]{:S(2)}) collective-permute-start(bf16[4,2,14,608]{3,1,2,0:T(2,128)(2,1)} %collective-permute-done.3), channel_id=1, source_target_pairs={{0,64},{1,449},{2,66},{3,451},{4,68},{5,453},{6,70},{7,455},{8,72}... | collective-permute-start | bytes 408584 | tf_op jit(solution)/shard_map/ppermute | solution.py:102
  74.6 11.7 %collective-permute-start.6 = (bf16[4,2,14,608]{3,1,2,0:T(2,128)(2,1)}, bf16[4,2,14,608]{3,1,2,0:T(2,128)(2,1)S(1)}, u32[]{:S(2)}, u32[]{:S(2)}) collective-permute-start(bf16[4,2,14,608]{3,1,2,0:T(2,128)(2,1)} %collective-permute-done.4), channel_id=1, source_target_pairs={{0,448},{1,65},{2,450},{3,67},{4,452},{5,69},{6,454},{7,71},{8,456... | collective-permute-start | bytes 408584 | tf_op jit(solution)/shard_map/ppermute | solution.py:108
  81.5 12.0 %collective-permute-start.7 = (bf16[4,2,14,608]{3,1,2,0:T(2,128)(2,1)S(1)}, bf16[4,2,14,608]{3,1,2,0:T(2,128)(2,1)S(1)}, u32[]{:S(2)}, u32[]{:S(2)}) collective-permute-start(bf16[4,2,14,608]{3,1,2,0:T(2,128)(2,1)S(1)} %collective-permute-done.5), channel_id=1, source_target_pairs={{0,64},{1,449},{2,66},{3,451},{4,68},{5,453},{6,70},{7,455},{8,72}... | collective-permute-start | bytes 408584 | tf_op jit(solution)/shard_map/ppermute | solution.py:102
  86.3 11.0 %collective-permute-start.8 = (bf16[4,2,14,608]{3,1,2,0:T(2,128)(2,1)S(1)}, bf16[4,2,14,608]{3,1,2,0:T(2,128)(2,1)S(1)}, u32[]{:S(2)}, u32[]{:S(2)}) collective-permute-start(bf16[4,2,14,608]{3,1,2,0:T(2,128)(2,1)S(1)} %collective-permute-done.6), channel_id=1, source_target_pairs={{0,448},{1,65},{2,450},{3,67},{4,452},{5,69},{6,454},{7,71},{8,456... | collective-permute-start | bytes 408584 | tf_op jit(solution)/shard_map/ppermute | solution.py:108
  94.3 14.3 %copy-start.1 = (f32[150,896]{1,0:T(8,128)S(1)}, f32[150,896]{1,0:T(8,128)}, u32[]{:S(2)}) copy-start(f32[150,896]{1,0:T(8,128)} %param.12) | copy-start | bytes 1612804
  94.3 14.3 %copy-start.2 = (f32[150,896]{1,0:T(8,128)S(1)}, f32[150,896]{1,0:T(8,128)}, u32[]{:S(2)}) copy-start(f32[150,896]{1,0:T(8,128)} %param.13) | copy-start | bytes 1612804
  100.1 20.2 %collective-permute-start.10 = (bf16[4,4,2,14,608]{4,2,3,1,0:T(2,128)(2,1)S(1)}, bf16[4,4,2,14,608]{4,2,3,1,0:T(2,128)(2,1)S(1)}, u32[]{:S(2)}, u32[]{:S(2)}) collective-permute-start(bf16[4,4,2,14,608]{4,2,3,1,0:T(2,128)(2,1)S(1)} %get-tuple-element.15), channel_id=1, source_target_pairs={{0,480},{1,33},{2,482},{3,35},{4,484},{5,37},{6,486},{7,39},{8,488... | collective-permute-start | bytes 1634312 | tf_op jit(solution)/shard_map/ppermute | solution.py:117
  106.6 9.7 %collective-permute-start.9 = (bf16[4,2,14,608]{3,1,2,0:T(2,128)(2,1)S(1)}, bf16[4,2,14,608]{3,1,2,0:T(2,128)(2,1)S(1)}, u32[]{:S(2)}, u32[]{:S(2)}) collective-permute-start(bf16[4,2,14,608]{3,1,2,0:T(2,128)(2,1)S(1)} %collective-permute-done.7), channel_id=1, source_target_pairs={{0,64},{1,449},{2,66},{3,451},{4,68},{5,453},{6,70},{7,455},{8,72}... | collective-permute-start | bytes 408584 | tf_op jit(solution)/shard_map/ppermute | solution.py:102
  109.9 12.8 %collective-permute-start.11 = (bf16[4,4,2,14,608]{4,2,3,1,0:T(2,128)(2,1)S(1)}, bf16[4,4,2,14,608]{4,2,3,1,0:T(2,128)(2,1)S(1)}, u32[]{:S(2)}, u32[]{:S(2)}) collective-permute-start(bf16[4,4,2,14,608]{4,2,3,1,0:T(2,128)(2,1)S(1)} %get-tuple-element.14), channel_id=1, source_target_pairs={{0,32},{1,481},{2,34},{3,483},{4,36},{5,485},{6,38},{7,487},{8,40}... | collective-permute-start | bytes 1634312 | tf_op jit(solution)/shard_map/ppermute | solution.py:117
